TPU v7x, 32 devices: a whole 2x2x4 slice. The times are simulated.
32 devices in a mesh: ctx: 16 (over z, y, x), head: 2 (over core).
Axes of the slice: x: 2, y: 2, z: 4, core: 2. Of those that a mesh axis runs over, the one named last changes fastest.
Arguments:
- queries: bfloat16 [4096, 4096], P('ctx', 'head')
- keys: bfloat16 [4096, 1024], P('ctx', 'head')
- values: bfloat16 [4096, 1024], P('ctx', 'head'), may hold values from -6 to 6
- positions: int32 [4096], P('ctx'), may hold values from 0 to 6143, as said below
- retrieval: int32 [4], replicated, may hold values from 0 to 7, as said below
- yarn_scale: int32 [1], replicated, may hold values from 2 to 8
- out_weight: bfloat16 [4096, 4096], P('head', 'ctx'), may hold values from -0.125 to 0.125
Outputs:
- layer_out: bfloat16 [4096, 4096], P('ctx', 'head')
Inputs may be any that keep to these rules, and one draw needn't show every extreme that they name: positions start at 0 and rise by 1 or 2 from one token to the next, by 2 at exactly 2048 of the steps. `retrieval`: 4 different KV-head indices.
All inputs are finite; a program needn't handle non-finite values.
Results may differ from a plain program's by a relative error of at most 0.014.
The roundings to bfloat16 on the way count: a program that leaves them out, or rounds other values in their place, can miss the bound.
Values may be sent and summed in bfloat16 or wider, within the bound.
No kernel may reach another device: no remote copies, remote signals or barrier semaphores. Data moves between devices by JAX's collectives and lax.ppermute only.
A program may use at most 128 MiB of HBM per device.

v0:
```python
from functools import partial
import math

import jax
import jax.numpy as jnp
from jax import lax
from jax.sharding import PartitionSpec as P

HEAD_SIZE = 128
SINK = 64
WINDOW = 256
ORIG_CTX = 8192
QUERY_PER_KEY = 4


rope_base = 500000.0
neg_big = -1e30


def yarn_tables(positions, yarn_scale):
    half_size = HEAD_SIZE // 2
    factor = yarn_scale[0].astype(jnp.float32)
    freq_index = jnp.arange(half_size, dtype=jnp.float32)
    base_freq = jnp.power(jnp.float32(rope_base), -2.0 * freq_index / HEAD_SIZE)
    wave_ratio = ORIG_CTX * base_freq / (2.0 * math.pi)
    ramp_weight = jnp.clip((wave_ratio - 1.0) / 31.0, 0.0, 1.0)
    yarn_freq = base_freq * ramp_weight + base_freq / factor * (1.0 - ramp_weight)
    angles = positions.astype(jnp.float32)[:, None] * yarn_freq[None, :]
    mscale = 0.1 * jnp.log(factor) + 1.0
    return (jnp.cos(angles) * mscale, jnp.sin(angles) * mscale)


def apply_rotary(x, cosine_lookup, sine_lookup, head_count):
    row_count = x.shape[0]
    shaped = x.astype(jnp.float32).reshape(row_count, head_count, HEAD_SIZE)
    lower_half = shaped[..., : HEAD_SIZE // 2]
    upper_half = shaped[..., HEAD_SIZE // 2 :]
    cosine = cosine_lookup[:, None, :]
    sine_part = sine_lookup[:, None, :]
    rotated = jnp.concatenate(
        [
            lower_half * cosine - upper_half * sine_part,
            upper_half * cosine + lower_half * sine_part,
        ],
        axis=-1,
    )
    return rotated.reshape(row_count, head_count * HEAD_SIZE).astype(jnp.bfloat16)


def update(query_rows, key_block, value_block, visible, partial_state):
    row_max, totals, accum = partial_state
    scores = jnp.einsum(
        "rhgd,khd->hgrk", query_rows, key_block, preferred_element_type=jnp.float32
    ) * (1.0 / math.sqrt(HEAD_SIZE))
    mask_full = visible[:, None]
    scores = jnp.where(mask_full, scores, neg_big)
    new_max = jnp.maximum(row_max, jnp.max(scores, axis=-1))
    weights = jnp.where(mask_full, jnp.exp(scores - new_max[..., None]), 0.0)
    rescale = jnp.exp(row_max - new_max)
    totals = totals * rescale + jnp.sum(weights, axis=-1)
    accum = accum * rescale[..., None] + jnp.einsum(
        "hgrk,khd->hgrd",
        weights.astype(jnp.bfloat16),
        value_block,
        preferred_element_type=jnp.float32,
    )
    return (new_max, totals, accum)


def attend(query_sets, rotated_key, values, flags, kv_local):
    shaped_sets = []
    initial = []
    for query_rows, query_index in query_sets:
        row_count = query_rows.shape[0]
        shaped_sets.append(
            (query_rows.reshape(row_count, kv_local, QUERY_PER_KEY, HEAD_SIZE), query_index)
        )
        initial.append(
            (
                jnp.full((kv_local, QUERY_PER_KEY, row_count), neg_big, jnp.float32),
                jnp.zeros((kv_local, QUERY_PER_KEY, row_count), jnp.float32),
                jnp.zeros((kv_local, QUERY_PER_KEY, row_count, HEAD_SIZE), jnp.float32),
            )
        )
    initial = tuple(initial)
    key_shard = lax.all_gather(rotated_key, "ctx", axis=0, tiled=True)
    value_shard = lax.all_gather(values, "ctx", axis=0, tiled=True)
    shard_rows = key_shard.shape[0]
    sub_rows = math.gcd(shard_rows, 512)
    turn_count = shard_rows // sub_rows

    def one_turn(j, inner_states):
        key_block = lax.dynamic_slice_in_dim(key_shard, j * sub_rows, sub_rows, 0).reshape(
            sub_rows, kv_local, HEAD_SIZE
        )
        value_block = lax.dynamic_slice_in_dim(value_shard, j * sub_rows, sub_rows, 0).reshape(
            sub_rows, kv_local, HEAD_SIZE
        )
        key_index = j * sub_rows + jnp.arange(sub_rows, dtype=jnp.int32)
        updated = []
        for (query_rows, query_index), partial_state in zip(shaped_sets, inner_states):
            causal = key_index[None, :] <= query_index[:, None]
            nearby = (key_index[None, :] < SINK) | (
                key_index[None, :] > query_index[:, None] - WINDOW
            )
            visible = causal[None] & (flags[:, None, None] | nearby[None])
            updated.append(
                lax.cond(
                    jnp.any(visible),
                    partial(update, query_rows, key_block, value_block, visible),
                    lambda keep_state: keep_state,
                    partial_state,
                )
            )
        return tuple(updated)

    final = lax.fori_loop(0, turn_count, one_turn, initial)
    results = []
    for (query_rows, query_index), (row_max, totals, accum) in zip(shaped_sets, final):
        output = accum / totals[..., None]
        results.append(
            output.transpose(2, 0, 1, 3)
            .reshape(query_rows.shape[0], kv_local * QUERY_PER_KEY * HEAD_SIZE)
            .astype(jnp.bfloat16)
        )
    return results


def shards(queries, keys, values, positions, retrieval, yarn_scale, out_weight):
    rows_dev = queries.shape[0]
    kv_local = keys.shape[1] // HEAD_SIZE
    cosine_lookup, sine_lookup = yarn_tables(positions, yarn_scale)
    rotated_query = apply_rotary(queries, cosine_lookup, sine_lookup, kv_local * QUERY_PER_KEY)
    rotated_key = apply_rotary(keys, cosine_lookup, sine_lookup, kv_local)
    ctx_index = lax.axis_index("ctx")
    head_ids = lax.axis_index("head") * kv_local + jnp.arange(kv_local, dtype=jnp.int32)
    flags = jnp.any(head_ids[:, None] == retrieval[None, :], axis=1)
    own_index = ctx_index * rows_dev + jnp.arange(rows_dev, dtype=jnp.int32)
    attended = attend(((rotated_query, own_index),), rotated_key, values, flags, kv_local)[0]
    partials = jnp.dot(
        attended,
        lax.all_gather(out_weight, "ctx", axis=1, tiled=True),
        preferred_element_type=jnp.float32,
    )
    return lax.psum_scatter(partials.astype(jnp.bfloat16), "head", scatter_dimension=1, tiled=True)


def solution(mesh):
    return jax.shard_map(
        shards,
        mesh=mesh,
        in_specs=(
            P("ctx", "head"),
            P("ctx", "head"),
            P("ctx", "head"),
            P("ctx"),
            P(),
            P(),
            P("head", "ctx"),
        ),
        out_specs=P("ctx", "head"),
        check_vma=False,
    )
```

profile of v0, /device:TPU:0, one launch (start us, length us, event | category | flops | bytes accessed | tf_op | source)
XLA Modules:
  0.0 449.2 jit_solution(7395130143101550300)
XLA Ops:
  7.3 1.1 copy.51
  8.4 0.8 convert_element_type.48
  9.2 0.3 fusion.13
  9.5 0.1 subtract_convert_fusion.1
  9.6 0.7 pad_maximum_fusion.1
  10.3 0.0 all-gather.6.cloned.1.call-start
  10.4 0.8 copy.42
  11.3 0.7 all-gather.8.cloned.1.call-update
  12.0 0.1 copy.41
  12.1 0.1 copy.39
  12.2 0.2 convert_bitcast_fusion
  12.5 0.4 copy.54
  12.9 0.2 copy-done.4
  13.1 0.2 compare_reduce_fusion
  13.3 0.7 fusion.17
  14.0 1.4 subtract_convert_fusion
  15.4 0.6 pad_maximum_fusion
  16.0 84.0 %all-gather.4.cloned.1.call-done = bf16[4096,512]{0,1:T(8,128)(2,1)} async-done(((bf16[256,512]{0,1:T(8,128)(2,1)}), bf16[4096,512]{0,1:T(8,128)(2,1)}) %all-gather.4.cloned.1.call-update) | async-done | bytes 4194320 | tf_op jit(solution)/shard_map/all_gather | solution.py:86
  100.0 87.7 %all-gather.6.cloned.1.call-done = bf16[4096,512]{0,1:T(8,128)(2,1)} async-done(((bf16[256,512]{0,1:T(8,128)(2,1)}), bf16[4096,512]{0,1:T(8,128)(2,1)}) %all-gather.6.cloned.1.call-update) | async-done | bytes 4194320 | tf_op jit(solution)/shard_map/all_gather | solution.py:87
  187.7 1.6 broadcast_in_dim.68
  189.3 29.0 %while.20 = (s32[]{:T(128)}, f32[4,4,256]{2,1,0:T(4,128)S(1)}, f32[4,4,256]{2,1,0:T(4,128)S(1)}, f32[4,4,256,128]{3,2,1,0:T(8,128)}, pred[4]{0:T(512)(128)(4,1)S...) while((s32[]{:T(128)}, f32[4,4,256]{2,1,0:T(4,128)S(1)}, ...), condition=%wide.region_7.8_spmd.clone, body=%wide.region_1.7_spmd.clone.sunk | while | flops 1104029696 | bytes 53224808 | solution.py:117
  189.3 0.2 broadcast_compare_fusion.5
  189.5 1.4 fusion.24
  191.5 10.4 %conditional.3 = ((f32[4,4,256]{2,1,0:T(4,128)S(1)}, f32[4,4,256]{2,1,0:T(4,128)S(1)}, f32[4,4,256,128]{3,2,1,0:T(8,128)})) conditional(s32[]{:T(128)} %convert_element_type.65, (f32[4,4,256]{2,1,0:T(4,128)S(1)}, f32[4,4,256]{2,1,0:T(4,128)S(1)}, f32[4,4,256,128]{3,2,1,0:T(8,128)}) %tuple.78, (pred[4,256,512]{1,2,0:T(8,128)(4,1)S(1)}, s32[]{:T(128)}, ...), branch_computations={%region_3.3_spmd, %region_4.6_spmd} | conditional | flops 1102061568 | bytes 52166780 | solution.py:108
  191.6 1.3 constant_dynamic-slice_fusion
  192.8 1.9 fusion.2
  194.8 2.1 fusion.4
  196.9 3.6 multiply_add_fusion
  200.6 1.4 copy-done.1
  201.9 0.2 broadcast_compare_fusion.5
  202.2 1.4 fusion.24
  204.3 0.2 broadcast_compare_fusion.5
  204.5 1.4 fusion.24
  206.6 0.2 broadcast_compare_fusion.5
  206.9 1.4 fusion.24
  209.0 0.2 broadcast_compare_fusion.5
  209.2 1.4 fusion.24
  211.3 0.2 broadcast_compare_fusion.5
  211.5 1.4 fusion.24
  213.6 0.2 broadcast_compare_fusion.5
  213.9 1.4 fusion.24
  216.0 0.2 broadcast_compare_fusion.5
  216.2 1.4 fusion.24
  218.3 1.9 copy.43
  220.2 0.2 divide_convert_fusion
  220.4 202.8 %all-gather.8.cloned.1.call-done = bf16[2048,4096]{1,0:T(8,128)(2,1)} async-done(((bf16[2048,256]{1,0:T(8,128)(2,1)}), bf16[2048,4096]{1,0:T(8,128)(2,1)}) %all-gather.8.cloned.1.call-update) | async-done | bytes 16777232 | tf_op jit(solution)/shard_map/all_gather | solution.py:142
  423.2 11.5 %convolution_convert_fusion = bf16[256,4096]{1,0:T(8,128)(2,1)} fusion(bf16[256,2048]{0,1:T(8,128)(2,1)S(1)} %bitcast.49, bf16[2048,4096]{1,0:T(8,128)(2,1)} %all-gather.8.cloned.1.call-done), kind=kOutput, calls=%fused_computation.23 | convolution fusion | flops 4296015872 | bytes 19922944 | tf_op jit(solution)/shard_map/dot_general | solution.py:140
  434.7 8.0 %reduce-scatter.2.cloned.1.call-done = bf16[256,2048]{1,0:T(8,128)(2,1)} async-done(((bf16[256,4096]{1,0:T(8,128)(2,1)}), bf16[256,2048]{1,0:T(8,128)(2,1)}) %reduce-scatter.2.cloned.1.call-update) | async-done | bytes 1048592 | tf_op jit(solution)/shard_map/reduce_scatter | solution.py:145
  (52 shorter events, 0.4 us)
Async XLA Ops:
  6.5 3.8 copy-start.3
  6.5 93.4 %all-gather.4.cloned.1.call-start = ((), (), s32[]{:S(2)}) async-start(), calls=%async_computation.1 | async-start | bytes 4456448 | tf_op jit(solution)/shard_map/all_gather | solution.py:86
  8.4 3.8 copy-start.2
  10.3 177.4 %all-gather.6.cloned.1.call-start = ((), (), s32[]{:S(2)}) async-start(), calls=%async_computation.2 | async-start | bytes 4456448 | tf_op jit(solution)/shard_map/all_gather | solution.py:87
  11.2 411.9 %all-gather.8.cloned.1.call-start = ((), (), s32[]{:S(2)}) async-start(), calls=%async_computation.3 | async-start | bytes 17825792 | tf_op jit(solution)/shard_map/all_gather | solution.py:142
  12.0 430.7 %reduce-scatter.2.cloned.1.call-start = ((), (), s32[]{:S(2)}) async-start(), calls=%async_computation.4 | async-start | bytes 3145728 | tf_op jit(solution)/shard_map/reduce_scatter | solution.py:145
  12.5 0.7 copy-start.4
  194.7 2.2 copy-start
  200.6 1.4 copy-start.1
Sparse Core Ops, SparseCore 0:
  10.4 89.4 all-gather.3
  102.7 84.9 all-gather.5
  190.4 232.7 all-gather.7
  434.8 7.8 reduce-scatter.1
where the time goes:
time: 450 us; the launch traced here: 449 us
  waiting for transfers between devices  383 us (85%)
  other arithmetic  19.6 us (4%)
  matrix products  17 us (4%)
  between operations  14 us (3%)
  local copies, waits for them, and re-layouts  9.6 us (2%)
  loops' own time  5.67 us (1%)
    all_gather x1, waiting for transfers between devices, shards(): lax.all_gather(out_weight, 'ctx', axis=1, tiled=True)  203 us
    all_gather x1, waiting for transfers between devices, attend(): value_shard = lax.all_gather(values, 'ctx', axis=0, tiled=True)  87.7 us
    all_gather x1, waiting for transfers between devices, attend(): key_shard = lax.all_gather(rotated_key, 'ctx', axis=0, tiled=True)  84 us
    dot_general x1, matrix products, shards(): jnp.dot(attended, lax.all_gather(out_weight, 'ctx', axis=1, tiled=True),...  11.5 us
    reduce_or x8, other arithmetic, one_turn(): jnp.any(visible)  11.1 us
  transfers between devices with their start and end apart: 4, of which 4 were waited for; matrix products, arithmetic and copies ran while one was open for 7% of the time, Pallas kernels for 0%

commit v1 on v0

--- a/solution.py
+++ b/solution.py
@@ -4,7 +4,7 @@
 import jax
 import jax.numpy as jnp
 from jax import lax
-from jax.sharding import PartitionSpec as P
+from jax.sharding import Mesh, PartitionSpec as P
 
 HEAD_SIZE = 128
 SINK = 64
@@ -83,8 +83,12 @@
             )
         )
     initial = tuple(initial)
-    key_shard = lax.all_gather(rotated_key, "ctx", axis=0, tiled=True)
-    value_shard = lax.all_gather(values, "ctx", axis=0, tiled=True)
+    kv_width = rotated_key.shape[1]
+    kv_shard = lax.all_gather(
+        jnp.concatenate([rotated_key, values], axis=1), CTX, axis=0, tiled=True
+    )
+    key_shard = kv_shard[:, :kv_width]
+    value_shard = kv_shard[:, kv_width:]
     shard_rows = key_shard.shape[0]
     sub_rows = math.gcd(shard_rows, 512)
     turn_count = shard_rows // sub_rows
@@ -126,38 +130,68 @@
     return results
 
 
+CTX = ("cz", "cb")
+
+
+def project(attended, w_local, head_count):
+    rows = attended.shape[0]
+    col_width = w_local.shape[1]
+    plane = lax.psum(1, "cb")
+    line = lax.psum(1, "cz")
+    a_plane = lax.all_gather(attended, "cb", axis=0, tiled=True)
+    w_line = lax.all_gather(w_local, "cz", axis=1, tiled=True)
+    part = jnp.dot(a_plane, w_line, preferred_element_type=jnp.float32)
+    reduced = lax.psum_scatter(part, "head", scatter_dimension=1, tiled=True).astype(jnp.bfloat16)
+    per_head = line // head_count
+    pieces = reduced.reshape(plane, rows, per_head * col_width)
+    got = lax.all_to_all(pieces, "cb", 0, 0, tiled=False)
+    return (
+        got.reshape(plane, rows, per_head, col_width)
+        .transpose(1, 2, 0, 3)
+        .reshape(rows, per_head * plane * col_width)
+    )
+
+
 def shards(queries, keys, values, positions, retrieval, yarn_scale, out_weight):
     rows_dev = queries.shape[0]
     kv_local = keys.shape[1] // HEAD_SIZE
     cosine_lookup, sine_lookup = yarn_tables(positions, yarn_scale)
     rotated_query = apply_rotary(queries, cosine_lookup, sine_lookup, kv_local * QUERY_PER_KEY)
     rotated_key = apply_rotary(keys, cosine_lookup, sine_lookup, kv_local)
-    ctx_index = lax.axis_index("ctx")
+    ctx_index = lax.axis_index("cz") * lax.psum(1, "cb") + lax.axis_index("cb")
     head_ids = lax.axis_index("head") * kv_local + jnp.arange(kv_local, dtype=jnp.int32)
     flags = jnp.any(head_ids[:, None] == retrieval[None, :], axis=1)
     own_index = ctx_index * rows_dev + jnp.arange(rows_dev, dtype=jnp.int32)
     attended = attend(((rotated_query, own_index),), rotated_key, values, flags, kv_local)[0]
-    partials = jnp.dot(
-        attended,
-        lax.all_gather(out_weight, "ctx", axis=1, tiled=True),
-        preferred_element_type=jnp.float32,
-    )
-    return lax.psum_scatter(partials.astype(jnp.bfloat16), "head", scatter_dimension=1, tiled=True)
+    return project(attended, out_weight, lax.psum(1, "head"))
+
+
+def grid_of(ctx_count, head_count):
+    best = None
+    for plane in range(1, ctx_count + 1):
+        line = ctx_count // plane
+        if ctx_count % plane == 0 and line % head_count == 0 and plane <= line:
+            best = (line, plane)
+    return best
 
 
 def solution(mesh):
+    ctx_count = mesh.shape["ctx"]
+    head_count = mesh.shape["head"]
+    line, plane = grid_of(ctx_count, head_count)
+    grid = Mesh(mesh.devices.reshape(line, plane, head_count), ("cz", "cb", "head"))
     return jax.shard_map(
         shards,
-        mesh=mesh,
+        mesh=grid,
         in_specs=(
-            P("ctx", "head"),
-            P("ctx", "head"),
-            P("ctx", "head"),
-            P("ctx"),
+            P(CTX, "head"),
+            P(CTX, "head"),
+            P(CTX, "head"),
+            P(CTX),
             P(),
             P(),
-            P("head", "ctx"),
+            P("head", CTX),
         ),
-        out_specs=P("ctx", "head"),
+        out_specs=P(CTX, "head"),
         check_vma=False,
     )

time: 450 us -> 365 us (0.81)
  waiting for transfers between devices: 383 us -> 265 us
  blocking collectives: 0 us -> 18.3 us
  local copies, waits for them, and re-layouts: 9.6 us -> 20.1 us
  other arithmetic: 19.6 us -> 24.4 us
    all_gather x3, waiting for transfers between devices: 374 us -> 253 us  [the longest x1 130 us: attend(): lax.all_gather(jnp.concatenate([rotated_key, values], axis=1), CTX, axis=...]
    all_to_all x0 -> x1, blocking collectives: none -> 18.3 us  [project(): got = lax.all_to_all(pieces, 'cb', 0, 0, tiled=False)]
    slice x0 -> x1, local copies, waits for them, and re-layouts: none -> 6.04 us  [attend(): value_shard = kv_shard[:, kv_width:]]
  transfers between devices with their start and end apart: 4 -> 4, of which waited for: 4 -> 4; matrix products, arithmetic and copies ran while one was open for 7% -> 11% of each run, Pallas kernels for 0% -> 0%
where the time goes in v1:
time: 365 us; the launch traced here: 364 us
  waiting for transfers between devices  265 us (73%)
  other arithmetic  24.4 us (7%)
  local copies, waits for them, and re-layouts  20.1 us (6%)
  blocking collectives  18.3 us (5%)
  matrix products  15.5 us (4%)
  between operations  14.1 us (4%)
  loops' own time  6.11 us (2%)
    all_gather x1, waiting for transfers between devices, attend(): lax.all_gather(jnp.concatenate([rotated_key, values], axis=1), CTX, axis=...  130 us
    all_gather x1, waiting for transfers between devices, project(): a_plane = lax.all_gather(attended, 'cb', axis=0, tiled=True)  83.2 us
    all_gather x1, waiting for transfers between devices, project(): w_line = lax.all_gather(w_local, 'cz', axis=1, tiled=True)  39.4 us
    all_to_all x1, blocking collectives, project(): got = lax.all_to_all(pieces, 'cb', 0, 0, tiled=False)  18.3 us
    reduce_scatter x1, waiting for transfers between devices, project(): lax.psum_scatter(part, 'head', scatter_dimension=1, tiled=True)  12 us
    reduce_or x8, other arithmetic, one_turn(): jnp.any(visible)  11.5 us
    dot_general x1, matrix products, project(): part = jnp.dot(a_plane, w_line, preferred_element_type=jnp.float32)  10 us
  transfers between devices with their start and end apart: 4, of which 4 were waited for; matrix products, arithmetic and copies ran while one was open for 11% of the time, Pallas kernels for 0%

profile of v1, /device:TPU:0, one launch (start us, length us, event | category | flops | bytes accessed | tf_op | source)
XLA Modules:
  0.0 364.2 jit_solution(13397331591921731845)
XLA Ops:
  7.3 1.1 copy.29
  8.4 1.1 copy.43
  9.5 0.7 convert_element_type.48
  10.2 0.3 fusion.13
  10.6 0.8 pad_maximum_fusion.1
  11.5 0.7 all-gather.8.cloned.1.call-update
  12.5 0.2 convert_bitcast_fusion
  12.8 0.4 copy.46
  13.2 2.0 fusion.18
  15.4 2.9 subtract_convert_fusion
  18.3 0.6 pad_maximum_fusion
  18.9 129.9 %all-gather.4.cloned.1.call-done = bf16[4096,1024]{0,1:T(8,128)(2,1)} async-done(((bf16[256,1024]{0,1:T(8,128)(2,1)}), bf16[4096,1024]{0,1:T(8,128)(2,1)}) %all-gather.4.cloned.1.call-update) | async-done | bytes 8388624 | tf_op jit(solution)/shard_map/all_gather | solution.py:87
  148.8 6.0 %fusion.17 = (bf16[4096,512]{0,1:T(8,128)(2,1)}, bf16[4096,512]{0,1:T(8,128)(2,1)}) fusion(bf16[4096,1024]{0,1:T(8,128)(2,1)} %all-gather.4.cloned.1.call-done), kind=kLoop, calls=%fused_computation.42 | loop fusion | bytes 16777216 | tf_op jit(solution)/shard_map/slice | solution.py:91
  154.9 1.6 broadcast_in_dim.68
  156.4 29.9 %while.20 = (s32[]{:T(128)}, f32[4,4,256]{2,1,0:T(4,128)S(1)}, f32[4,4,256]{2,1,0:T(4,128)S(1)}, f32[4,4,256,128]{3,2,1,0:T(8,128)}, pred[4]{0:T(512)(128)(4,1)S...) while((s32[]{:T(128)}, f32[4,4,256]{2,1,0:T(4,128)S(1)}, ...), condition=%wide.region_7.8_spmd.clone, body=%wide.region_1.7_spmd.clone.sunk | while | flops 1104029696 | bytes 53224808 | solution.py:121
  156.5 0.2 broadcast_compare_fusion.5
  156.7 1.4 fusion.26
  158.8 10.4 %conditional.3 = ((f32[4,4,256]{2,1,0:T(4,128)S(1)}, f32[4,4,256]{2,1,0:T(4,128)S(1)}, f32[4,4,256,128]{3,2,1,0:T(8,128)})) conditional(s32[]{:T(128)} %convert_element_type.64, (f32[4,4,256]{2,1,0:T(4,128)S(1)}, f32[4,4,256]{2,1,0:T(4,128)S(1)}, f32[4,4,256,128]{3,2,1,0:T(8,128)}) %tuple.79, (pred[4,256,512]{1,2,0:T(8,128)(4,1)S(1)}, s32[]{:T(128)}, ...), branch_computations={%region_3.3_spmd, %region_4.6_spmd} | conditional | flops 1102061568 | bytes 52166780 | solution.py:112
  158.9 1.3 constant_dynamic-slice_fusion
  160.2 1.9 fusion.2
  162.1 2.1 fusion.4
  164.2 3.6 multiply_add_fusion
  167.9 1.3 copy-done.1
  169.2 0.2 broadcast_compare_fusion.5
  169.5 1.4 fusion.26
  171.7 0.2 broadcast_compare_fusion.5
  171.9 1.4 fusion.26
  174.1 0.2 broadcast_compare_fusion.5
  174.4 1.4 fusion.26
  176.6 0.2 broadcast_compare_fusion.5
  176.8 1.4 fusion.26
  179.0 0.2 broadcast_compare_fusion.5
  179.3 1.4 fusion.26
  181.5 0.2 broadcast_compare_fusion.5
  181.7 1.4 fusion.26
  183.9 0.2 broadcast_compare_fusion.5
  184.2 1.4 fusion.26
  186.3 1.9 copy.34
  188.3 1.2 divide_convert_fusion
  189.7 39.4 %all-gather.8.cloned.1.call-done = bf16[2048,1024]{1,0:T(8,128)(2,1)} async-done(((bf16[2048,256]{1,0:T(8,128)(2,1)}), bf16[2048,1024]{1,0:T(8,128)(2,1)}) %all-gather.8.cloned.1.call-update) | async-done | bytes 4194320 | tf_op jit(solution)/shard_map/all_gather | solution.py:142
  229.2 83.2 %all-gather.6.cloned.1.call-done = bf16[1024,2048]{0,1:T(8,128)(2,1)} async-done(((bf16[256,2048]{0,1:T(8,128)(2,1)}), bf16[1024,2048]{0,1:T(8,128)(2,1)}) %all-gather.6.cloned.1.call-update) | async-done | bytes 4194320 | tf_op jit(solution)/shard_map/all_gather | solution.py:141
  312.4 10.0 %fusion.19 = f32[1024,1024]{1,0:T(8,128)} fusion(bf16[1024,2048]{0,1:T(8,128)(2,1)} %all-gather.6.cloned.1.call-done, bf16[2048,1024]{1,0:T(8,128)(2,1)} %all-gather.8.cloned.1.call-done), kind=kOutput, calls=%fused_computation.44 | convolution fusion | flops 4294967296 | bytes 12582912 | tf_op jit(solution)/shard_map/dot_general | solution.py:143
  322.4 12.0 %reduce-scatter.2.cloned.1.call-done = f32[1024,512]{1,0:T(8,128)} async-done(((f32[1024,1024]{1,0:T(8,128)}), f32[1024,512]{1,0:T(8,128)}) %reduce-scatter.2.cloned.1.call-update) | async-done | bytes 2097168 | tf_op jit(solution)/shard_map/reduce_scatter | solution.py:144
  334.4 1.7 convert_element_type.56
  336.2 18.3 %all_to_all.5 = bf16[4,256,512]{2,1,0:T(8,128)(2,1)S(1)} all-to-all(bf16[4,256,512]{2,1,0:T(8,128)(2,1)S(1)} %bitcast.54), channel_id=1, replica_groups=mesh['cz'=4,'cb'=4,'head'=2] {'cb'}, dimensions={0} | all-to-all | bytes 2097152 | tf_op jit(solution)/shard_map/all_to_all | solution.py:147
  354.4 0.3 reshape.225
  354.7 1.4 copy.52
  356.1 1.6 reshape.226
  (57 shorter events, 1.1 us)
Async XLA Ops:
  6.5 6.0 %copy-start.2 = (bf16[256,2048]{1,0:T(8,128)(2,1)S(1)}, bf16[256,2048]{1,0:T(8,128)(2,1)}, u32[]{:S(2)}) copy-start(bf16[256,2048]{1,0:T(8,128)(2,1)} %param.11) | copy-start | bytes 3145732
  6.5 142.3 %all-gather.4.cloned.1.call-start = ((), (), s32[]{:S(2)}) async-start(), calls=%async_computation.2 | async-start | bytes 8912896 | tf_op jit(solution)/shard_map/all_gather | solution.py:87
  11.5 217.7 %all-gather.8.cloned.1.call-start = ((), (), s32[]{:S(2)}) async-start(), calls=%async_computation.4 | async-start | bytes 5242880 | tf_op jit(solution)/shard_map/all_gather | solution.py:142
  12.2 300.1 %all-gather.6.cloned.1.call-start = ((), (), s32[]{:S(2)}) async-start(), calls=%async_computation.3 | async-start | bytes 5242880 | tf_op jit(solution)/shard_map/all_gather | solution.py:141
  13.1 2.0 copy-start.3
  162.1 2.2 copy-start
  167.9 1.3 copy-start.1
  189.5 144.9 %reduce-scatter.2.cloned.1.call-start = ((), (), s32[]{:S(2)}) async-start(), calls=%async_computation.5 | async-start | bytes 6291456 | tf_op jit(solution)/shard_map/reduce_scatter | solution.py:144
Sparse Core Ops, SparseCore 0:
  11.6 137.1 all-gather.3
  150.4 78.7 all-gather.7
  231.0 81.3 all-gather.5
  322.5 11.8 reduce-scatter.1

commit v2 on v1

--- a/solution.py
+++ b/solution.py
@@ -133,6 +133,99 @@
 CTX = ("cz", "cb")
 
 
+def head_exchange(x, head_count):
+    if head_count == 2:
+        other = lax.ppermute(x, "head", [(0, 1), (1, 0)])
+        first = lax.axis_index("head") == 0
+        return jnp.stack([jnp.where(first, x, other), jnp.where(first, other, x)])
+    return lax.all_gather(x, "head", axis=0, tiled=False)
+
+
+def duo_attend(rotated_query, rotated_key, values, retrieval, kv_local, head_count, ctx_index):
+    rows = rotated_query.shape[0]
+    ctx_count = lax.psum(1, CTX)
+    kv_total = kv_local * head_count
+    ret_count = retrieval.shape[0]
+    ret_per = ret_count // head_count
+    run_per = (kv_total - ret_count) // head_count
+    me = lax.axis_index("head")
+    is_ret = jnp.any(jnp.arange(kv_total, dtype=jnp.int32)[:, None] == retrieval[None, :], axis=1)
+    order = jnp.argsort(is_ret.astype(jnp.int32), stable=True)
+    run_ids = lax.dynamic_slice_in_dim(order, me * run_per, run_per)
+    ret_ids = lax.dynamic_slice_in_dim(order, kv_total - ret_count + me * ret_per, ret_per)
+
+    q_all = head_exchange(rotated_query.reshape(rows, kv_local, QUERY_PER_KEY, HEAD_SIZE), head_count)
+    q_all = q_all.transpose(1, 0, 2, 3, 4).reshape(rows, kv_total, QUERY_PER_KEY, HEAD_SIZE)
+    kv_own = jnp.stack(
+        [rotated_key.reshape(rows, kv_local, HEAD_SIZE), values.reshape(rows, kv_local, HEAD_SIZE)], axis=2
+    )
+    kv_all = head_exchange(kv_own, head_count)
+    kv_all = kv_all.transpose(1, 0, 2, 3, 4).reshape(rows, kv_total, 2, HEAD_SIZE)
+
+    own_index = ctx_index * rows + jnp.arange(rows, dtype=jnp.int32)
+    inv_root = 1.0 / math.sqrt(HEAD_SIZE)
+
+    run_kv = jnp.take(kv_all, run_ids, axis=1)
+    prev_kv = lax.ppermute(run_kv, CTX, [(i, i + 1) for i in range(ctx_count - 1)])
+    sink_kv = lax.psum(jnp.where(ctx_index == 0, run_kv[:SINK], jnp.zeros_like(run_kv[:SINK])), CTX)
+    near_kv = jnp.concatenate([sink_kv, prev_kv, run_kv], axis=0)
+    sink_index = jnp.arange(SINK, dtype=jnp.int32)
+    window_index = (ctx_index - 1) * rows + jnp.arange(2 * rows, dtype=jnp.int32)
+    causal_sink = sink_index[None, :] <= own_index[:, None]
+    in_window = (
+        (window_index[None, :] <= own_index[:, None])
+        & (window_index[None, :] > own_index[:, None] - WINDOW)
+        & (window_index[None, :] >= SINK)
+    )
+    near_visible = jnp.concatenate([causal_sink, in_window], axis=1)[None]
+    q_run = jnp.take(q_all, run_ids, axis=1)
+    start = (
+        jnp.full((run_per, QUERY_PER_KEY, rows), neg_big, jnp.float32),
+        jnp.zeros((run_per, QUERY_PER_KEY, rows), jnp.float32),
+        jnp.zeros((run_per, QUERY_PER_KEY, rows, HEAD_SIZE), jnp.float32),
+    )
+    _, run_totals, run_accum = update(
+        q_run, near_kv[:, :, 0], near_kv[:, :, 1], near_visible, start
+    )
+    run_out = run_accum / run_totals[..., None]
+
+    ret_kv = jnp.take(kv_all, ret_ids, axis=1)
+    ret_shard = lax.all_gather(ret_kv.reshape(rows, ret_per * 2 * HEAD_SIZE), CTX, axis=0, tiled=True)
+    ret_shard = ret_shard.reshape(ctx_count * rows, ret_per, 2, HEAD_SIZE)
+    q_ret = jnp.take(q_all, ret_ids, axis=1)
+    sub_rows = math.gcd(ctx_count * rows, 512)
+    turn_count = (ctx_index * rows + rows + sub_rows - 1) // sub_rows
+
+    def one_turn(j, state):
+        block = lax.dynamic_slice_in_dim(ret_shard, j * sub_rows, sub_rows, 0)
+        key_index = j * sub_rows + jnp.arange(sub_rows, dtype=jnp.int32)
+        visible = (key_index[None, :] <= own_index[:, None])[None]
+        return update(q_ret, block[:, :, 0], block[:, :, 1], visible, state)
+
+    start = (
+        jnp.full((ret_per, QUERY_PER_KEY, rows), neg_big, jnp.float32),
+        jnp.zeros((ret_per, QUERY_PER_KEY, rows), jnp.float32),
+        jnp.zeros((ret_per, QUERY_PER_KEY, rows, HEAD_SIZE), jnp.float32),
+    )
+    _, ret_totals, ret_accum = lax.fori_loop(0, turn_count, one_turn, start)
+    ret_out = ret_accum / ret_totals[..., None]
+
+    done = jnp.concatenate([ret_out, run_out], axis=0).astype(jnp.bfloat16)
+    slots = head_exchange(done, head_count).reshape(kv_total, QUERY_PER_KEY, rows, HEAD_SIZE)
+    placed = jnp.concatenate(
+        [
+            jnp.concatenate(
+                [order[kv_total - ret_count + h * ret_per : kv_total - ret_count + (h + 1) * ret_per],
+                 order[h * run_per : (h + 1) * run_per]]
+            )
+            for h in range(head_count)
+        ]
+    )
+    slot_of = jnp.argsort(placed)
+    home = jnp.take(slots, lax.dynamic_slice_in_dim(slot_of, me * kv_local, kv_local), axis=0)
+    return home.transpose(2, 0, 1, 3).reshape(rows, kv_local * QUERY_PER_KEY * HEAD_SIZE)
+
+
 def project(attended, w_local, head_count):
     rows = attended.shape[0]
     col_width = w_local.shape[1]
@@ -162,8 +255,21 @@
     head_ids = lax.axis_index("head") * kv_local + jnp.arange(kv_local, dtype=jnp.int32)
     flags = jnp.any(head_ids[:, None] == retrieval[None, :], axis=1)
     own_index = ctx_index * rows_dev + jnp.arange(rows_dev, dtype=jnp.int32)
-    attended = attend(((rotated_query, own_index),), rotated_key, values, flags, kv_local)[0]
-    return project(attended, out_weight, lax.psum(1, "head"))
+    head_count = lax.psum(1, "head")
+    kv_total = kv_local * head_count
+    ret_count = retrieval.shape[0]
+    if (
+        ret_count % head_count == 0
+        and (kv_total - ret_count) % head_count == 0
+        and ret_count < kv_total
+        and rows_dev >= max(SINK, WINDOW)
+    ):
+        attended = duo_attend(
+            rotated_query, rotated_key, values, retrieval, kv_local, head_count, ctx_index
+        )
+    else:
+        attended = attend(((rotated_query, own_index),), rotated_key, values, flags, kv_local)[0]
+    return project(attended, out_weight, head_count)
 
 
 def grid_of(ctx_count, head_count):

time: 365 us -> 395 us (1.082)
  waiting for transfers between devices: 265 us -> 305 us
  other arithmetic: 24.4 us -> 14.1 us
  starting transfers between devices: 0.3 us -> 6.47 us
  loops' own time: 6.11 us -> 0.27 us
  matrix products: 15.5 us -> 20.3 us
  local copies, waits for them, and re-layouts: 20.1 us -> 15.6 us
    psum x0 -> x1, waiting for transfers between devices: none -> 94.8 us  [duo_attend(): lax.psum(jnp.where(ctx_index == 0, run_kv[:SINK], jnp.zeros_like(run_kv[:...]
    all_gather x1, waiting for transfers between devices: 130 us -> 79.8 us  [duo_attend(): lax.all_gather(ret_kv.reshape(rows, ret_per * 2 * HEAD_SIZE), CTX, axis=0...]
    all_gather x1, waiting for transfers between devices: 83.2 us -> 52.3 us  [project(): a_plane = lax.all_gather(attended, 'cb', axis=0, tiled=True)]
    all_gather x1, waiting for transfers between devices: 39.4 us -> 64.7 us  [project(): w_line = lax.all_gather(w_local, 'cz', axis=1, tiled=True)]
    reduce_or x9 -> x1, other arithmetic: 11.7 us -> 0.74 us  [duo_attend(): jnp.any(jnp.arange(kv_total, dtype=jnp.int32)[:, None] == retrieval[None,...]
    ppermute x0 -> x4, starting transfers between devices: none -> 6.3 us  [the longest x1 5.53 us: duo_attend(): lax.ppermute(run_kv, CTX, [(i, i + 1) for i in range(ctx_count - 1)])]
    slice x1, local copies, waits for them, and re-layouts: 6.04 us -> 0.07 us  [duo_attend(): order[kv_total - ret_count + h * ret_per:kv_total - ret_count + (h + 1) *...]
    another operation x9 -> x1, loops' own time: 6.11 us -> 0.27 us  [duo_attend(): _, ret_totals, ret_accum = lax.fori_loop(0, turn_count, one_turn, start)]
  transfers between devices with their start and end apart: 4 -> 9, of which waited for: 4 -> 6; matrix products, arithmetic and copies ran while one was open for 11% -> 7% of each run, Pallas kernels for 0% -> 0%
where the time goes in v2:
time: 395 us; the launch traced here: 394 us
  waiting for transfers between devices  305 us (77%)
  matrix products  20.3 us (5%)
  blocking collectives  18.3 us (5%)
  local copies, waits for them, and re-layouts  15.6 us (4%)
  between operations  14.2 us (4%)
  other arithmetic  14.1 us (4%)
  starting transfers between devices  6.47 us (2%)
    psum x1, waiting for transfers between devices, duo_attend(): lax.psum(jnp.where(ctx_index == 0, run_kv[:SINK], jnp.zeros_like(run_kv[:...  94.8 us
    all_gather x1, waiting for transfers between devices, duo_attend(): lax.all_gather(ret_kv.reshape(rows, ret_per * 2 * HEAD_SIZE), CTX, axis=0...  79.8 us
    all_gather x1, waiting for transfers between devices, project(): w_line = lax.all_gather(w_local, 'cz', axis=1, tiled=True)  64.7 us
    all_gather x1, waiting for transfers between devices, project(): a_plane = lax.all_gather(attended, 'cb', axis=0, tiled=True)  52.3 us
    all_to_all x1, blocking collectives, project(): got = lax.all_to_all(pieces, 'cb', 0, 0, tiled=False)  18.3 us
    reduce_scatter x1, waiting for transfers between devices, project(): lax.psum_scatter(part, 'head', scatter_dimension=1, tiled=True)  12 us
    dot_general x1, matrix products, project(): part = jnp.dot(a_plane, w_line, preferred_element_type=jnp.float32)  10 us
  transfers between devices with their start and end apart: 9, of which 6 were waited for; matrix products, arithmetic and copies ran while one was open for 7% of the time, Pallas kernels for 0%

profile of v2, /device:TPU:0, one launch (start us, length us, event | category | flops | bytes accessed | tf_op | source)
XLA Modules:
  0.0 394.5 jit_solution(9107826275673010215)
XLA Ops:
  7.2 0.7 convert_element_type.38
  7.9 1.1 copy.33
  9.0 1.1 copy.32
  10.2 0.3 fusion.36
  10.6 0.6 collective-permute-start
  11.2 0.7 fusion.38
  11.9 1.0 sort.34
  13.0 0.2 select_bitcast_fusion.7
  13.3 0.7 copy.34
  14.0 0.6 gather_fusion.3
  14.7 0.6 slice_select_fusion
  15.4 0.6 gather_fusion.1
  16.1 0.9 copy.35
  17.3 0.2 convert_bitcast_fusion
  17.5 0.4 copy.54
  17.9 0.7 fusion.45
  18.6 1.4 subtract_convert_fusion
  20.0 0.6 pad_maximum_fusion.2
  20.8 0.2 and_and_fusion
  21.0 5.5 %collective-permute-start.2 = (bf16[256,2,2,128]{3,0,1,2:T(8,128)(2,1)S(1)}, bf16[256,2,2,128]{3,0,1,2:T(8,128)(2,1)}, u32[]{:S(2)}, u32[]{:S(2)}) collective-permute-start(bf16[256,2,2,128]{3,0,1,2:T(8,128)(2,1)S(1)} %fusion.32), channel_id=1, source_target_pairs={{0,2},{2,4},{4,6},{6,8},{8,10},{10,12},{12,14},{14,16},{16,18},{18... | collective-permute-start | bytes 786440 | tf_op jit(solution)/shard_map/ppermute | solution.py:169
  26.6 94.8 %all-reduce.2.cloned.1.call-done = bf16[64,2,2,128]{3,0,1,2:T(8,128)(2,1)} async-done(((bf16[64,2,2,128]{3,0,1,2:T(8,128)(2,1)}), bf16[64,2,2,128]{3,0,1,2:T(8,128)(2,1)}) %all-reduce.2.cloned.1.call-update) | async-done | bytes 65552 | tf_op jit(solution)/shard_map/psum | solution.py:170
  121.4 1.0 pad_maximum_fusion.4
  122.6 0.2 pad_maximum_fusion
  122.8 1.4 gather_fusion.4
  124.2 0.6 gather_fusion.2
  124.8 2.0 fusion.17
  126.8 1.2 fusion.18
  128.1 2.0 divide_convert_fusion
  130.2 79.8 %all-gather.4.cloned.1.call-done = bf16[4096,512]{0,1:T(8,128)(2,1)} async-done(((bf16[256,512]{0,1:T(8,128)(2,1)}), bf16[4096,512]{0,1:T(8,128)(2,1)}) %all-gather.4.cloned.1.call-update) | async-done | bytes 4194320 | tf_op jit(solution)/shard_map/all_gather | solution.py:193
  210.0 9.7 %while.15 = (s32[]{:T(128)}, f32[2,4,256]{2,1,0:T(4,128)S(1)}, f32[2,4,256]{2,1,0:T(4,128)S(1)}, f32[2,4,256,128]{3,2,1,0:T(8,128)S(1)}, s32[]{:T(128)}, /*index...) while((s32[]{:T(128)}, f32[2,4,256]{2,1,0:T(4,128)S(1)}, ...), condition=%wide.region_6.9_spmd.clone, body=%wide.region_3.8_spmd.clone.sunk | while | flops 551162624 | bytes 33167600 | solution.py:210
  210.4 1.8 fusion.58
  212.3 1.9 copy-done
  214.3 1.0 fusion.59
  215.3 4.4 %fusion.60 = f32[2,4,256,128]{3,2,1,0:T(8,128)S(1)} fusion(f32[2,512,256,4]{2,1,3,0:T(8,128)} %copy-done, f32[2,4,256]{2,1,0:T(4,128)S(1)} %max.13, pred[256,512]{0,1:T(8,128)(4,1)S(1)} %broadcast_compare_fusion.3, f32[2,4,256,128]{3,2,1,0:T(8,128)S(1)} %get-tuple-element.231, f32[2,4,256]{2,1,0:T(4,128)S(1)} %bitcast.163, ...), kind=kOutput, calls=%fused_computation.13.clone.1 | convolution fusion | flops 274202624 | bytes 6701064 | tf_op jit(solution)/shard_map/while/body/hgrk,khd->hgrd/dot_general | solution.py:61
  219.7 0.3 divide_convert_fusion.1
  220.4 1.0 sort.35
  221.4 1.4 collective-permute-done.3
  223.2 0.7 gather_fusion
  224.2 1.3 copy.42
  225.5 64.7 %all-gather.8.cloned.1.call-done = bf16[2048,1024]{1,0:T(8,128)(2,1)} async-done(((bf16[2048,256]{1,0:T(8,128)(2,1)}), bf16[2048,1024]{1,0:T(8,128)(2,1)}) %all-gather.8.cloned.1.call-update) | async-done | bytes 4194320 | tf_op jit(solution)/shard_map/all_gather | solution.py:235
  290.3 52.3 %all-gather.6.cloned.1.call-done = bf16[1024,2048]{0,1:T(8,128)(2,1)} async-done(((bf16[256,2048]{0,1:T(8,128)(2,1)}), bf16[1024,2048]{0,1:T(8,128)(2,1)}) %all-gather.6.cloned.1.call-update) | async-done | bytes 4194320 | tf_op jit(solution)/shard_map/all_gather | solution.py:234
  342.6 10.0 %fusion.47 = f32[1024,1024]{1,0:T(8,128)} fusion(bf16[1024,2048]{0,1:T(8,128)(2,1)} %all-gather.6.cloned.1.call-done, bf16[2048,1024]{1,0:T(8,128)(2,1)} %all-gather.8.cloned.1.call-done), kind=kOutput, calls=%fused_computation.105 | convolution fusion | flops 4294967296 | bytes 12582912 | tf_op jit(solution)/shard_map/dot_general | solution.py:236
  352.7 12.0 %reduce-scatter.2.cloned.1.call-done = f32[1024,512]{1,0:T(8,128)} async-done(((f32[1024,1024]{1,0:T(8,128)}), f32[1024,512]{1,0:T(8,128)}) %reduce-scatter.2.cloned.1.call-update) | async-done | bytes 2097168 | tf_op jit(solution)/shard_map/reduce_scatter | solution.py:237
  364.7 1.7 convert_element_type.43
  366.4 18.3 %all_to_all.5 = bf16[4,256,512]{2,1,0:T(8,128)(2,1)S(1)} all-to-all(bf16[4,256,512]{2,1,0:T(8,128)(2,1)S(1)} %bitcast.148), channel_id=1, replica_groups=mesh['cz'=4,'cb'=4,'head'=2] {'cb'}, dimensions={0} | all-to-all | bytes 2097152 | tf_op jit(solution)/shard_map/all_to_all | solution.py:240
  384.7 0.3 reshape.220
  385.0 1.4 copy.63
  386.3 1.6 reshape.221
  (59 shorter events, 2.6 us)
Async XLA Ops:
  6.5 114.9 %all-reduce.2.cloned.1.call-start = ((), (), s32[]{:S(2)}) async-start(), calls=%async_computation.3 | async-start | bytes 131072 | tf_op jit(solution)/shard_map/psum | solution.py:170
  10.6 2.4 collective-permute-start
  13.2 4.1 %copy-start.1 = (bf16[256,2048]{1,0:T(8,128)(2,1)S(1)}, bf16[256,2048]{1,0:T(8,128)(2,1)}, u32[]{:S(2)}) copy-start(bf16[256,2048]{1,0:T(8,128)(2,1)} %param.13) | copy-start | bytes 3145732
  15.4 194.6 %all-gather.4.cloned.1.call-start = ((), (), s32[]{:S(2)}) async-start(), calls=%async_computation.2 | async-start | bytes 4456448 | tf_op jit(solution)/shard_map/all_gather | solution.py:193
  17.0 273.3 %all-gather.8.cloned.1.call-start = ((), (), s32[]{:S(2)}) async-start(), calls=%async_computation.5 | async-start | bytes 5242880 | tf_op jit(solution)/shard_map/all_gather | solution.py:235
  20.5 101.9 %collective-permute-start.1 = (bf16[256,4,4,128]{3,0,2,1:T(8,128)(2,1)S(1)}, bf16[256,4,4,128]{3,0,2,1:T(8,128)(2,1)S(1)}, u32[]{:S(2)}, u32[]{:S(2)}) collective-permute-start(bf16[256,4,4,128]{3,0,2,1:T(8,128)(2,1)S(1)} %bitcast.146), channel_id=1, source_target_pairs={{0,1},{1,0},{2,3},{3,2},{4,5},{5,4},{6,7},{7,6},{8,9},{9,8},{10,11... | collective-permute-start | bytes 3145736 | tf_op jit(solution)/shard_map/ppermute | solution.py:138
  20.7 321.9 %all-gather.6.cloned.1.call-start = ((), (), s32[]{:S(2)}) async-start(), calls=%async_computation.4 | async-start | bytes 5242880 | tf_op jit(solution)/shard_map/all_gather | solution.py:234
  21.0 100.4 %collective-permute-start.2 = (bf16[256,2,2,128]{3,0,1,2:T(8,128)(2,1)S(1)}, bf16[256,2,2,128]{3,0,1,2:T(8,128)(2,1)}, u32[]{:S(2)}, u32[]{:S(2)}) collective-permute-start(bf16[256,2,2,128]{3,0,1,2:T(8,128)(2,1)S(1)} %fusion.32), channel_id=1, source_target_pairs={{0,2},{2,4},{4,6},{6,8},{8,10},{10,12},{12,14},{14,16},{16,18},{18... | collective-permute-start | bytes 786440 | tf_op jit(solution)/shard_map/ppermute | solution.py:169
  212.3 2.0 copy-start
  220.2 2.7 collective-permute-start.3
  225.5 139.2 %reduce-scatter.2.cloned.1.call-start = ((), (), s32[]{:S(2)}) async-start(), calls=%async_computation.6 | async-start | bytes 6291456 | tf_op jit(solution)/shard_map/reduce_scatter | solution.py:237
Sparse Core Ops, SparseCore 0:
  15.5 105.8 all-reduce.1
  124.1 85.7 all-gather.3
  211.5 78.7 all-gather.7
  292.0 50.6 all-gather.5
  352.8 11.8 reduce-scatter.1

commit v3 on v2

--- a/solution.py
+++ b/solution.py
@@ -167,7 +167,13 @@
 
     run_kv = jnp.take(kv_all, run_ids, axis=1)
     prev_kv = lax.ppermute(run_kv, CTX, [(i, i + 1) for i in range(ctx_count - 1)])
-    sink_kv = lax.psum(jnp.where(ctx_index == 0, run_kv[:SINK], jnp.zeros_like(run_kv[:SINK])), CTX)
+    sink_kv = run_kv[:SINK]
+    have = 1
+    while have < ctx_count:
+        pairs = [(i, i + have) for i in range(have) if i + have < ctx_count]
+        got = lax.ppermute(sink_kv, CTX, pairs)
+        sink_kv = jnp.where((ctx_index >= have) & (ctx_index < 2 * have), got, sink_kv)
+        have *= 2
     near_kv = jnp.concatenate([sink_kv, prev_kv, run_kv], axis=0)
     sink_index = jnp.arange(SINK, dtype=jnp.int32)
     window_index = (ctx_index - 1) * rows + jnp.arange(2 * rows, dtype=jnp.int32)

time: 395 us -> 296 us (0.75)
  waiting for transfers between devices: 305 us -> 200 us
  starting transfers between devices: 6.47 us -> 13.8 us
    psum x1 -> x0, waiting for transfers between devices: 94.8 us -> none  [duo_attend(): lax.psum(jnp.where(ctx_index == 0, run_kv[:SINK], jnp.zeros_like(run_kv[:...]
    all_gather x1, waiting for transfers between devices: 79.8 us -> 62.7 us  [duo_attend(): lax.all_gather(ret_kv.reshape(rows, ret_per * 2 * HEAD_SIZE), CTX, axis=0...]
    ppermute x0 -> x4, starting transfers between devices: none -> 8.69 us  [duo_attend(): got = lax.ppermute(sink_kv, CTX, pairs)]
    ppermute x0 -> x4, waiting for transfers between devices: none -> 5.5 us  [duo_attend(): got = lax.ppermute(sink_kv, CTX, pairs)]
  transfers between devices with their start and end apart: 9 -> 12, of which waited for: 6 -> 9; matrix products, arithmetic and copies ran while one was open for 7% -> 9% of each run, Pallas kernels for 0% -> 0%
where the time goes in v3:
time: 296 us; the launch traced here: 295 us
  waiting for transfers between devices  200 us (68%)
  matrix products  20.2 us (7%)
  blocking collectives  18.3 us (6%)
  local copies, waits for them, and re-layouts  14.8 us (5%)
  between operations  14.3 us (5%)
  starting transfers between devices  13.8 us (5%)
  other arithmetic  13.4 us (5%)
    all_gather x1, waiting for transfers between devices, project(): w_line = lax.all_gather(w_local, 'cz', axis=1, tiled=True)  64.8 us
    all_gather x1, waiting for transfers between devices, duo_attend(): lax.all_gather(ret_kv.reshape(rows, ret_per * 2 * HEAD_SIZE), CTX, axis=0...  62.7 us
    all_gather x1, waiting for transfers between devices, project(): a_plane = lax.all_gather(attended, 'cb', axis=0, tiled=True)  52.5 us
    all_to_all x1, blocking collectives, project(): got = lax.all_to_all(pieces, 'cb', 0, 0, tiled=False)  18.3 us
    reduce_scatter x1, waiting for transfers between devices, project(): lax.psum_scatter(part, 'head', scatter_dimension=1, tiled=True)  12 us
    dot_general x1, matrix products, project(): part = jnp.dot(a_plane, w_line, preferred_element_type=jnp.float32)  10 us
    ppermute x4, starting transfers between devices, duo_attend(): got = lax.ppermute(sink_kv, CTX, pairs)  8.69 us
    dot_general x2, matrix products, update(): jnp.einsum('hgrk,khd->hgrd', weights.astype(jnp.bfloat16), value_block, p...  6.42 us
  transfers between devices with their start and end apart: 12, of which 9 were waited for; matrix products, arithmetic and copies ran while one was open for 9% of the time, Pallas kernels for 0%

profile of v3, /device:TPU:0, one launch (start us, length us, event | category | flops | bytes accessed | tf_op | source)
XLA Modules:
  0.0 295.4 jit_solution(3231720207045080559)
XLA Ops:
  7.2 0.7 convert_element_type.38
  7.9 1.1 copy.33
  9.0 1.1 copy.32
  10.6 0.6 collective-permute-start
  11.2 0.7 fusion.38
  11.9 1.0 sort.34
  13.3 0.7 copy.34
  14.0 0.6 gather_fusion.1
  14.7 0.9 copy.35
  16.1 0.4 copy.54
  16.5 0.7 fusion.45
  17.2 1.4 subtract_convert_fusion
  18.5 0.6 pad_maximum_fusion.2
  19.4 0.6 gather_fusion.3
  20.1 4.8 %collective-permute-start.2 = (bf16[64,2,2,128]{3,0,1,2:T(8,128)(2,1)S(1)}, bf16[64,2,2,128]{3,0,1,2:T(8,128)(2,1)S(1)}, u32[]{:S(2)}, u32[]{:S(2)}) collective-permute-start(bf16[64,2,2,128]{3,0,1,2:T(8,128)(2,1)S(1)} %slice.66), channel_id=1, source_target_pairs={{0,2},{1,3}} | collective-permute-start | bytes 196616 | tf_op jit(solution)/shard_map/ppermute | solution.py:174
  24.9 1.9 collective-permute-done.2
  26.8 1.3 collective-permute-start.3
  28.3 1.8 collective-permute-done.3
  30.1 1.3 collective-permute-start.4
  31.5 4.2 %collective-permute-start.6 = (bf16[256,2,2,128]{3,0,1,2:T(8,128)(2,1)S(1)}, bf16[256,2,2,128]{3,0,1,2:T(8,128)(2,1)S(1)}, u32[]{:S(2)}, u32[]{:S(2)}) collective-permute-start(bf16[256,2,2,128]{3,0,1,2:T(8,128)(2,1)S(1)} %fusion.32), channel_id=1, source_target_pairs={{0,2},{2,4},{4,6},{6,8},{8,10},{10,12},{12,14},{14,16},{16,18},{18... | collective-permute-start | bytes 786440 | tf_op jit(solution)/shard_map/ppermute | solution.py:169
  35.7 1.3 collective-permute-start.5
  37.0 1.9 collective-permute-done.5
  38.9 1.4 collective-permute-done.6
  40.2 0.9 pad_maximum_fusion.4
  41.4 0.6 gather_fusion.4
  42.1 0.6 gather_fusion.2
  42.8 1.9 fusion.17
  44.7 1.2 fusion.18
  46.0 2.0 divide_convert_fusion
  48.0 62.7 %all-gather.4.cloned.1.call-done = bf16[4096,512]{0,1:T(8,128)(2,1)} async-done(((bf16[256,512]{0,1:T(8,128)(2,1)}), bf16[4096,512]{0,1:T(8,128)(2,1)}) %all-gather.4.cloned.1.call-update) | async-done | bytes 4194320 | tf_op jit(solution)/shard_map/all_gather | solution.py:199
  110.9 9.6 %while.15 = (s32[]{:T(128)}, f32[2,4,256]{2,1,0:T(4,128)S(1)}, f32[2,4,256]{2,1,0:T(4,128)S(1)}, f32[2,4,256,128]{3,2,1,0:T(8,128)S(1)}, s32[]{:T(128)}, /*index...) while((s32[]{:T(128)}, f32[2,4,256]{2,1,0:T(4,128)S(1)}, ...), condition=%wide.region_6.9_spmd.clone, body=%wide.region_3.8_spmd.clone.sunk | while | flops 551162624 | bytes 33167600 | solution.py:216
  111.3 1.8 fusion.58
  113.1 1.9 copy-done
  115.1 1.0 fusion.59
  116.1 4.4 %fusion.60 = f32[2,4,256,128]{3,2,1,0:T(8,128)S(1)} fusion(f32[2,512,256,4]{2,1,3,0:T(8,128)} %copy-done, f32[2,4,256]{2,1,0:T(4,128)S(1)} %max.13, pred[256,512]{0,1:T(8,128)(4,1)S(1)} %broadcast_compare_fusion.3, f32[2,4,256,128]{3,2,1,0:T(8,128)S(1)} %get-tuple-element.231, f32[2,4,256]{2,1,0:T(4,128)S(1)} %bitcast.163, ...), kind=kOutput, calls=%fused_computation.13.clone.1 | convolution fusion | flops 274202624 | bytes 6701064 | tf_op jit(solution)/shard_map/while/body/hgrk,khd->hgrd/dot_general | solution.py:61
  120.5 0.3 divide_convert_fusion.1
  121.2 1.0 sort.35
  122.3 1.4 collective-permute-done.7
  124.0 0.7 gather_fusion
  125.0 1.3 copy.42
  126.4 64.8 %all-gather.8.cloned.1.call-done = bf16[2048,1024]{1,0:T(8,128)(2,1)} async-done(((bf16[2048,256]{1,0:T(8,128)(2,1)}), bf16[2048,1024]{1,0:T(8,128)(2,1)}) %all-gather.8.cloned.1.call-update) | async-done | bytes 4194320 | tf_op jit(solution)/shard_map/all_gather | solution.py:241
  191.1 52.5 %all-gather.6.cloned.1.call-done = bf16[1024,2048]{0,1:T(8,128)(2,1)} async-done(((bf16[256,2048]{0,1:T(8,128)(2,1)}), bf16[1024,2048]{0,1:T(8,128)(2,1)}) %all-gather.6.cloned.1.call-update) | async-done | bytes 4194320 | tf_op jit(solution)/shard_map/all_gather | solution.py:240
  243.6 10.0 %fusion.47 = f32[1024,1024]{1,0:T(8,128)} fusion(bf16[1024,2048]{0,1:T(8,128)(2,1)} %all-gather.6.cloned.1.call-done, bf16[2048,1024]{1,0:T(8,128)(2,1)} %all-gather.8.cloned.1.call-done), kind=kOutput, calls=%fused_computation.108 | convolution fusion | flops 4294967296 | bytes 12582912 | tf_op jit(solution)/shard_map/dot_general | solution.py:242
  253.6 12.0 %reduce-scatter.2.cloned.1.call-done = f32[1024,512]{1,0:T(8,128)} async-done(((f32[1024,1024]{1,0:T(8,128)}), f32[1024,512]{1,0:T(8,128)}) %reduce-scatter.2.cloned.1.call-update) | async-done | bytes 2097168 | tf_op jit(solution)/shard_map/reduce_scatter | solution.py:243
  265.7 1.7 convert_element_type.43
  267.4 18.3 %all_to_all.5 = bf16[4,256,512]{2,1,0:T(8,128)(2,1)S(1)} all-to-all(bf16[4,256,512]{2,1,0:T(8,128)(2,1)S(1)} %bitcast.148), channel_id=1, replica_groups=mesh['cz'=4,'cb'=4,'head'=2] {'cb'}, dimensions={0} | all-to-all | bytes 2097152 | tf_op jit(solution)/shard_map/all_to_all | solution.py:246
  286.0 1.4 copy.63
  287.3 1.6 reshape.221
  (70 shorter events, 4.0 us)
Async XLA Ops:
  6.5 104.3 %all-gather.4.cloned.1.call-start = ((), (), s32[]{:S(2)}) async-start(), calls=%async_computation.2 | async-start | bytes 4456448 | tf_op jit(solution)/shard_map/all_gather | solution.py:199
  10.6 2.4 collective-permute-start
  13.0 2.9 copy-start.1
  15.6 175.5 %all-gather.8.cloned.1.call-start = ((), (), s32[]{:S(2)}) async-start(), calls=%async_computation.4 | async-start | bytes 5242880 | tf_op jit(solution)/shard_map/all_gather | solution.py:241
  19.1 22.0 %collective-permute-start.1 = (bf16[256,4,4,128]{3,0,2,1:T(8,128)(2,1)S(1)}, bf16[256,4,4,128]{3,0,2,1:T(8,128)(2,1)S(1)}, u32[]{:S(2)}, u32[]{:S(2)}) collective-permute-start(bf16[256,4,4,128]{3,0,2,1:T(8,128)(2,1)S(1)} %bitcast.146), channel_id=1, source_target_pairs={{0,1},{1,0},{2,3},{3,2},{4,5},{5,4},{6,7},{7,6},{8,9},{9,8},{10,11... | collective-permute-start | bytes 3145736 | tf_op jit(solution)/shard_map/ppermute | solution.py:138
  19.3 224.3 %all-gather.6.cloned.1.call-start = ((), (), s32[]{:S(2)}) async-start(), calls=%async_computation.3 | async-start | bytes 5242880 | tf_op jit(solution)/shard_map/all_gather | solution.py:240
  20.1 6.7 %collective-permute-start.2 = (bf16[64,2,2,128]{3,0,1,2:T(8,128)(2,1)S(1)}, bf16[64,2,2,128]{3,0,1,2:T(8,128)(2,1)S(1)}, u32[]{:S(2)}, u32[]{:S(2)}) collective-permute-start(bf16[64,2,2,128]{3,0,1,2:T(8,128)(2,1)S(1)} %slice.66), channel_id=1, source_target_pairs={{0,2},{1,3}} | collective-permute-start | bytes 196616 | tf_op jit(solution)/shard_map/ppermute | solution.py:174
  26.8 3.3 %collective-permute-start.3 = (bf16[64,2,2,128]{3,0,1,2:T(8,128)(2,1)S(1)}, bf16[64,2,2,128]{3,0,1,2:T(8,128)(2,1)S(1)}, u32[]{:S(2)}, u32[]{:S(2)}) collective-permute-start(bf16[64,2,2,128]{3,0,1,2:T(8,128)(2,1)S(1)} %broadcast_select_fusion), channel_id=1, source_target_pairs={{0,4},{2,6},{1,5},{3,7}} | collective-permute-start | bytes 196616 | tf_op jit(solution)/shard_map/ppermute | solution.py:174
  30.1 5.5 %collective-permute-start.4 = (bf16[64,2,2,128]{3,0,1,2:T(8,128)(2,1)S(1)}, bf16[64,2,2,128]{3,0,1,2:T(8,128)(2,1)S(1)}, u32[]{:S(2)}, u32[]{:S(2)}) collective-permute-start(bf16[64,2,2,128]{3,0,1,2:T(8,128)(2,1)S(1)} %broadcast_select_fusion.1), channel_id=1, source_target_pairs={{0,8},{2,10},{4,12},{6,14},{1,9},{3,11},{5,13},{7,15}} | collective-permute-start | bytes 196616 | tf_op jit(solution)/shard_map/ppermute | solution.py:174
  31.5 8.8 %collective-permute-start.6 = (bf16[256,2,2,128]{3,0,1,2:T(8,128)(2,1)S(1)}, bf16[256,2,2,128]{3,0,1,2:T(8,128)(2,1)S(1)}, u32[]{:S(2)}, u32[]{:S(2)}) collective-permute-start(bf16[256,2,2,128]{3,0,1,2:T(8,128)(2,1)S(1)} %fusion.32), channel_id=1, source_target_pairs={{0,2},{2,4},{4,6},{6,8},{8,10},{10,12},{12,14},{14,16},{16,18},{18... | collective-permute-start | bytes 786440 | tf_op jit(solution)/shard_map/ppermute | solution.py:169
  35.7 3.2 %collective-permute-start.5 = (bf16[64,2,2,128]{3,0,1,2:T(8,128)(2,1)S(1)}, bf16[64,2,2,128]{3,0,1,2:T(8,128)(2,1)S(1)}, u32[]{:S(2)}, u32[]{:S(2)}) collective-permute-start(bf16[64,2,2,128]{3,0,1,2:T(8,128)(2,1)S(1)} %broadcast_select_fusion.2), channel_id=1, source_target_pairs={{0,16},{2,18},{4,20},{6,22},{8,24},{10,26},{12,28},{14,30},{1,17},... | collective-permute-start | bytes 196616 | tf_op jit(solution)/shard_map/ppermute | solution.py:174
  44.7 1.3 copy-start.2
  113.1 2.0 copy-start
  121.0 2.7 collective-permute-start.7
  126.3 139.4 %reduce-scatter.2.cloned.1.call-start = ((), (), s32[]{:S(2)}) async-start(), calls=%async_computation.5 | async-start | bytes 6291456 | tf_op jit(solution)/shard_map/reduce_scatter | solution.py:243
Sparse Core Ops, SparseCore 0:
  15.7 95.0 all-gather.3
  112.4 78.7 all-gather.7
  192.9 50.6 all-gather.5
  253.8 11.8 reduce-scatter.1

commit v4 on v3

--- a/solution.py
+++ b/solution.py
@@ -5,6 +5,7 @@
 import jax.numpy as jnp
 from jax import lax
 from jax.sharding import Mesh, PartitionSpec as P
+
 
 HEAD_SIZE = 128
 SINK = 64
@@ -163,7 +164,6 @@
     kv_all = kv_all.transpose(1, 0, 2, 3, 4).reshape(rows, kv_total, 2, HEAD_SIZE)
 
     own_index = ctx_index * rows + jnp.arange(rows, dtype=jnp.int32)
-    inv_root = 1.0 / math.sqrt(HEAD_SIZE)
 
     run_kv = jnp.take(kv_all, run_ids, axis=1)
     prev_kv = lax.ppermute(run_kv, CTX, [(i, i + 1) for i in range(ctx_count - 1)])
@@ -232,15 +232,32 @@
     return home.transpose(2, 0, 1, 3).reshape(rows, kv_local * QUERY_PER_KEY * HEAD_SIZE)
 
 
+def line_gather(w_local, line):
+    me = lax.axis_index("cz")
+    pieces = [w_local] + [
+        lax.ppermute(w_local, "cz", [(i, (i + shift) % line) for i in range(line)])
+        for shift in range(1, line)
+    ]
+    return jnp.take(jnp.stack(pieces), (me - jnp.arange(line)) % line, axis=0)
+
+
 def project(attended, w_local, head_count):
     rows = attended.shape[0]
     col_width = w_local.shape[1]
     plane = lax.psum(1, "cb")
     line = lax.psum(1, "cz")
     a_plane = lax.all_gather(attended, "cb", axis=0, tiled=True)
-    w_line = lax.all_gather(w_local, "cz", axis=1, tiled=True)
-    part = jnp.dot(a_plane, w_line, preferred_element_type=jnp.float32)
-    reduced = lax.psum_scatter(part, "head", scatter_dimension=1, tiled=True).astype(jnp.bfloat16)
+    part = jnp.einsum(
+        "tk,lkc->tlc", a_plane, line_gather(w_local, line), preferred_element_type=jnp.float32
+    ).reshape(a_plane.shape[0], line * col_width)
+    if head_count == 2:
+        half = part.shape[1] // 2
+        me = lax.axis_index("head")
+        mine = lax.dynamic_slice_in_dim(part, me * half, half, axis=1)
+        other = lax.dynamic_slice_in_dim(part, (1 - me) * half, half, axis=1)
+        reduced = (mine + lax.ppermute(other, "head", [(0, 1), (1, 0)])).astype(jnp.bfloat16)
+    else:
+        reduced = lax.psum_scatter(part, "head", scatter_dimension=1, tiled=True).astype(jnp.bfloat16)
     per_head = line // head_count
     pieces = reduced.reshape(plane, rows, per_head * col_width)
     got = lax.all_to_all(pieces, "cb", 0, 0, tiled=False)
@@ -251,7 +268,7 @@
     )
 
 
-def shards(queries, keys, values, positions, retrieval, yarn_scale, out_weight):
+def layer(queries, keys, values, positions, retrieval, yarn_scale, out_weight):
     rows_dev = queries.shape[0]
     kv_local = keys.shape[1] // HEAD_SIZE
     cosine_lookup, sine_lookup = yarn_tables(positions, yarn_scale)
@@ -293,7 +310,7 @@
     line, plane = grid_of(ctx_count, head_count)
     grid = Mesh(mesh.devices.reshape(line, plane, head_count), ("cz", "cb", "head"))
     return jax.shard_map(
-        shards,
+        layer,
         mesh=grid,
         in_specs=(
             P(CTX, "head"),

time: 296 us -> 335 us (1.13)
  the two profiles are of different devices: /device:TPU:0 before, /device:TPU:16 now
where the time goes in v4:
time: 335 us; the launch traced here: 334 us
  waiting for transfers between devices  168 us (50%)
  matrix products  40.8 us (12%)
  local copies, waits for them, and re-layouts  34.1 us (10%)
  starting transfers between devices  27.2 us (8%)
  blocking collectives  26.5 us (8%)
  other arithmetic  22.3 us (7%)
  between operations  14.7 us (4%)
    ppermute x3, waiting for transfers between devices, line_gather(): lax.ppermute(w_local, 'cz', [(i, (i + shift) % line) for i in range(line)])  89.9 us
    all_gather x1, waiting for transfers between devices, duo_attend(): lax.all_gather(ret_kv.reshape(rows, ret_per * 2 * HEAD_SIZE), CTX, axis=0...  62.8 us
    all_to_all x1, blocking collectives, project(): got = lax.all_to_all(pieces, 'cb', 0, 0, tiled=False)  26.5 us
    dot_general x6, matrix products, update(): jnp.einsum('hgrk,khd->hgrd', weights.astype(jnp.bfloat16), value_block, p...  21.9 us
    ppermute x3, starting transfers between devices, line_gather(): lax.ppermute(w_local, 'cz', [(i, (i + shift) % line) for i in range(line)])  19.8 us
    dot_general x6, matrix products, update(): jnp.einsum('rhgd,khd->hgrk', query_rows, key_block, preferred_element_typ...  11.2 us
    ppermute x4, waiting for transfers between devices, duo_attend(): got = lax.ppermute(sink_kv, CTX, pairs)  10.9 us
    while x15, local copies, waits for them, and re-layouts  9.81 us
  transfers between devices with their start and end apart: 14, of which 8 were waited for; matrix products, arithmetic and copies ran while one was open for 8% of the time, Pallas kernels for 0%

profile of v4, /device:TPU:16, one launch (start us, length us, event | category | flops | bytes accessed | tf_op | source)
XLA Modules:
  0.0 334.1 jit_solution(10531579112183013991)
XLA Ops:
  7.9 1.1 copy.40
  9.0 1.1 copy.39
  16.7 1.4 subtract_convert_fusion
  22.2 3.4 %collective-permute-start.6 = (bf16[256,2,2,128]{3,0,1,2:T(8,128)(2,1)S(1)}, bf16[256,2,2,128]{3,0,1,2:T(8,128)(2,1)S(1)}, u32[]{:S(2)}, u32[]{:S(2)}) collective-permute-start(bf16[256,2,2,128]{3,0,1,2:T(8,128)(2,1)S(1)} %fusion.37), channel_id=1, source_target_pairs={{0,2},{2,4},{4,6},{6,8},{8,10},{10,12},{12,14},{14,16},{16,18},{18... | collective-permute-start | bytes 786440 | tf_op jit(solution)/shard_map/ppermute | solution.py:169
  25.7 1.3 collective-permute-start.5
  27.0 10.9 %collective-permute-done.5 = bf16[64,2,2,128]{3,0,1,2:T(8,128)(2,1)S(1)} collective-permute-done((bf16[64,2,2,128]{3,0,1,2:T(8,128)(2,1)S(1)}, bf16[64,2,2,128]{3,0,1,2:T(8,128)(2,1)S(1)}, u32[]{:S(2)}, u32[]{:S(2)}) %collective-permute-start.5) | collective-permute-done | bytes 65568 | tf_op jit(solution)/shard_map/ppermute | solution.py:174
  40.4 1.9 fusion.21
  42.4 1.2 fusion.22
  43.7 2.0 divide_convert_fusion
  45.7 62.8 %all-gather.3.cloned.1.call-done = bf16[4096,512]{0,1:T(8,128)(2,1)} async-done(((bf16[256,512]{0,1:T(8,128)(2,1)}), bf16[4096,512]{0,1:T(8,128)(2,1)}) %all-gather.3.cloned.1.call-update) | async-done | bytes 4194320 | tf_op jit(solution)/shard_map/all_gather | solution.py:199
  108.6 45.5 %while.15 = (s32[]{:T(128)}, f32[2,4,256]{2,1,0:T(4,128)S(1)}, f32[2,4,256]{2,1,0:T(4,128)S(1)}, f32[2,4,256,128]{3,2,1,0:T(8,128)S(1)}, s32[]{:T(128)}, /*index...) while((s32[]{:T(128)}, f32[2,4,256]{2,1,0:T(4,128)S(1)}, ...), condition=%wide.region_6.9_spmd.clone, body=%wide.region_3.8_spmd.clone.sunk | while | flops 551162624 | bytes 33167600 | solution.py:216
  109.0 1.8 fusion.64
  110.9 2.0 copy-done
  112.9 1.0 fusion.65
  113.9 4.0 %fusion.66 = f32[2,4,256,128]{3,2,1,0:T(8,128)S(1)} fusion(f32[2,512,256,4]{2,1,3,0:T(8,128)} %copy-done, f32[2,4,256]{2,1,0:T(4,128)S(1)} %max.13, pred[256,512]{0,1:T(8,128)(4,1)S(1)} %broadcast_compare_fusion.3, f32[2,4,256,128]{3,2,1,0:T(8,128)S(1)} %get-tuple-element.233, f32[2,4,256]{2,1,0:T(4,128)S(1)} %bitcast.175, ...), kind=kOutput, calls=%fused_computation.14.clone.1 | convolution fusion | flops 274202624 | bytes 6701064 | tf_op jit(solution)/shard_map/while/body/hgrk,khd->hgrd/dot_general | solution.py:62
  118.1 1.8 fusion.64
  120.0 2.0 copy-done
  121.9 1.0 fusion.65
  123.0 4.0 %fusion.66 = f32[2,4,256,128]{3,2,1,0:T(8,128)S(1)} fusion(f32[2,512,256,4]{2,1,3,0:T(8,128)} %copy-done, f32[2,4,256]{2,1,0:T(4,128)S(1)} %max.13, pred[256,512]{0,1:T(8,128)(4,1)S(1)} %broadcast_compare_fusion.3, f32[2,4,256,128]{3,2,1,0:T(8,128)S(1)} %get-tuple-element.233, f32[2,4,256]{2,1,0:T(4,128)S(1)} %bitcast.175, ...), kind=kOutput, calls=%fused_computation.14.clone.1 | convolution fusion | flops 274202624 | bytes 6701064 | tf_op jit(solution)/shard_map/while/body/hgrk,khd->hgrd/dot_general | solution.py:62
  127.1 1.8 fusion.64
  129.0 2.0 copy-done
  131.0 1.0 fusion.65
  132.0 4.0 %fusion.66 = f32[2,4,256,128]{3,2,1,0:T(8,128)S(1)} fusion(f32[2,512,256,4]{2,1,3,0:T(8,128)} %copy-done, f32[2,4,256]{2,1,0:T(4,128)S(1)} %max.13, pred[256,512]{0,1:T(8,128)(4,1)S(1)} %broadcast_compare_fusion.3, f32[2,4,256,128]{3,2,1,0:T(8,128)S(1)} %get-tuple-element.233, f32[2,4,256]{2,1,0:T(4,128)S(1)} %bitcast.175, ...), kind=kOutput, calls=%fused_computation.14.clone.1 | convolution fusion | flops 274202624 | bytes 6701064 | tf_op jit(solution)/shard_map/while/body/hgrk,khd->hgrd/dot_general | solution.py:62
  136.2 1.8 fusion.64
  138.1 2.0 copy-done
  140.0 1.0 fusion.65
  141.1 4.0 %fusion.66 = f32[2,4,256,128]{3,2,1,0:T(8,128)S(1)} fusion(f32[2,512,256,4]{2,1,3,0:T(8,128)} %copy-done, f32[2,4,256]{2,1,0:T(4,128)S(1)} %max.13, pred[256,512]{0,1:T(8,128)(4,1)S(1)} %broadcast_compare_fusion.3, f32[2,4,256,128]{3,2,1,0:T(8,128)S(1)} %get-tuple-element.233, f32[2,4,256]{2,1,0:T(4,128)S(1)} %bitcast.175, ...), kind=kOutput, calls=%fused_computation.14.clone.1 | convolution fusion | flops 274202624 | bytes 6701064 | tf_op jit(solution)/shard_map/while/body/hgrk,khd->hgrd/dot_general | solution.py:62
  145.2 1.8 fusion.64
  147.1 2.0 copy-done
  149.1 1.0 fusion.65
  150.1 4.0 %fusion.66 = f32[2,4,256,128]{3,2,1,0:T(8,128)S(1)} fusion(f32[2,512,256,4]{2,1,3,0:T(8,128)} %copy-done, f32[2,4,256]{2,1,0:T(4,128)S(1)} %max.13, pred[256,512]{0,1:T(8,128)(4,1)S(1)} %broadcast_compare_fusion.3, f32[2,4,256,128]{3,2,1,0:T(8,128)S(1)} %get-tuple-element.233, f32[2,4,256]{2,1,0:T(4,128)S(1)} %bitcast.175, ...), kind=kOutput, calls=%fused_computation.14.clone.1 | convolution fusion | flops 274202624 | bytes 6701064 | tf_op jit(solution)/shard_map/while/body/hgrk,khd->hgrd/dot_general | solution.py:62
  154.8 1.0 sort.35
  155.8 1.4 collective-permute-done.7
  159.4 1.6 reshape.275
  161.1 19.8 %collective-permute-start.9 = (bf16[2048,256]{1,0:T(8,128)(2,1)S(1)}, bf16[2048,256]{1,0:T(8,128)(2,1)S(1)}, u32[]{:S(2)}, u32[]{:S(2)}) collective-permute-start(bf16[2048,256]{1,0:T(8,128)(2,1)S(1)} %copy-done.2), channel_id=1, source_target_pairs={{0,16},{8,24},{16,0},{24,8},{1,17},{9,25},{17,1},{25,9},{2,18},{10... | collective-permute-start | bytes 3145736 | tf_op jit(solution)/shard_map/ppermute | solution.py:238
  180.9 21.6 %collective-permute-done.10 = bf16[2048,256]{1,0:T(8,128)(2,1)S(1)} collective-permute-done((bf16[2048,256]{1,0:T(8,128)(2,1)S(1)}, bf16[2048,256]{1,0:T(8,128)(2,1)S(1)}, u32[]{:S(2)}, u32[]{:S(2)}) %collective-permute-start.10) | collective-permute-done | bytes 1048608 | tf_op jit(solution)/shard_map/ppermute | solution.py:238
  202.5 49.0 %collective-permute-done.9 = bf16[2048,256]{1,0:T(8,128)(2,1)S(1)} collective-permute-done((bf16[2048,256]{1,0:T(8,128)(2,1)S(1)}, bf16[2048,256]{1,0:T(8,128)(2,1)S(1)}, u32[]{:S(2)}, u32[]{:S(2)}) %collective-permute-start.9) | collective-permute-done | bytes 1048608 | tf_op jit(solution)/shard_map/ppermute | solution.py:238
  251.5 19.3 %collective-permute-done.8 = bf16[2048,256]{1,0:T(8,128)(2,1)} collective-permute-done((bf16[2048,256]{1,0:T(8,128)(2,1)S(1)}, bf16[2048,256]{1,0:T(8,128)(2,1)}, u32[]{:S(2)}, u32[]{:S(2)}) %collective-permute-start.8) | collective-permute-done | bytes 1048608 | tf_op jit(solution)/shard_map/ppermute | solution.py:238
  270.8 3.3 pad_maximum_fusion
  274.1 5.0 %gather_fusion.1 = bf16[4,2048,256]{2,1,0:T(8,128)(2,1)} fusion(bf16[4,2048,256]{2,1,0:T(8,128)(2,1)} %pad_maximum_fusion, s32[1024]{0:T(1024)S(1)} %pad_clamp_fusion), kind=kCustom, calls=%fused_computation.5 | custom fusion | bytes 8388624 | tf_op jit(solution)/shard_map/jit(_take)/gather | solution.py:241
  279.1 7.8 %fusion.17 = f32[1024,4,256]{0,2,1:T(8,128)S(1)} fusion(bf16[1024,2048]{1,0:T(8,128)(2,1)} %all-gather.5.cloned.1.call-done, bf16[4,2048,256]{2,1,0:T(8,128)(2,1)} %gather_fusion.1, pred[4]{0:T(512)(128)(4,1)S(1)} %compare_and_fusion.2), kind=kOutput, calls=%fused_computation.31 | convolution fusion | flops 4297064448 | bytes 12582916 | tf_op jit(solution)/shard_map/tk,lkc->tlc/dot_general | solution.py:250
  286.9 1.8 constant_dynamic-slice_fusion
  288.7 2.9 copy.66
  291.6 1.8 copy.65
  293.4 2.7 collective-permute-done.11
  296.1 2.6 add_convert_fusion
  298.7 26.5 %all_to_all.5 = bf16[4,256,512]{2,1,0:T(8,128)(2,1)S(1)} all-to-all(bf16[4,256,512]{2,1,0:T(8,128)(2,1)S(1)} %bitcast.156), channel_id=1, replica_groups=mesh['cz'=4,'cb'=4,'head'=2] {'cb'}, dimensions={0} | all-to-all | bytes 2097152 | tf_op jit(solution)/shard_map/all_to_all | solution.py:263
  325.8 1.4 copy.55
  (127 shorter events, 18.3 us)
Async XLA Ops:
  6.5 102.0 %all-gather.3.cloned.1.call-start = ((), (), s32[]{:S(2)}) async-start(), calls=%async_computation.1 | async-start | bytes 4456448 | tf_op jit(solution)/shard_map/all_gather | solution.py:199
  10.6 2.0 collective-permute-start
  12.5 2.9 copy-start.1
  15.1 263.9 %all-gather.5.cloned.1.call-start = ((), (), s32[]{:S(2)}) async-start(), calls=%async_computation.2 | async-start | bytes 5242880 | tf_op jit(solution)/shard_map/all_gather | solution.py:249
  18.7 20.1 %collective-permute-start.1 = (bf16[256,4,4,128]{3,0,2,1:T(8,128)(2,1)S(1)}, bf16[256,4,4,128]{3,0,2,1:T(8,128)(2,1)S(1)}, u32[]{:S(2)}, u32[]{:S(2)}) collective-permute-start(bf16[256,4,4,128]{3,0,2,1:T(8,128)(2,1)S(1)} %bitcast.154), channel_id=1, source_target_pairs={{0,1},{1,0},{2,3},{3,2},{4,5},{5,4},{6,7},{7,6},{8,9},{9,8},{10,11... | collective-permute-start | bytes 3145736 | tf_op jit(solution)/shard_map/ppermute | solution.py:139
  19.9 0.7 collective-permute-start.2
  20.6 0.9 collective-permute-start.3
  21.5 4.1 %collective-permute-start.4 = (bf16[64,2,2,128]{3,0,1,2:T(8,128)(2,1)S(1)}, bf16[64,2,2,128]{3,0,1,2:T(8,128)(2,1)S(1)}, u32[]{:S(2)}, u32[]{:S(2)}) collective-permute-start(bf16[64,2,2,128]{3,0,1,2:T(8,128)(2,1)S(1)} %broadcast_select_fusion.1), channel_id=1, source_target_pairs={{0,8},{2,10},{4,12},{6,14},{1,9},{3,11},{5,13},{7,15}} | collective-permute-start | bytes 196616 | tf_op jit(solution)/shard_map/ppermute | solution.py:174
  22.2 15.7 %collective-permute-start.6 = (bf16[256,2,2,128]{3,0,1,2:T(8,128)(2,1)S(1)}, bf16[256,2,2,128]{3,0,1,2:T(8,128)(2,1)S(1)}, u32[]{:S(2)}, u32[]{:S(2)}) collective-permute-start(bf16[256,2,2,128]{3,0,1,2:T(8,128)(2,1)S(1)} %fusion.37), channel_id=1, source_target_pairs={{0,2},{2,4},{4,6},{6,8},{8,10},{10,12},{12,14},{14,16},{16,18},{18... | collective-permute-start | bytes 786440 | tf_op jit(solution)/shard_map/ppermute | solution.py:169
  25.7 12.2 %collective-permute-start.5 = (bf16[64,2,2,128]{3,0,1,2:T(8,128)(2,1)S(1)}, bf16[64,2,2,128]{3,0,1,2:T(8,128)(2,1)S(1)}, u32[]{:S(2)}, u32[]{:S(2)}) collective-permute-start(bf16[64,2,2,128]{3,0,1,2:T(8,128)(2,1)S(1)} %broadcast_select_fusion.2), channel_id=1, source_target_pairs={{0,16},{2,18},{4,20},{6,22},{8,24},{10,26},{12,28},{14,30},{1,17},... | collective-permute-start | bytes 196616 | tf_op jit(solution)/shard_map/ppermute | solution.py:174
  42.4 1.3 copy-start.3
  110.9 2.0 copy-start
  119.9 2.0 copy-start
  129.0 2.0 copy-start
  138.0 2.0 copy-start
  147.1 2.0 copy-start
  154.6 2.7 collective-permute-start.7
  158.4 2.6 copy-start.2
  161.0 41.5 %collective-permute-start.10 = (bf16[2048,256]{1,0:T(8,128)(2,1)S(1)}, bf16[2048,256]{1,0:T(8,128)(2,1)S(1)}, u32[]{:S(2)}, u32[]{:S(2)}) collective-permute-start(bf16[2048,256]{1,0:T(8,128)(2,1)S(1)} %copy-done.2), channel_id=1, source_target_pairs={{0,24},{8,0},{16,8},{24,16},{1,25},{9,1},{17,9},{25,17},{2,26},{10... | collective-permute-start | bytes 3145736 | tf_op jit(solution)/shard_map/ppermute | solution.py:238
  161.1 90.4 %collective-permute-start.9 = (bf16[2048,256]{1,0:T(8,128)(2,1)S(1)}, bf16[2048,256]{1,0:T(8,128)(2,1)S(1)}, u32[]{:S(2)}, u32[]{:S(2)}) collective-permute-start(bf16[2048,256]{1,0:T(8,128)(2,1)S(1)} %copy-done.2), channel_id=1, source_target_pairs={{0,16},{8,24},{16,0},{24,8},{1,17},{9,25},{17,1},{25,9},{2,18},{10... | collective-permute-start | bytes 3145736 | tf_op jit(solution)/shard_map/ppermute | solution.py:238
  180.9 89.9 %collective-permute-start.8 = (bf16[2048,256]{1,0:T(8,128)(2,1)S(1)}, bf16[2048,256]{1,0:T(8,128)(2,1)}, u32[]{:S(2)}, u32[]{:S(2)}) collective-permute-start(bf16[2048,256]{1,0:T(8,128)(2,1)S(1)} %copy-done.2), channel_id=1, source_target_pairs={{0,8},{8,16},{16,24},{24,0},{1,9},{9,17},{17,25},{25,1},{2,10},{10... | collective-permute-start | bytes 3145736 | tf_op jit(solution)/shard_map/ppermute | solution.py:238
  291.6 4.5 %collective-permute-start.11 = (f32[1024,512]{1,0:T(8,128)}, f32[1024,512]{1,0:T(8,128)}, u32[]{:S(2)}, u32[]{:S(2)}) collective-permute-start(f32[1024,512]{1,0:T(8,128)} %copy.66), channel_id=1, source_target_pairs={{0,1},{1,0},{2,3},{3,2},{4,5},{5,4},{6,7},{7,6},{8,9},{9,8},{10,11... | collective-permute-start | bytes 6291464 | tf_op jit(solution)/shard_map/ppermute | solution.py:258
Sparse Core Ops, SparseCore 0:
  15.3 93.2 all-gather.2
  161.1 78.0 all-gather.4

commit v5 on v4

--- a/solution.py
+++ b/solution.py
@@ -232,13 +232,13 @@
     return home.transpose(2, 0, 1, 3).reshape(rows, kv_local * QUERY_PER_KEY * HEAD_SIZE)
 
 
-def line_gather(w_local, line):
-    me = lax.axis_index("cz")
-    pieces = [w_local] + [
-        lax.ppermute(w_local, "cz", [(i, (i + shift) % line) for i in range(line)])
-        for shift in range(1, line)
-    ]
-    return jnp.take(jnp.stack(pieces), (me - jnp.arange(line)) % line, axis=0)
+def plane_exchange(pieces, plane):
+    me = lax.axis_index("cb")
+    got = [lax.dynamic_index_in_dim(pieces, me, 0, keepdims=False)]
+    for shift in range(1, plane):
+        send = lax.dynamic_index_in_dim(pieces, (me + shift) % plane, 0, keepdims=False)
+        got.append(lax.ppermute(send, "cb", [(i, (i + shift) % plane) for i in range(plane)]))
+    return jnp.take(jnp.stack(got), (me - jnp.arange(plane)) % plane, axis=0)
 
 
 def project(attended, w_local, head_count):
@@ -247,9 +247,8 @@
     plane = lax.psum(1, "cb")
     line = lax.psum(1, "cz")
     a_plane = lax.all_gather(attended, "cb", axis=0, tiled=True)
-    part = jnp.einsum(
-        "tk,lkc->tlc", a_plane, line_gather(w_local, line), preferred_element_type=jnp.float32
-    ).reshape(a_plane.shape[0], line * col_width)
+    w_line = lax.all_gather(w_local, "cz", axis=1, tiled=True)
+    part = jnp.dot(a_plane, w_line, preferred_element_type=jnp.float32)
     if head_count == 2:
         half = part.shape[1] // 2
         me = lax.axis_index("head")
@@ -260,7 +259,7 @@
         reduced = lax.psum_scatter(part, "head", scatter_dimension=1, tiled=True).astype(jnp.bfloat16)
     per_head = line // head_count
     pieces = reduced.reshape(plane, rows, per_head * col_width)
-    got = lax.all_to_all(pieces, "cb", 0, 0, tiled=False)
+    got = plane_exchange(pieces, plane)
     return (
         got.reshape(plane, rows, per_head, col_width)
         .transpose(1, 2, 0, 3)

time: 335 us -> 287 us (0.86)
  the two profiles are of different devices: /device:TPU:16 before, /device:TPU:0 now
where the time goes in v5:
time: 287 us; the launch traced here: 286 us
  waiting for transfers between devices  204 us (71%)
  matrix products  17.8 us (6%)
  local copies, waits for them, and re-layouts  17.7 us (6%)
  starting transfers between devices  17.3 us (6%)
  other arithmetic  14.6 us (5%)
  between operations  14.4 us (5%)
    all_gather x1, waiting for transfers between devices, project(): w_line = lax.all_gather(w_local, 'cz', axis=1, tiled=True)  64.8 us
    all_gather x1, waiting for transfers between devices, duo_attend(): lax.all_gather(ret_kv.reshape(rows, ret_per * 2 * HEAD_SIZE), CTX, axis=0...  62.7 us
    all_gather x1, waiting for transfers between devices, project(): a_plane = lax.all_gather(attended, 'cb', axis=0, tiled=True)  52.5 us
    ppermute x3, waiting for transfers between devices, plane_exchange(): lax.ppermute(send, 'cb', [(i, (i + shift) % plane) for i in range(plane)])  11.6 us
    ppermute x4, starting transfers between devices, duo_attend(): got = lax.ppermute(sink_kv, CTX, pairs)  8.69 us
    dot_general x1, matrix products, project(): part = jnp.dot(a_plane, w_line, preferred_element_type=jnp.float32)  7.58 us
    dot_general x2, matrix products, update(): jnp.einsum('hgrk,khd->hgrd', weights.astype(jnp.bfloat16), value_block, p...  6.41 us
  transfers between devices with their start and end apart: 15, of which 11 were waited for; matrix products, arithmetic and copies ran while one was open for 9% of the time, Pallas kernels for 0%

profile of v5, /device:TPU:0, one launch (start us, length us, event | category | flops | bytes accessed | tf_op | source)
XLA Modules:
  0.0 286.4 jit_solution(9222968145880632521)
XLA Ops:
  7.2 0.7 convert_element_type.38
  7.9 1.1 copy.33
  9.0 1.1 copy.32
  11.2 0.7 fusion.39
  11.9 1.0 sort.34
  13.3 0.7 copy.34
  14.7 0.9 copy.35
  16.5 0.7 fusion.49
  17.2 1.4 subtract_convert_fusion
  20.1 4.8 %collective-permute-start.2 = (bf16[64,2,2,128]{3,0,1,2:T(8,128)(2,1)S(1)}, bf16[64,2,2,128]{3,0,1,2:T(8,128)(2,1)S(1)}, u32[]{:S(2)}, u32[]{:S(2)}) collective-permute-start(bf16[64,2,2,128]{3,0,1,2:T(8,128)(2,1)S(1)} %slice.68), channel_id=1, source_target_pairs={{0,2},{1,3}} | collective-permute-start | bytes 196616 | tf_op jit(solution)/shard_map/ppermute | solution.py:174
  24.9 1.9 collective-permute-done.2
  26.8 1.3 collective-permute-start.3
  28.3 1.8 collective-permute-done.3
  30.1 1.3 collective-permute-start.4
  31.5 4.2 %collective-permute-start.6 = (bf16[256,2,2,128]{3,0,1,2:T(8,128)(2,1)S(1)}, bf16[256,2,2,128]{3,0,1,2:T(8,128)(2,1)S(1)}, u32[]{:S(2)}, u32[]{:S(2)}) collective-permute-start(bf16[256,2,2,128]{3,0,1,2:T(8,128)(2,1)S(1)} %fusion.33), channel_id=1, source_target_pairs={{0,2},{2,4},{4,6},{6,8},{8,10},{10,12},{12,14},{14,16},{16,18},{18... | collective-permute-start | bytes 786440 | tf_op jit(solution)/shard_map/ppermute | solution.py:169
  35.7 1.3 collective-permute-start.5
  37.0 1.9 collective-permute-done.5
  38.9 1.4 collective-permute-done.6
  40.2 0.9 pad_maximum_fusion.5
  41.4 0.6 gather_fusion.5
  42.1 0.6 gather_fusion.3
  42.8 1.9 fusion.17
  44.7 1.2 fusion.18
  46.0 2.0 divide_convert_fusion
  48.0 62.7 %all-gather.4.cloned.1.call-done = bf16[4096,512]{0,1:T(8,128)(2,1)} async-done(((bf16[256,512]{0,1:T(8,128)(2,1)}), bf16[4096,512]{0,1:T(8,128)(2,1)}) %all-gather.4.cloned.1.call-update) | async-done | bytes 4194320 | tf_op jit(solution)/shard_map/all_gather | solution.py:199
  110.9 9.6 %while.15 = (s32[]{:T(128)}, f32[2,4,256]{2,1,0:T(4,128)S(1)}, f32[2,4,256]{2,1,0:T(4,128)S(1)}, f32[2,4,256,128]{3,2,1,0:T(8,128)S(1)}, s32[]{:T(128)}, /*index...) while((s32[]{:T(128)}, f32[2,4,256]{2,1,0:T(4,128)S(1)}, ...), condition=%wide.region_6.9_spmd.clone, body=%wide.region_3.8_spmd.clone.sunk | while | flops 551162624 | bytes 33167600 | solution.py:216
  111.3 1.8 fusion.62
  113.1 1.9 copy-done
  115.1 1.0 fusion.63
  116.1 4.4 %fusion.64 = f32[2,4,256,128]{3,2,1,0:T(8,128)S(1)} fusion(f32[2,512,256,4]{2,1,3,0:T(8,128)} %copy-done, f32[2,4,256]{2,1,0:T(4,128)S(1)} %max.13, pred[256,512]{0,1:T(8,128)(4,1)S(1)} %broadcast_compare_fusion.3, f32[2,4,256,128]{3,2,1,0:T(8,128)S(1)} %get-tuple-element.236, f32[2,4,256]{2,1,0:T(4,128)S(1)} %bitcast.175, ...), kind=kOutput, calls=%fused_computation.14.clone.1 | convolution fusion | flops 274202624 | bytes 6701064 | tf_op jit(solution)/shard_map/while/body/hgrk,khd->hgrd/dot_general | solution.py:62
  121.2 1.0 sort.35
  122.3 1.4 collective-permute-done.7
  124.0 0.7 gather_fusion
  125.0 1.3 copy.42
  126.3 64.8 %all-gather.8.cloned.1.call-done = bf16[2048,1024]{1,0:T(8,128)(2,1)} async-done(((bf16[2048,256]{1,0:T(8,128)(2,1)}), bf16[2048,1024]{1,0:T(8,128)(2,1)}) %all-gather.8.cloned.1.call-update) | async-done | bytes 4194320 | tf_op jit(solution)/shard_map/all_gather | solution.py:250
  191.1 52.5 %all-gather.6.cloned.1.call-done = bf16[1024,2048]{0,1:T(8,128)(2,1)} async-done(((bf16[256,2048]{0,1:T(8,128)(2,1)}), bf16[1024,2048]{0,1:T(8,128)(2,1)}) %all-gather.6.cloned.1.call-update) | async-done | bytes 4194320 | tf_op jit(solution)/shard_map/all_gather | solution.py:249
  243.6 7.6 %fusion.51 = f32[1024,1024]{1,0:T(8,128)S(1)} fusion(bf16[1024,2048]{0,1:T(8,128)(2,1)} %all-gather.6.cloned.1.call-done, bf16[2048,1024]{1,0:T(8,128)(2,1)} %all-gather.8.cloned.1.call-done), kind=kOutput, calls=%fused_computation.130 | convolution fusion | flops 4294967296 | bytes 12582912 | tf_op jit(solution)/shard_map/dot_general | solution.py:251
  251.2 1.9 copy-done.1
  253.1 1.5 constant_dynamic-slice_fusion.1
  254.7 4.4 %collective-permute-done.8 = f32[1024,512]{1,0:T(8,128)S(1)} collective-permute-done((f32[1024,512]{1,0:T(8,128)}, f32[1024,512]{1,0:T(8,128)S(1)}, u32[]{:S(2)}, u32[]{:S(2)}) %collective-permute-start.8) | collective-permute-done | bytes 2097184 | tf_op jit(solution)/shard_map/ppermute | solution.py:257
  259.1 1.9 add_convert_fusion
  261.1 1.5 collective-permute-start.11
  262.6 1.5 collective-permute-start.10
  264.7 5.7 %collective-permute-done.11 = bf16[256,512]{1,0:T(8,128)(2,1)S(1)} collective-permute-done((bf16[256,512]{1,0:T(8,128)(2,1)S(1)}, bf16[256,512]{1,0:T(8,128)(2,1)S(1)}, u32[]{:S(2)}, u32[]{:S(2)}) %collective-permute-start.11) | collective-permute-done | bytes 262176 | tf_op jit(solution)/shard_map/ppermute | solution.py:240
  270.3 6.0 %collective-permute-done.10 = bf16[256,512]{1,0:T(8,128)(2,1)S(1)} collective-permute-done((bf16[256,512]{1,0:T(8,128)(2,1)S(1)}, bf16[256,512]{1,0:T(8,128)(2,1)S(1)}, u32[]{:S(2)}, u32[]{:S(2)}) %collective-permute-start.10) | collective-permute-done | bytes 262176 | tf_op jit(solution)/shard_map/ppermute | solution.py:240
  276.4 0.6 gather_fusion.1
  277.4 0.9 fusion.26
  278.3 1.6 reshape.273
  (82 shorter events, 7.9 us)
Async XLA Ops:
  6.5 104.3 %all-gather.4.cloned.1.call-start = ((), (), s32[]{:S(2)}) async-start(), calls=%async_computation | async-start | bytes 4456448 | tf_op jit(solution)/shard_map/all_gather | solution.py:199
  10.6 2.4 collective-permute-start
  13.0 2.9 copy-start.2
  15.6 175.5 %all-gather.8.cloned.1.call-start = ((), (), s32[]{:S(2)}) async-start(), calls=%async_computation.2 | async-start | bytes 5242880 | tf_op jit(solution)/shard_map/all_gather | solution.py:250
  19.1 22.0 %collective-permute-start.1 = (bf16[256,4,4,128]{3,0,2,1:T(8,128)(2,1)S(1)}, bf16[256,4,4,128]{3,0,2,1:T(8,128)(2,1)S(1)}, u32[]{:S(2)}, u32[]{:S(2)}) collective-permute-start(bf16[256,4,4,128]{3,0,2,1:T(8,128)(2,1)S(1)} %bitcast.156), channel_id=1, source_target_pairs={{0,1},{1,0},{2,3},{3,2},{4,5},{5,4},{6,7},{7,6},{8,9},{9,8},{10,11... | collective-permute-start | bytes 3145736 | tf_op jit(solution)/shard_map/ppermute | solution.py:139
  19.3 224.3 %all-gather.6.cloned.1.call-start = ((), (), s32[]{:S(2)}) async-start(), calls=%async_computation.1 | async-start | bytes 5242880 | tf_op jit(solution)/shard_map/all_gather | solution.py:249
  20.1 6.7 %collective-permute-start.2 = (bf16[64,2,2,128]{3,0,1,2:T(8,128)(2,1)S(1)}, bf16[64,2,2,128]{3,0,1,2:T(8,128)(2,1)S(1)}, u32[]{:S(2)}, u32[]{:S(2)}) collective-permute-start(bf16[64,2,2,128]{3,0,1,2:T(8,128)(2,1)S(1)} %slice.68), channel_id=1, source_target_pairs={{0,2},{1,3}} | collective-permute-start | bytes 196616 | tf_op jit(solution)/shard_map/ppermute | solution.py:174
  26.8 3.3 %collective-permute-start.3 = (bf16[64,2,2,128]{3,0,1,2:T(8,128)(2,1)S(1)}, bf16[64,2,2,128]{3,0,1,2:T(8,128)(2,1)S(1)}, u32[]{:S(2)}, u32[]{:S(2)}) collective-permute-start(bf16[64,2,2,128]{3,0,1,2:T(8,128)(2,1)S(1)} %broadcast_select_fusion), channel_id=1, source_target_pairs={{0,4},{2,6},{1,5},{3,7}} | collective-permute-start | bytes 196616 | tf_op jit(solution)/shard_map/ppermute | solution.py:174
  30.1 5.5 %collective-permute-start.4 = (bf16[64,2,2,128]{3,0,1,2:T(8,128)(2,1)S(1)}, bf16[64,2,2,128]{3,0,1,2:T(8,128)(2,1)S(1)}, u32[]{:S(2)}, u32[]{:S(2)}) collective-permute-start(bf16[64,2,2,128]{3,0,1,2:T(8,128)(2,1)S(1)} %broadcast_select_fusion.1), channel_id=1, source_target_pairs={{0,8},{2,10},{4,12},{6,14},{1,9},{3,11},{5,13},{7,15}} | collective-permute-start | bytes 196616 | tf_op jit(solution)/shard_map/ppermute | solution.py:174
  31.5 8.8 %collective-permute-start.6 = (bf16[256,2,2,128]{3,0,1,2:T(8,128)(2,1)S(1)}, bf16[256,2,2,128]{3,0,1,2:T(8,128)(2,1)S(1)}, u32[]{:S(2)}, u32[]{:S(2)}) collective-permute-start(bf16[256,2,2,128]{3,0,1,2:T(8,128)(2,1)S(1)} %fusion.33), channel_id=1, source_target_pairs={{0,2},{2,4},{4,6},{6,8},{8,10},{10,12},{12,14},{14,16},{16,18},{18... | collective-permute-start | bytes 786440 | tf_op jit(solution)/shard_map/ppermute | solution.py:169
  35.7 3.2 %collective-permute-start.5 = (bf16[64,2,2,128]{3,0,1,2:T(8,128)(2,1)S(1)}, bf16[64,2,2,128]{3,0,1,2:T(8,128)(2,1)S(1)}, u32[]{:S(2)}, u32[]{:S(2)}) collective-permute-start(bf16[64,2,2,128]{3,0,1,2:T(8,128)(2,1)S(1)} %broadcast_select_fusion.2), channel_id=1, source_target_pairs={{0,16},{2,18},{4,20},{6,22},{8,24},{10,26},{12,28},{14,30},{1,17},... | collective-permute-start | bytes 196616 | tf_op jit(solution)/shard_map/ppermute | solution.py:174
  44.7 1.3 copy-start.3
  113.1 2.0 copy-start
  121.0 2.7 collective-permute-start.7
  251.2 2.0 copy-start.1
  254.7 4.4 %collective-permute-start.8 = (f32[1024,512]{1,0:T(8,128)}, f32[1024,512]{1,0:T(8,128)S(1)}, u32[]{:S(2)}, u32[]{:S(2)}) collective-permute-start(f32[1024,512]{1,0:T(8,128)} %constant_dynamic-slice_fusion.1), channel_id=1, source_target_pairs={{0,1},{1,0},{2,3},{3,2},{4,5},{5,4},{6,7},{7,6},{8,9},{9,8},{10,11... | collective-permute-start | bytes 6291464 | tf_op jit(solution)/shard_map/ppermute | solution.py:257
  261.1 9.2 %collective-permute-start.11 = (bf16[256,512]{1,0:T(8,128)(2,1)S(1)}, bf16[256,512]{1,0:T(8,128)(2,1)S(1)}, u32[]{:S(2)}, u32[]{:S(2)}) collective-permute-start(bf16[256,512]{1,0:T(8,128)(2,1)S(1)} %get-tuple-element.136), channel_id=1, source_target_pairs={{0,6},{2,0},{4,2},{6,4},{1,7},{3,1},{5,3},{7,5},{8,14},{10,8},{12,... | collective-permute-start | bytes 786440 | tf_op jit(solution)/shard_map/ppermute | solution.py:240
  262.6 13.7 %collective-permute-start.10 = (bf16[256,512]{1,0:T(8,128)(2,1)S(1)}, bf16[256,512]{1,0:T(8,128)(2,1)S(1)}, u32[]{:S(2)}, u32[]{:S(2)}) collective-permute-start(bf16[256,512]{1,0:T(8,128)(2,1)S(1)} %get-tuple-element.137), channel_id=1, source_target_pairs={{0,4},{2,6},{4,0},{6,2},{1,5},{3,7},{5,1},{7,3},{8,12},{10,14},{12... | collective-permute-start | bytes 786440 | tf_op jit(solution)/shard_map/ppermute | solution.py:240
  264.1 12.2 %collective-permute-start.9 = (bf16[256,512]{1,0:T(8,128)(2,1)S(1)}, bf16[256,512]{1,0:T(8,128)(2,1)S(1)}, u32[]{:S(2)}, u32[]{:S(2)}) collective-permute-start(bf16[256,512]{1,0:T(8,128)(2,1)S(1)} %get-tuple-element.138), channel_id=1, source_target_pairs={{0,2},{2,4},{4,6},{6,0},{1,3},{3,5},{5,7},{7,1},{8,10},{10,12},{12... | collective-permute-start | bytes 786440 | tf_op jit(solution)/shard_map/ppermute | solution.py:240
Sparse Core Ops, SparseCore 0:
  15.7 95.0 all-gather.3
  112.3 78.7 all-gather.7
  192.9 50.6 all-gather.5

commit v6 on v5

--- a/solution.py
+++ b/solution.py
@@ -199,7 +199,7 @@
     ret_shard = lax.all_gather(ret_kv.reshape(rows, ret_per * 2 * HEAD_SIZE), CTX, axis=0, tiled=True)
     ret_shard = ret_shard.reshape(ctx_count * rows, ret_per, 2, HEAD_SIZE)
     q_ret = jnp.take(q_all, ret_ids, axis=1)
-    sub_rows = math.gcd(ctx_count * rows, 512)
+    sub_rows = math.gcd(ctx_count * rows, 2048)
     turn_count = (ctx_index * rows + rows + sub_rows - 1) // sub_rows
 
     def one_turn(j, state):
@@ -232,6 +232,16 @@
     return home.transpose(2, 0, 1, 3).reshape(rows, kv_local * QUERY_PER_KEY * HEAD_SIZE)
 
 
+def plane_gather(block, plane):
+    me = lax.axis_index("cb")
+    got = [block] + [
+        lax.ppermute(block, "cb", [(i, (i + shift) % plane) for i in range(plane)])
+        for shift in range(1, plane)
+    ]
+    ordered = jnp.take(jnp.stack(got), (me - jnp.arange(plane)) % plane, axis=0)
+    return ordered.reshape(plane * block.shape[0], block.shape[1])
+
+
 def plane_exchange(pieces, plane):
     me = lax.axis_index("cb")
     got = [lax.dynamic_index_in_dim(pieces, me, 0, keepdims=False)]
@@ -246,7 +256,7 @@
     col_width = w_local.shape[1]
     plane = lax.psum(1, "cb")
     line = lax.psum(1, "cz")
-    a_plane = lax.all_gather(attended, "cb", axis=0, tiled=True)
+    a_plane = plane_gather(attended, plane)
     w_line = lax.all_gather(w_local, "cz", axis=1, tiled=True)
     part = jnp.dot(a_plane, w_line, preferred_element_type=jnp.float32)
     if head_count == 2:

time: 287 us -> 266 us (0.927)
  the two profiles are of different devices: /device:TPU:0 before, /device:TPU:16 now
where the time goes in v6:
time: 266 us; the launch traced here: 265 us
  waiting for transfers between devices  138 us (52%)
  matrix products  38.3 us (14%)
  other arithmetic  31.4 us (12%)
  local copies, waits for them, and re-layouts  30.3 us (11%)
  between operations  14.7 us (6%)
  starting transfers between devices  12.5 us (5%)
    all_gather x1, waiting for transfers between devices, duo_attend(): lax.all_gather(ret_kv.reshape(rows, ret_per * 2 * HEAD_SIZE), CTX, axis=0...  63 us
    ppermute x3, waiting for transfers between devices, plane_gather(): lax.ppermute(block, 'cb', [(i, (i + shift) % plane) for i in range(plane)])  46 us
    dot_general x3, matrix products, update(): jnp.einsum('hgrk,khd->hgrd', weights.astype(jnp.bfloat16), value_block, p...  20.5 us
    ppermute x3, waiting for transfers between devices, plane_exchange(): lax.ppermute(send, 'cb', [(i, (i + shift) % plane) for i in range(plane)])  11.6 us
    gather x2, local copies, waits for them, and re-layouts, plane_gather(): ordered = jnp.take(jnp.stack(got), (me - jnp.arange(plane)) % plane, axis=0)  11.2 us
    ppermute x4, waiting for transfers between devices, duo_attend(): got = lax.ppermute(sink_kv, CTX, pairs)  11 us
    dot_general x3, matrix products, update(): jnp.einsum('rhgd,khd->hgrk', query_rows, key_block, preferred_element_typ...  10.3 us
    reduce_sum x3, other arithmetic, update(): totals = totals * rescale + jnp.sum(weights, axis=-1)  9.27 us
  transfers between devices with their start and end apart: 17, of which 9 were waited for; matrix products, arithmetic and copies ran while one was open for 28% of the time, Pallas kernels for 0%

profile of v6, /device:TPU:16, one launch (start us, length us, event | category | flops | bytes accessed | tf_op | source)
XLA Modules:
  0.0 265.2 jit_solution(15255686371154739626)
XLA Ops:
  7.2 0.7 convert_element_type.38
  7.9 1.1 copy.35
  9.0 1.1 copy.34
  10.7 0.7 fusion.39
  11.4 1.0 sort.34
  14.3 0.9 copy.37
  16.7 1.4 subtract_convert_fusion
  22.3 3.4 %collective-permute-start.6 = (bf16[256,2,2,128]{3,0,1,2:T(8,128)(2,1)S(1)}, bf16[256,2,2,128]{3,0,1,2:T(8,128)(2,1)S(1)}, u32[]{:S(2)}, u32[]{:S(2)}) collective-permute-start(bf16[256,2,2,128]{3,0,1,2:T(8,128)(2,1)S(1)} %fusion.33), channel_id=1, source_target_pairs={{0,2},{2,4},{4,6},{6,8},{8,10},{10,12},{12,14},{14,16},{16,18},{18... | collective-permute-start | bytes 786440 | tf_op jit(solution)/shard_map/ppermute | solution.py:169
  25.8 1.3 collective-permute-start.5
  27.1 11.0 %collective-permute-done.5 = bf16[64,2,2,128]{3,0,1,2:T(8,128)(2,1)S(1)} collective-permute-done((bf16[64,2,2,128]{3,0,1,2:T(8,128)(2,1)S(1)}, bf16[64,2,2,128]{3,0,1,2:T(8,128)(2,1)S(1)}, u32[]{:S(2)}, u32[]{:S(2)}) %collective-permute-start.5) | collective-permute-done | bytes 65568 | tf_op jit(solution)/shard_map/ppermute | solution.py:174
  38.1 0.9 pad_maximum_fusion.6
  40.6 1.9 fusion.17
  42.6 1.2 fusion.18
  43.9 2.0 divide_convert_fusion
  45.9 63.0 %all-gather.3.cloned.1.call-done = bf16[4096,512]{0,1:T(8,128)(2,1)} async-done(((bf16[256,512]{0,1:T(8,128)(2,1)}), bf16[4096,512]{0,1:T(8,128)(2,1)}) %all-gather.3.cloned.1.call-update) | async-done | bytes 4194320 | tf_op jit(solution)/shard_map/all_gather | solution.py:199
  109.0 40.3 %while.15 = (s32[]{:T(128)}, f32[2,4,256]{2,1,0:T(4,128)S(1)}, f32[2,4,256]{2,1,0:T(4,128)S(1)}, f32[2,4,256,128]{3,2,1,0:T(8,128)S(1)}, s32[]{:T(128)}, /*index...) while((s32[]{:T(128)}, f32[2,4,256]{2,1,0:T(4,128)S(1)}, ...), condition=%wide.region_6.9_spmd.clone, body=%wide.region_3.8_spmd.clone.sunk | while | flops 2203064576 | bytes 124405992 | solution.py:216
  109.7 4.2 %fusion.62 = (f32[2,4,256]{2,1,0:T(4,128)S(1)}, f32[2,2048,256,4]{2,1,3,0:T(8,128)S(1)}) fusion(pred[256,2048]{0,1:T(8,128)(4,1)S(1)} %broadcast_compare_fusion.3, bf16[256,2,4,128]{3,0,2,1:T(8,128)(2,1)S(1)} %get-tuple-element.252, bf16[4096,2,2,128]{0,3,2,1:T(8,128)(2,1)} %get-tuple-element.251, s32[]{:T(128)S(6)} %select_n.371), kind=kOutput, calls=%fused_computation.10.clone.1 | convolution fusion | flops 1086322688 | bytes 18882564 | tf_op jit(solution)/shard_map/while/body/rhgd,khd->hgrk/dot_general | solution.py:53
  113.9 4.1 %fusion.63 = f32[2,4,256]{2,1,0:T(4,128)S(1)} fusion(f32[2,2048,256,4]{2,1,3,0:T(8,128)S(1)} %get-tuple-element.217, f32[2,4,256]{2,1,0:T(4,128)S(1)} %max.13, pred[256,2048]{0,1:T(8,128)(4,1)S(1)} %broadcast_compare_fusion.3), kind=kLoop, calls=%fused_computation.12.clone.1 | loop fusion | flops 20969472 | bytes 17317888 | tf_op jit(solution)/shard_map/while/body/reduce_sum | solution.py:61
  118.0 2.3 copy-done
  120.3 9.3 %fusion.64 = f32[2,4,256,128]{3,2,1,0:T(8,128)S(1)} fusion(f32[2,2048,256,4]{2,1,3,0:T(8,128)} %copy-done, f32[2,4,256]{2,1,0:T(4,128)S(1)} %max.13, pred[256,2048]{0,1:T(8,128)(4,1)S(1)} %broadcast_compare_fusion.3, bf16[4096,2,2,128]{0,3,2,1:T(8,128)(2,1)} %get-tuple-element.251, s32[]{:T(128)S(6)} %select_n.371, s32[]{:T(128)S(6)} %add.327, ...), kind=kOutput, calls=%fused_computation.15.clone.1 | convolution fusion | flops 1095237632 | bytes 20463624 | tf_op jit(solution)/shard_map/while/body/hgrk,khd->hgrd/dot_general | solution.py:62
  130.2 4.2 %fusion.62 = (f32[2,4,256]{2,1,0:T(4,128)S(1)}, f32[2,2048,256,4]{2,1,3,0:T(8,128)S(1)}) fusion(pred[256,2048]{0,1:T(8,128)(4,1)S(1)} %broadcast_compare_fusion.3, bf16[256,2,4,128]{3,0,2,1:T(8,128)(2,1)S(1)} %get-tuple-element.252, bf16[4096,2,2,128]{0,3,2,1:T(8,128)(2,1)} %get-tuple-element.251, s32[]{:T(128)S(6)} %select_n.371), kind=kOutput, calls=%fused_computation.10.clone.1 | convolution fusion | flops 1086322688 | bytes 18882564 | tf_op jit(solution)/shard_map/while/body/rhgd,khd->hgrk/dot_general | solution.py:53
  134.4 4.1 %fusion.63 = f32[2,4,256]{2,1,0:T(4,128)S(1)} fusion(f32[2,2048,256,4]{2,1,3,0:T(8,128)S(1)} %get-tuple-element.217, f32[2,4,256]{2,1,0:T(4,128)S(1)} %max.13, pred[256,2048]{0,1:T(8,128)(4,1)S(1)} %broadcast_compare_fusion.3), kind=kLoop, calls=%fused_computation.12.clone.1 | loop fusion | flops 20969472 | bytes 17317888 | tf_op jit(solution)/shard_map/while/body/reduce_sum | solution.py:61
  138.5 1.7 copy-done
  140.2 9.1 %fusion.64 = f32[2,4,256,128]{3,2,1,0:T(8,128)S(1)} fusion(f32[2,2048,256,4]{2,1,3,0:T(8,128)} %copy-done, f32[2,4,256]{2,1,0:T(4,128)S(1)} %max.13, pred[256,2048]{0,1:T(8,128)(4,1)S(1)} %broadcast_compare_fusion.3, bf16[4096,2,2,128]{0,3,2,1:T(8,128)(2,1)} %get-tuple-element.251, s32[]{:T(128)S(6)} %select_n.371, s32[]{:T(128)S(6)} %add.327, ...), kind=kOutput, calls=%fused_computation.15.clone.1 | convolution fusion | flops 1095237632 | bytes 20463624 | tf_op jit(solution)/shard_map/while/body/hgrk,khd->hgrd/dot_general | solution.py:62
  149.7 1.1 pad_maximum_fusion.4
  150.9 1.0 sort.35
  152.0 1.6 collective-permute-done.7
  153.9 0.7 gather_fusion
  155.4 0.8 collective-permute-start.10
  156.8 0.7 collective-permute-start.8
  157.6 23.9 %collective-permute-done.10 = bf16[256,2048]{0,1:T(8,128)(2,1)S(1)} collective-permute-done((bf16[256,2048]{0,1:T(8,128)(2,1)S(1)}, bf16[256,2048]{0,1:T(8,128)(2,1)S(1)}, u32[]{:S(2)}, u32[]{:S(2)}) %collective-permute-start.10) | collective-permute-done | bytes 1048608 | tf_op jit(solution)/shard_map/ppermute | solution.py:238
  181.5 22.1 %collective-permute-done.9 = bf16[256,2048]{0,1:T(8,128)(2,1)S(1)} collective-permute-done((bf16[256,2048]{0,1:T(8,128)(2,1)S(1)}, bf16[256,2048]{0,1:T(8,128)(2,1)S(1)}, u32[]{:S(2)}, u32[]{:S(2)}) %collective-permute-start.9) | collective-permute-done | bytes 1048608 | tf_op jit(solution)/shard_map/ppermute | solution.py:238
  203.6 3.2 %pad_maximum_fusion = bf16[4,256,2048]{1,2,0:T(8,128)(2,1)} fusion(bf16[1,256,2048]{1,2,0:T(8,128)(2,1)S(1)} %bitcast.177, bf16[1,256,2048]{1,2,0:T(8,128)(2,1)S(1)} %bitcast.178, bf16[1,256,2048]{1,2,0:T(8,128)(2,1)} %bitcast.35, bf16[1,256,2048]{1,2,0:T(8,128)(2,1)S(1)} %bitcast.169), kind=kLoop, calls=%fused_computation.31 | loop fusion | flops 6291456 | bytes 8388608 | tf_op jit(solution)/shard_map/stack | solution.py:241
  206.8 5.0 %gather_fusion.1 = bf16[4,256,2048]{1,2,0:T(8,128)(2,1)} fusion(bf16[4,256,2048]{1,2,0:T(8,128)(2,1)} %pad_maximum_fusion, s32[1024]{0:T(1024)S(1)} %pad_clamp_fusion), kind=kCustom, calls=%fused_computation.5 | custom fusion | bytes 8388624 | tf_op jit(solution)/shard_map/jit(_take)/gather | solution.py:241
  211.8 6.3 %copy.46 = bf16[4,256,2048]{2,1,0:T(8,128)(2,1)} copy(bf16[4,256,2048]{1,2,0:T(8,128)(2,1)} %gather_fusion.1) | data formatting | bytes 8388608 | tf_op jit(solution)/shard_map/jit(_take)/gather | solution.py:241
  218.1 4.6 %bitcast_select_fusion.2 = bf16[1024,2048]{1,0:T(8,128)(2,1)} fusion(bf16[4,256,2048]{2,1,0:T(8,128)(2,1)} %copy.46, pred[1024]{0:T(1024)(128)(4,1)S(1)} %broadcast_in_dim.116), kind=kLoop, calls=%fused_computation.32 | loop fusion | flops 2097152 | bytes 8389632 | tf_op jit(solution)/shard_map/jit(_take)/select_n | solution.py:241
  222.7 7.5 %fusion.51 = f32[1024,1024]{1,0:T(8,128)S(1)} fusion(bf16[1024,2048]{1,0:T(8,128)(2,1)} %bitcast_select_fusion.2, bf16[2048,1024]{1,0:T(8,128)(2,1)} %all-gather.5.cloned.1.call-done), kind=kOutput, calls=%fused_computation.133 | convolution fusion | flops 4294967296 | bytes 12582912 | tf_op jit(solution)/shard_map/dot_general | solution.py:261
  230.2 1.9 copy-done.1
  232.1 1.5 constant_dynamic-slice_fusion.1
  233.7 4.4 %collective-permute-done.11 = f32[1024,512]{1,0:T(8,128)S(1)} collective-permute-done((f32[1024,512]{1,0:T(8,128)}, f32[1024,512]{1,0:T(8,128)S(1)}, u32[]{:S(2)}, u32[]{:S(2)}) %collective-permute-start.11) | collective-permute-done | bytes 2097184 | tf_op jit(solution)/shard_map/ppermute | solution.py:267
  238.0 1.9 add_convert_fusion
  240.1 1.0 collective-permute-start.14
  241.1 0.9 collective-permute-start.13
  242.0 1.2 collective-permute-start.12
  243.3 6.1 %collective-permute-done.14 = bf16[256,512]{1,0:T(8,128)(2,1)S(1)} collective-permute-done((bf16[256,512]{1,0:T(8,128)(2,1)S(1)}, bf16[256,512]{1,0:T(8,128)(2,1)S(1)}, u32[]{:S(2)}, u32[]{:S(2)}) %collective-permute-start.14) | collective-permute-done | bytes 262176 | tf_op jit(solution)/shard_map/ppermute | solution.py:250
  249.3 5.5 %collective-permute-done.13 = bf16[256,512]{1,0:T(8,128)(2,1)S(1)} collective-permute-done((bf16[256,512]{1,0:T(8,128)(2,1)S(1)}, bf16[256,512]{1,0:T(8,128)(2,1)S(1)}, u32[]{:S(2)}, u32[]{:S(2)}) %collective-permute-start.13) | collective-permute-done | bytes 262176 | tf_op jit(solution)/shard_map/ppermute | solution.py:250
  255.9 0.9 fusion.26
  256.8 1.6 reshape.276
  (102 shorter events, 14.3 us)
Async XLA Ops:
  6.5 102.4 %all-gather.3.cloned.1.call-start = ((), (), s32[]{:S(2)}) async-start(), calls=%async_computation | async-start | bytes 4456448 | tf_op jit(solution)/shard_map/all_gather | solution.py:199
  10.6 2.0 collective-permute-start
  12.5 2.9 %copy-start.2 = (bf16[256,2048]{1,0:T(8,128)(2,1)S(1)}, bf16[256,2048]{1,0:T(8,128)(2,1)}, u32[]{:S(2)}) copy-start(bf16[256,2048]{1,0:T(8,128)(2,1)} %param.13) | copy-start | bytes 3145732
  15.2 207.5 %all-gather.5.cloned.1.call-start = ((), (), s32[]{:S(2)}) async-start(), calls=%async_computation.1 | async-start | bytes 5242880 | tf_op jit(solution)/shard_map/all_gather | solution.py:260
  18.7 20.3 %collective-permute-start.1 = (bf16[256,4,4,128]{3,0,2,1:T(8,128)(2,1)S(1)}, bf16[256,4,4,128]{3,0,2,1:T(8,128)(2,1)S(1)}, u32[]{:S(2)}, u32[]{:S(2)}) collective-permute-start(bf16[256,4,4,128]{3,0,2,1:T(8,128)(2,1)S(1)} %bitcast.163), channel_id=1, source_target_pairs={{0,1},{1,0},{2,3},{3,2},{4,5},{5,4},{6,7},{7,6},{8,9},{9,8},{10,11... | collective-permute-start | bytes 3145736 | tf_op jit(solution)/shard_map/ppermute | solution.py:139
  20.0 0.7 collective-permute-start.2
  20.7 0.9 collective-permute-start.3
  21.6 4.1 %collective-permute-start.4 = (bf16[64,2,2,128]{3,0,1,2:T(8,128)(2,1)S(1)}, bf16[64,2,2,128]{3,0,1,2:T(8,128)(2,1)S(1)}, u32[]{:S(2)}, u32[]{:S(2)}) collective-permute-start(bf16[64,2,2,128]{3,0,1,2:T(8,128)(2,1)S(1)} %broadcast_select_fusion.1), channel_id=1, source_target_pairs={{0,8},{2,10},{4,12},{6,14},{1,9},{3,11},{5,13},{7,15}} | collective-permute-start | bytes 196616 | tf_op jit(solution)/shard_map/ppermute | solution.py:174
  22.3 15.8 %collective-permute-start.6 = (bf16[256,2,2,128]{3,0,1,2:T(8,128)(2,1)S(1)}, bf16[256,2,2,128]{3,0,1,2:T(8,128)(2,1)S(1)}, u32[]{:S(2)}, u32[]{:S(2)}) collective-permute-start(bf16[256,2,2,128]{3,0,1,2:T(8,128)(2,1)S(1)} %fusion.33), channel_id=1, source_target_pairs={{0,2},{2,4},{4,6},{6,8},{8,10},{10,12},{12,14},{14,16},{16,18},{18... | collective-permute-start | bytes 786440 | tf_op jit(solution)/shard_map/ppermute | solution.py:169
  25.8 12.3 %collective-permute-start.5 = (bf16[64,2,2,128]{3,0,1,2:T(8,128)(2,1)S(1)}, bf16[64,2,2,128]{3,0,1,2:T(8,128)(2,1)S(1)}, u32[]{:S(2)}, u32[]{:S(2)}) collective-permute-start(bf16[64,2,2,128]{3,0,1,2:T(8,128)(2,1)S(1)} %broadcast_select_fusion.2), channel_id=1, source_target_pairs={{0,16},{2,18},{4,20},{6,22},{8,24},{10,26},{12,28},{14,30},{1,17},... | collective-permute-start | bytes 196616 | tf_op jit(solution)/shard_map/ppermute | solution.py:174
  42.6 1.3 copy-start.3
  113.9 6.4 %copy-start = (f32[2,2048,256,4]{2,1,3,0:T(8,128)}, f32[2,2048,256,4]{2,1,3,0:T(8,128)S(1)}, u32[]{:S(2)}) copy-start(f32[2,2048,256,4]{2,1,3,0:T(8,128)S(1)} %get-tuple-element.217) | copy-start | bytes 50331652 | tf_op jit(solution)/shard_map/while
  134.4 5.7 %copy-start = (f32[2,2048,256,4]{2,1,3,0:T(8,128)}, f32[2,2048,256,4]{2,1,3,0:T(8,128)S(1)}, u32[]{:S(2)}) copy-start(f32[2,2048,256,4]{2,1,3,0:T(8,128)S(1)} %get-tuple-element.217) | copy-start | bytes 50331652 | tf_op jit(solution)/shard_map/while
  150.7 2.9 %collective-permute-start.7 = (bf16[4,4,256,128]{3,2,1,0:T(8,128)(2,1)}, bf16[4,4,256,128]{3,2,1,0:T(8,128)(2,1)S(1)}, u32[]{:S(2)}, u32[]{:S(2)}) collective-permute-start(bf16[4,4,256,128]{3,2,1,0:T(8,128)(2,1)} %pad_maximum_fusion.4), channel_id=1, source_target_pairs={{0,1},{1,0},{2,3},{3,2},{4,5},{5,4},{6,7},{7,6},{8,9},{9,8},{10,11... | collective-permute-start | bytes 3145736 | tf_op jit(solution)/shard_map/ppermute | solution.py:139
  155.4 26.1 %collective-permute-start.10 = (bf16[256,2048]{0,1:T(8,128)(2,1)S(1)}, bf16[256,2048]{0,1:T(8,128)(2,1)S(1)}, u32[]{:S(2)}, u32[]{:S(2)}) collective-permute-start(bf16[256,2048]{0,1:T(8,128)(2,1)S(1)} %bitcast.166), channel_id=1, source_target_pairs={{0,6},{2,0},{4,2},{6,4},{1,7},{3,1},{5,3},{7,5},{8,14},{10,8},{12,... | collective-permute-start | bytes 3145736 | tf_op jit(solution)/shard_map/ppermute | solution.py:238
  156.2 47.4 %collective-permute-start.9 = (bf16[256,2048]{0,1:T(8,128)(2,1)S(1)}, bf16[256,2048]{0,1:T(8,128)(2,1)S(1)}, u32[]{:S(2)}, u32[]{:S(2)}) collective-permute-start(bf16[256,2048]{0,1:T(8,128)(2,1)S(1)} %bitcast.167), channel_id=1, source_target_pairs={{0,4},{2,6},{4,0},{6,2},{1,5},{3,7},{5,1},{7,3},{8,12},{10,14},{12... | collective-permute-start | bytes 3145736 | tf_op jit(solution)/shard_map/ppermute | solution.py:238
  156.8 46.8 %collective-permute-start.8 = (bf16[256,2048]{0,1:T(8,128)(2,1)S(1)}, bf16[256,2048]{0,1:T(8,128)(2,1)}, u32[]{:S(2)}, u32[]{:S(2)}) collective-permute-start(bf16[256,2048]{0,1:T(8,128)(2,1)S(1)} %bitcast.168), channel_id=1, source_target_pairs={{0,2},{2,4},{4,6},{6,0},{1,3},{3,5},{5,7},{7,1},{8,10},{10,12},{12... | collective-permute-start | bytes 3145736 | tf_op jit(solution)/shard_map/ppermute | solution.py:238
  230.2 2.0 copy-start.1
  233.7 4.4 %collective-permute-start.11 = (f32[1024,512]{1,0:T(8,128)}, f32[1024,512]{1,0:T(8,128)S(1)}, u32[]{:S(2)}, u32[]{:S(2)}) collective-permute-start(f32[1024,512]{1,0:T(8,128)} %constant_dynamic-slice_fusion.1), channel_id=1, source_target_pairs={{0,1},{1,0},{2,3},{3,2},{4,5},{5,4},{6,7},{7,6},{8,9},{9,8},{10,11... | collective-permute-start | bytes 6291464 | tf_op jit(solution)/shard_map/ppermute | solution.py:267
  240.1 9.2 %collective-permute-start.14 = (bf16[256,512]{1,0:T(8,128)(2,1)S(1)}, bf16[256,512]{1,0:T(8,128)(2,1)S(1)}, u32[]{:S(2)}, u32[]{:S(2)}) collective-permute-start(bf16[256,512]{1,0:T(8,128)(2,1)S(1)} %get-tuple-element.136), channel_id=1, source_target_pairs={{0,6},{2,0},{4,2},{6,4},{1,7},{3,1},{5,3},{7,5},{8,14},{10,8},{12,... | collective-permute-start | bytes 786440 | tf_op jit(solution)/shard_map/ppermute | solution.py:250
  241.1 13.7 %collective-permute-start.13 = (bf16[256,512]{1,0:T(8,128)(2,1)S(1)}, bf16[256,512]{1,0:T(8,128)(2,1)S(1)}, u32[]{:S(2)}, u32[]{:S(2)}) collective-permute-start(bf16[256,512]{1,0:T(8,128)(2,1)S(1)} %get-tuple-element.137), channel_id=1, source_target_pairs={{0,4},{2,6},{4,0},{6,2},{1,5},{3,7},{5,1},{7,3},{8,12},{10,14},{12... | collective-permute-start | bytes 786440 | tf_op jit(solution)/shard_map/ppermute | solution.py:250
  242.0 12.8 %collective-permute-start.12 = (bf16[256,512]{1,0:T(8,128)(2,1)S(1)}, bf16[256,512]{1,0:T(8,128)(2,1)S(1)}, u32[]{:S(2)}, u32[]{:S(2)}) collective-permute-start(bf16[256,512]{1,0:T(8,128)(2,1)S(1)} %get-tuple-element.138), channel_id=1, source_target_pairs={{0,2},{2,4},{4,6},{6,0},{1,3},{3,5},{5,7},{7,1},{8,10},{10,12},{12... | collective-permute-start | bytes 786440 | tf_op jit(solution)/shard_map/ppermute | solution.py:250
Sparse Core Ops, SparseCore 0:
  15.3 93.5 all-gather.2
  110.4 78.7 all-gather.4

commit v7 on v6

--- a/solution.py
+++ b/solution.py
@@ -216,20 +216,54 @@
     _, ret_totals, ret_accum = lax.fori_loop(0, turn_count, one_turn, start)
     ret_out = ret_accum / ret_totals[..., None]
 
-    done = jnp.concatenate([ret_out, run_out], axis=0).astype(jnp.bfloat16)
-    slots = head_exchange(done, head_count).reshape(kv_total, QUERY_PER_KEY, rows, HEAD_SIZE)
-    placed = jnp.concatenate(
-        [
-            jnp.concatenate(
-                [order[kv_total - ret_count + h * ret_per : kv_total - ret_count + (h + 1) * ret_per],
-                 order[h * run_per : (h + 1) * run_per]]
-            )
-            for h in range(head_count)
-        ]
-    )
-    slot_of = jnp.argsort(placed)
-    home = jnp.take(slots, lax.dynamic_slice_in_dim(slot_of, me * kv_local, kv_local), axis=0)
-    return home.transpose(2, 0, 1, 3).reshape(rows, kv_local * QUERY_PER_KEY * HEAD_SIZE)
+    return (
+        ret_out.transpose(2, 0, 1, 3).reshape(rows, ret_per * QUERY_PER_KEY * HEAD_SIZE).astype(jnp.bfloat16),
+        run_out.transpose(2, 0, 1, 3).reshape(rows, run_per * QUERY_PER_KEY * HEAD_SIZE).astype(jnp.bfloat16),
+        jnp.concatenate([ret_ids, run_ids]),
+    )
+
+
+def plane_pieces(block, plane):
+    return [block] + [
+        lax.ppermute(block, "cb", [(i, (i + shift) % plane) for i in range(plane)])
+        for shift in range(1, plane)
+    ]
+
+
+def project_assigned(att_ret, att_run, ids, w_local, head_count):
+    rows = att_ret.shape[0]
+    col_width = w_local.shape[1]
+    plane = lax.psum(1, "cb")
+    line = lax.psum(1, "cz")
+    group_rows = QUERY_PER_KEY * HEAD_SIZE
+    w_all = head_exchange(w_local.reshape(-1, group_rows, col_width), head_count)
+    w_all = w_all.reshape(-1, group_rows, col_width)
+    w_mine = jnp.take(w_all, ids, axis=0).reshape(-1, col_width)
+    w_line = lax.all_gather(w_mine, "cz", axis=1, tiled=True)
+    ret_rows = att_ret.shape[1]
+    run_stack = jnp.concatenate(plane_pieces(att_run, plane), axis=0)
+    ret_stack = jnp.concatenate(plane_pieces(att_ret, plane), axis=0)
+    part = jnp.dot(ret_stack, w_line[:ret_rows], preferred_element_type=jnp.float32) + jnp.dot(
+        run_stack, w_line[ret_rows:], preferred_element_type=jnp.float32
+    )
+    half = part.shape[1] // 2
+    me = lax.axis_index("head")
+    mine = lax.dynamic_slice_in_dim(part, me * half, half, axis=1)
+    other = lax.dynamic_slice_in_dim(part, (1 - me) * half, half, axis=1)
+    reduced = (mine + lax.ppermute(other, "head", [(0, 1), (1, 0)])).astype(jnp.bfloat16)
+    me_cb = lax.axis_index("cb")
+    blocks = reduced.reshape(plane, rows, half)
+    got = [blocks[0]] + [
+        lax.ppermute(blocks[(-shift) % plane], "cb", [(i, (i + shift) % plane) for i in range(plane)])
+        for shift in range(1, plane)
+    ]
+    got = jnp.take(jnp.stack(got), (me_cb - jnp.arange(plane)) % plane, axis=0)
+    per_head = line // head_count
+    return (
+        got.reshape(plane, rows, per_head, col_width)
+        .transpose(1, 2, 0, 3)
+        .reshape(rows, per_head * plane * col_width)
+    )
 
 
 def plane_gather(block, plane):
@@ -296,9 +330,10 @@
         and ret_count < kv_total
         and rows_dev >= max(SINK, WINDOW)
     ):
-        attended = duo_attend(
+        att_ret, att_run, ids = duo_attend(
             rotated_query, rotated_key, values, retrieval, kv_local, head_count, ctx_index
         )
+        return project_assigned(att_ret, att_run, ids, out_weight, head_count)
     else:
         attended = attend(((rotated_query, own_index),), rotated_key, values, flags, kv_local)[0]
     return project(attended, out_weight, head_count)

time: 266 us -> 240 us (0.902)
  the two profiles are of different devices: /device:TPU:16 before, /device:TPU:0 now
where the time goes in v7:
time: 240 us; the launch traced here: 239 us
  waiting for transfers between devices  121 us (50%)
  matrix products  29.5 us (12%)
  starting transfers between devices  27.3 us (11%)
  other arithmetic  23.9 us (10%)
  local copies, waits for them, and re-layouts  22.6 us (9%)
  between operations  14.7 us (6%)
    all_gather x1, waiting for transfers between devices, project_assigned(): w_line = lax.all_gather(w_mine, 'cz', axis=1, tiled=True)  57 us
    all_gather x1, waiting for transfers between devices, duo_attend(): lax.all_gather(ret_kv.reshape(rows, ret_per * 2 * HEAD_SIZE), CTX, axis=0...  40.9 us
    dot_general x2, matrix products, update(): jnp.einsum('hgrk,khd->hgrd', weights.astype(jnp.bfloat16), value_block, p...  13.9 us
    ppermute x3, waiting for transfers between devices, project_assigned(): lax.ppermute(blocks[-shift % plane], 'cb', [(i, (i + shift) % plane) for...  10.5 us
    ppermute x6, starting transfers between devices, plane_pieces(): lax.ppermute(block, 'cb', [(i, (i + shift) % plane) for i in range(plane)])  8.95 us
    ppermute x4, starting transfers between devices, duo_attend(): got = lax.ppermute(sink_kv, CTX, pairs)  8.35 us
    ppermute x4, waiting for transfers between devices, duo_attend(): got = lax.ppermute(sink_kv, CTX, pairs)  6.47 us
    dot_general x2, matrix products, update(): jnp.einsum('rhgd,khd->hgrk', query_rows, key_block, preferred_element_typ...  6.32 us
  transfers between devices with their start and end apart: 20, of which 9 were waited for; matrix products, arithmetic and copies ran while one was open for 21% of the time, Pallas kernels for 0%

profile of v7, /device:TPU:0, one launch (start us, length us, event | category | flops | bytes accessed | tf_op | source)
XLA Modules:
  0.0 239.1 jit_solution(18269070544392005684)
XLA Ops:
  7.9 1.1 copy.33
  9.1 1.1 copy.34
  11.5 1.0 sort.17
  17.1 1.4 subtract_convert_fusion
  22.6 4.5 %collective-permute-start.6 = (bf16[64,2,2,128]{3,0,1,2:T(8,128)(2,1)S(1)}, bf16[64,2,2,128]{3,0,1,2:T(8,128)(2,1)S(1)}, u32[]{:S(2)}, u32[]{:S(2)}) collective-permute-start(bf16[64,2,2,128]{3,0,1,2:T(8,128)(2,1)S(1)} %slice.84), channel_id=1, source_target_pairs={{0,2},{1,3}} | collective-permute-start | bytes 196616 | tf_op jit(solution)/shard_map/ppermute | solution.py:174
  27.9 2.8 %collective-permute-done.6 = bf16[64,2,2,128]{3,0,1,2:T(8,128)(2,1)S(1)} collective-permute-done((bf16[64,2,2,128]{3,0,1,2:T(8,128)(2,1)S(1)}, bf16[64,2,2,128]{3,0,1,2:T(8,128)(2,1)S(1)}, u32[]{:S(2)}, u32[]{:S(2)}) %collective-permute-start.6) | collective-permute-done | bytes 65568 | tf_op jit(solution)/shard_map/ppermute | solution.py:174
  30.6 1.3 collective-permute-start.7
  32.0 1.9 collective-permute-done.7
  33.8 1.3 collective-permute-start.8
  35.9 4.4 %collective-permute-start.10 = (bf16[256,2,2,128]{3,0,1,2:T(8,128)(2,1)S(1)}, bf16[256,2,2,128]{3,0,1,2:T(8,128)(2,1)S(1)}, u32[]{:S(2)}, u32[]{:S(2)}) collective-permute-start(bf16[256,2,2,128]{3,0,1,2:T(8,128)(2,1)S(1)} %fusion.59), channel_id=1, source_target_pairs={{0,2},{2,4},{4,6},{6,8},{8,10},{10,12},{12,14},{14,16},{16,18},{18... | collective-permute-start | bytes 786440 | tf_op jit(solution)/shard_map/ppermute | solution.py:169
  40.3 1.3 collective-permute-start.9
  41.7 1.8 collective-permute-done.9
  43.5 1.6 collective-permute-done.10
  45.1 0.9 pad_maximum_fusion.4
  46.0 1.4 select_bitcast_fusion.3
  47.6 1.5 gather_fusion.5
  49.1 2.1 fusion.17
  51.3 2.1 copy-done.1
  53.4 1.1 fusion.18
  54.5 1.5 gather_fusion.3
  56.1 4.6 %divide_convert_fusion = bf16[256,2,4,128]{0,3,2,1:T(8,128)(2,1)} fusion(f32[2,576,256,4]{2,1,3,0:T(8,128)} %copy-done.1, f32[2,4,256]{2,1,0:T(4,128)S(1)} %get-tuple-element.140, pred[256,576]{0,1:T(8,128)(4,1)S(1)} %pad_add_fusion, f32[256,2,4]{0,2,1:T(4,128)S(1)} %bitcast_add_fusion, f32[256,2,4]{0,2,1:T(4,128)S(1)} %get-tuple-element.139, ...), kind=kOutput, calls=%fused_computation.67 | convolution fusion | flops 308674560 | bytes 5709824 | tf_op jit(solution)/shard_map/hgrk,khd->hgrd/dot_general | solution.py:62
  60.7 2.4 %collective-permute-start.11 = (bf16[256,1024]{0,1:T(8,128)(2,1)}, bf16[256,1024]{0,1:T(8,128)(2,1)}, u32[]{:S(2)}, u32[]{:S(2)}) collective-permute-start(bf16[256,1024]{0,1:T(8,128)(2,1)} %bitcast.43), channel_id=1, source_target_pairs={{0,2},{2,4},{4,6},{6,0},{1,3},{3,5},{5,7},{7,1},{8,10},{10,12},{12... | collective-permute-start | bytes 1572872 | tf_op jit(solution)/shard_map/ppermute | solution.py:228
  63.1 2.1 collective-permute-start.12
  65.2 1.2 collective-permute-start.13
  66.4 1.4 select_bitcast_fusion.1
  68.6 1.2 select_bitcast_fusion.4
  69.8 1.3 bitcast_select_fusion.2
  71.2 40.9 %all-gather.3.cloned.1.call-done = bf16[4096,512]{0,1:T(8,128)(2,1)} async-done(((bf16[256,512]{0,1:T(8,128)(2,1)}), bf16[4096,512]{0,1:T(8,128)(2,1)}) %all-gather.3.cloned.1.call-update) | async-done | bytes 4194320 | tf_op jit(solution)/shard_map/all_gather | solution.py:199
  112.2 20.7 %while.15 = (s32[]{:T(128)}, f32[2,4,256]{2,1,0:T(4,128)S(1)}, f32[2,4,256]{2,1,0:T(4,128)S(1)}, f32[2,4,256,128]{3,2,1,0:T(8,128)S(1)}, s32[]{:T(128)}, /*index...) while((s32[]{:T(128)}, f32[2,4,256]{2,1,0:T(4,128)S(1)}, ...), condition=%wide.region_5.8_spmd.clone, body=%wide.region_2.7_spmd.clone.sunk | while | flops 2203064576 | bytes 124405992 | solution.py:216
  112.9 4.2 %fusion.86 = (f32[2,4,256]{2,1,0:T(4,128)S(1)}, f32[2,2048,256,4]{2,1,3,0:T(8,128)S(1)}) fusion(pred[256,2048]{0,1:T(8,128)(4,1)S(1)} %broadcast_compare_fusion.3, bf16[256,2,4,128]{3,0,2,1:T(8,128)(2,1)S(1)} %get-tuple-element.243, bf16[4096,2,2,128]{0,3,2,1:T(8,128)(2,1)} %get-tuple-element.242, s32[]{:T(128)S(6)} %select_n.340), kind=kOutput, calls=%fused_computation.9.clone.1 | convolution fusion | flops 1086322688 | bytes 18882564 | tf_op jit(solution)/shard_map/while/body/rhgd,khd->hgrk/dot_general | solution.py:53
  117.1 4.1 %fusion.87 = f32[2,4,256]{2,1,0:T(4,128)S(1)} fusion(f32[2,2048,256,4]{2,1,3,0:T(8,128)S(1)} %get-tuple-element.208, f32[2,4,256]{2,1,0:T(4,128)S(1)} %max.13, pred[256,2048]{0,1:T(8,128)(4,1)S(1)} %broadcast_compare_fusion.3), kind=kLoop, calls=%fused_computation.11.clone.1 | loop fusion | flops 20969472 | bytes 17317888 | tf_op jit(solution)/shard_map/while/body/reduce_sum | solution.py:61
  121.2 2.3 copy-done
  123.5 9.3 %fusion.88 = f32[2,4,256,128]{3,2,1,0:T(8,128)S(1)} fusion(f32[2,2048,256,4]{2,1,3,0:T(8,128)} %copy-done, f32[2,4,256]{2,1,0:T(4,128)S(1)} %max.13, pred[256,2048]{0,1:T(8,128)(4,1)S(1)} %broadcast_compare_fusion.3, bf16[4096,2,2,128]{0,3,2,1:T(8,128)(2,1)} %get-tuple-element.242, s32[]{:T(128)S(6)} %select_n.340, s32[]{:T(128)S(6)} %add.300, ...), kind=kOutput, calls=%fused_computation.14.clone.1 | convolution fusion | flops 1095237632 | bytes 20463624 | tf_op jit(solution)/shard_map/while/body/hgrk,khd->hgrd/dot_general | solution.py:62
  133.4 3.1 %collective-permute-start.3 = (bf16[256,1024]{0,1:T(8,128)(2,1)S(1)}, bf16[256,1024]{0,1:T(8,128)(2,1)S(1)}, u32[]{:S(2)}, u32[]{:S(2)}) collective-permute-start(bf16[256,1024]{0,1:T(8,128)(2,1)S(1)} %bitcast.189), channel_id=1, source_target_pairs={{0,4},{2,6},{4,0},{6,2},{1,5},{3,7},{5,1},{7,3},{8,12},{10,14},{12... | collective-permute-start | bytes 1572872 | tf_op jit(solution)/shard_map/ppermute | solution.py:228
  136.5 57.0 %all-gather.5.cloned.1.call-done = bf16[2048,1024]{1,0:T(8,128)(2,1)} async-done(((bf16[2048,256]{1,0:T(8,128)(2,1)}), bf16[2048,1024]{1,0:T(8,128)(2,1)}) %all-gather.5.cloned.1.call-update) | async-done | bytes 4194320 | tf_op jit(solution)/shard_map/all_gather | solution.py:242
  193.5 4.8 %fusion.23 = f32[1024,1024]{1,0:T(8,128)S(1)} fusion(bf16[2048,1024]{1,0:T(8,128)(2,1)} %all-gather.5.cloned.1.call-done, bf16[256,1024]{0,1:T(8,128)(2,1)} %collective-permute-done.13, bf16[256,1024]{0,1:T(8,128)(2,1)} %collective-permute-done.12, bf16[256,1024]{0,1:T(8,128)(2,1)} %collective-permute-done.11, bf16[256,1024]{0,1:T(8,128)(2,1)} %bitcast.43), kind=kOutput, calls=%fused_computation.35 | convolution fusion | flops 2155872256 | bytes 8388608 | tf_op jit(solution)/shard_map/dot_general | solution.py:246
  198.3 4.5 %fusion.41 = f32[1024,1024]{1,0:T(8,128)} fusion(f32[1024,1024]{1,0:T(8,128)S(1)} %fusion.23, bf16[2048,1024]{1,0:T(8,128)(2,1)S(1)} %copy-done.10, bf16[256,1024]{0,1:T(8,128)(2,1)S(1)} %collective-permute-done.4, bf16[256,1024]{0,1:T(8,128)(2,1)S(1)} %collective-permute-done.3, bf16[256,1024]{0,1:T(8,128)(2,1)S(1)} %collective-permute-done.2, ...), kind=kOutput, calls=%fused_computation.60 | convolution fusion | flops 2156920832 | bytes 12582912 | tf_op jit(solution)/shard_map/dot_general | solution.py:246
  202.8 3.1 %constant_dynamic-slice_fusion = f32[1024,512]{1,0:T(8,128)} fusion(f32[1024,1024]{1,0:T(8,128)} %fusion.41, s32[]{:T(128)S(6)} %select_n.195), kind=kLoop, calls=%fused_computation.141 | loop fusion | bytes 4194308 | tf_op jit(solution)/shard_map/dynamic_slice | solution.py:252
  205.9 4.4 %collective-permute-done.14 = f32[1024,512]{1,0:T(8,128)S(1)} collective-permute-done((f32[1024,512]{1,0:T(8,128)}, f32[1024,512]{1,0:T(8,128)S(1)}, u32[]{:S(2)}, u32[]{:S(2)}) %collective-permute-start.14) | collective-permute-done | bytes 2097184 | tf_op jit(solution)/shard_map/ppermute | solution.py:253
  210.3 1.9 add_convert_fusion
  212.4 1.5 collective-permute-start.15
  213.9 1.5 collective-permute-start.16
  215.3 1.5 collective-permute-start.17
  216.8 5.7 %collective-permute-done.15 = bf16[256,512]{1,0:T(8,128)(2,1)S(1)} collective-permute-done((bf16[256,512]{1,0:T(8,128)(2,1)S(1)}, bf16[256,512]{1,0:T(8,128)(2,1)S(1)}, u32[]{:S(2)}, u32[]{:S(2)}) %collective-permute-start.15) | collective-permute-done | bytes 262176 | tf_op jit(solution)/shard_map/ppermute | solution.py:257
  222.5 4.7 %collective-permute-done.16 = bf16[256,512]{1,0:T(8,128)(2,1)S(1)} collective-permute-done((bf16[256,512]{1,0:T(8,128)(2,1)S(1)}, bf16[256,512]{1,0:T(8,128)(2,1)S(1)}, u32[]{:S(2)}, u32[]{:S(2)}) %collective-permute-start.16) | collective-permute-done | bytes 262176 | tf_op jit(solution)/shard_map/ppermute | solution.py:257
  228.4 1.0 fusion.52
  229.3 1.4 copy.44
  230.7 1.6 reshape.372
  (110 shorter events, 15.5 us)
Async XLA Ops:
  6.5 4.9 %copy-start.11 = (s32[4]{0:T(128)S(1)}, s32[4]{0:T(128)}, u32[]{:S(2)}) copy-start(s32[4]{0:T(128)} %param.17) | copy-start | bytes 52
  6.5 105.5 %all-gather.3.cloned.1.call-start = ((), (), s32[]{:S(2)}) async-start(), calls=%async_computation | async-start | bytes 4456448 | tf_op jit(solution)/shard_map/all_gather | solution.py:199
  10.6 2.5 %collective-permute-start = (bf16[256,4,2,128]{0,3,1,2:T(8,128)(2,1)S(1)}, bf16[256,4,2,128]{0,3,1,2:T(8,128)(2,1)S(1)}, u32[]{:S(2)}, u32[]{:S(2)}) collective-permute-start(bf16[256,4,2,128]{0,3,1,2:T(8,128)(2,1)S(1)} %pad_maximum_fusion.5), channel_id=1, source_target_pairs={{0,1},{1,0},{2,3},{3,2},{4,5},{5,4},{6,7},{7,6},{8,9},{9,8},{10,11... | collective-permute-start | bytes 1572872 | tf_op jit(solution)/shard_map/ppermute | solution.py:139
  11.3 4.5 %copy-start.2 = (bf16[256,2048]{1,0:T(8,128)(2,1)S(1)}, bf16[256,2048]{1,0:T(8,128)(2,1)}, u32[]{:S(2)}) copy-start(bf16[256,2048]{1,0:T(8,128)(2,1)} %param.13) | copy-start | bytes 3145732
  13.1 2.9 %copy-start.5 = (pred[2]{0:T(512)(128)(4,1)}, pred[2]{0:T(512)(128)(4,1)S(1)}, u32[]{:S(2)}) copy-start(pred[2]{0:T(512)(128)(4,1)S(1)} %get-tuple-element.117) | copy-start | bytes 10
  13.1 6.6 %copy-start.8 = (s32[2]{0:T(128)}, s32[2]{0:T(128)S(1)}, u32[]{:S(2)}) copy-start(s32[2]{0:T(128)S(1)} %get-tuple-element.118) | copy-start | bytes 28
  13.1 7.2 %copy-start.9 = (s32[2]{0:T(128)}, s32[2]{0:T(128)S(1)}, u32[]{:S(2)}) copy-start(s32[2]{0:T(128)S(1)} %get-tuple-element.144) | copy-start | bytes 28
  13.1 2.9 %copy-start.4 = (s32[1024]{0:T(1024)}, s32[1024]{0:T(1024)S(1)}, u32[]{:S(2)}) copy-start(s32[1024]{0:T(1024)S(1)} %pad_clamp_fusion.3) | copy-start | bytes 12292
  15.7 177.8 %all-gather.5.cloned.1.call-start = ((), (), s32[]{:S(2)}) async-start(), calls=%async_computation.1 | async-start | bytes 5242880 | tf_op jit(solution)/shard_map/all_gather | solution.py:242
  17.1 2.0 copy-start.3
  19.1 26.9 %collective-permute-start.1 = (bf16[256,4,4,128]{3,0,2,1:T(8,128)(2,1)S(1)}, bf16[256,4,4,128]{3,0,2,1:T(8,128)(2,1)}, u32[]{:S(2)}, u32[]{:S(2)}) collective-permute-start(bf16[256,4,4,128]{3,0,2,1:T(8,128)(2,1)S(1)} %bitcast.175), channel_id=1, source_target_pairs={{0,1},{1,0},{2,3},{3,2},{4,5},{5,4},{6,7},{7,6},{8,9},{9,8},{10,11... | collective-permute-start | bytes 3145736 | tf_op jit(solution)/shard_map/ppermute | solution.py:139
  19.2 47.3 %collective-permute-start.5 = (bf16[4,512,256]{2,1,0:T(8,128)(2,1)S(1)}, bf16[4,512,256]{2,1,0:T(8,128)(2,1)}, u32[]{:S(2)}, u32[]{:S(2)}) collective-permute-start(bf16[4,512,256]{2,1,0:T(8,128)(2,1)S(1)} %bitcast.182), channel_id=1, source_target_pairs={{0,1},{1,0},{2,3},{3,2},{4,5},{5,4},{6,7},{7,6},{8,9},{9,8},{10,11... | collective-permute-start | bytes 3145736 | tf_op jit(solution)/shard_map/ppermute | solution.py:139
  22.6 8.0 %collective-permute-start.6 = (bf16[64,2,2,128]{3,0,1,2:T(8,128)(2,1)S(1)}, bf16[64,2,2,128]{3,0,1,2:T(8,128)(2,1)S(1)}, u32[]{:S(2)}, u32[]{:S(2)}) collective-permute-start(bf16[64,2,2,128]{3,0,1,2:T(8,128)(2,1)S(1)} %slice.84), channel_id=1, source_target_pairs={{0,2},{1,3}} | collective-permute-start | bytes 196616 | tf_op jit(solution)/shard_map/ppermute | solution.py:174
  30.6 3.2 %collective-permute-start.7 = (bf16[64,2,2,128]{3,0,1,2:T(8,128)(2,1)S(1)}, bf16[64,2,2,128]{3,0,1,2:T(8,128)(2,1)S(1)}, u32[]{:S(2)}, u32[]{:S(2)}) collective-permute-start(bf16[64,2,2,128]{3,0,1,2:T(8,128)(2,1)S(1)} %broadcast_select_fusion.1), channel_id=1, source_target_pairs={{0,4},{2,6},{1,5},{3,7}} | collective-permute-start | bytes 196616 | tf_op jit(solution)/shard_map/ppermute | solution.py:174
  33.8 6.4 %collective-permute-start.8 = (bf16[64,2,2,128]{3,0,1,2:T(8,128)(2,1)S(1)}, bf16[64,2,2,128]{3,0,1,2:T(8,128)(2,1)S(1)}, u32[]{:S(2)}, u32[]{:S(2)}) collective-permute-start(bf16[64,2,2,128]{3,0,1,2:T(8,128)(2,1)S(1)} %broadcast_select_fusion.2), channel_id=1, source_target_pairs={{0,8},{2,10},{4,12},{6,14},{1,9},{3,11},{5,13},{7,15}} | collective-permute-start | bytes 196616 | tf_op jit(solution)/shard_map/ppermute | solution.py:174
  35.9 9.2 %collective-permute-start.10 = (bf16[256,2,2,128]{3,0,1,2:T(8,128)(2,1)S(1)}, bf16[256,2,2,128]{3,0,1,2:T(8,128)(2,1)S(1)}, u32[]{:S(2)}, u32[]{:S(2)}) collective-permute-start(bf16[256,2,2,128]{3,0,1,2:T(8,128)(2,1)S(1)} %fusion.59), channel_id=1, source_target_pairs={{0,2},{2,4},{4,6},{6,8},{8,10},{10,12},{12,14},{14,16},{16,18},{18... | collective-permute-start | bytes 786440 | tf_op jit(solution)/shard_map/ppermute | solution.py:169
  40.3 3.2 %collective-permute-start.9 = (bf16[64,2,2,128]{3,0,1,2:T(8,128)(2,1)S(1)}, bf16[64,2,2,128]{3,0,1,2:T(8,128)(2,1)S(1)}, u32[]{:S(2)}, u32[]{:S(2)}) collective-permute-start(bf16[64,2,2,128]{3,0,1,2:T(8,128)(2,1)S(1)} %broadcast_select_fusion.3), channel_id=1, source_target_pairs={{0,16},{2,18},{4,20},{6,22},{8,24},{10,26},{12,28},{14,30},{1,17},... | collective-permute-start | bytes 196616 | tf_op jit(solution)/shard_map/ppermute | solution.py:174
  46.0 3.2 %copy-start.7 = (pred[2]{0:T(512)(128)(4,1)S(1)}, pred[2]{0:T(512)(128)(4,1)}, u32[]{:S(2)}) copy-start(pred[2]{0:T(512)(128)(4,1)} %get-tuple-element.143) | copy-start | bytes 10
  51.2 2.2 copy-start.1
  60.7 75.8 %collective-permute-start.11 = (bf16[256,1024]{0,1:T(8,128)(2,1)}, bf16[256,1024]{0,1:T(8,128)(2,1)}, u32[]{:S(2)}, u32[]{:S(2)}) collective-permute-start(bf16[256,1024]{0,1:T(8,128)(2,1)} %bitcast.43), channel_id=1, source_target_pairs={{0,2},{2,4},{4,6},{6,0},{1,3},{3,5},{5,7},{7,1},{8,10},{10,12},{12... | collective-permute-start | bytes 1572872 | tf_op jit(solution)/shard_map/ppermute | solution.py:228
  63.1 73.4 %collective-permute-start.12 = (bf16[256,1024]{0,1:T(8,128)(2,1)}, bf16[256,1024]{0,1:T(8,128)(2,1)}, u32[]{:S(2)}, u32[]{:S(2)}) collective-permute-start(bf16[256,1024]{0,1:T(8,128)(2,1)} %bitcast.43), channel_id=1, source_target_pairs={{0,4},{2,6},{4,0},{6,2},{1,5},{3,7},{5,1},{7,3},{8,12},{10,14},{12... | collective-permute-start | bytes 1572872 | tf_op jit(solution)/shard_map/ppermute | solution.py:228
  65.2 71.3 %collective-permute-start.13 = (bf16[256,1024]{0,1:T(8,128)(2,1)}, bf16[256,1024]{0,1:T(8,128)(2,1)}, u32[]{:S(2)}, u32[]{:S(2)}) collective-permute-start(bf16[256,1024]{0,1:T(8,128)(2,1)} %bitcast.43), channel_id=1, source_target_pairs={{0,6},{2,0},{4,2},{6,4},{1,7},{3,1},{5,3},{7,5},{8,14},{10,8},{12,... | collective-permute-start | bytes 1572872 | tf_op jit(solution)/shard_map/ppermute | solution.py:228
  67.8 0.8 copy-start.6
  117.1 6.4 %copy-start = (f32[2,2048,256,4]{2,1,3,0:T(8,128)}, f32[2,2048,256,4]{2,1,3,0:T(8,128)S(1)}, u32[]{:S(2)}) copy-start(f32[2,2048,256,4]{2,1,3,0:T(8,128)S(1)} %get-tuple-element.208) | copy-start | bytes 50331652 | tf_op jit(solution)/shard_map/while
  133.3 65.0 %collective-permute-start.2 = (bf16[256,1024]{0,1:T(8,128)(2,1)S(1)}, bf16[256,1024]{0,1:T(8,128)(2,1)S(1)}, u32[]{:S(2)}, u32[]{:S(2)}) collective-permute-start(bf16[256,1024]{0,1:T(8,128)(2,1)S(1)} %bitcast.188), channel_id=1, source_target_pairs={{0,2},{2,4},{4,6},{6,0},{1,3},{3,5},{5,7},{7,1},{8,10},{10,12},{12... | collective-permute-start | bytes 1572872 | tf_op jit(solution)/shard_map/ppermute | solution.py:228
  133.4 64.9 %collective-permute-start.3 = (bf16[256,1024]{0,1:T(8,128)(2,1)S(1)}, bf16[256,1024]{0,1:T(8,128)(2,1)S(1)}, u32[]{:S(2)}, u32[]{:S(2)}) collective-permute-start(bf16[256,1024]{0,1:T(8,128)(2,1)S(1)} %bitcast.189), channel_id=1, source_target_pairs={{0,4},{2,6},{4,0},{6,2},{1,5},{3,7},{5,1},{7,3},{8,12},{10,14},{12... | collective-permute-start | bytes 1572872 | tf_op jit(solution)/shard_map/ppermute | solution.py:228
  136.5 61.8 %collective-permute-start.4 = (bf16[256,1024]{0,1:T(8,128)(2,1)S(1)}, bf16[256,1024]{0,1:T(8,128)(2,1)S(1)}, u32[]{:S(2)}, u32[]{:S(2)}) collective-permute-start(bf16[256,1024]{0,1:T(8,128)(2,1)S(1)} %bitcast.190), channel_id=1, source_target_pairs={{0,6},{2,0},{4,2},{6,4},{1,7},{3,1},{5,3},{7,5},{8,14},{10,8},{12,... | collective-permute-start | bytes 1572872 | tf_op jit(solution)/shard_map/ppermute | solution.py:228
  193.5 4.8 %copy-start.10 = (bf16[2048,1024]{1,0:T(8,128)(2,1)S(1)}, bf16[2048,1024]{1,0:T(8,128)(2,1)}, u32[]{:S(2)}) copy-start(bf16[2048,1024]{1,0:T(8,128)(2,1)} %all-gather.5.cloned.1.call-done) | copy-start | bytes 12582916
  205.9 4.4 %collective-permute-start.14 = (f32[1024,512]{1,0:T(8,128)}, f32[1024,512]{1,0:T(8,128)S(1)}, u32[]{:S(2)}, u32[]{:S(2)}) collective-permute-start(f32[1024,512]{1,0:T(8,128)} %constant_dynamic-slice_fusion), channel_id=1, source_target_pairs={{0,1},{1,0},{2,3},{3,2},{4,5},{5,4},{6,7},{7,6},{8,9},{9,8},{10,11... | collective-permute-start | bytes 6291464 | tf_op jit(solution)/shard_map/ppermute | solution.py:253
  212.4 10.2 %collective-permute-start.15 = (bf16[256,512]{1,0:T(8,128)(2,1)S(1)}, bf16[256,512]{1,0:T(8,128)(2,1)S(1)}, u32[]{:S(2)}, u32[]{:S(2)}) collective-permute-start(bf16[256,512]{1,0:T(8,128)(2,1)S(1)} %get-tuple-element.134), channel_id=1, source_target_pairs={{0,2},{2,4},{4,6},{6,0},{1,3},{3,5},{5,7},{7,1},{8,10},{10,12},{12... | collective-permute-start | bytes 786440 | tf_op jit(solution)/shard_map/ppermute | solution.py:257
  213.9 13.4 %collective-permute-start.16 = (bf16[256,512]{1,0:T(8,128)(2,1)S(1)}, bf16[256,512]{1,0:T(8,128)(2,1)S(1)}, u32[]{:S(2)}, u32[]{:S(2)}) collective-permute-start(bf16[256,512]{1,0:T(8,128)(2,1)S(1)} %get-tuple-element.133), channel_id=1, source_target_pairs={{0,4},{2,6},{4,0},{6,2},{1,5},{3,7},{5,1},{7,3},{8,12},{10,14},{12... | collective-permute-start | bytes 786440 | tf_op jit(solution)/shard_map/ppermute | solution.py:257
  215.3 12.0 %collective-permute-start.17 = (bf16[256,512]{1,0:T(8,128)(2,1)S(1)}, bf16[256,512]{1,0:T(8,128)(2,1)S(1)}, u32[]{:S(2)}, u32[]{:S(2)}) collective-permute-start(bf16[256,512]{1,0:T(8,128)(2,1)S(1)} %get-tuple-element.132), channel_id=1, source_target_pairs={{0,6},{2,0},{4,2},{6,4},{1,7},{3,1},{5,3},{7,5},{8,14},{10,8},{12,... | collective-permute-start | bytes 786440 | tf_op jit(solution)/shard_map/ppermute | solution.py:257
Sparse Core Ops, SparseCore 0:
  15.8 96.1 all-gather.2
  113.6 79.7 all-gather.4

commit v8 on v7

--- a/solution.py
+++ b/solution.py
@@ -239,13 +239,19 @@
     w_all = head_exchange(w_local.reshape(-1, group_rows, col_width), head_count)
     w_all = w_all.reshape(-1, group_rows, col_width)
     w_mine = jnp.take(w_all, ids, axis=0).reshape(-1, col_width)
-    w_line = lax.all_gather(w_mine, "cz", axis=1, tiled=True)
     ret_rows = att_ret.shape[1]
+    w_ret = lax.all_gather(w_mine[:ret_rows], "cz", axis=1, tiled=True)
+    me_cz = lax.axis_index("cz")
+    w_run = [w_mine[ret_rows:]] + [
+        lax.ppermute(w_mine[ret_rows:], "cz", [(i, (i + shift) % line) for i in range(line)])
+        for shift in range(1, line)
+    ]
+    w_run = jnp.take(jnp.stack(w_run), (me_cz - jnp.arange(line)) % line, axis=0)
     run_stack = jnp.concatenate(plane_pieces(att_run, plane), axis=0)
     ret_stack = jnp.concatenate(plane_pieces(att_ret, plane), axis=0)
-    part = jnp.dot(ret_stack, w_line[:ret_rows], preferred_element_type=jnp.float32) + jnp.dot(
-        run_stack, w_line[ret_rows:], preferred_element_type=jnp.float32
-    )
+    part = jnp.dot(ret_stack, w_ret, preferred_element_type=jnp.float32) + jnp.einsum(
+        "tk,lkc->tlc", run_stack, w_run, preferred_element_type=jnp.float32
+    ).reshape(run_stack.shape[0], line * col_width)
     half = part.shape[1] // 2
     me = lax.axis_index("head")
     mine = lax.dynamic_slice_in_dim(part, me * half, half, axis=1)

time: 240 us -> 248 us (1.033)
  the two profiles are of different devices: /device:TPU:0 before, /device:TPU:17 now
where the time goes in v8:
time: 248 us; the launch traced here: 247 us
  waiting for transfers between devices  73.9 us (30%)
  starting transfers between devices  54.2 us (22%)
  matrix products  42.9 us (17%)
  local copies, waits for them, and re-layouts  31.5 us (13%)
  other arithmetic  29.6 us (12%)
  between operations  14.7 us (6%)
    ppermute x6, starting transfers between devices, plane_pieces(): lax.ppermute(block, 'cb', [(i, (i + shift) % plane) for i in range(plane)])  38.5 us
    ppermute x3, waiting for transfers between devices, project_assigned(): lax.ppermute(w_mine[ret_rows:], 'cz', [(i, (i + shift) % line) for i in r...  23.3 us
    dot_general x3, matrix products, update(): jnp.einsum('hgrk,khd->hgrd', weights.astype(jnp.bfloat16), value_block, p...  20.6 us
    all_gather x1, waiting for transfers between devices, duo_attend(): lax.all_gather(ret_kv.reshape(rows, ret_per * 2 * HEAD_SIZE), CTX, axis=0...  12.8 us
    ppermute x3, waiting for transfers between devices, project_assigned(): lax.ppermute(blocks[-shift % plane], 'cb', [(i, (i + shift) % plane) for...  11.9 us
    ppermute x6, waiting for transfers between devices, plane_pieces(): lax.ppermute(block, 'cb', [(i, (i + shift) % plane) for i in range(plane)])  11.2 us
    ppermute x4, waiting for transfers between devices, duo_attend(): got = lax.ppermute(sink_kv, CTX, pairs)  10.6 us
    dot_general x3, matrix products, update(): jnp.einsum('rhgd,khd->hgrk', query_rows, key_block, preferred_element_typ...  10.4 us
  transfers between devices with their start and end apart: 23, of which 8 were waited for; matrix products, arithmetic and copies ran while one was open for 32% of the time, Pallas kernels for 0%

profile of v8, /device:TPU:17, one launch (start us, length us, event | category | flops | bytes accessed | tf_op | source)
XLA Modules:
  0.0 247.0 jit_solution(9624237565766733872)
XLA Ops:
  7.9 1.1 copy.50
  9.1 1.1 copy.51
  12.1 1.0 sort.17
  17.8 1.4 subtract_convert_fusion
  26.2 3.1 %collective-permute-start.10 = (bf16[256,2,2,128]{3,0,1,2:T(8,128)(2,1)S(1)}, bf16[256,2,2,128]{3,0,1,2:T(8,128)(2,1)S(1)}, u32[]{:S(2)}, u32[]{:S(2)}) collective-permute-start(bf16[256,2,2,128]{3,0,1,2:T(8,128)(2,1)S(1)} %fusion.57), channel_id=1, source_target_pairs={{0,2},{2,4},{4,6},{6,8},{8,10},{10,12},{12,14},{14,16},{16,18},{18... | collective-permute-start | bytes 786440 | tf_op jit(solution)/shard_map/ppermute | solution.py:169
  29.3 1.3 collective-permute-start.9
  30.7 10.6 %collective-permute-done.9 = bf16[64,2,2,128]{3,0,1,2:T(8,128)(2,1)S(1)} collective-permute-done((bf16[64,2,2,128]{3,0,1,2:T(8,128)(2,1)S(1)}, bf16[64,2,2,128]{3,0,1,2:T(8,128)(2,1)S(1)}, u32[]{:S(2)}, u32[]{:S(2)}) %collective-permute-start.9) | collective-permute-done | bytes 65568 | tf_op jit(solution)/shard_map/ppermute | solution.py:174
  42.2 1.4 select_bitcast_fusion.1
  43.8 1.7 gather_fusion
  45.5 1.4 broadcast_select_fusion.1
  48.3 4.1 %collective-permute-start.15 = (bf16[1024,256]{1,0:T(8,128)(2,1)S(1)}, bf16[1024,256]{1,0:T(8,128)(2,1)}, u32[]{:S(2)}, u32[]{:S(2)}) collective-permute-start(bf16[1024,256]{1,0:T(8,128)(2,1)S(1)} %bitcast.193), channel_id=1, source_target_pairs={{0,16},{8,24},{16,0},{24,8},{1,17},{9,25},{17,1},{25,9},{2,18},{10... | collective-permute-start | bytes 1572872 | tf_op jit(solution)/shard_map/ppermute | solution.py:246
  52.4 1.4 select_bitcast_fusion.3
  54.8 2.0 fusion.17
  56.8 1.1 fusion.18
  58.0 2.1 divide_convert_fusion
  60.8 2.0 copy.64
  62.9 1.0 collective-permute-start.11
  63.9 1.5 collective-permute-start.12
  66.1 33.5 %collective-permute-start.13 = (bf16[256,1024]{1,0:T(8,128)(2,1)}, bf16[256,1024]{1,0:T(8,128)(2,1)}, u32[]{:S(2)}, u32[]{:S(2)}) collective-permute-start(bf16[256,1024]{1,0:T(8,128)(2,1)} %copy.64), channel_id=1, source_target_pairs={{0,6},{2,0},{4,2},{6,4},{1,7},{3,1},{5,3},{7,5},{8,14},{10,8},{12,... | collective-permute-start | bytes 1572872 | tf_op jit(solution)/shard_map/ppermute | solution.py:228
  99.6 22.7 %collective-permute-done.16 = bf16[1024,256]{1,0:T(8,128)(2,1)} collective-permute-done((bf16[1024,256]{1,0:T(8,128)(2,1)S(1)}, bf16[1024,256]{1,0:T(8,128)(2,1)}, u32[]{:S(2)}, u32[]{:S(2)}) %collective-permute-start.16) | collective-permute-done | bytes 524320 | tf_op jit(solution)/shard_map/ppermute | solution.py:246
  122.4 1.6 pad_maximum_fusion.2
  124.0 2.1 gather_fusion.1
  126.1 12.8 %all-gather.3.cloned.1.call-done = bf16[4096,512]{0,1:T(8,128)(2,1)} async-done(((bf16[256,512]{0,1:T(8,128)(2,1)}), bf16[4096,512]{0,1:T(8,128)(2,1)}) %all-gather.3.cloned.1.call-update) | async-done | bytes 4194320 | tf_op jit(solution)/shard_map/all_gather | solution.py:199
  139.0 39.7 %while.15 = (s32[]{:T(128)}, f32[2,4,256]{2,1,0:T(4,128)S(1)}, f32[2,4,256]{2,1,0:T(4,128)S(1)}, f32[2,4,256,128]{3,2,1,0:T(8,128)S(1)}, s32[]{:T(128)}, /*index...) while((s32[]{:T(128)}, f32[2,4,256]{2,1,0:T(4,128)S(1)}, ...), condition=%wide.region_5.8_spmd.clone, body=%wide.region_2.7_spmd.clone.sunk | while | flops 2203064576 | bytes 124405992 | solution.py:216
  139.5 4.2 %fusion.90 = (f32[2,4,256]{2,1,0:T(4,128)S(1)}, f32[2,2048,256,4]{2,1,3,0:T(8,128)S(1)}) fusion(pred[256,2048]{0,1:T(8,128)(4,1)S(1)} %broadcast_compare_fusion.3, bf16[256,2,4,128]{3,0,2,1:T(8,128)(2,1)S(1)} %get-tuple-element.245, bf16[4096,2,2,128]{0,3,2,1:T(8,128)(2,1)} %get-tuple-element.244, s32[]{:T(128)S(6)} %select_n.396), kind=kOutput, calls=%fused_computation.10.clone.1 | convolution fusion | flops 1086322688 | bytes 18882564 | tf_op jit(solution)/shard_map/while/body/rhgd,khd->hgrk/dot_general | solution.py:53
  143.7 4.1 %fusion.91 = f32[2,4,256]{2,1,0:T(4,128)S(1)} fusion(f32[2,2048,256,4]{2,1,3,0:T(8,128)S(1)} %get-tuple-element.210, f32[2,4,256]{2,1,0:T(4,128)S(1)} %max.13, pred[256,2048]{0,1:T(8,128)(4,1)S(1)} %broadcast_compare_fusion.3), kind=kLoop, calls=%fused_computation.12.clone.1 | loop fusion | flops 20969472 | bytes 17317888 | tf_op jit(solution)/shard_map/while/body/reduce_sum | solution.py:61
  147.8 1.9 copy-done
  149.7 9.3 %fusion.92 = f32[2,4,256,128]{3,2,1,0:T(8,128)S(1)} fusion(f32[2,2048,256,4]{2,1,3,0:T(8,128)} %copy-done, f32[2,4,256]{2,1,0:T(4,128)S(1)} %max.13, pred[256,2048]{0,1:T(8,128)(4,1)S(1)} %broadcast_compare_fusion.3, bf16[4096,2,2,128]{0,3,2,1:T(8,128)(2,1)} %get-tuple-element.244, s32[]{:T(128)S(6)} %select_n.396, s32[]{:T(128)S(6)} %add.350, ...), kind=kOutput, calls=%fused_computation.15.clone.1 | convolution fusion | flops 1095237632 | bytes 20463624 | tf_op jit(solution)/shard_map/while/body/hgrk,khd->hgrd/dot_general | solution.py:62
  159.5 4.2 %fusion.90 = (f32[2,4,256]{2,1,0:T(4,128)S(1)}, f32[2,2048,256,4]{2,1,3,0:T(8,128)S(1)}) fusion(pred[256,2048]{0,1:T(8,128)(4,1)S(1)} %broadcast_compare_fusion.3, bf16[256,2,4,128]{3,0,2,1:T(8,128)(2,1)S(1)} %get-tuple-element.245, bf16[4096,2,2,128]{0,3,2,1:T(8,128)(2,1)} %get-tuple-element.244, s32[]{:T(128)S(6)} %select_n.396), kind=kOutput, calls=%fused_computation.10.clone.1 | convolution fusion | flops 1086322688 | bytes 18882564 | tf_op jit(solution)/shard_map/while/body/rhgd,khd->hgrk/dot_general | solution.py:53
  163.7 4.1 %fusion.91 = f32[2,4,256]{2,1,0:T(4,128)S(1)} fusion(f32[2,2048,256,4]{2,1,3,0:T(8,128)S(1)} %get-tuple-element.210, f32[2,4,256]{2,1,0:T(4,128)S(1)} %max.13, pred[256,2048]{0,1:T(8,128)(4,1)S(1)} %broadcast_compare_fusion.3), kind=kLoop, calls=%fused_computation.12.clone.1 | loop fusion | flops 20969472 | bytes 17317888 | tf_op jit(solution)/shard_map/while/body/reduce_sum | solution.py:61
  167.8 1.6 copy-done
  169.4 9.2 %fusion.92 = f32[2,4,256,128]{3,2,1,0:T(8,128)S(1)} fusion(f32[2,2048,256,4]{2,1,3,0:T(8,128)} %copy-done, f32[2,4,256]{2,1,0:T(4,128)S(1)} %max.13, pred[256,2048]{0,1:T(8,128)(4,1)S(1)} %broadcast_compare_fusion.3, bf16[4096,2,2,128]{0,3,2,1:T(8,128)(2,1)} %get-tuple-element.244, s32[]{:T(128)S(6)} %select_n.396, s32[]{:T(128)S(6)} %add.350, ...), kind=kOutput, calls=%fused_computation.15.clone.1 | convolution fusion | flops 1095237632 | bytes 20463624 | tf_op jit(solution)/shard_map/while/body/hgrk,khd->hgrd/dot_general | solution.py:62
  179.2 2.2 collective-permute-start.3
  181.6 6.7 %fusion.31 = f32[1024,4,256]{0,2,1:T(8,128)} fusion(bf16[256,1024]{1,0:T(8,128)(2,1)} %collective-permute-done.13, bf16[256,1024]{1,0:T(8,128)(2,1)} %collective-permute-done.12, bf16[256,1024]{1,0:T(8,128)(2,1)} %collective-permute-done.11, bf16[256,1024]{1,0:T(8,128)(2,1)} %copy.64, bf16[4,1024,256]{2,1,0:T(8,128)(2,1)} %gather_fusion.1, ...), kind=kOutput, calls=%fused_computation.47 | convolution fusion | flops 2156920832 | bytes 8388612 | tf_op jit(solution)/shard_map/tk,lkc->tlc/dot_general | solution.py:252
  188.3 5.4 %copy.74 = f32[1024,1024]{1,0:T(8,128)} copy(f32[1024,1024]{0,1:T(8,128)} %bitcast.185) | data formatting | bytes 8388608 | tf_op jit(solution)/shard_map/reshape | solution.py:254
  193.7 11.2 %collective-permute-done.3 = bf16[256,1024]{0,1:T(8,128)(2,1)S(1)} collective-permute-done((bf16[256,1024]{0,1:T(8,128)(2,1)S(1)}, bf16[256,1024]{0,1:T(8,128)(2,1)S(1)}, u32[]{:S(2)}, u32[]{:S(2)}) %collective-permute-start.3) | collective-permute-done | bytes 524320 | tf_op jit(solution)/shard_map/ppermute | solution.py:228
  204.9 5.2 %fusion.40 = f32[1024,1024]{1,0:T(8,128)S(1)} fusion(f32[1024,1024]{1,0:T(8,128)} %copy.74, bf16[1024,1024]{1,0:T(8,128)(2,1)} %all-gather.5.cloned.1.call-done, bf16[256,1024]{0,1:T(8,128)(2,1)S(1)} %collective-permute-done.4, bf16[256,1024]{0,1:T(8,128)(2,1)S(1)} %collective-permute-done.3, bf16[256,1024]{0,1:T(8,128)(2,1)S(1)} %collective-permute-done.2, ...), kind=kOutput, calls=%fused_computation.62 | convolution fusion | flops 2156920832 | bytes 12582912 | tf_op jit(solution)/shard_map/dot_general | solution.py:252
  210.1 2.0 copy-done.1
  212.1 1.6 constant_dynamic-slice_fusion
  214.3 4.0 %collective-permute-done.17 = f32[1024,512]{1,0:T(8,128)S(1)} collective-permute-done((f32[1024,512]{1,0:T(8,128)}, f32[1024,512]{1,0:T(8,128)S(1)}, u32[]{:S(2)}, u32[]{:S(2)}) %collective-permute-start.17) | collective-permute-done | bytes 2097184 | tf_op jit(solution)/shard_map/ppermute | solution.py:259
  218.3 1.9 add_convert_fusion
  220.4 1.2 collective-permute-start.18
  222.3 0.9 collective-permute-start.20
  223.3 5.6 %collective-permute-done.18 = bf16[256,512]{1,0:T(8,128)(2,1)S(1)} collective-permute-done((bf16[256,512]{1,0:T(8,128)(2,1)S(1)}, bf16[256,512]{1,0:T(8,128)(2,1)S(1)}, u32[]{:S(2)}, u32[]{:S(2)}) %collective-permute-start.18) | collective-permute-done | bytes 262176 | tf_op jit(solution)/shard_map/ppermute | solution.py:263
  228.9 6.3 %collective-permute-done.19 = bf16[256,512]{1,0:T(8,128)(2,1)S(1)} collective-permute-done((bf16[256,512]{1,0:T(8,128)(2,1)S(1)}, bf16[256,512]{1,0:T(8,128)(2,1)S(1)}, u32[]{:S(2)}, u32[]{:S(2)}) %collective-permute-start.19) | collective-permute-done | bytes 262176 | tf_op jit(solution)/shard_map/ppermute | solution.py:263
  236.2 1.0 fusion.50
  237.2 1.4 copy.67
  238.6 1.6 reshape.431
  (131 shorter events, 23.3 us)
Async XLA Ops:
  6.5 132.3 %all-gather.3.cloned.1.call-start = ((), (), s32[]{:S(2)}) async-start(), calls=%async_computation | async-start | bytes 4456448 | tf_op jit(solution)/shard_map/all_gather | solution.py:199
  10.6 3.1 %collective-permute-start = (bf16[256,4,2,128]{0,3,1,2:T(8,128)(2,1)S(1)}, bf16[256,4,2,128]{0,3,1,2:T(8,128)(2,1)S(1)}, u32[]{:S(2)}, u32[]{:S(2)}) collective-permute-start(bf16[256,4,2,128]{0,3,1,2:T(8,128)(2,1)S(1)} %pad_maximum_fusion.6), channel_id=1, source_target_pairs={{0,1},{1,0},{2,3},{3,2},{4,5},{5,4},{6,7},{7,6},{8,9},{9,8},{10,11... | collective-permute-start | bytes 1572872 | tf_op jit(solution)/shard_map/ppermute | solution.py:139
  13.6 2.9 %copy-start.6 = (pred[2]{0:T(512)(128)(4,1)}, pred[2]{0:T(512)(128)(4,1)S(1)}, u32[]{:S(2)}) copy-start(pred[2]{0:T(512)(128)(4,1)S(1)} %get-tuple-element.117) | copy-start | bytes 10
  13.6 6.8 %copy-start.9 = (s32[2]{0:T(128)}, s32[2]{0:T(128)S(1)}, u32[]{:S(2)}) copy-start(s32[2]{0:T(128)S(1)} %get-tuple-element.118) | copy-start | bytes 28
  13.6 7.4 %copy-start.10 = (s32[2]{0:T(128)}, s32[2]{0:T(128)S(1)}, u32[]{:S(2)}) copy-start(s32[2]{0:T(128)S(1)} %get-tuple-element.146) | copy-start | bytes 28
  13.6 2.8 %copy-start.5 = (s32[1024]{0:T(1024)}, s32[1024]{0:T(1024)S(1)}, u32[]{:S(2)}) copy-start(s32[1024]{0:T(1024)S(1)} %pad_clamp_fusion.4) | copy-start | bytes 12292
  13.7 2.8 %copy-start.2 = (bf16[256,2048]{1,0:T(8,128)(2,1)S(1)}, bf16[256,2048]{1,0:T(8,128)(2,1)}, u32[]{:S(2)}) copy-start(bf16[256,2048]{1,0:T(8,128)(2,1)} %param.13) | copy-start | bytes 3145732
  16.2 177.5 %all-gather.5.cloned.1.call-start = ((), (), s32[]{:S(2)}) async-start(), calls=%async_computation.1 | async-start | bytes 2621440 | tf_op jit(solution)/shard_map/all_gather | solution.py:243
  17.8 2.1 copy-start.3
  19.8 32.6 %collective-permute-start.1 = (bf16[256,4,4,128]{3,0,2,1:T(8,128)(2,1)S(1)}, bf16[256,4,4,128]{3,0,2,1:T(8,128)(2,1)}, u32[]{:S(2)}, u32[]{:S(2)}) collective-permute-start(bf16[256,4,4,128]{3,0,2,1:T(8,128)(2,1)S(1)} %bitcast.183), channel_id=1, source_target_pairs={{0,1},{1,0},{2,3},{3,2},{4,5},{5,4},{6,7},{7,6},{8,9},{9,8},{10,11... | collective-permute-start | bytes 3145736 | tf_op jit(solution)/shard_map/ppermute | solution.py:139
  19.9 22.3 %collective-permute-start.5 = (bf16[4,512,256]{2,1,0:T(8,128)(2,1)S(1)}, bf16[4,512,256]{2,1,0:T(8,128)(2,1)}, u32[]{:S(2)}, u32[]{:S(2)}) collective-permute-start(bf16[4,512,256]{2,1,0:T(8,128)(2,1)S(1)} %bitcast.196), channel_id=1, source_target_pairs={{0,1},{1,0},{2,3},{3,2},{4,5},{5,4},{6,7},{7,6},{8,9},{9,8},{10,11... | collective-permute-start | bytes 3145736 | tf_op jit(solution)/shard_map/ppermute | solution.py:139
  23.3 0.7 collective-permute-start.6
  24.0 0.7 collective-permute-start.7
  24.8 4.5 %collective-permute-start.8 = (bf16[64,2,2,128]{3,0,1,2:T(8,128)(2,1)S(1)}, bf16[64,2,2,128]{3,0,1,2:T(8,128)(2,1)S(1)}, u32[]{:S(2)}, u32[]{:S(2)}) collective-permute-start(bf16[64,2,2,128]{3,0,1,2:T(8,128)(2,1)S(1)} %broadcast_select_fusion.3), channel_id=1, source_target_pairs={{0,8},{2,10},{4,12},{6,14},{1,9},{3,11},{5,13},{7,15}} | collective-permute-start | bytes 196616 | tf_op jit(solution)/shard_map/ppermute | solution.py:174
  26.2 15.1 %collective-permute-start.10 = (bf16[256,2,2,128]{3,0,1,2:T(8,128)(2,1)S(1)}, bf16[256,2,2,128]{3,0,1,2:T(8,128)(2,1)S(1)}, u32[]{:S(2)}, u32[]{:S(2)}) collective-permute-start(bf16[256,2,2,128]{3,0,1,2:T(8,128)(2,1)S(1)} %fusion.57), channel_id=1, source_target_pairs={{0,2},{2,4},{4,6},{6,8},{8,10},{10,12},{12,14},{14,16},{16,18},{18... | collective-permute-start | bytes 786440 | tf_op jit(solution)/shard_map/ppermute | solution.py:169
  29.3 12.0 %collective-permute-start.9 = (bf16[64,2,2,128]{3,0,1,2:T(8,128)(2,1)S(1)}, bf16[64,2,2,128]{3,0,1,2:T(8,128)(2,1)S(1)}, u32[]{:S(2)}, u32[]{:S(2)}) collective-permute-start(bf16[64,2,2,128]{3,0,1,2:T(8,128)(2,1)S(1)} %broadcast_select_fusion.4), channel_id=1, source_target_pairs={{0,16},{2,18},{4,20},{6,22},{8,24},{10,26},{12,28},{14,30},{1,17},... | collective-permute-start | bytes 196616 | tf_op jit(solution)/shard_map/ppermute | solution.py:174
  47.9 6.9 %copy-start.8 = (pred[2]{0:T(512)(128)(4,1)S(1)}, pred[2]{0:T(512)(128)(4,1)}, u32[]{:S(2)}) copy-start(pred[2]{0:T(512)(128)(4,1)} %get-tuple-element.145) | copy-start | bytes 10
  47.9 18.3 %collective-permute-start.14 = (bf16[1024,256]{1,0:T(8,128)(2,1)S(1)}, bf16[1024,256]{1,0:T(8,128)(2,1)}, u32[]{:S(2)}, u32[]{:S(2)}) collective-permute-start(bf16[1024,256]{1,0:T(8,128)(2,1)S(1)} %bitcast.192), channel_id=1, source_target_pairs={{0,8},{8,16},{16,24},{24,0},{1,9},{9,17},{17,25},{25,1},{2,10},{10... | collective-permute-start | bytes 1572872 | tf_op jit(solution)/shard_map/ppermute | solution.py:246
  48.3 51.3 %collective-permute-start.15 = (bf16[1024,256]{1,0:T(8,128)(2,1)S(1)}, bf16[1024,256]{1,0:T(8,128)(2,1)}, u32[]{:S(2)}, u32[]{:S(2)}) collective-permute-start(bf16[1024,256]{1,0:T(8,128)(2,1)S(1)} %bitcast.193), channel_id=1, source_target_pairs={{0,16},{8,24},{16,0},{24,8},{1,17},{9,25},{17,1},{25,9},{2,18},{10... | collective-permute-start | bytes 1572872 | tf_op jit(solution)/shard_map/ppermute | solution.py:246
  52.4 70.0 %collective-permute-start.16 = (bf16[1024,256]{1,0:T(8,128)(2,1)S(1)}, bf16[1024,256]{1,0:T(8,128)(2,1)}, u32[]{:S(2)}, u32[]{:S(2)}) collective-permute-start(bf16[1024,256]{1,0:T(8,128)(2,1)S(1)} %bitcast.194), channel_id=1, source_target_pairs={{0,24},{8,0},{16,8},{24,16},{1,25},{9,1},{17,9},{25,17},{2,26},{10... | collective-permute-start | bytes 1572872 | tf_op jit(solution)/shard_map/ppermute | solution.py:246
  54.8 3.2 %copy-start.4 = (bf16[576,2,2,128]{3,0,1,2:T(8,128)(2,1)S(1)}, bf16[576,2,2,128]{3,0,1,2:T(8,128)(2,1)}, u32[]{:S(2)}) copy-start(bf16[576,2,2,128]{3,0,1,2:T(8,128)(2,1)} %pad_maximum_fusion.5) | copy-start | bytes 1769476
  57.9 7.5 %copy-start.7 = (pred[2]{0:T(512)(128)(4,1)S(1)}, pred[2]{0:T(512)(128)(4,1)}, u32[]{:S(2)}) copy-start(pred[2]{0:T(512)(128)(4,1)} %copy-done.6) | copy-start | bytes 10
  62.9 118.5 %collective-permute-start.11 = (bf16[256,1024]{1,0:T(8,128)(2,1)}, bf16[256,1024]{1,0:T(8,128)(2,1)}, u32[]{:S(2)}, u32[]{:S(2)}) collective-permute-start(bf16[256,1024]{1,0:T(8,128)(2,1)} %copy.64), channel_id=1, source_target_pairs={{0,2},{2,4},{4,6},{6,0},{1,3},{3,5},{5,7},{7,1},{8,10},{10,12},{12... | collective-permute-start | bytes 1572872 | tf_op jit(solution)/shard_map/ppermute | solution.py:228
  63.9 117.7 %collective-permute-start.12 = (bf16[256,1024]{1,0:T(8,128)(2,1)}, bf16[256,1024]{1,0:T(8,128)(2,1)}, u32[]{:S(2)}, u32[]{:S(2)}) collective-permute-start(bf16[256,1024]{1,0:T(8,128)(2,1)} %copy.64), channel_id=1, source_target_pairs={{0,4},{2,6},{4,0},{6,2},{1,5},{3,7},{5,1},{7,3},{8,12},{10,14},{12... | collective-permute-start | bytes 1572872 | tf_op jit(solution)/shard_map/ppermute | solution.py:228
  66.1 115.4 %collective-permute-start.13 = (bf16[256,1024]{1,0:T(8,128)(2,1)}, bf16[256,1024]{1,0:T(8,128)(2,1)}, u32[]{:S(2)}, u32[]{:S(2)}) collective-permute-start(bf16[256,1024]{1,0:T(8,128)(2,1)} %copy.64), channel_id=1, source_target_pairs={{0,6},{2,0},{4,2},{6,4},{1,7},{3,1},{5,3},{7,5},{8,14},{10,8},{12,... | collective-permute-start | bytes 1572872 | tf_op jit(solution)/shard_map/ppermute | solution.py:228
  143.7 5.9 %copy-start = (f32[2,2048,256,4]{2,1,3,0:T(8,128)}, f32[2,2048,256,4]{2,1,3,0:T(8,128)S(1)}, u32[]{:S(2)}) copy-start(f32[2,2048,256,4]{2,1,3,0:T(8,128)S(1)} %get-tuple-element.210) | copy-start | bytes 50331652 | tf_op jit(solution)/shard_map/while
  163.7 5.7 %copy-start = (f32[2,2048,256,4]{2,1,3,0:T(8,128)}, f32[2,2048,256,4]{2,1,3,0:T(8,128)S(1)}, u32[]{:S(2)}) copy-start(f32[2,2048,256,4]{2,1,3,0:T(8,128)S(1)} %get-tuple-element.210) | copy-start | bytes 50331652 | tf_op jit(solution)/shard_map/while
  179.1 14.6 %collective-permute-start.2 = (bf16[256,1024]{0,1:T(8,128)(2,1)S(1)}, bf16[256,1024]{0,1:T(8,128)(2,1)S(1)}, u32[]{:S(2)}, u32[]{:S(2)}) collective-permute-start(bf16[256,1024]{0,1:T(8,128)(2,1)S(1)} %bitcast.202), channel_id=1, source_target_pairs={{0,2},{2,4},{4,6},{6,0},{1,3},{3,5},{5,7},{7,1},{8,10},{10,12},{12... | collective-permute-start | bytes 1572872 | tf_op jit(solution)/shard_map/ppermute | solution.py:228
  179.2 25.7 %collective-permute-start.3 = (bf16[256,1024]{0,1:T(8,128)(2,1)S(1)}, bf16[256,1024]{0,1:T(8,128)(2,1)S(1)}, u32[]{:S(2)}, u32[]{:S(2)}) collective-permute-start(bf16[256,1024]{0,1:T(8,128)(2,1)S(1)} %bitcast.203), channel_id=1, source_target_pairs={{0,4},{2,6},{4,0},{6,2},{1,5},{3,7},{5,1},{7,3},{8,12},{10,14},{12... | collective-permute-start | bytes 1572872 | tf_op jit(solution)/shard_map/ppermute | solution.py:228
  181.4 23.5 %collective-permute-start.4 = (bf16[256,1024]{0,1:T(8,128)(2,1)S(1)}, bf16[256,1024]{0,1:T(8,128)(2,1)S(1)}, u32[]{:S(2)}, u32[]{:S(2)}) collective-permute-start(bf16[256,1024]{0,1:T(8,128)(2,1)S(1)} %bitcast.204), channel_id=1, source_target_pairs={{0,6},{2,0},{4,2},{6,4},{1,7},{3,1},{5,3},{7,5},{8,14},{10,8},{12,... | collective-permute-start | bytes 1572872 | tf_op jit(solution)/shard_map/ppermute | solution.py:228
  210.1 2.0 copy-start.1
  213.7 4.6 %collective-permute-start.17 = (f32[1024,512]{1,0:T(8,128)}, f32[1024,512]{1,0:T(8,128)S(1)}, u32[]{:S(2)}, u32[]{:S(2)}) collective-permute-start(f32[1024,512]{1,0:T(8,128)} %constant_dynamic-slice_fusion), channel_id=1, source_target_pairs={{0,1},{1,0},{2,3},{3,2},{4,5},{5,4},{6,7},{7,6},{8,9},{9,8},{10,11... | collective-permute-start | bytes 6291464 | tf_op jit(solution)/shard_map/ppermute | solution.py:259
  220.4 8.5 %collective-permute-start.18 = (bf16[256,512]{1,0:T(8,128)(2,1)S(1)}, bf16[256,512]{1,0:T(8,128)(2,1)S(1)}, u32[]{:S(2)}, u32[]{:S(2)}) collective-permute-start(bf16[256,512]{1,0:T(8,128)(2,1)S(1)} %get-tuple-element.134), channel_id=1, source_target_pairs={{0,2},{2,4},{4,6},{6,0},{1,3},{3,5},{5,7},{7,1},{8,10},{10,12},{12... | collective-permute-start | bytes 786440 | tf_op jit(solution)/shard_map/ppermute | solution.py:263
  221.6 13.6 %collective-permute-start.19 = (bf16[256,512]{1,0:T(8,128)(2,1)S(1)}, bf16[256,512]{1,0:T(8,128)(2,1)S(1)}, u32[]{:S(2)}, u32[]{:S(2)}) collective-permute-start(bf16[256,512]{1,0:T(8,128)(2,1)S(1)} %get-tuple-element.133), channel_id=1, source_target_pairs={{0,4},{2,6},{4,0},{6,2},{1,5},{3,7},{5,1},{7,3},{8,12},{10,14},{12... | collective-permute-start | bytes 786440 | tf_op jit(solution)/shard_map/ppermute | solution.py:263
  222.3 12.9 %collective-permute-start.20 = (bf16[256,512]{1,0:T(8,128)(2,1)S(1)}, bf16[256,512]{1,0:T(8,128)(2,1)S(1)}, u32[]{:S(2)}, u32[]{:S(2)}) collective-permute-start(bf16[256,512]{1,0:T(8,128)(2,1)S(1)} %get-tuple-element.132), channel_id=1, source_target_pairs={{0,6},{2,0},{4,2},{6,4},{1,7},{3,1},{5,3},{7,5},{8,14},{10,8},{12,... | collective-permute-start | bytes 786440 | tf_op jit(solution)/shard_map/ppermute | solution.py:263
Sparse Core Ops, SparseCore 0:
  16.4 122.4 all-gather.2
  140.4 45.6 all-gather.4

commit v9 on v7

--- a/solution.py
+++ b/solution.py
@@ -243,14 +243,17 @@
     ret_rows = att_ret.shape[1]
     run_stack = jnp.concatenate(plane_pieces(att_run, plane), axis=0)
     ret_stack = jnp.concatenate(plane_pieces(att_ret, plane), axis=0)
-    part = jnp.dot(ret_stack, w_line[:ret_rows], preferred_element_type=jnp.float32) + jnp.dot(
-        run_stack, w_line[ret_rows:], preferred_element_type=jnp.float32
-    )
-    half = part.shape[1] // 2
+    half = w_line.shape[1] // 2
     me = lax.axis_index("head")
-    mine = lax.dynamic_slice_in_dim(part, me * half, half, axis=1)
-    other = lax.dynamic_slice_in_dim(part, (1 - me) * half, half, axis=1)
-    reduced = (mine + lax.ppermute(other, "head", [(0, 1), (1, 0)])).astype(jnp.bfloat16)
+
+    def product(columns):
+        w_half = lax.dynamic_slice_in_dim(w_line, columns * half, half, axis=1)
+        return jnp.dot(ret_stack, w_half[:ret_rows], preferred_element_type=jnp.float32) + jnp.dot(
+            run_stack, w_half[ret_rows:], preferred_element_type=jnp.float32
+        )
+
+    sent = lax.ppermute(product(1 - me), "head", [(0, 1), (1, 0)])
+    reduced = (product(me) + sent).astype(jnp.bfloat16)
     me_cb = lax.axis_index("cb")
     blocks = reduced.reshape(plane, rows, half)
     got = [blocks[0]] + [

time: 240 us -> 237 us (0.988)
  waiting for transfers between devices: 121 us -> 126 us
  local copies, waits for them, and re-layouts: 22.6 us -> 18.8 us
  starting transfers between devices: 27.3 us -> 24.4 us
    all_gather x1, waiting for transfers between devices: 57 us -> 62.4 us  [project_assigned(): w_line = lax.all_gather(w_mine, 'cz', axis=1, tiled=True)]
    ppermute x1, waiting for transfers between devices: 4.37 us -> 0.01 us  [project_assigned(): sent = lax.ppermute(product(1 - me), 'head', [(0, 1), (1, 0)])]
    dot_general x2 -> x4, matrix products: 9.29 us -> 12.7 us  [the longest x2 6.38 us: product(): jnp.dot(ret_stack, w_half[:ret_rows], preferred_element_type=jnp.float32)]
    dynamic_slice x1 -> x0, local copies, waits for them, and re-layouts: 3.11 us -> none  [project_assigned(): other = lax.dynamic_slice_in_dim(part, (1 - me) * half, half, axis=1)]
    ppermute x3, waiting for transfers between devices: 10.5 us -> 12.9 us  [project_assigned(): lax.ppermute(blocks[-shift % plane], 'cb', [(i, (i + shift) % plane) for...]
    unnamed x27 -> x35, local copies, waits for them, and re-layouts: 5.45 us -> 7.04 us
  transfers between devices with their start and end apart: 20 -> 20, of which waited for: 9 -> 8; matrix products, arithmetic and copies ran while one was open for 21% -> 23% of each run, Pallas kernels for 0% -> 0%
where the time goes in v9:
time: 237 us; the launch traced here: 236 us
  waiting for transfers between devices  126 us (53%)
  matrix products  30.8 us (13%)
  starting transfers between devices  24.4 us (10%)
  other arithmetic  21.5 us (9%)
  local copies, waits for them, and re-layouts  18.8 us (8%)
  between operations  14.7 us (6%)
    all_gather x1, waiting for transfers between devices, project_assigned(): w_line = lax.all_gather(w_mine, 'cz', axis=1, tiled=True)  62.4 us
    all_gather x1, waiting for transfers between devices, duo_attend(): lax.all_gather(ret_kv.reshape(rows, ret_per * 2 * HEAD_SIZE), CTX, axis=0...  42.1 us
    ppermute x3, waiting for transfers between devices, project_assigned(): lax.ppermute(blocks[-shift % plane], 'cb', [(i, (i + shift) % plane) for...  12.9 us
    dot_general x2, matrix products, update(): jnp.einsum('hgrk,khd->hgrd', weights.astype(jnp.bfloat16), value_block, p...  11.9 us
    ppermute x4, starting transfers between devices, duo_attend(): got = lax.ppermute(sink_kv, CTX, pairs)  8.34 us
    unnamed x35, local copies, waits for them, and re-layouts  7.04 us
    ppermute x6, starting transfers between devices, plane_pieces(): lax.ppermute(block, 'cb', [(i, (i + shift) % plane) for i in range(plane)])  6.96 us
    dot_general x2, matrix products, product(): jnp.dot(ret_stack, w_half[:ret_rows], preferred_element_type=jnp.float32)  6.38 us
  transfers between devices with their start and end apart: 20, of which 8 were waited for; matrix products, arithmetic and copies ran while one was open for 23% of the time, Pallas kernels for 0%

profile of v9, /device:TPU:0, one launch (start us, length us, event | category | flops | bytes accessed | tf_op | source)
XLA Modules:
  0.0 236.1 jit_solution(10631851837818443404)
XLA Ops:
  7.9 1.1 copy.33
  9.1 1.1 copy.34
  11.6 1.0 sort.17
  14.9 0.9 copy.36
  17.2 1.4 subtract_convert_fusion
  22.6 4.5 %collective-permute-start.6 = (bf16[64,2,2,128]{3,0,1,2:T(8,128)(2,1)S(1)}, bf16[64,2,2,128]{3,0,1,2:T(8,128)(2,1)S(1)}, u32[]{:S(2)}, u32[]{:S(2)}) collective-permute-start(bf16[64,2,2,128]{3,0,1,2:T(8,128)(2,1)S(1)} %slice.91), channel_id=1, source_target_pairs={{0,2},{1,3}} | collective-permute-start | bytes 196616 | tf_op jit(solution)/shard_map/ppermute | solution.py:174
  27.8 2.7 %collective-permute-done.6 = bf16[64,2,2,128]{3,0,1,2:T(8,128)(2,1)S(1)} collective-permute-done((bf16[64,2,2,128]{3,0,1,2:T(8,128)(2,1)S(1)}, bf16[64,2,2,128]{3,0,1,2:T(8,128)(2,1)S(1)}, u32[]{:S(2)}, u32[]{:S(2)}) %collective-permute-start.6) | collective-permute-done | bytes 65568 | tf_op jit(solution)/shard_map/ppermute | solution.py:174
  30.5 1.3 collective-permute-start.7
  31.8 1.9 collective-permute-done.7
  33.7 1.3 collective-permute-start.8
  35.0 0.8 fusion.53
  35.8 4.4 %collective-permute-start.10 = (bf16[256,2,2,128]{3,0,1,2:T(8,128)(2,1)S(1)}, bf16[256,2,2,128]{3,0,1,2:T(8,128)(2,1)S(1)}, u32[]{:S(2)}, u32[]{:S(2)}) collective-permute-start(bf16[256,2,2,128]{3,0,1,2:T(8,128)(2,1)S(1)} %fusion.43), channel_id=1, source_target_pairs={{0,2},{2,4},{4,6},{6,8},{8,10},{10,12},{12,14},{14,16},{16,18},{18... | collective-permute-start | bytes 786440 | tf_op jit(solution)/shard_map/ppermute | solution.py:169
  40.2 1.3 collective-permute-start.9
  41.5 1.8 collective-permute-done.9
  43.4 1.7 collective-permute-done.10
  45.1 0.9 pad_maximum_fusion.6
  46.3 1.5 gather_fusion.5
  47.9 2.0 fusion.17
  49.9 2.1 copy-done
  52.1 1.1 fusion.18
  53.2 1.5 gather_fusion.3
  54.8 4.6 %divide_convert_fusion = bf16[256,2,4,128]{0,3,2,1:T(8,128)(2,1)} fusion(f32[2,576,256,4]{2,1,3,0:T(8,128)} %copy-done, f32[2,4,256]{2,1,0:T(4,128)S(1)} %get-tuple-element.140, pred[256,576]{0,1:T(8,128)(4,1)S(1)} %pad_add_fusion, f32[256,2,4]{0,2,1:T(4,128)S(1)} %bitcast_add_fusion, f32[256,2,4]{0,2,1:T(4,128)S(1)} %get-tuple-element.139, ...), kind=kOutput, calls=%fused_computation.58 | convolution fusion | flops 308674560 | bytes 5709824 | tf_op jit(solution)/shard_map/hgrk,khd->hgrd/dot_general | solution.py:62
  59.3 4.0 %collective-permute-start.13 = (bf16[256,1024]{0,1:T(8,128)(2,1)}, bf16[256,1024]{0,1:T(8,128)(2,1)}, u32[]{:S(2)}, u32[]{:S(2)}) collective-permute-start(bf16[256,1024]{0,1:T(8,128)(2,1)} %bitcast.43), channel_id=1, source_target_pairs={{0,6},{2,0},{4,2},{6,4},{1,7},{3,1},{5,3},{7,5},{8,14},{10,8},{12,... | collective-permute-start | bytes 1572872 | tf_op jit(solution)/shard_map/ppermute | solution.py:228
  63.3 0.9 collective-permute-start.11
  64.2 1.4 select_bitcast_fusion.1
  66.4 1.2 select_bitcast_fusion.4
  67.6 1.3 bitcast_select_fusion.2
  68.9 42.1 %all-gather.3.cloned.1.call-done = bf16[4096,512]{0,1:T(8,128)(2,1)} async-done(((bf16[256,512]{0,1:T(8,128)(2,1)}), bf16[4096,512]{0,1:T(8,128)(2,1)}) %all-gather.3.cloned.1.call-update) | async-done | bytes 4194320 | tf_op jit(solution)/shard_map/all_gather | solution.py:199
  111.1 16.3 %while.15 = (s32[]{:T(128)}, f32[2,4,256]{2,1,0:T(4,128)S(1)}, f32[2,4,256]{2,1,0:T(4,128)S(1)}, f32[2,4,256,128]{3,2,1,0:T(8,128)S(1)}, s32[]{:T(128)}, /*index...) while((s32[]{:T(128)}, f32[2,4,256]{2,1,0:T(4,128)S(1)}, ...), condition=%wide.region_5.8_spmd.clone, body=%wide.region_2.7_spmd.clone.sunk | while | flops 2203064576 | bytes 57297100 | solution.py:216
  111.8 4.2 %fusion.74 = (f32[2,4,256]{2,1,0:T(4,128)S(1)}, f32[2,2048,256,4]{2,1,3,0:T(8,128)S(1)}) fusion(pred[256,2048]{0,1:T(8,128)(4,1)S(1)} %broadcast_compare_fusion.3, bf16[256,2,4,128]{3,0,2,1:T(8,128)(2,1)S(1)} %get-tuple-element.243, bf16[4096,2,2,128]{0,3,2,1:T(8,128)(2,1)} %get-tuple-element.242, s32[]{:T(128)S(6)} %select_n.340), kind=kOutput, calls=%fused_computation.9.clone.1 | convolution fusion | flops 1086322688 | bytes 18882564 | tf_op jit(solution)/shard_map/while/body/rhgd,khd->hgrk/dot_general | solution.py:53
  116.1 4.0 %fusion.75 = f32[2,4,256]{2,1,0:T(4,128)S(1)} fusion(f32[2,2048,256,4]{2,1,3,0:T(8,128)S(1)} %get-tuple-element.208, f32[2,4,256]{2,1,0:T(4,128)S(1)} %max.13, pred[256,2048]{0,1:T(8,128)(4,1)S(1)} %broadcast_compare_fusion.3), kind=kLoop, calls=%fused_computation.11.clone.1 | loop fusion | flops 20969472 | bytes 17317888 | tf_op jit(solution)/shard_map/while/body/reduce_sum | solution.py:61
  120.1 7.3 %fusion.76 = f32[2,4,256,128]{3,2,1,0:T(8,128)S(1)} fusion(f32[2,2048,256,4]{2,1,3,0:T(8,128)S(1)} %get-tuple-element.208, f32[2,4,256]{2,1,0:T(4,128)S(1)} %max.13, pred[256,2048]{0,1:T(8,128)(4,1)S(1)} %broadcast_compare_fusion.3, bf16[4096,2,2,128]{0,3,2,1:T(8,128)(2,1)} %get-tuple-element.242, s32[]{:T(128)S(6)} %select_n.340, s32[]{:T(128)S(6)} %add.307, ...), kind=kOutput, calls=%fused_computation.14.clone.1 | convolution fusion | flops 1095237632 | bytes 20463624 | tf_op jit(solution)/shard_map/while/body/hgrk,khd->hgrd/dot_general | solution.py:62
  127.9 1.3 collective-permute-start.4
  129.2 0.8 collective-permute-start.2
  130.0 62.4 %all-gather.5.cloned.1.call-done = bf16[2048,1024]{1,0:T(8,128)(2,1)} async-done(((bf16[2048,256]{1,0:T(8,128)(2,1)}), bf16[2048,1024]{1,0:T(8,128)(2,1)}) %all-gather.5.cloned.1.call-update) | async-done | bytes 4194320 | tf_op jit(solution)/shard_map/all_gather | solution.py:242
  192.4 3.1 %fusion.29 = f32[1024,512]{1,0:T(8,128)S(1)} fusion(bf16[2048,1024]{1,0:T(8,128)(2,1)} %all-gather.5.cloned.1.call-done, s32[]{:T(128)S(6)} %add.227, s32[]{:T(128)S(6)} %select_n.195, bf16[256,1024]{0,1:T(8,128)(2,1)} %collective-permute-done.13, bf16[256,1024]{0,1:T(8,128)(2,1)} %collective-permute-done.12, ...), kind=kOutput, calls=%fused_computation.47 | convolution fusion | flops 1082130432 | bytes 5242888 | tf_op jit(solution)/shard_map/dot_general | solution.py:251
  195.6 0.8 copy-done.10
  196.4 0.8 copy-done.12
  197.2 3.9 %convolution_add_fusion = f32[1024,512]{1,0:T(8,128)} fusion(f32[1024,512]{1,0:T(8,128)S(1)} %fusion.29, bf16[2048,1024]{1,0:T(8,128)(2,1)} %all-gather.5.cloned.1.call-done, s32[]{:T(128)S(6)} %select_n.195, bf16[256,1024]{0,1:T(8,128)(2,1)S(1)} %collective-permute-done.4, bf16[256,1024]{0,1:T(8,128)(2,1)S(1)} %collective-permute-done.3, ...), kind=kOutput, calls=%fused_computation.44 | convolution fusion | flops 1082654720 | bytes 7340036 | tf_op jit(solution)/shard_map/dot_general | solution.py:251
  201.1 3.2 %fusion.32 = f32[1024,512]{1,0:T(8,128)S(1)} fusion(bf16[2048,1024]{1,0:T(8,128)(2,1)} %all-gather.5.cloned.1.call-done, s32[]{:T(128)S(6)} %add.227, s32[]{:T(128)S(6)} %select_n.184, bf16[256,1024]{0,1:T(8,128)(2,1)} %collective-permute-done.13, bf16[256,1024]{0,1:T(8,128)(2,1)} %collective-permute-done.12, ...), kind=kOutput, calls=%fused_computation.50 | convolution fusion | flops 1082130432 | bytes 5242888 | tf_op jit(solution)/shard_map/dot_general | solution.py:251
  204.3 2.5 %fusion.34 = f32[1024,512]{1,0:T(8,128)S(1)} fusion(bf16[2048,1024]{1,0:T(8,128)(2,1)} %all-gather.5.cloned.1.call-done, s32[]{:T(128)S(6)} %select_n.184, bf16[256,1024]{0,1:T(8,128)(2,1)S(1)} %collective-permute-done.4, bf16[256,1024]{0,1:T(8,128)(2,1)S(1)} %copy-done.11, bf16[256,1024]{0,1:T(8,128)(2,1)S(1)} %copy-done.13, ...), kind=kOutput, calls=%fused_computation.52 | convolution fusion | flops 1082130432 | bytes 5242884 | tf_op jit(solution)/shard_map/dot_general | solution.py:251
  206.8 0.8 add_convert_fusion
  207.8 2.4 %collective-permute-start.17 = (bf16[256,512]{1,0:T(8,128)(2,1)S(1)}, bf16[256,512]{1,0:T(8,128)(2,1)S(1)}, u32[]{:S(2)}, u32[]{:S(2)}) collective-permute-start(bf16[256,512]{1,0:T(8,128)(2,1)S(1)} %get-tuple-element.132), channel_id=1, source_target_pairs={{0,6},{2,0},{4,2},{6,4},{1,7},{3,1},{5,3},{7,5},{8,14},{10,8},{12,... | collective-permute-start | bytes 786440 | tf_op jit(solution)/shard_map/ppermute | solution.py:260
  211.4 5.6 %collective-permute-done.17 = bf16[256,512]{1,0:T(8,128)(2,1)S(1)} collective-permute-done((bf16[256,512]{1,0:T(8,128)(2,1)S(1)}, bf16[256,512]{1,0:T(8,128)(2,1)S(1)}, u32[]{:S(2)}, u32[]{:S(2)}) %collective-permute-start.17) | collective-permute-done | bytes 262176 | tf_op jit(solution)/shard_map/ppermute | solution.py:260
  217.0 7.3 %collective-permute-done.16 = bf16[256,512]{1,0:T(8,128)(2,1)S(1)} collective-permute-done((bf16[256,512]{1,0:T(8,128)(2,1)S(1)}, bf16[256,512]{1,0:T(8,128)(2,1)S(1)}, u32[]{:S(2)}, u32[]{:S(2)}) %collective-permute-start.16) | collective-permute-done | bytes 262176 | tf_op jit(solution)/shard_map/ppermute | solution.py:260
  225.3 1.0 fusion.36
  226.3 1.4 copy.44
  227.7 1.6 reshape.372
  (117 shorter events, 15.1 us)
Async XLA Ops:
  6.5 4.9 %copy-start.14 = (s32[4]{0:T(128)S(1)}, s32[4]{0:T(128)}, u32[]{:S(2)}) copy-start(s32[4]{0:T(128)} %param.17) | copy-start | bytes 52
  6.5 104.5 %all-gather.3.cloned.1.call-start = ((), (), s32[]{:S(2)}) async-start(), calls=%async_computation | async-start | bytes 4456448 | tf_op jit(solution)/shard_map/all_gather | solution.py:199
  10.6 2.6 %collective-permute-start = (bf16[256,4,2,128]{0,3,1,2:T(8,128)(2,1)S(1)}, bf16[256,4,2,128]{0,3,1,2:T(8,128)(2,1)S(1)}, u32[]{:S(2)}, u32[]{:S(2)}) collective-permute-start(bf16[256,4,2,128]{0,3,1,2:T(8,128)(2,1)S(1)} %pad_maximum_fusion.7), channel_id=1, source_target_pairs={{0,1},{1,0},{2,3},{3,2},{4,5},{5,4},{6,7},{7,6},{8,9},{9,8},{10,11... | collective-permute-start | bytes 1572872 | tf_op jit(solution)/shard_map/ppermute | solution.py:139
  11.2 53.0 %collective-permute-start.5 = (bf16[4,512,256]{2,1,0:T(8,128)(2,1)}, bf16[4,512,256]{2,1,0:T(8,128)(2,1)}, u32[]{:S(2)}, u32[]{:S(2)}) collective-permute-start(bf16[4,512,256]{2,1,0:T(8,128)(2,1)} %bitcast.182), channel_id=1, source_target_pairs={{0,1},{1,0},{2,3},{3,2},{4,5},{5,4},{6,7},{7,6},{8,9},{9,8},{10,11... | collective-permute-start | bytes 3145736 | tf_op jit(solution)/shard_map/ppermute | solution.py:139
  11.3 4.5 %copy-start.1 = (bf16[256,2048]{1,0:T(8,128)(2,1)S(1)}, bf16[256,2048]{1,0:T(8,128)(2,1)}, u32[]{:S(2)}) copy-start(bf16[256,2048]{1,0:T(8,128)(2,1)} %param.13) | copy-start | bytes 3145732
  13.2 2.9 %copy-start.5 = (pred[2]{0:T(512)(128)(4,1)}, pred[2]{0:T(512)(128)(4,1)S(1)}, u32[]{:S(2)}) copy-start(pred[2]{0:T(512)(128)(4,1)S(1)} %get-tuple-element.117) | copy-start | bytes 10
  13.2 6.5 %copy-start.8 = (s32[2]{0:T(128)}, s32[2]{0:T(128)S(1)}, u32[]{:S(2)}) copy-start(s32[2]{0:T(128)S(1)} %get-tuple-element.118) | copy-start | bytes 28
  13.2 7.1 %copy-start.9 = (s32[2]{0:T(128)}, s32[2]{0:T(128)S(1)}, u32[]{:S(2)}) copy-start(s32[2]{0:T(128)S(1)} %get-tuple-element.144) | copy-start | bytes 28
  13.2 2.9 %copy-start.4 = (s32[1024]{0:T(1024)}, s32[1024]{0:T(1024)S(1)}, u32[]{:S(2)}) copy-start(s32[1024]{0:T(1024)S(1)} %pad_clamp_fusion.3) | copy-start | bytes 12292
  15.8 176.6 %all-gather.5.cloned.1.call-start = ((), (), s32[]{:S(2)}) async-start(), calls=%async_computation.1 | async-start | bytes 5242880 | tf_op jit(solution)/shard_map/all_gather | solution.py:242
  19.2 26.8 %collective-permute-start.1 = (bf16[256,4,4,128]{3,0,2,1:T(8,128)(2,1)S(1)}, bf16[256,4,4,128]{3,0,2,1:T(8,128)(2,1)S(1)}, u32[]{:S(2)}, u32[]{:S(2)}) collective-permute-start(bf16[256,4,4,128]{3,0,2,1:T(8,128)(2,1)S(1)} %bitcast.175), channel_id=1, source_target_pairs={{0,1},{1,0},{2,3},{3,2},{4,5},{5,4},{6,7},{7,6},{8,9},{9,8},{10,11... | collective-permute-start | bytes 3145736 | tf_op jit(solution)/shard_map/ppermute | solution.py:139
  22.6 7.9 %collective-permute-start.6 = (bf16[64,2,2,128]{3,0,1,2:T(8,128)(2,1)S(1)}, bf16[64,2,2,128]{3,0,1,2:T(8,128)(2,1)S(1)}, u32[]{:S(2)}, u32[]{:S(2)}) collective-permute-start(bf16[64,2,2,128]{3,0,1,2:T(8,128)(2,1)S(1)} %slice.91), channel_id=1, source_target_pairs={{0,2},{1,3}} | collective-permute-start | bytes 196616 | tf_op jit(solution)/shard_map/ppermute | solution.py:174
  30.5 3.2 %collective-permute-start.7 = (bf16[64,2,2,128]{3,0,1,2:T(8,128)(2,1)S(1)}, bf16[64,2,2,128]{3,0,1,2:T(8,128)(2,1)S(1)}, u32[]{:S(2)}, u32[]{:S(2)}) collective-permute-start(bf16[64,2,2,128]{3,0,1,2:T(8,128)(2,1)S(1)} %broadcast_select_fusion.1), channel_id=1, source_target_pairs={{0,4},{2,6},{1,5},{3,7}} | collective-permute-start | bytes 196616 | tf_op jit(solution)/shard_map/ppermute | solution.py:174
  33.7 6.5 %collective-permute-start.8 = (bf16[64,2,2,128]{3,0,1,2:T(8,128)(2,1)S(1)}, bf16[64,2,2,128]{3,0,1,2:T(8,128)(2,1)S(1)}, u32[]{:S(2)}, u32[]{:S(2)}) collective-permute-start(bf16[64,2,2,128]{3,0,1,2:T(8,128)(2,1)S(1)} %broadcast_select_fusion.2), channel_id=1, source_target_pairs={{0,8},{2,10},{4,12},{6,14},{1,9},{3,11},{5,13},{7,15}} | collective-permute-start | bytes 196616 | tf_op jit(solution)/shard_map/ppermute | solution.py:174
  35.8 9.4 %collective-permute-start.10 = (bf16[256,2,2,128]{3,0,1,2:T(8,128)(2,1)S(1)}, bf16[256,2,2,128]{3,0,1,2:T(8,128)(2,1)S(1)}, u32[]{:S(2)}, u32[]{:S(2)}) collective-permute-start(bf16[256,2,2,128]{3,0,1,2:T(8,128)(2,1)S(1)} %fusion.43), channel_id=1, source_target_pairs={{0,2},{2,4},{4,6},{6,8},{8,10},{10,12},{12,14},{14,16},{16,18},{18... | collective-permute-start | bytes 786440 | tf_op jit(solution)/shard_map/ppermute | solution.py:169
  40.2 3.2 %collective-permute-start.9 = (bf16[64,2,2,128]{3,0,1,2:T(8,128)(2,1)S(1)}, bf16[64,2,2,128]{3,0,1,2:T(8,128)(2,1)S(1)}, u32[]{:S(2)}, u32[]{:S(2)}) collective-permute-start(bf16[64,2,2,128]{3,0,1,2:T(8,128)(2,1)S(1)} %broadcast_select_fusion.3), channel_id=1, source_target_pairs={{0,16},{2,18},{4,20},{6,22},{8,24},{10,26},{12,28},{14,30},{1,17},... | collective-permute-start | bytes 196616 | tf_op jit(solution)/shard_map/ppermute | solution.py:174
  46.0 1.9 copy-start.7
  46.1 1.8 copy-start.3
  49.9 2.2 copy-start
  54.8 9.5 %copy-start.2 = (bf16[2048,256]{1,0:T(8,128)(2,1)S(1)}, bf16[2048,256]{1,0:T(8,128)(2,1)}, u32[]{:S(2)}) copy-start(bf16[2048,256]{1,0:T(8,128)(2,1)} %param.19) | copy-start | bytes 3145732
  59.3 69.9 %collective-permute-start.13 = (bf16[256,1024]{0,1:T(8,128)(2,1)}, bf16[256,1024]{0,1:T(8,128)(2,1)}, u32[]{:S(2)}, u32[]{:S(2)}) collective-permute-start(bf16[256,1024]{0,1:T(8,128)(2,1)} %bitcast.43), channel_id=1, source_target_pairs={{0,6},{2,0},{4,2},{6,4},{1,7},{3,1},{5,3},{7,5},{8,14},{10,8},{12,... | collective-permute-start | bytes 1572872 | tf_op jit(solution)/shard_map/ppermute | solution.py:228
  63.3 66.7 %collective-permute-start.12 = (bf16[256,1024]{0,1:T(8,128)(2,1)}, bf16[256,1024]{0,1:T(8,128)(2,1)}, u32[]{:S(2)}, u32[]{:S(2)}) collective-permute-start(bf16[256,1024]{0,1:T(8,128)(2,1)} %bitcast.43), channel_id=1, source_target_pairs={{0,4},{2,6},{4,0},{6,2},{1,5},{3,7},{5,1},{7,3},{8,12},{10,14},{12... | collective-permute-start | bytes 1572872 | tf_op jit(solution)/shard_map/ppermute | solution.py:228
  63.3 66.7 %collective-permute-start.11 = (bf16[256,1024]{0,1:T(8,128)(2,1)}, bf16[256,1024]{0,1:T(8,128)(2,1)}, u32[]{:S(2)}, u32[]{:S(2)}) collective-permute-start(bf16[256,1024]{0,1:T(8,128)(2,1)} %bitcast.43), channel_id=1, source_target_pairs={{0,2},{2,4},{4,6},{6,0},{1,3},{3,5},{5,7},{7,1},{8,10},{10,12},{12... | collective-permute-start | bytes 1572872 | tf_op jit(solution)/shard_map/ppermute | solution.py:228
  65.6 0.8 copy-start.6
  127.9 67.7 %collective-permute-start.4 = (bf16[256,1024]{0,1:T(8,128)(2,1)S(1)}, bf16[256,1024]{0,1:T(8,128)(2,1)S(1)}, u32[]{:S(2)}, u32[]{:S(2)}) collective-permute-start(bf16[256,1024]{0,1:T(8,128)(2,1)S(1)} %bitcast.188), channel_id=1, source_target_pairs={{0,6},{2,0},{4,2},{6,4},{1,7},{3,1},{5,3},{7,5},{8,14},{10,8},{12,... | collective-permute-start | bytes 1572872 | tf_op jit(solution)/shard_map/ppermute | solution.py:228
  129.2 66.4 %collective-permute-start.3 = (bf16[256,1024]{0,1:T(8,128)(2,1)S(1)}, bf16[256,1024]{0,1:T(8,128)(2,1)S(1)}, u32[]{:S(2)}, u32[]{:S(2)}) collective-permute-start(bf16[256,1024]{0,1:T(8,128)(2,1)S(1)} %bitcast.189), channel_id=1, source_target_pairs={{0,4},{2,6},{4,0},{6,2},{1,5},{3,7},{5,1},{7,3},{8,12},{10,14},{12... | collective-permute-start | bytes 1572872 | tf_op jit(solution)/shard_map/ppermute | solution.py:228
  129.2 66.4 %collective-permute-start.2 = (bf16[256,1024]{0,1:T(8,128)(2,1)S(1)}, bf16[256,1024]{0,1:T(8,128)(2,1)S(1)}, u32[]{:S(2)}, u32[]{:S(2)}) collective-permute-start(bf16[256,1024]{0,1:T(8,128)(2,1)S(1)} %bitcast.190), channel_id=1, source_target_pairs={{0,2},{2,4},{4,6},{6,0},{1,3},{3,5},{5,7},{7,1},{8,10},{10,12},{12... | collective-permute-start | bytes 1572872 | tf_op jit(solution)/shard_map/ppermute | solution.py:228
  195.6 0.8 copy-start.10
  196.4 0.8 copy-start.12
  201.1 5.8 %collective-permute-start.14 = (f32[1024,512]{1,0:T(8,128)}, f32[1024,512]{1,0:T(8,128)S(1)}, u32[]{:S(2)}, u32[]{:S(2)}) collective-permute-start(f32[1024,512]{1,0:T(8,128)} %convolution_add_fusion), channel_id=1, source_target_pairs={{0,1},{1,0},{2,3},{3,2},{4,5},{5,4},{6,7},{7,6},{8,9},{9,8},{10,11... | collective-permute-start | bytes 6291464 | tf_op jit(solution)/shard_map/ppermute | solution.py:255
  201.1 3.2 %copy-start.11 = (bf16[256,1024]{0,1:T(8,128)(2,1)S(1)}, bf16[256,1024]{0,1:T(8,128)(2,1)}, u32[]{:S(2)}) copy-start(bf16[256,1024]{0,1:T(8,128)(2,1)} %copy-done.10) | copy-start | bytes 1572868
  201.1 3.2 %copy-start.13 = (bf16[256,1024]{0,1:T(8,128)(2,1)S(1)}, bf16[256,1024]{0,1:T(8,128)(2,1)}, u32[]{:S(2)}) copy-start(bf16[256,1024]{0,1:T(8,128)(2,1)} %copy-done.12) | copy-start | bytes 1572868
  207.8 9.2 %collective-permute-start.17 = (bf16[256,512]{1,0:T(8,128)(2,1)S(1)}, bf16[256,512]{1,0:T(8,128)(2,1)S(1)}, u32[]{:S(2)}, u32[]{:S(2)}) collective-permute-start(bf16[256,512]{1,0:T(8,128)(2,1)S(1)} %get-tuple-element.132), channel_id=1, source_target_pairs={{0,6},{2,0},{4,2},{6,4},{1,7},{3,1},{5,3},{7,5},{8,14},{10,8},{12,... | collective-permute-start | bytes 786440 | tf_op jit(solution)/shard_map/ppermute | solution.py:260
  210.2 14.1 %collective-permute-start.16 = (bf16[256,512]{1,0:T(8,128)(2,1)S(1)}, bf16[256,512]{1,0:T(8,128)(2,1)S(1)}, u32[]{:S(2)}, u32[]{:S(2)}) collective-permute-start(bf16[256,512]{1,0:T(8,128)(2,1)S(1)} %get-tuple-element.133), channel_id=1, source_target_pairs={{0,4},{2,6},{4,0},{6,2},{1,5},{3,7},{5,1},{7,3},{8,12},{10,14},{12... | collective-permute-start | bytes 786440 | tf_op jit(solution)/shard_map/ppermute | solution.py:260
  210.8 13.5 %collective-permute-start.15 = (bf16[256,512]{1,0:T(8,128)(2,1)S(1)}, bf16[256,512]{1,0:T(8,128)(2,1)S(1)}, u32[]{:S(2)}, u32[]{:S(2)}) collective-permute-start(bf16[256,512]{1,0:T(8,128)(2,1)S(1)} %get-tuple-element.134), channel_id=1, source_target_pairs={{0,2},{2,4},{4,6},{6,0},{1,3},{3,5},{5,7},{7,1},{8,10},{10,12},{12... | collective-permute-start | bytes 786440 | tf_op jit(solution)/shard_map/ppermute | solution.py:260
Sparse Core Ops, SparseCore 0:
  15.9 95.0 all-gather.2
  112.6 79.7 all-gather.4

commit v10 on v9

--- a/solution.py
+++ b/solution.py
@@ -196,8 +196,9 @@
     run_out = run_accum / run_totals[..., None]
 
     ret_kv = jnp.take(kv_all, ret_ids, axis=1)
-    ret_shard = lax.all_gather(ret_kv.reshape(rows, ret_per * 2 * HEAD_SIZE), CTX, axis=0, tiled=True)
-    ret_shard = ret_shard.reshape(ctx_count * rows, ret_per, 2, HEAD_SIZE)
+    along = lax.all_gather(ret_kv.reshape(rows, ret_per * 2 * HEAD_SIZE), "cz", axis=0, tiled=False)
+    ret_shard = lax.all_gather(along, "cb", axis=0, tiled=False)
+    ret_shard = ret_shard.transpose(1, 0, 2, 3).reshape(ctx_count * rows, ret_per, 2, HEAD_SIZE)
     q_ret = jnp.take(q_all, ret_ids, axis=1)
     sub_rows = math.gcd(ctx_count * rows, 2048)
     turn_count = (ctx_index * rows + rows + sub_rows - 1) // sub_rows

time: 237 us -> 253 us (1.068)
  local copies, waits for them, and re-layouts: 18.8 us -> 36.1 us
  starting transfers between devices: 24.4 us -> 33.7 us
  waiting for transfers between devices: 126 us -> 118 us
    all_gather x1, waiting for transfers between devices: 62.4 us -> 47.6 us  [project_assigned(): w_line = lax.all_gather(w_mine, 'cz', axis=1, tiled=True)]
    ppermute x6, starting transfers between devices: 6.96 us -> 17.2 us  [plane_pieces(): lax.ppermute(block, 'cb', [(i, (i + shift) % plane) for i in range(plane)])]
    reshape x0 -> x1, local copies, waits for them, and re-layouts: none -> 6.95 us  [duo_attend(): ret_shard.transpose(1, 0, 2, 3)]
    slice x0 -> x1, local copies, waits for them, and re-layouts: none -> 5.46 us  [one_turn(): return update(q_ret, block[:, :, 0], block[:, :, 1], visible, state)]
    all_gather x1 -> x2, waiting for transfers between devices: 42.1 us -> 46.8 us  [the longest x1 26.3 us: duo_attend(): lax.all_gather(ret_kv.reshape(rows, ret_per * 2 * HEAD_SIZE), 'cz', axis=...]
    all_gather x0 -> x1, local copies, waits for them, and re-layouts: none -> 4.61 us  [duo_attend(): ret_shard = lax.all_gather(along, 'cb', axis=0, tiled=False)]
    ppermute x1, waiting for transfers between devices: 1.74 us -> 4.31 us  [duo_attend(): lax.ppermute(run_kv, CTX, [(i, i + 1) for i in range(ctx_count - 1)])]
    unnamed x35 -> x33, local copies, waits for them, and re-layouts: 7.04 us -> 7.17 us
  transfers between devices with their start and end apart: 20 -> 21, of which waited for: 8 -> 9; matrix products, arithmetic and copies ran while one was open for 23% -> 26% of each run, Pallas kernels for 0% -> 0%
where the time goes in v10:
time: 253 us; the launch traced here: 252 us
  waiting for transfers between devices  118 us (47%)
  local copies, waits for them, and re-layouts  36.1 us (14%)
  starting transfers between devices  33.7 us (13%)
  matrix products  28.3 us (11%)
  other arithmetic  21.8 us (9%)
  between operations  14.4 us (6%)
    all_gather x1, waiting for transfers between devices, project_assigned(): w_line = lax.all_gather(w_mine, 'cz', axis=1, tiled=True)  47.6 us
    all_gather x1, waiting for transfers between devices, duo_attend(): lax.all_gather(ret_kv.reshape(rows, ret_per * 2 * HEAD_SIZE), 'cz', axis=...  26.3 us
    all_gather x1, waiting for transfers between devices, duo_attend(): ret_shard = lax.all_gather(along, 'cb', axis=0, tiled=False)  20.5 us
    ppermute x6, starting transfers between devices, plane_pieces(): lax.ppermute(block, 'cb', [(i, (i + shift) % plane) for i in range(plane)])  17.2 us
    ppermute x3, waiting for transfers between devices, project_assigned(): lax.ppermute(blocks[-shift % plane], 'cb', [(i, (i + shift) % plane) for...  12.9 us
    dot_general x2, matrix products, update(): jnp.einsum('hgrk,khd->hgrd', weights.astype(jnp.bfloat16), value_block, p...  10.8 us
    ppermute x4, starting transfers between devices, duo_attend(): got = lax.ppermute(sink_kv, CTX, pairs)  7.25 us
    unnamed x33, local copies, waits for them, and re-layouts  7.17 us
  transfers between devices with their start and end apart: 21, of which 9 were waited for; matrix products, arithmetic and copies ran while one was open for 26% of the time, Pallas kernels for 0%

profile of v10, /device:TPU:0, one launch (start us, length us, event | category | flops | bytes accessed | tf_op | source)
XLA Modules:
  0.0 252.1 jit_solution(6340634579636782364)
XLA Ops:
  7.9 1.1 copy.50
  9.1 1.1 copy.51
  11.9 1.0 sort.17
  15.3 0.8 copy.54
  17.9 1.4 subtract_convert_fusion
  20.4 26.3 %all-gather.5.cloned.1.call-done = bf16[4,256,512]{2,1,0:T(8,128)(2,1)} async-done(((bf16[1,256,512]{2,1,0:T(8,128)(2,1)}), bf16[4,256,512]{2,1,0:T(8,128)(2,1)}) %all-gather.5.cloned.1.call-update) | async-done | bytes 1048592 | tf_op jit(solution)/shard_map/all_gather | solution.py:199
  49.7 3.4 %collective-permute-start.6 = (bf16[64,2,2,128]{3,0,1,2:T(8,128)(2,1)S(1)}, bf16[64,2,2,128]{3,0,1,2:T(8,128)(2,1)S(1)}, u32[]{:S(2)}, u32[]{:S(2)}) collective-permute-start(bf16[64,2,2,128]{3,0,1,2:T(8,128)(2,1)S(1)} %slice.91), channel_id=1, source_target_pairs={{0,2},{1,3}} | collective-permute-start | bytes 196616 | tf_op jit(solution)/shard_map/ppermute | solution.py:174
  53.8 1.2 collective-permute-done.6
  54.9 1.3 collective-permute-start.7
  56.3 2.9 %collective-permute-done.7 = bf16[64,2,2,128]{3,0,1,2:T(8,128)(2,1)S(1)} collective-permute-done((bf16[64,2,2,128]{3,0,1,2:T(8,128)(2,1)S(1)}, bf16[64,2,2,128]{3,0,1,2:T(8,128)(2,1)S(1)}, u32[]{:S(2)}, u32[]{:S(2)}) %collective-permute-start.7) | collective-permute-done | bytes 65568 | tf_op jit(solution)/shard_map/ppermute | solution.py:174
  59.2 1.3 collective-permute-start.8
  61.2 4.4 %collective-permute-start.10 = (bf16[256,2,2,128]{3,0,1,2:T(8,128)(2,1)S(1)}, bf16[256,2,2,128]{3,0,1,2:T(8,128)(2,1)S(1)}, u32[]{:S(2)}, u32[]{:S(2)}) collective-permute-start(bf16[256,2,2,128]{3,0,1,2:T(8,128)(2,1)S(1)} %fusion.41), channel_id=1, source_target_pairs={{0,2},{2,4},{4,6},{6,8},{8,10},{10,12},{12,14},{14,16},{16,18},{18... | collective-permute-start | bytes 786440 | tf_op jit(solution)/shard_map/ppermute | solution.py:169
  65.6 1.3 collective-permute-start.9
  67.0 1.8 collective-permute-done.9
  68.8 4.3 %collective-permute-done.10 = bf16[256,2,2,128]{3,0,1,2:T(8,128)(2,1)S(1)} collective-permute-done((bf16[256,2,2,128]{3,0,1,2:T(8,128)(2,1)S(1)}, bf16[256,2,2,128]{3,0,1,2:T(8,128)(2,1)S(1)}, u32[]{:S(2)}, u32[]{:S(2)}) %collective-permute-start.10) | collective-permute-done | bytes 262176 | tf_op jit(solution)/shard_map/ppermute | solution.py:169
  73.2 0.9 pad_maximum_fusion.6
  74.4 1.5 gather_fusion.5
  75.9 2.0 fusion.15
  77.9 2.3 copy-done
  80.2 1.1 fusion.16
  81.4 1.5 gather_fusion.3
  82.9 4.5 %divide_convert_fusion = bf16[256,2,4,128]{0,3,2,1:T(8,128)(2,1)} fusion(f32[2,576,256,4]{2,1,3,0:T(8,128)} %copy-done, f32[2,4,256]{2,1,0:T(4,128)S(1)} %get-tuple-element.150, pred[256,576]{0,1:T(8,128)(4,1)S(1)} %pad_add_fusion, f32[256,2,4]{0,2,1:T(4,128)S(1)} %bitcast_add_fusion, f32[256,2,4]{0,2,1:T(4,128)S(1)} %get-tuple-element.149, ...), kind=kOutput, calls=%fused_computation.59 | convolution fusion | flops 308674560 | bytes 5709824 | tf_op jit(solution)/shard_map/hgrk,khd->hgrd/dot_general | solution.py:62
  87.4 3.5 %collective-permute-start.13 = (bf16[256,1024]{0,1:T(8,128)(2,1)}, bf16[256,1024]{0,1:T(8,128)(2,1)}, u32[]{:S(2)}, u32[]{:S(2)}) collective-permute-start(bf16[256,1024]{0,1:T(8,128)(2,1)} %bitcast.44), channel_id=1, source_target_pairs={{0,6},{2,0},{4,2},{6,4},{1,7},{3,1},{5,3},{7,5},{8,14},{10,8},{12,... | collective-permute-start | bytes 1572872 | tf_op jit(solution)/shard_map/ppermute | solution.py:229
  91.4 1.5 collective-permute-start.11
  92.9 1.4 select_bitcast_fusion.1
  95.1 1.2 select_bitcast_fusion.4
  96.3 1.3 bitcast_select_fusion.2
  97.6 20.5 %all-gather.9.cloned.1.call-done = bf16[16,256,512]{2,1,0:T(8,128)(2,1)} async-done(((bf16[4,256,512]{2,1,0:T(8,128)(2,1)}), bf16[16,256,512]{2,1,0:T(8,128)(2,1)}) %all-gather.9.cloned.1.call-update) | async-done | bytes 4194320 | tf_op jit(solution)/shard_map/all_gather | solution.py:200
  118.1 4.6 %copy.90 = bf16[4,4,256,512]{3,2,0,1:T(8,128)(2,1)} copy(bf16[4,4,256,512]{3,2,1,0:T(8,128)(2,1)} %bitcast.180) | data formatting | bytes 8388608 | tf_op jit(solution)/shard_map/all_gather | solution.py:200
  122.7 7.0 %reshape.362 = bf16[4096,2,2,128]{3,2,1,0:T(2,128)(2,1)} reshape(bf16[4,4,256,512]{3,2,1,0:T(8,128)(2,1)} %bitcast.174) | data formatting | bytes 8388608 | tf_op jit(solution)/shard_map/reshape | solution.py:201
  129.8 19.3 %while.15 = (s32[]{:T(128)}, f32[2,4,256]{2,1,0:T(4,128)S(1)}, f32[2,4,256]{2,1,0:T(4,128)S(1)}, f32[2,4,256,128]{3,2,1,0:T(8,128)S(1)}, s32[]{:T(128)}, /*index...) while((s32[]{:T(128)}, f32[2,4,256]{2,1,0:T(4,128)S(1)}, ...), condition=%wide.region_5.8_spmd.clone, body=%wide.region_2.7_spmd.clone.sunk | while | flops 2203064576 | bytes 61491400 | solution.py:217
  130.5 5.5 %constant_dynamic-slice_fusion.3 = (bf16[2048,2,1,128]{3,2,1,0:T(2,128)(2,1)S(1)}, bf16[2048,2,1,128]{3,2,1,0:T(2,128)(2,1)S(1)}) fusion(bf16[4096,2,2,128]{3,2,1,0:T(2,128)(2,1)} %get-tuple-element.256, s32[]{:T(128)S(6)} %select_n.340, s32[]{:T(128)S(6)} %add.307), kind=kLoop, calls=%fused_computation.24.clone.1 | loop fusion | bytes 4194312 | tf_op jit(solution)/shard_map/while/body/slice | solution.py:210
  135.9 2.7 %fusion.72 = (f32[2,4,256]{2,1,0:T(4,128)S(1)}, f32[2,2048,256,4]{2,1,3,0:T(8,128)S(1)}) fusion(pred[256,2048]{0,1:T(8,128)(4,1)S(1)} %broadcast_compare_fusion.3, bf16[256,2,4,128]{3,0,2,1:T(8,128)(2,1)S(1)} %get-tuple-element.257, bf16[2048,2,1,128]{3,2,1,0:T(2,128)(2,1)S(1)} %get-tuple-element.219), kind=kOutput, calls=%fused_computation.9.clone.1 | convolution fusion | flops 1086322688 | bytes 18882560 | tf_op jit(solution)/shard_map/while/body/rhgd,khd->hgrk/dot_general | solution.py:53
  138.7 4.0 %fusion.73 = f32[2,4,256]{2,1,0:T(4,128)S(1)} fusion(f32[2,2048,256,4]{2,1,3,0:T(8,128)S(1)} %get-tuple-element.221, f32[2,4,256]{2,1,0:T(4,128)S(1)} %max.13, pred[256,2048]{0,1:T(8,128)(4,1)S(1)} %broadcast_compare_fusion.3), kind=kLoop, calls=%fused_computation.11.clone.1 | loop fusion | flops 20969472 | bytes 17317888 | tf_op jit(solution)/shard_map/while/body/reduce_sum | solution.py:61
  142.8 6.3 %fusion.74 = f32[2,4,256,128]{3,2,1,0:T(8,128)S(1)} fusion(f32[2,2048,256,4]{2,1,3,0:T(8,128)S(1)} %get-tuple-element.221, f32[2,4,256]{2,1,0:T(4,128)S(1)} %max.13, pred[256,2048]{0,1:T(8,128)(4,1)S(1)} %broadcast_compare_fusion.3, bf16[2048,2,1,128]{3,2,1,0:T(2,128)(2,1)S(1)} %get-tuple-element.224, ...), kind=kOutput, calls=%fused_computation.14.clone.1 | convolution fusion | flops 1095237632 | bytes 20463616 | tf_op jit(solution)/shard_map/while/body/hgrk,khd->hgrd/dot_general | solution.py:62
  149.5 10.1 %collective-permute-start.4 = (bf16[256,1024]{0,1:T(8,128)(2,1)S(1)}, bf16[256,1024]{0,1:T(8,128)(2,1)S(1)}, u32[]{:S(2)}, u32[]{:S(2)}) collective-permute-start(bf16[256,1024]{0,1:T(8,128)(2,1)S(1)} %bitcast.192), channel_id=1, source_target_pairs={{0,6},{2,0},{4,2},{6,4},{1,7},{3,1},{5,3},{7,5},{8,14},{10,8},{12,... | collective-permute-start | bytes 1572872 | tf_op jit(solution)/shard_map/ppermute | solution.py:229
  159.6 1.6 collective-permute-start.3
  161.2 47.6 %all-gather.7.cloned.1.call-done = bf16[2048,1024]{1,0:T(8,128)(2,1)} async-done(((bf16[2048,256]{1,0:T(8,128)(2,1)}), bf16[2048,1024]{1,0:T(8,128)(2,1)}) %all-gather.7.cloned.1.call-update) | async-done | bytes 4194320 | tf_op jit(solution)/shard_map/all_gather | solution.py:243
  208.8 3.1 %fusion.27 = f32[1024,512]{1,0:T(8,128)S(1)} fusion(bf16[2048,1024]{1,0:T(8,128)(2,1)} %all-gather.7.cloned.1.call-done, s32[]{:T(128)S(6)} %add.227, s32[]{:T(128)S(6)} %select_n.195, bf16[256,1024]{0,1:T(8,128)(2,1)} %collective-permute-done.13, bf16[256,1024]{0,1:T(8,128)(2,1)} %collective-permute-done.12, ...), kind=kOutput, calls=%fused_computation.48 | convolution fusion | flops 1082130432 | bytes 5242888 | tf_op jit(solution)/shard_map/dot_general | solution.py:252
  213.6 3.9 %convolution_add_fusion = f32[1024,512]{1,0:T(8,128)} fusion(f32[1024,512]{1,0:T(8,128)S(1)} %fusion.27, bf16[2048,1024]{1,0:T(8,128)(2,1)} %all-gather.7.cloned.1.call-done, s32[]{:T(128)S(6)} %select_n.195, bf16[256,1024]{0,1:T(8,128)(2,1)S(1)} %collective-permute-done.4, bf16[256,1024]{0,1:T(8,128)(2,1)S(1)} %collective-permute-done.3, ...), kind=kOutput, calls=%fused_computation.45 | convolution fusion | flops 1082654720 | bytes 7340036 | tf_op jit(solution)/shard_map/dot_general | solution.py:252
  217.4 3.2 %fusion.30 = f32[1024,512]{1,0:T(8,128)S(1)} fusion(bf16[2048,1024]{1,0:T(8,128)(2,1)} %all-gather.7.cloned.1.call-done, s32[]{:T(128)S(6)} %add.227, s32[]{:T(128)S(6)} %select_n.184, bf16[256,1024]{0,1:T(8,128)(2,1)} %collective-permute-done.13, bf16[256,1024]{0,1:T(8,128)(2,1)} %collective-permute-done.12, ...), kind=kOutput, calls=%fused_computation.51 | convolution fusion | flops 1082130432 | bytes 5242888 | tf_op jit(solution)/shard_map/dot_general | solution.py:252
  220.7 2.5 fusion.32
  224.1 2.4 collective-permute-start.17
  227.8 5.6 %collective-permute-done.17 = bf16[256,512]{1,0:T(8,128)(2,1)S(1)} collective-permute-done((bf16[256,512]{1,0:T(8,128)(2,1)S(1)}, bf16[256,512]{1,0:T(8,128)(2,1)S(1)}, u32[]{:S(2)}, u32[]{:S(2)}) %collective-permute-start.17) | collective-permute-done | bytes 262176 | tf_op jit(solution)/shard_map/ppermute | solution.py:261
  233.4 7.2 %collective-permute-done.16 = bf16[256,512]{1,0:T(8,128)(2,1)S(1)} collective-permute-done((bf16[256,512]{1,0:T(8,128)(2,1)S(1)}, bf16[256,512]{1,0:T(8,128)(2,1)S(1)}, u32[]{:S(2)}, u32[]{:S(2)}) %collective-permute-start.16) | collective-permute-done | bytes 262176 | tf_op jit(solution)/shard_map/ppermute | solution.py:261
  241.7 1.0 fusion.34
  242.7 1.4 copy.63
  244.0 1.6 reshape.368
  (122 shorter events, 19.4 us)
Async XLA Ops:
  6.5 40.2 %all-gather.5.cloned.1.call-start = ((), (), s32[]{:S(2)}) async-start(), calls=%async_computation | async-start | bytes 1310720 | tf_op jit(solution)/shard_map/all_gather | solution.py:199
  10.6 2.9 %collective-permute-start = (bf16[256,4,2,128]{0,3,1,2:T(8,128)(2,1)S(1)}, bf16[256,4,2,128]{0,3,1,2:T(8,128)(2,1)S(1)}, u32[]{:S(2)}, u32[]{:S(2)}) collective-permute-start(bf16[256,4,2,128]{0,3,1,2:T(8,128)(2,1)S(1)} %pad_maximum_fusion.7), channel_id=1, source_target_pairs={{0,1},{1,0},{2,3},{3,2},{4,5},{5,4},{6,7},{7,6},{8,9},{9,8},{10,11... | collective-permute-start | bytes 1572872 | tf_op jit(solution)/shard_map/ppermute | solution.py:139
  13.4 2.8 %copy-start.5 = (pred[2]{0:T(512)(128)(4,1)}, pred[2]{0:T(512)(128)(4,1)S(1)}, u32[]{:S(2)}) copy-start(pred[2]{0:T(512)(128)(4,1)S(1)} %get-tuple-element.125) | copy-start | bytes 10
  13.4 33.4 %copy-start.8 = (s32[2]{0:T(128)}, s32[2]{0:T(128)S(1)}, u32[]{:S(2)}) copy-start(s32[2]{0:T(128)S(1)} %get-tuple-element.126) | copy-start | bytes 28
  13.4 34.0 %copy-start.9 = (s32[2]{0:T(128)}, s32[2]{0:T(128)S(1)}, u32[]{:S(2)}) copy-start(s32[2]{0:T(128)S(1)} %get-tuple-element.154) | copy-start | bytes 28
  13.5 2.7 %copy-start.4 = (s32[1024]{0:T(1024)}, s32[1024]{0:T(1024)S(1)}, u32[]{:S(2)}) copy-start(s32[1024]{0:T(1024)S(1)} %pad_clamp_fusion.3) | copy-start | bytes 12292
  13.5 3.1 %copy-start.1 = (bf16[256,2048]{1,0:T(8,128)(2,1)S(1)}, bf16[256,2048]{1,0:T(8,128)(2,1)}, u32[]{:S(2)}) copy-start(bf16[256,2048]{1,0:T(8,128)(2,1)} %param.13) | copy-start | bytes 3145732
  16.2 101.9 %all-gather.9.cloned.1.call-start = ((), (), s32[]{:S(2)}) async-start(), calls=%async_computation.2 | async-start | bytes 5242880 | tf_op jit(solution)/shard_map/all_gather | solution.py:200
  16.3 76.6 %collective-permute-start.5 = (bf16[4,512,256]{2,1,0:T(8,128)(2,1)}, bf16[4,512,256]{2,1,0:T(8,128)(2,1)}, u32[]{:S(2)}, u32[]{:S(2)}) collective-permute-start(bf16[4,512,256]{2,1,0:T(8,128)(2,1)} %bitcast.186), channel_id=1, source_target_pairs={{0,1},{1,0},{2,3},{3,2},{4,5},{5,4},{6,7},{7,6},{8,9},{9,8},{10,11... | collective-permute-start | bytes 3145736 | tf_op jit(solution)/shard_map/ppermute | solution.py:139
  19.8 54.2 %collective-permute-start.1 = (bf16[256,4,4,128]{3,0,2,1:T(8,128)(2,1)S(1)}, bf16[256,4,4,128]{3,0,2,1:T(8,128)(2,1)S(1)}, u32[]{:S(2)}, u32[]{:S(2)}) collective-permute-start(bf16[256,4,4,128]{3,0,2,1:T(8,128)(2,1)S(1)} %bitcast.178), channel_id=1, source_target_pairs={{0,1},{1,0},{2,3},{3,2},{4,5},{5,4},{6,7},{7,6},{8,9},{9,8},{10,11... | collective-permute-start | bytes 3145736 | tf_op jit(solution)/shard_map/ppermute | solution.py:139
  46.8 162.0 %all-gather.7.cloned.1.call-start = ((), (), s32[]{:S(2)}) async-start(), calls=%async_computation.1 | async-start | bytes 5242880 | tf_op jit(solution)/shard_map/all_gather | solution.py:243
  49.7 5.3 %collective-permute-start.6 = (bf16[64,2,2,128]{3,0,1,2:T(8,128)(2,1)S(1)}, bf16[64,2,2,128]{3,0,1,2:T(8,128)(2,1)S(1)}, u32[]{:S(2)}, u32[]{:S(2)}) collective-permute-start(bf16[64,2,2,128]{3,0,1,2:T(8,128)(2,1)S(1)} %slice.91), channel_id=1, source_target_pairs={{0,2},{1,3}} | collective-permute-start | bytes 196616 | tf_op jit(solution)/shard_map/ppermute | solution.py:174
  54.9 4.2 %collective-permute-start.7 = (bf16[64,2,2,128]{3,0,1,2:T(8,128)(2,1)S(1)}, bf16[64,2,2,128]{3,0,1,2:T(8,128)(2,1)S(1)}, u32[]{:S(2)}, u32[]{:S(2)}) collective-permute-start(bf16[64,2,2,128]{3,0,1,2:T(8,128)(2,1)S(1)} %broadcast_select_fusion.1), channel_id=1, source_target_pairs={{0,4},{2,6},{1,5},{3,7}} | collective-permute-start | bytes 196616 | tf_op jit(solution)/shard_map/ppermute | solution.py:174
  59.2 6.4 %collective-permute-start.8 = (bf16[64,2,2,128]{3,0,1,2:T(8,128)(2,1)S(1)}, bf16[64,2,2,128]{3,0,1,2:T(8,128)(2,1)S(1)}, u32[]{:S(2)}, u32[]{:S(2)}) collective-permute-start(bf16[64,2,2,128]{3,0,1,2:T(8,128)(2,1)S(1)} %broadcast_select_fusion.2), channel_id=1, source_target_pairs={{0,8},{2,10},{4,12},{6,14},{1,9},{3,11},{5,13},{7,15}} | collective-permute-start | bytes 196616 | tf_op jit(solution)/shard_map/ppermute | solution.py:174
  61.2 12.0 %collective-permute-start.10 = (bf16[256,2,2,128]{3,0,1,2:T(8,128)(2,1)S(1)}, bf16[256,2,2,128]{3,0,1,2:T(8,128)(2,1)S(1)}, u32[]{:S(2)}, u32[]{:S(2)}) collective-permute-start(bf16[256,2,2,128]{3,0,1,2:T(8,128)(2,1)S(1)} %fusion.41), channel_id=1, source_target_pairs={{0,2},{2,4},{4,6},{6,8},{8,10},{10,12},{12,14},{14,16},{16,18},{18... | collective-permute-start | bytes 786440 | tf_op jit(solution)/shard_map/ppermute | solution.py:169
  65.6 3.2 %collective-permute-start.9 = (bf16[64,2,2,128]{3,0,1,2:T(8,128)(2,1)S(1)}, bf16[64,2,2,128]{3,0,1,2:T(8,128)(2,1)S(1)}, u32[]{:S(2)}, u32[]{:S(2)}) collective-permute-start(bf16[64,2,2,128]{3,0,1,2:T(8,128)(2,1)S(1)} %broadcast_select_fusion.3), channel_id=1, source_target_pairs={{0,16},{2,18},{4,20},{6,22},{8,24},{10,26},{12,28},{14,30},{1,17},... | collective-permute-start | bytes 196616 | tf_op jit(solution)/shard_map/ppermute | solution.py:174
  74.0 1.9 copy-start.7
  74.2 1.7 copy-start.3
  77.9 2.3 copy-start
  82.9 10.0 %copy-start.2 = (bf16[2048,256]{1,0:T(8,128)(2,1)S(1)}, bf16[2048,256]{1,0:T(8,128)(2,1)}, u32[]{:S(2)}) copy-start(bf16[2048,256]{1,0:T(8,128)(2,1)} %param.19) | copy-start | bytes 3145732
  87.4 73.8 %collective-permute-start.13 = (bf16[256,1024]{0,1:T(8,128)(2,1)}, bf16[256,1024]{0,1:T(8,128)(2,1)}, u32[]{:S(2)}, u32[]{:S(2)}) collective-permute-start(bf16[256,1024]{0,1:T(8,128)(2,1)} %bitcast.44), channel_id=1, source_target_pairs={{0,6},{2,0},{4,2},{6,4},{1,7},{3,1},{5,3},{7,5},{8,14},{10,8},{12,... | collective-permute-start | bytes 1572872 | tf_op jit(solution)/shard_map/ppermute | solution.py:229
  90.9 70.2 %collective-permute-start.12 = (bf16[256,1024]{0,1:T(8,128)(2,1)}, bf16[256,1024]{0,1:T(8,128)(2,1)}, u32[]{:S(2)}, u32[]{:S(2)}) collective-permute-start(bf16[256,1024]{0,1:T(8,128)(2,1)} %bitcast.44), channel_id=1, source_target_pairs={{0,4},{2,6},{4,0},{6,2},{1,5},{3,7},{5,1},{7,3},{8,12},{10,14},{12... | collective-permute-start | bytes 1572872 | tf_op jit(solution)/shard_map/ppermute | solution.py:229
  91.4 69.8 %collective-permute-start.11 = (bf16[256,1024]{0,1:T(8,128)(2,1)}, bf16[256,1024]{0,1:T(8,128)(2,1)}, u32[]{:S(2)}, u32[]{:S(2)}) collective-permute-start(bf16[256,1024]{0,1:T(8,128)(2,1)} %bitcast.44), channel_id=1, source_target_pairs={{0,2},{2,4},{4,6},{6,0},{1,3},{3,5},{5,7},{7,1},{8,10},{10,12},{12... | collective-permute-start | bytes 1572872 | tf_op jit(solution)/shard_map/ppermute | solution.py:229
  94.3 0.8 copy-start.6
  149.5 62.5 %collective-permute-start.4 = (bf16[256,1024]{0,1:T(8,128)(2,1)S(1)}, bf16[256,1024]{0,1:T(8,128)(2,1)S(1)}, u32[]{:S(2)}, u32[]{:S(2)}) collective-permute-start(bf16[256,1024]{0,1:T(8,128)(2,1)S(1)} %bitcast.192), channel_id=1, source_target_pairs={{0,6},{2,0},{4,2},{6,4},{1,7},{3,1},{5,3},{7,5},{8,14},{10,8},{12,... | collective-permute-start | bytes 1572872 | tf_op jit(solution)/shard_map/ppermute | solution.py:229
  159.6 52.4 %collective-permute-start.3 = (bf16[256,1024]{0,1:T(8,128)(2,1)S(1)}, bf16[256,1024]{0,1:T(8,128)(2,1)S(1)}, u32[]{:S(2)}, u32[]{:S(2)}) collective-permute-start(bf16[256,1024]{0,1:T(8,128)(2,1)S(1)} %bitcast.193), channel_id=1, source_target_pairs={{0,4},{2,6},{4,0},{6,2},{1,5},{3,7},{5,1},{7,3},{8,12},{10,14},{12... | collective-permute-start | bytes 1572872 | tf_op jit(solution)/shard_map/ppermute | solution.py:229
  161.2 50.8 %collective-permute-start.2 = (bf16[256,1024]{0,1:T(8,128)(2,1)S(1)}, bf16[256,1024]{0,1:T(8,128)(2,1)S(1)}, u32[]{:S(2)}, u32[]{:S(2)}) collective-permute-start(bf16[256,1024]{0,1:T(8,128)(2,1)S(1)} %bitcast.194), channel_id=1, source_target_pairs={{0,2},{2,4},{4,6},{6,0},{1,3},{3,5},{5,7},{7,1},{8,10},{10,12},{12... | collective-permute-start | bytes 1572872 | tf_op jit(solution)/shard_map/ppermute | solution.py:229
  212.0 0.8 copy-start.10
  212.8 0.8 copy-start.12
  217.4 5.8 %collective-permute-start.14 = (f32[1024,512]{1,0:T(8,128)}, f32[1024,512]{1,0:T(8,128)S(1)}, u32[]{:S(2)}, u32[]{:S(2)}) collective-permute-start(f32[1024,512]{1,0:T(8,128)} %convolution_add_fusion), channel_id=1, source_target_pairs={{0,1},{1,0},{2,3},{3,2},{4,5},{5,4},{6,7},{7,6},{8,9},{9,8},{10,11... | collective-permute-start | bytes 6291464 | tf_op jit(solution)/shard_map/ppermute | solution.py:256
  217.4 3.2 %copy-start.11 = (bf16[256,1024]{0,1:T(8,128)(2,1)S(1)}, bf16[256,1024]{0,1:T(8,128)(2,1)}, u32[]{:S(2)}) copy-start(bf16[256,1024]{0,1:T(8,128)(2,1)} %copy-done.10) | copy-start | bytes 1572868
  217.4 3.2 %copy-start.13 = (bf16[256,1024]{0,1:T(8,128)(2,1)S(1)}, bf16[256,1024]{0,1:T(8,128)(2,1)}, u32[]{:S(2)}) copy-start(bf16[256,1024]{0,1:T(8,128)(2,1)} %copy-done.12) | copy-start | bytes 1572868
  224.1 9.2 %collective-permute-start.17 = (bf16[256,512]{1,0:T(8,128)(2,1)S(1)}, bf16[256,512]{1,0:T(8,128)(2,1)S(1)}, u32[]{:S(2)}, u32[]{:S(2)}) collective-permute-start(bf16[256,512]{1,0:T(8,128)(2,1)S(1)} %get-tuple-element.142), channel_id=1, source_target_pairs={{0,6},{2,0},{4,2},{6,4},{1,7},{3,1},{5,3},{7,5},{8,14},{10,8},{12,... | collective-permute-start | bytes 786440 | tf_op jit(solution)/shard_map/ppermute | solution.py:261
  226.6 14.0 %collective-permute-start.16 = (bf16[256,512]{1,0:T(8,128)(2,1)S(1)}, bf16[256,512]{1,0:T(8,128)(2,1)S(1)}, u32[]{:S(2)}, u32[]{:S(2)}) collective-permute-start(bf16[256,512]{1,0:T(8,128)(2,1)S(1)} %get-tuple-element.143), channel_id=1, source_target_pairs={{0,4},{2,6},{4,0},{6,2},{1,5},{3,7},{5,1},{7,3},{8,12},{10,14},{12... | collective-permute-start | bytes 786440 | tf_op jit(solution)/shard_map/ppermute | solution.py:261
  227.1 13.5 %collective-permute-start.15 = (bf16[256,512]{1,0:T(8,128)(2,1)S(1)}, bf16[256,512]{1,0:T(8,128)(2,1)S(1)}, u32[]{:S(2)}, u32[]{:S(2)}) collective-permute-start(bf16[256,512]{1,0:T(8,128)(2,1)S(1)} %get-tuple-element.144), channel_id=1, source_target_pairs={{0,2},{2,4},{4,6},{6,0},{1,3},{3,5},{5,7},{7,1},{8,10},{10,12},{12... | collective-permute-start | bytes 786440 | tf_op jit(solution)/shard_map/ppermute | solution.py:261
Sparse Core Ops, SparseCore 0:
  16.3 30.3 all-gather.4
  48.6 69.4 all-gather.8
  119.7 89.0 all-gather.6

commit v11 on v9

--- a/solution.py
+++ b/solution.py
@@ -196,7 +196,12 @@
     run_out = run_accum / run_totals[..., None]
 
     ret_kv = jnp.take(kv_all, ret_ids, axis=1)
-    ret_shard = lax.all_gather(ret_kv.reshape(rows, ret_per * 2 * HEAD_SIZE), CTX, axis=0, tiled=True)
+    payload = ret_kv.reshape(rows, ret_per * 2 * HEAD_SIZE)
+    got = [payload] + [
+        lax.ppermute(payload, CTX, [(i, i + shift) for i in range(ctx_count - shift)])
+        for shift in range(1, ctx_count)
+    ]
+    ret_shard = jnp.take(jnp.stack(got), (ctx_index - jnp.arange(ctx_count)) % ctx_count, axis=0)
     ret_shard = ret_shard.reshape(ctx_count * rows, ret_per, 2, HEAD_SIZE)
     q_ret = jnp.take(q_all, ret_ids, axis=1)
     sub_rows = math.gcd(ctx_count * rows, 2048)

time: 237 us -> 333 us (1.41)
  starting transfers between devices: 24.4 us -> 129 us
  waiting for transfers between devices: 126 us -> 85.5 us
  local copies, waits for them, and re-layouts: 18.8 us -> 47.7 us
    ppermute x0 -> x15, starting transfers between devices: none -> 105 us  [duo_attend(): lax.ppermute(payload, CTX, [(i, i + shift) for i in range(ctx_count - shi...]
    all_gather x1 -> x0, waiting for transfers between devices: 42.1 us -> none  [duo_attend(): lax.all_gather(ret_kv.reshape(rows, ret_per * 2 * HEAD_SIZE), CTX, axis=0...]
    gather x0 -> x3, local copies, waits for them, and re-layouts: none -> 18.9 us  [duo_attend(): jnp.take(jnp.stack(got), (ctx_index - jnp.arange(ctx_count)) % ctx_count,...]
    unnamed x35 -> x32, local copies, waits for them, and re-layouts: 7.04 us -> 17.3 us
    select_n x0 -> x2, other arithmetic: none -> 4.58 us  [duo_attend(): jnp.take(jnp.stack(got), (ctx_index - jnp.arange(ctx_count)) % ctx_count,...]
    ppermute x0 -> x15, waiting for transfers between devices: none -> 3.5 us  [duo_attend(): lax.ppermute(payload, CTX, [(i, i + shift) for i in range(ctx_count - shi...]
  transfers between devices with their start and end apart: 20 -> 34, of which waited for: 8 -> 10; matrix products, arithmetic and copies ran while one was open for 23% -> 26% of each run, Pallas kernels for 0% -> 0%
where the time goes in v11:
time: 333 us; the launch traced here: 332 us
  starting transfers between devices  129 us (39%)
  waiting for transfers between devices  85.5 us (26%)
  local copies, waits for them, and re-layouts  47.7 us (14%)
  matrix products  31 us (9%)
  other arithmetic  24.3 us (7%)
  between operations  14.9 us (4%)
    ppermute x15, starting transfers between devices, duo_attend(): lax.ppermute(payload, CTX, [(i, i + shift) for i in range(ctx_count - shi...  105 us
    all_gather x1, waiting for transfers between devices, project_assigned(): w_line = lax.all_gather(w_mine, 'cz', axis=1, tiled=True)  64.4 us
    gather x3, local copies, waits for them, and re-layouts, duo_attend(): jnp.take(jnp.stack(got), (ctx_index - jnp.arange(ctx_count)) % ctx_count,...  18.9 us
    unnamed x32, local copies, waits for them, and re-layouts  17.3 us
    ppermute x3, waiting for transfers between devices, project_assigned(): lax.ppermute(blocks[-shift % plane], 'cb', [(i, (i + shift) % plane) for...  12.9 us
    dot_general x2, matrix products, update(): jnp.einsum('hgrk,khd->hgrd', weights.astype(jnp.bfloat16), value_block, p...  11.8 us
    ppermute x4, starting transfers between devices, duo_attend(): got = lax.ppermute(sink_kv, CTX, pairs)  8.31 us
    dot_general x2, matrix products, product(): jnp.dot(ret_stack, w_half[:ret_rows], preferred_element_type=jnp.float32)  6.7 us
  transfers between devices with their start and end apart: 34, of which 10 were waited for; matrix products, arithmetic and copies ran while one was open for 26% of the time, Pallas kernels for 0%

profile of v11, /device:TPU:0, one launch (start us, length us, event | category | flops | bytes accessed | tf_op | source)
XLA Modules:
  0.0 332.2 jit_solution(14371596885433189965)
XLA Ops:
  13.5 1.4 subtract_convert_fusion
  19.6 4.4 %collective-permute-start.21 = (bf16[64,2,2,128]{3,0,1,2:T(8,128)(2,1)S(1)}, bf16[64,2,2,128]{3,0,1,2:T(8,128)(2,1)S(1)}, u32[]{:S(2)}, u32[]{:S(2)}) collective-permute-start(bf16[64,2,2,128]{3,0,1,2:T(8,128)(2,1)S(1)} %slice.93), channel_id=1, source_target_pairs={{0,2},{1,3}} | collective-permute-start | bytes 196616 | tf_op jit(solution)/shard_map/ppermute | solution.py:174
  24.1 1.9 collective-permute-done.21
  30.8 1.3 collective-permute-start.15
  32.1 3.8 %collective-permute-start.1 = (bf16[256,512]{0,1:T(8,128)(2,1)S(1)}, bf16[256,512]{0,1:T(8,128)(2,1)S(1)}, u32[]{:S(2)}, u32[]{:S(2)}) collective-permute-start(bf16[256,512]{0,1:T(8,128)(2,1)S(1)} %bitcast.219), channel_id=1, source_target_pairs={{0,2},{2,4},{4,6},{6,8},{8,10},{10,12},{12,14},{14,16},{16,18},{18... | collective-permute-start | bytes 786440 | tf_op jit(solution)/shard_map/ppermute | solution.py:201
  38.0 1.4 collective-permute-done.24
  39.4 4.0 %collective-permute-start.2 = (bf16[256,512]{0,1:T(8,128)(2,1)S(1)}, bf16[256,512]{0,1:T(8,128)(2,1)S(1)}, u32[]{:S(2)}, u32[]{:S(2)}) collective-permute-start(bf16[256,512]{0,1:T(8,128)(2,1)S(1)} %bitcast.221), channel_id=1, source_target_pairs={{0,4},{2,6},{4,8},{6,10},{8,12},{10,14},{12,16},{14,18},{16,20},{1... | collective-permute-start | bytes 786440 | tf_op jit(solution)/shard_map/ppermute | solution.py:201
  43.4 4.3 %collective-permute-start.3 = (bf16[256,512]{0,1:T(8,128)(2,1)S(1)}, bf16[256,512]{0,1:T(8,128)(2,1)S(1)}, u32[]{:S(2)}, u32[]{:S(2)}) collective-permute-start(bf16[256,512]{0,1:T(8,128)(2,1)S(1)} %bitcast.222), channel_id=1, source_target_pairs={{0,6},{2,8},{4,10},{6,12},{8,14},{10,16},{12,18},{14,20},{16,22},{... | collective-permute-start | bytes 786440 | tf_op jit(solution)/shard_map/ppermute | solution.py:201
  48.4 7.6 %collective-permute-start.4 = (bf16[256,512]{0,1:T(8,128)(2,1)S(1)}, bf16[256,512]{0,1:T(8,128)(2,1)S(1)}, u32[]{:S(2)}, u32[]{:S(2)}) collective-permute-start(bf16[256,512]{0,1:T(8,128)(2,1)S(1)} %bitcast.223), channel_id=1, source_target_pairs={{0,8},{2,10},{4,12},{6,14},{8,16},{10,18},{12,20},{14,22},{16,24},... | collective-permute-start | bytes 786440 | tf_op jit(solution)/shard_map/ppermute | solution.py:201
  56.8 6.7 %collective-permute-start.5 = (bf16[256,512]{0,1:T(8,128)(2,1)S(1)}, bf16[256,512]{0,1:T(8,128)(2,1)S(1)}, u32[]{:S(2)}, u32[]{:S(2)}) collective-permute-start(bf16[256,512]{0,1:T(8,128)(2,1)S(1)} %bitcast.224), channel_id=1, source_target_pairs={{0,10},{2,12},{4,14},{6,16},{8,18},{10,20},{12,22},{14,24},{16,26}... | collective-permute-start | bytes 786440 | tf_op jit(solution)/shard_map/ppermute | solution.py:201
  64.2 3.8 %collective-permute-start.6 = (bf16[256,512]{0,1:T(8,128)(2,1)S(1)}, bf16[256,512]{0,1:T(8,128)(2,1)S(1)}, u32[]{:S(2)}, u32[]{:S(2)}) collective-permute-start(bf16[256,512]{0,1:T(8,128)(2,1)S(1)} %bitcast.225), channel_id=1, source_target_pairs={{0,12},{2,14},{4,16},{6,18},{8,20},{10,22},{12,24},{14,26},{16,28}... | collective-permute-start | bytes 786440 | tf_op jit(solution)/shard_map/ppermute | solution.py:201
  69.0 27.4 %collective-permute-start.7 = (bf16[256,512]{0,1:T(8,128)(2,1)S(1)}, bf16[256,512]{0,1:T(8,128)(2,1)S(1)}, u32[]{:S(2)}, u32[]{:S(2)}) collective-permute-start(bf16[256,512]{0,1:T(8,128)(2,1)S(1)} %bitcast.226), channel_id=1, source_target_pairs={{0,14},{2,16},{4,18},{6,20},{8,22},{10,24},{12,26},{14,28},{16,30}... | collective-permute-start | bytes 786440 | tf_op jit(solution)/shard_map/ppermute | solution.py:201
  97.1 1.3 collective-permute-start.8
  99.1 1.6 collective-permute-done.7
  100.7 1.3 collective-permute-start.9
  106.4 24.2 %collective-permute-start.11 = (bf16[256,512]{0,1:T(8,128)(2,1)S(1)}, bf16[256,512]{0,1:T(8,128)(2,1)S(1)}, u32[]{:S(2)}, u32[]{:S(2)}) collective-permute-start(bf16[256,512]{0,1:T(8,128)(2,1)S(1)} %bitcast.230), channel_id=1, source_target_pairs={{0,22},{2,24},{4,26},{6,28},{8,30},{1,23},{3,25},{5,27},{7,29},{9,... | collective-permute-start | bytes 786440 | tf_op jit(solution)/shard_map/ppermute | solution.py:201
  131.3 6.3 %collective-permute-start.12 = (bf16[256,512]{0,1:T(8,128)(2,1)S(1)}, bf16[256,512]{0,1:T(8,128)(2,1)S(1)}, u32[]{:S(2)}, u32[]{:S(2)}) collective-permute-start(bf16[256,512]{0,1:T(8,128)(2,1)S(1)} %bitcast.231), channel_id=1, source_target_pairs={{0,24},{2,26},{4,28},{6,30},{1,25},{3,27},{5,29},{7,31}} | collective-permute-start | bytes 786440 | tf_op jit(solution)/shard_map/ppermute | solution.py:201
  138.3 5.3 %collective-permute-start.13 = (bf16[256,512]{0,1:T(8,128)(2,1)S(1)}, bf16[256,512]{0,1:T(8,128)(2,1)S(1)}, u32[]{:S(2)}, u32[]{:S(2)}) collective-permute-start(bf16[256,512]{0,1:T(8,128)(2,1)S(1)} %bitcast.232), channel_id=1, source_target_pairs={{0,26},{2,28},{4,30},{1,27},{3,29},{5,31}} | collective-permute-start | bytes 786440 | tf_op jit(solution)/shard_map/ppermute | solution.py:201
  144.3 6.4 %collective-permute-start.14 = (bf16[256,512]{0,1:T(8,128)(2,1)S(1)}, bf16[256,512]{0,1:T(8,128)(2,1)S(1)}, u32[]{:S(2)}, u32[]{:S(2)}) collective-permute-start(bf16[256,512]{0,1:T(8,128)(2,1)S(1)} %bitcast.233), channel_id=1, source_target_pairs={{0,28},{2,30},{1,29},{3,31}} | collective-permute-start | bytes 786440 | tf_op jit(solution)/shard_map/ppermute | solution.py:201
  151.5 4.7 %collective-permute-start.25 = (bf16[256,2,2,128]{3,0,1,2:T(8,128)(2,1)S(1)}, bf16[256,2,2,128]{3,0,1,2:T(8,128)(2,1)S(1)}, u32[]{:S(2)}, u32[]{:S(2)}) collective-permute-start(bf16[256,2,2,128]{3,0,1,2:T(8,128)(2,1)S(1)} %fusion.43), channel_id=1, source_target_pairs={{0,2},{2,4},{4,6},{6,8},{8,10},{10,12},{12,14},{14,16},{16,18},{18... | collective-permute-start | bytes 786440 | tf_op jit(solution)/shard_map/ppermute | solution.py:169
  158.4 5.0 %gather_fusion = bf16[16,256,512]{1,2,0:T(8,128)(2,1)} fusion(bf16[16,256,512]{1,2,0:T(8,128)(2,1)} %bitcast_dynamic-update-slice_fusion, s32[1024]{0:T(1024)S(1)} %pad_clamp_fusion.3), kind=kCustom, calls=%fused_computation.4 | custom fusion | bytes 8388672 | tf_op jit(solution)/shard_map/jit(_take)/gather | solution.py:204
  163.3 6.6 %copy.42 = bf16[16,256,512]{1,0,2:T(8,128)(2,1)} copy(bf16[16,256,512]{1,2,0:T(8,128)(2,1)} %gather_fusion) | data formatting | bytes 8388608 | tf_op jit(solution)/shard_map/jit(_take)/gather | solution.py:204
  169.9 7.4 %gather.25 = bf16[4096,2,2,128]{0,3,2,1:T(8,128)(2,1)} reshape(bf16[16,256,512]{1,0,2:T(8,128)(2,1)} %copy.42) | data formatting | bytes 8388608 | tf_op jit(solution)/shard_map/jit(_take)/gather | solution.py:204
  177.3 4.6 %broadcast_select_fusion = bf16[4096,2,2,128]{0,3,2,1:T(8,128)(2,1)} fusion(bf16[4096,2,2,128]{0,3,2,1:T(8,128)(2,1)} %gather.25, pred[4096]{0:T(1024)(128)(4,1)S(1)} %broadcast_in_dim.118), kind=kLoop, calls=%fused_computation.31 | loop fusion | flops 2097152 | bytes 8392704 | tf_op jit(solution)/shard_map/jit(_take)/select_n | solution.py:204
  181.9 1.4 select_bitcast_fusion.3
  183.5 1.4 gather_fusion.6
  184.9 2.0 fusion.17
  186.9 2.1 copy-done
  190.2 1.4 gather_fusion.4
  191.6 4.5 %divide_convert_fusion = bf16[256,2,4,128]{0,3,2,1:T(8,128)(2,1)} fusion(f32[2,576,256,4]{2,1,3,0:T(8,128)} %copy-done, f32[2,4,256]{2,1,0:T(4,128)S(1)} %get-tuple-element.140, pred[256,576]{0,1:T(8,128)(4,1)S(1)} %pad_add_fusion, f32[256,2,4]{0,2,1:T(4,128)S(1)} %bitcast_add_fusion, f32[256,2,4]{0,2,1:T(4,128)S(1)} %get-tuple-element.139, ...), kind=kOutput, calls=%fused_computation.60 | convolution fusion | flops 308674560 | bytes 5709824 | tf_op jit(solution)/shard_map/hgrk,khd->hgrd/dot_general | solution.py:62
  196.2 1.5 collective-permute-start.27
  198.2 1.4 select_bitcast_fusion.1
  200.4 1.3 bitcast_select_fusion.2
  203.0 16.3 %while.15 = (s32[]{:T(128)}, f32[2,4,256]{2,1,0:T(4,128)S(1)}, f32[2,4,256]{2,1,0:T(4,128)S(1)}, f32[2,4,256,128]{3,2,1,0:T(8,128)S(1)}, s32[]{:T(128)}, /*index...) while((s32[]{:T(128)}, f32[2,4,256]{2,1,0:T(4,128)S(1)}, ...), condition=%wide.region_5.8_spmd.clone, body=%wide.region_2.7_spmd.clone.sunk | while | flops 2203064576 | bytes 57297100 | solution.py:221
  203.8 4.2 %fusion.77 = (f32[2,4,256]{2,1,0:T(4,128)S(1)}, f32[2,2048,256,4]{2,1,3,0:T(8,128)S(1)}) fusion(pred[256,2048]{0,1:T(8,128)(4,1)S(1)} %broadcast_compare_fusion.3, bf16[256,2,4,128]{3,0,2,1:T(8,128)(2,1)S(1)} %get-tuple-element.245, bf16[4096,2,2,128]{0,3,2,1:T(8,128)(2,1)} %get-tuple-element.244, s32[]{:T(128)S(6)} %select_n.400), kind=kOutput, calls=%fused_computation.10.clone.1 | convolution fusion | flops 1086322688 | bytes 18882564 | tf_op jit(solution)/shard_map/while/body/rhgd,khd->hgrk/dot_general | solution.py:53
  208.0 4.0 %fusion.78 = f32[2,4,256]{2,1,0:T(4,128)S(1)} fusion(f32[2,2048,256,4]{2,1,3,0:T(8,128)S(1)} %get-tuple-element.210, f32[2,4,256]{2,1,0:T(4,128)S(1)} %max.13, pred[256,2048]{0,1:T(8,128)(4,1)S(1)} %broadcast_compare_fusion.3), kind=kLoop, calls=%fused_computation.12.clone.1 | loop fusion | flops 20969472 | bytes 17317888 | tf_op jit(solution)/shard_map/while/body/reduce_sum | solution.py:61
  212.1 7.3 %fusion.79 = f32[2,4,256,128]{3,2,1,0:T(8,128)S(1)} fusion(f32[2,2048,256,4]{2,1,3,0:T(8,128)S(1)} %get-tuple-element.210, f32[2,4,256]{2,1,0:T(4,128)S(1)} %max.13, pred[256,2048]{0,1:T(8,128)(4,1)S(1)} %broadcast_compare_fusion.3, bf16[4096,2,2,128]{0,3,2,1:T(8,128)(2,1)} %get-tuple-element.244, s32[]{:T(128)S(6)} %select_n.400, s32[]{:T(128)S(6)} %add.359, ...), kind=kOutput, calls=%fused_computation.15.clone.1 | convolution fusion | flops 1095237632 | bytes 20463624 | tf_op jit(solution)/shard_map/while/body/hgrk,khd->hgrd/dot_general | solution.py:62
  219.8 2.4 collective-permute-start.19
  223.9 64.4 %all-gather.2.cloned.1.call-done = bf16[2048,1024]{1,0:T(8,128)(2,1)} async-done(((bf16[2048,256]{1,0:T(8,128)(2,1)}), bf16[2048,1024]{1,0:T(8,128)(2,1)}) %all-gather.2.cloned.1.call-update) | async-done | bytes 4194320 | tf_op jit(solution)/shard_map/all_gather | solution.py:247
  288.3 3.1 fusion.29
  293.1 3.9 %convolution_add_fusion = f32[1024,512]{1,0:T(8,128)} fusion(f32[1024,512]{1,0:T(8,128)S(1)} %fusion.29, bf16[2048,1024]{1,0:T(8,128)(2,1)} %all-gather.2.cloned.1.call-done, s32[]{:T(128)S(6)} %select_n.238, bf16[256,1024]{0,1:T(8,128)(2,1)S(1)} %collective-permute-done.19, bf16[256,1024]{0,1:T(8,128)(2,1)S(1)} %collective-permute-done.18, ...), kind=kOutput, calls=%fused_computation.46 | convolution fusion | flops 1082654720 | bytes 7340036 | tf_op jit(solution)/shard_map/dot_general | solution.py:256
  297.0 2.8 fusion.34
  299.8 3.1 fusion.32
  303.9 2.4 collective-permute-start.32
  307.5 5.6 %collective-permute-done.32 = bf16[256,512]{1,0:T(8,128)(2,1)S(1)} collective-permute-done((bf16[256,512]{1,0:T(8,128)(2,1)S(1)}, bf16[256,512]{1,0:T(8,128)(2,1)S(1)}, u32[]{:S(2)}, u32[]{:S(2)}) %collective-permute-start.32) | collective-permute-done | bytes 262176 | tf_op jit(solution)/shard_map/ppermute | solution.py:265
  313.2 7.3 %collective-permute-done.31 = bf16[256,512]{1,0:T(8,128)(2,1)S(1)} collective-permute-done((bf16[256,512]{1,0:T(8,128)(2,1)S(1)}, bf16[256,512]{1,0:T(8,128)(2,1)S(1)}, u32[]{:S(2)}, u32[]{:S(2)}) %collective-permute-start.31) | collective-permute-done | bytes 262176 | tf_op jit(solution)/shard_map/ppermute | solution.py:265
  322.5 1.4 copy.50
  323.8 1.6 reshape.425
  (150 shorter events, 44.0 us)
Async XLA Ops:
  6.5 5.7 %copy-start.1 = (bf16[256,2048]{1,0:T(8,128)(2,1)S(1)}, bf16[256,2048]{1,0:T(8,128)(2,1)}, u32[]{:S(2)}) copy-start(bf16[256,2048]{1,0:T(8,128)(2,1)} %param.13) | copy-start | bytes 3145732
  6.5 281.8 %all-gather.2.cloned.1.call-start = ((), (), s32[]{:S(2)}) async-start(), calls=%async_computation | async-start | bytes 5242880 | tf_op jit(solution)/shard_map/all_gather | solution.py:247
  11.5 6.4 %collective-permute-start = (bf16[256,4,2,128]{0,3,1,2:T(8,128)(2,1)}, bf16[256,4,2,128]{0,3,1,2:T(8,128)(2,1)S(1)}, u32[]{:S(2)}, u32[]{:S(2)}) collective-permute-start(bf16[256,4,2,128]{0,3,1,2:T(8,128)(2,1)} %pad_maximum_fusion.7), channel_id=1, source_target_pairs={{0,1},{1,0},{2,3},{3,2},{4,5},{5,4},{6,7},{7,6},{8,9},{9,8},{10,11... | collective-permute-start | bytes 1572872 | tf_op jit(solution)/shard_map/ppermute | solution.py:139
  12.0 186.2 %collective-permute-start.20 = (bf16[4,512,256]{2,1,0:T(8,128)(2,1)}, bf16[4,512,256]{2,1,0:T(8,128)(2,1)}, u32[]{:S(2)}, u32[]{:S(2)}) collective-permute-start(bf16[4,512,256]{2,1,0:T(8,128)(2,1)} %bitcast.215), channel_id=1, source_target_pairs={{0,1},{1,0},{2,3},{3,2},{4,5},{5,4},{6,7},{7,6},{8,9},{9,8},{10,11... | collective-permute-start | bytes 3145736 | tf_op jit(solution)/shard_map/ppermute | solution.py:139
  13.5 2.5 copy-start.5
  15.5 166.4 %collective-permute-start.16 = (bf16[256,4,4,128]{3,0,2,1:T(8,128)(2,1)S(1)}, bf16[256,4,4,128]{3,0,2,1:T(8,128)(2,1)}, u32[]{:S(2)}, u32[]{:S(2)}) collective-permute-start(bf16[256,4,4,128]{3,0,2,1:T(8,128)(2,1)S(1)} %bitcast.208), channel_id=1, source_target_pairs={{0,1},{1,0},{2,3},{3,2},{4,5},{5,4},{6,7},{7,6},{8,9},{9,8},{10,11... | collective-permute-start | bytes 3145736 | tf_op jit(solution)/shard_map/ppermute | solution.py:139
  19.6 6.4 %collective-permute-start.21 = (bf16[64,2,2,128]{3,0,1,2:T(8,128)(2,1)S(1)}, bf16[64,2,2,128]{3,0,1,2:T(8,128)(2,1)S(1)}, u32[]{:S(2)}, u32[]{:S(2)}) collective-permute-start(bf16[64,2,2,128]{3,0,1,2:T(8,128)(2,1)S(1)} %slice.93), channel_id=1, source_target_pairs={{0,2},{1,3}} | collective-permute-start | bytes 196616 | tf_op jit(solution)/shard_map/ppermute | solution.py:174
  26.1 3.2 collective-permute-start.22
  29.3 6.6 %collective-permute-start.23 = (bf16[64,2,2,128]{3,0,1,2:T(8,128)(2,1)S(1)}, bf16[64,2,2,128]{3,0,1,2:T(8,128)(2,1)S(1)}, u32[]{:S(2)}, u32[]{:S(2)}) collective-permute-start(bf16[64,2,2,128]{3,0,1,2:T(8,128)(2,1)S(1)} %broadcast_select_fusion.3), channel_id=1, source_target_pairs={{0,8},{2,10},{4,12},{6,14},{1,9},{3,11},{5,13},{7,15}} | collective-permute-start | bytes 196616 | tf_op jit(solution)/shard_map/ppermute | solution.py:174
  30.8 126.8 %collective-permute-start.15 = (bf16[256,512]{0,1:T(8,128)(2,1)S(1)}, bf16[256,512]{0,1:T(8,128)(2,1)S(1)}, u32[]{:S(2)}, u32[]{:S(2)}) collective-permute-start(bf16[256,512]{0,1:T(8,128)(2,1)S(1)} %bitcast.218), channel_id=1, source_target_pairs={{0,30},{1,31}} | collective-permute-start | bytes 786440 | tf_op jit(solution)/shard_map/ppermute | solution.py:201
  32.1 11.3 %collective-permute-start.1 = (bf16[256,512]{0,1:T(8,128)(2,1)S(1)}, bf16[256,512]{0,1:T(8,128)(2,1)S(1)}, u32[]{:S(2)}, u32[]{:S(2)}) collective-permute-start(bf16[256,512]{0,1:T(8,128)(2,1)S(1)} %bitcast.219), channel_id=1, source_target_pairs={{0,2},{2,4},{4,6},{6,8},{8,10},{10,12},{12,14},{14,16},{16,18},{18... | collective-permute-start | bytes 786440 | tf_op jit(solution)/shard_map/ppermute | solution.py:201
  35.9 3.4 %collective-permute-start.24 = (bf16[64,2,2,128]{3,0,1,2:T(8,128)(2,1)S(1)}, bf16[64,2,2,128]{3,0,1,2:T(8,128)(2,1)S(1)}, u32[]{:S(2)}, u32[]{:S(2)}) collective-permute-start(bf16[64,2,2,128]{3,0,1,2:T(8,128)(2,1)S(1)} %broadcast_select_fusion.4), channel_id=1, source_target_pairs={{0,16},{2,18},{4,20},{6,22},{8,24},{10,26},{12,28},{14,30},{1,17},... | collective-permute-start | bytes 196616 | tf_op jit(solution)/shard_map/ppermute | solution.py:174
  39.4 9.1 %collective-permute-start.2 = (bf16[256,512]{0,1:T(8,128)(2,1)S(1)}, bf16[256,512]{0,1:T(8,128)(2,1)S(1)}, u32[]{:S(2)}, u32[]{:S(2)}) collective-permute-start(bf16[256,512]{0,1:T(8,128)(2,1)S(1)} %bitcast.221), channel_id=1, source_target_pairs={{0,4},{2,6},{4,8},{6,10},{8,12},{10,14},{12,16},{14,18},{16,20},{1... | collective-permute-start | bytes 786440 | tf_op jit(solution)/shard_map/ppermute | solution.py:201
  43.4 13.4 %collective-permute-start.3 = (bf16[256,512]{0,1:T(8,128)(2,1)S(1)}, bf16[256,512]{0,1:T(8,128)(2,1)S(1)}, u32[]{:S(2)}, u32[]{:S(2)}) collective-permute-start(bf16[256,512]{0,1:T(8,128)(2,1)S(1)} %bitcast.222), channel_id=1, source_target_pairs={{0,6},{2,8},{4,10},{6,12},{8,14},{10,16},{12,18},{14,20},{16,22},{... | collective-permute-start | bytes 786440 | tf_op jit(solution)/shard_map/ppermute | solution.py:201
  48.4 15.8 %collective-permute-start.4 = (bf16[256,512]{0,1:T(8,128)(2,1)S(1)}, bf16[256,512]{0,1:T(8,128)(2,1)S(1)}, u32[]{:S(2)}, u32[]{:S(2)}) collective-permute-start(bf16[256,512]{0,1:T(8,128)(2,1)S(1)} %bitcast.223), channel_id=1, source_target_pairs={{0,8},{2,10},{4,12},{6,14},{8,16},{10,18},{12,20},{14,22},{16,24},... | collective-permute-start | bytes 786440 | tf_op jit(solution)/shard_map/ppermute | solution.py:201
  56.8 12.2 %collective-permute-start.5 = (bf16[256,512]{0,1:T(8,128)(2,1)S(1)}, bf16[256,512]{0,1:T(8,128)(2,1)S(1)}, u32[]{:S(2)}, u32[]{:S(2)}) collective-permute-start(bf16[256,512]{0,1:T(8,128)(2,1)S(1)} %bitcast.224), channel_id=1, source_target_pairs={{0,10},{2,12},{4,14},{6,16},{8,18},{10,20},{12,22},{14,24},{16,26}... | collective-permute-start | bytes 786440 | tf_op jit(solution)/shard_map/ppermute | solution.py:201
  64.2 32.9 %collective-permute-start.6 = (bf16[256,512]{0,1:T(8,128)(2,1)S(1)}, bf16[256,512]{0,1:T(8,128)(2,1)S(1)}, u32[]{:S(2)}, u32[]{:S(2)}) collective-permute-start(bf16[256,512]{0,1:T(8,128)(2,1)S(1)} %bitcast.225), channel_id=1, source_target_pairs={{0,12},{2,14},{4,16},{6,18},{8,20},{10,22},{12,24},{14,26},{16,28}... | collective-permute-start | bytes 786440 | tf_op jit(solution)/shard_map/ppermute | solution.py:201
  69.0 31.7 %collective-permute-start.7 = (bf16[256,512]{0,1:T(8,128)(2,1)S(1)}, bf16[256,512]{0,1:T(8,128)(2,1)S(1)}, u32[]{:S(2)}, u32[]{:S(2)}) collective-permute-start(bf16[256,512]{0,1:T(8,128)(2,1)S(1)} %bitcast.226), channel_id=1, source_target_pairs={{0,14},{2,16},{4,18},{6,20},{8,22},{10,24},{12,26},{14,28},{16,30}... | collective-permute-start | bytes 786440 | tf_op jit(solution)/shard_map/ppermute | solution.py:201
  97.1 6.5 %collective-permute-start.8 = (bf16[256,512]{0,1:T(8,128)(2,1)S(1)}, bf16[256,512]{0,1:T(8,128)(2,1)S(1)}, u32[]{:S(2)}, u32[]{:S(2)}) collective-permute-start(bf16[256,512]{0,1:T(8,128)(2,1)S(1)} %bitcast.227), channel_id=1, source_target_pairs={{0,16},{2,18},{4,20},{6,22},{8,24},{10,26},{12,28},{14,30},{1,17},... | collective-permute-start | bytes 786440 | tf_op jit(solution)/shard_map/ppermute | solution.py:201
  100.7 5.7 %collective-permute-start.9 = (bf16[256,512]{0,1:T(8,128)(2,1)S(1)}, bf16[256,512]{0,1:T(8,128)(2,1)S(1)}, u32[]{:S(2)}, u32[]{:S(2)}) collective-permute-start(bf16[256,512]{0,1:T(8,128)(2,1)S(1)} %bitcast.228), channel_id=1, source_target_pairs={{0,18},{2,20},{4,22},{6,24},{8,26},{10,28},{12,30},{1,19},{3,21},{... | collective-permute-start | bytes 786440 | tf_op jit(solution)/shard_map/ppermute | solution.py:201
  103.6 27.7 %collective-permute-start.10 = (bf16[256,512]{0,1:T(8,128)(2,1)S(1)}, bf16[256,512]{0,1:T(8,128)(2,1)S(1)}, u32[]{:S(2)}, u32[]{:S(2)}) collective-permute-start(bf16[256,512]{0,1:T(8,128)(2,1)S(1)} %bitcast.229), channel_id=1, source_target_pairs={{0,20},{2,22},{4,24},{6,26},{8,28},{10,30},{1,21},{3,23},{5,25},{7... | collective-permute-start | bytes 786440 | tf_op jit(solution)/shard_map/ppermute | solution.py:201
  106.4 31.9 %collective-permute-start.11 = (bf16[256,512]{0,1:T(8,128)(2,1)S(1)}, bf16[256,512]{0,1:T(8,128)(2,1)S(1)}, u32[]{:S(2)}, u32[]{:S(2)}) collective-permute-start(bf16[256,512]{0,1:T(8,128)(2,1)S(1)} %bitcast.230), channel_id=1, source_target_pairs={{0,22},{2,24},{4,26},{6,28},{8,30},{1,23},{3,25},{5,27},{7,29},{9,... | collective-permute-start | bytes 786440 | tf_op jit(solution)/shard_map/ppermute | solution.py:201
  131.3 13.0 %collective-permute-start.12 = (bf16[256,512]{0,1:T(8,128)(2,1)S(1)}, bf16[256,512]{0,1:T(8,128)(2,1)S(1)}, u32[]{:S(2)}, u32[]{:S(2)}) collective-permute-start(bf16[256,512]{0,1:T(8,128)(2,1)S(1)} %bitcast.231), channel_id=1, source_target_pairs={{0,24},{2,26},{4,28},{6,30},{1,25},{3,27},{5,29},{7,31}} | collective-permute-start | bytes 786440 | tf_op jit(solution)/shard_map/ppermute | solution.py:201
  138.3 13.1 %collective-permute-start.13 = (bf16[256,512]{0,1:T(8,128)(2,1)S(1)}, bf16[256,512]{0,1:T(8,128)(2,1)S(1)}, u32[]{:S(2)}, u32[]{:S(2)}) collective-permute-start(bf16[256,512]{0,1:T(8,128)(2,1)S(1)} %bitcast.232), channel_id=1, source_target_pairs={{0,26},{2,28},{4,30},{1,27},{3,29},{5,31}} | collective-permute-start | bytes 786440 | tf_op jit(solution)/shard_map/ppermute | solution.py:201
  144.3 12.6 %collective-permute-start.14 = (bf16[256,512]{0,1:T(8,128)(2,1)S(1)}, bf16[256,512]{0,1:T(8,128)(2,1)S(1)}, u32[]{:S(2)}, u32[]{:S(2)}) collective-permute-start(bf16[256,512]{0,1:T(8,128)(2,1)S(1)} %bitcast.233), channel_id=1, source_target_pairs={{0,28},{2,30},{1,29},{3,31}} | collective-permute-start | bytes 786440 | tf_op jit(solution)/shard_map/ppermute | solution.py:201
  151.5 25.9 %collective-permute-start.25 = (bf16[256,2,2,128]{3,0,1,2:T(8,128)(2,1)S(1)}, bf16[256,2,2,128]{3,0,1,2:T(8,128)(2,1)S(1)}, u32[]{:S(2)}, u32[]{:S(2)}) collective-permute-start(bf16[256,2,2,128]{3,0,1,2:T(8,128)(2,1)S(1)} %fusion.43), channel_id=1, source_target_pairs={{0,2},{2,4},{4,6},{6,8},{8,10},{10,12},{12,14},{14,16},{16,18},{18... | collective-permute-start | bytes 786440 | tf_op jit(solution)/shard_map/ppermute | solution.py:169
  186.9 2.1 copy-start
  191.6 6.6 %copy-start.2 = (bf16[2048,256]{1,0:T(8,128)(2,1)S(1)}, bf16[2048,256]{1,0:T(8,128)(2,1)}, u32[]{:S(2)}) copy-start(bf16[2048,256]{1,0:T(8,128)(2,1)} %param.19) | copy-start | bytes 3145732
  196.2 26.6 %collective-permute-start.28 = (bf16[256,1024]{0,1:T(8,128)(2,1)}, bf16[256,1024]{0,1:T(8,128)(2,1)}, u32[]{:S(2)}, u32[]{:S(2)}) collective-permute-start(bf16[256,1024]{0,1:T(8,128)(2,1)} %bitcast.59), channel_id=1, source_target_pairs={{0,6},{2,0},{4,2},{6,4},{1,7},{3,1},{5,3},{7,5},{8,14},{10,8},{12,... | collective-permute-start | bytes 1572872 | tf_op jit(solution)/shard_map/ppermute | solution.py:233
  196.2 27.7 %collective-permute-start.27 = (bf16[256,1024]{0,1:T(8,128)(2,1)}, bf16[256,1024]{0,1:T(8,128)(2,1)}, u32[]{:S(2)}, u32[]{:S(2)}) collective-permute-start(bf16[256,1024]{0,1:T(8,128)(2,1)} %bitcast.59), channel_id=1, source_target_pairs={{0,4},{2,6},{4,0},{6,2},{1,5},{3,7},{5,1},{7,3},{8,12},{10,14},{12... | collective-permute-start | bytes 1572872 | tf_op jit(solution)/shard_map/ppermute | solution.py:233
  197.7 26.3 %collective-permute-start.26 = (bf16[256,1024]{0,1:T(8,128)(2,1)}, bf16[256,1024]{0,1:T(8,128)(2,1)}, u32[]{:S(2)}, u32[]{:S(2)}) collective-permute-start(bf16[256,1024]{0,1:T(8,128)(2,1)} %bitcast.59), channel_id=1, source_target_pairs={{0,2},{2,4},{4,6},{6,0},{1,3},{3,5},{5,7},{7,1},{8,10},{10,12},{12... | collective-permute-start | bytes 1572872 | tf_op jit(solution)/shard_map/ppermute | solution.py:233
  219.8 71.7 %collective-permute-start.19 = (bf16[256,1024]{0,1:T(8,128)(2,1)S(1)}, bf16[256,1024]{0,1:T(8,128)(2,1)S(1)}, u32[]{:S(2)}, u32[]{:S(2)}) collective-permute-start(bf16[256,1024]{0,1:T(8,128)(2,1)S(1)} %bitcast.236), channel_id=1, source_target_pairs={{0,6},{2,0},{4,2},{6,4},{1,7},{3,1},{5,3},{7,5},{8,14},{10,8},{12,... | collective-permute-start | bytes 1572872 | tf_op jit(solution)/shard_map/ppermute | solution.py:233
  222.2 69.3 %collective-permute-start.18 = (bf16[256,1024]{0,1:T(8,128)(2,1)S(1)}, bf16[256,1024]{0,1:T(8,128)(2,1)S(1)}, u32[]{:S(2)}, u32[]{:S(2)}) collective-permute-start(bf16[256,1024]{0,1:T(8,128)(2,1)S(1)} %bitcast.237), channel_id=1, source_target_pairs={{0,4},{2,6},{4,0},{6,2},{1,5},{3,7},{5,1},{7,3},{8,12},{10,14},{12... | collective-permute-start | bytes 1572872 | tf_op jit(solution)/shard_map/ppermute | solution.py:233
  222.8 68.7 %collective-permute-start.17 = (bf16[256,1024]{0,1:T(8,128)(2,1)S(1)}, bf16[256,1024]{0,1:T(8,128)(2,1)S(1)}, u32[]{:S(2)}, u32[]{:S(2)}) collective-permute-start(bf16[256,1024]{0,1:T(8,128)(2,1)S(1)} %bitcast.238), channel_id=1, source_target_pairs={{0,2},{2,4},{4,6},{6,0},{1,3},{3,5},{5,7},{7,1},{8,10},{10,12},{12... | collective-permute-start | bytes 1572872 | tf_op jit(solution)/shard_map/ppermute | solution.py:233
  291.5 0.8 copy-start.3
  292.3 0.8 copy-start.4
  297.0 6.0 %collective-permute-start.29 = (f32[1024,512]{1,0:T(8,128)}, f32[1024,512]{1,0:T(8,128)S(1)}, u32[]{:S(2)}, u32[]{:S(2)}) collective-permute-start(f32[1024,512]{1,0:T(8,128)} %convolution_add_fusion), channel_id=1, source_target_pairs={{0,1},{1,0},{2,3},{3,2},{4,5},{5,4},{6,7},{7,6},{8,9},{9,8},{10,11... | collective-permute-start | bytes 6291464 | tf_op jit(solution)/shard_map/ppermute | solution.py:260
  303.9 9.2 %collective-permute-start.32 = (bf16[256,512]{1,0:T(8,128)(2,1)S(1)}, bf16[256,512]{1,0:T(8,128)(2,1)S(1)}, u32[]{:S(2)}, u32[]{:S(2)}) collective-permute-start(bf16[256,512]{1,0:T(8,128)(2,1)S(1)} %get-tuple-element.132), channel_id=1, source_target_pairs={{0,6},{2,0},{4,2},{6,4},{1,7},{3,1},{5,3},{7,5},{8,14},{10,8},{12,... | collective-permute-start | bytes 786440 | tf_op jit(solution)/shard_map/ppermute | solution.py:265
  306.4 14.1 %collective-permute-start.31 = (bf16[256,512]{1,0:T(8,128)(2,1)S(1)}, bf16[256,512]{1,0:T(8,128)(2,1)S(1)}, u32[]{:S(2)}, u32[]{:S(2)}) collective-permute-start(bf16[256,512]{1,0:T(8,128)(2,1)S(1)} %get-tuple-element.133), channel_id=1, source_target_pairs={{0,4},{2,6},{4,0},{6,2},{1,5},{3,7},{5,1},{7,3},{8,12},{10,14},{12... | collective-permute-start | bytes 786440 | tf_op jit(solution)/shard_map/ppermute | solution.py:265
  306.9 13.5 %collective-permute-start.30 = (bf16[256,512]{1,0:T(8,128)(2,1)S(1)}, bf16[256,512]{1,0:T(8,128)(2,1)S(1)}, u32[]{:S(2)}, u32[]{:S(2)}) collective-permute-start(bf16[256,512]{1,0:T(8,128)(2,1)S(1)} %get-tuple-element.134), channel_id=1, source_target_pairs={{0,2},{2,4},{4,6},{6,0},{1,3},{3,5},{5,7},{7,1},{8,10},{10,12},{12... | collective-permute-start | bytes 786440 | tf_op jit(solution)/shard_map/ppermute | solution.py:265
Sparse Core Ops, SparseCore 0:
  201.9 86.4 all-gather.1

commit v12 on v9

--- a/solution.py
+++ b/solution.py
@@ -246,20 +246,23 @@
     half = w_line.shape[1] // 2
     me = lax.axis_index("head")
 
-    def product(columns):
+    def product(ret_part, run_part, columns):
         w_half = lax.dynamic_slice_in_dim(w_line, columns * half, half, axis=1)
-        return jnp.dot(ret_stack, w_half[:ret_rows], preferred_element_type=jnp.float32) + jnp.dot(
-            run_stack, w_half[ret_rows:], preferred_element_type=jnp.float32
-        )
-
-    sent = lax.ppermute(product(1 - me), "head", [(0, 1), (1, 0)])
-    reduced = (product(me) + sent).astype(jnp.bfloat16)
+        return jnp.dot(ret_part, w_half[:ret_rows], preferred_element_type=jnp.float32) + jnp.dot(
+            run_part, w_half[ret_rows:], preferred_element_type=jnp.float32
+        )
+
+    def reduced(ret_part, run_part):
+        sent = lax.ppermute(product(ret_part, run_part, 1 - me), "head", [(0, 1), (1, 0)])
+        return (product(ret_part, run_part, me) + sent).astype(jnp.bfloat16)
+
     me_cb = lax.axis_index("cb")
-    blocks = reduced.reshape(plane, rows, half)
-    got = [blocks[0]] + [
-        lax.ppermute(blocks[(-shift) % plane], "cb", [(i, (i + shift) % plane) for i in range(plane)])
+    far = reduced(ret_stack[rows:], run_stack[rows:]).reshape(plane - 1, rows, half)
+    got = [None] + [
+        lax.ppermute(far[(-shift) % plane - 1], "cb", [(i, (i + shift) % plane) for i in range(plane)])
         for shift in range(1, plane)
     ]
+    got[0] = reduced(ret_stack[:rows], run_stack[:rows])
     got = jnp.take(jnp.stack(got), (me_cb - jnp.arange(plane)) % plane, axis=0)
     per_head = line // head_count
     return (

time: 237 us -> 234 us (0.987)
  waiting for transfers between devices: 126 us -> 108 us
  local copies, waits for them, and re-layouts: 18.8 us -> 25.9 us
  starting transfers between devices: 24.4 us -> 28.5 us
  matrix products: 30.8 us -> 34.6 us
    all_gather x1, waiting for transfers between devices: 62.4 us -> 51.7 us  [project_assigned(): w_line = lax.all_gather(w_mine, 'cz', axis=1, tiled=True)]
    all_gather x1, waiting for transfers between devices: 42.1 us -> 31.9 us  [duo_attend(): lax.all_gather(ret_kv.reshape(rows, ret_per * 2 * HEAD_SIZE), CTX, axis=0...]
    ppermute x6, waiting for transfers between devices: 0.02 us -> 9.43 us  [plane_pieces(): lax.ppermute(block, 'cb', [(i, (i + shift) % plane) for i in range(plane)])]
    ppermute x4 -> x5, waiting for transfers between devices: 12.9 us -> 8.4 us  [the longest x3 8.39 us: project_assigned(): lax.ppermute(far[-shift % plane - 1], 'cb', [(i, (i + shift) % plane) for...]
    dot_general x2, matrix products: 11.9 us -> 14.7 us  [update(): jnp.einsum('hgrk,khd->hgrd', weights.astype(jnp.bfloat16), value_block, p...]
    ppermute x6, starting transfers between devices: 6.96 us -> 9.61 us  [plane_pieces(): lax.ppermute(block, 'cb', [(i, (i + shift) % plane) for i in range(plane)])]
    ppermute x4 -> x5, starting transfers between devices: 3.56 us -> 5.04 us  [the longest x3 4.47 us: project_assigned(): lax.ppermute(far[-shift % plane - 1], 'cb', [(i, (i + shift) % plane) for...]
    dot_general x4 -> x8, matrix products: 12.7 us -> 13.6 us  [the longest x4 7.64 us: product(): jnp.dot(run_part, w_half[ret_rows:], preferred_element_type=jnp.float32)]
  transfers between devices with their start and end apart: 20 -> 21, of which waited for: 8 -> 10; matrix products, arithmetic and copies ran while one was open for 23% -> 26% of each run, Pallas kernels for 0% -> 0%
where the time goes in v12:
time: 234 us
  waiting for transfers between devices  108 us (46%)
  matrix products  34.6 us (15%)
  starting transfers between devices  28.5 us (12%)
  local copies, waits for them, and re-layouts  25.9 us (11%)
  other arithmetic  21.5 us (9%)
  between operations  14.8 us (6%)
    all_gather x1, waiting for transfers between devices, project_assigned(): w_line = lax.all_gather(w_mine, 'cz', axis=1, tiled=True)  51.7 us
    all_gather x1, waiting for transfers between devices, duo_attend(): lax.all_gather(ret_kv.reshape(rows, ret_per * 2 * HEAD_SIZE), CTX, axis=0...  31.9 us
    dot_general x2, matrix products, update(): jnp.einsum('hgrk,khd->hgrd', weights.astype(jnp.bfloat16), value_block, p...  14.7 us
    ppermute x6, starting transfers between devices, plane_pieces(): lax.ppermute(block, 'cb', [(i, (i + shift) % plane) for i in range(plane)])  9.61 us
    ppermute x6, waiting for transfers between devices, plane_pieces(): lax.ppermute(block, 'cb', [(i, (i + shift) % plane) for i in range(plane)])  9.43 us
    ppermute x4, starting transfers between devices, duo_attend(): got = lax.ppermute(sink_kv, CTX, pairs)  8.73 us
    ppermute x3, waiting for transfers between devices, project_assigned(): lax.ppermute(far[-shift % plane - 1], 'cb', [(i, (i + shift) % plane) for...  8.39 us
    unnamed x35, local copies, waits for them, and re-layouts  7.76 us
  transfers between devices with their start and end apart: 21, of which 10 were waited for; matrix products, arithmetic and copies ran while one was open for 26% of the time, Pallas kernels for 0%

profile of v12, /device:TPU:0, one launch (start us, length us, event | category | flops | bytes accessed | tf_op | source)
XLA Modules:
  0.0 233.5 jit_solution(2019721716432638222)
XLA Ops:
  9.1 1.1 copy.34
  17.3 1.4 subtract_convert_fusion
  21.6 4.8 %collective-permute-start.3 = (bf16[64,2,2,128]{3,0,1,2:T(8,128)(2,1)S(1)}, bf16[64,2,2,128]{3,0,1,2:T(8,128)(2,1)S(1)}, u32[]{:S(2)}, u32[]{:S(2)}) collective-permute-start(bf16[64,2,2,128]{3,0,1,2:T(8,128)(2,1)S(1)} %slice.87), channel_id=1, source_target_pairs={{0,2},{1,3}} | collective-permute-start | bytes 196616 | tf_op jit(solution)/shard_map/ppermute | solution.py:174
  26.5 3.0 %collective-permute-done.3 = bf16[64,2,2,128]{3,0,1,2:T(8,128)(2,1)S(1)} collective-permute-done((bf16[64,2,2,128]{3,0,1,2:T(8,128)(2,1)S(1)}, bf16[64,2,2,128]{3,0,1,2:T(8,128)(2,1)S(1)}, u32[]{:S(2)}, u32[]{:S(2)}) %collective-permute-start.3) | collective-permute-done | bytes 65568 | tf_op jit(solution)/shard_map/ppermute | solution.py:174
  29.5 1.3 collective-permute-start.4
  31.5 1.1 collective-permute-done.4
  32.7 1.3 collective-permute-start.5
  34.0 4.4 %collective-permute-start.7 = (bf16[256,2,2,128]{3,0,1,2:T(8,128)(2,1)S(1)}, bf16[256,2,2,128]{3,0,1,2:T(8,128)(2,1)S(1)}, u32[]{:S(2)}, u32[]{:S(2)}) collective-permute-start(bf16[256,2,2,128]{3,0,1,2:T(8,128)(2,1)S(1)} %fusion.52), channel_id=1, source_target_pairs={{0,2},{2,4},{4,6},{6,8},{8,10},{10,12},{12,14},{14,16},{16,18},{18... | collective-permute-start | bytes 786440 | tf_op jit(solution)/shard_map/ppermute | solution.py:169
  38.5 1.3 collective-permute-start.6
  39.8 1.8 collective-permute-done.6
  43.1 1.4 select_bitcast_fusion.3
  44.7 1.4 gather_fusion.5
  46.2 2.1 fusion.17
  48.3 2.1 copy-done.2
  50.4 1.1 fusion.18
  51.6 1.5 gather_fusion.3
  53.1 4.5 %divide_convert_fusion = bf16[256,2,4,128]{0,3,2,1:T(8,128)(2,1)} fusion(f32[2,576,256,4]{2,1,3,0:T(8,128)} %copy-done.2, f32[2,4,256]{2,1,0:T(4,128)S(1)} %get-tuple-element.139, pred[256,576]{0,1:T(8,128)(4,1)S(1)} %pad_add_fusion, f32[256,2,4]{0,2,1:T(4,128)S(1)} %bitcast_add_fusion, f32[256,2,4]{0,2,1:T(4,128)S(1)} %get-tuple-element.138, ...), kind=kOutput, calls=%fused_computation.54 | convolution fusion | flops 308674560 | bytes 5709824 | tf_op jit(solution)/shard_map/hgrk,khd->hgrd/dot_general | solution.py:62
  57.5 2.5 %collective-permute-start.12 = (bf16[256,1024]{0,1:T(8,128)(2,1)}, bf16[256,1024]{0,1:T(8,128)(2,1)}, u32[]{:S(2)}, u32[]{:S(2)}) collective-permute-start(bf16[256,1024]{0,1:T(8,128)(2,1)} %bitcast.42), channel_id=1, source_target_pairs={{0,2},{2,4},{4,6},{6,0},{1,3},{3,5},{5,7},{7,1},{8,10},{10,12},{12... | collective-permute-start | bytes 1572872 | tf_op jit(solution)/shard_map/ppermute | solution.py:228
  60.0 2.5 %collective-permute-start.13 = (bf16[256,1024]{0,1:T(8,128)(2,1)}, bf16[256,1024]{0,1:T(8,128)(2,1)}, u32[]{:S(2)}, u32[]{:S(2)}) collective-permute-start(bf16[256,1024]{0,1:T(8,128)(2,1)} %bitcast.42), channel_id=1, source_target_pairs={{0,4},{2,6},{4,0},{6,2},{1,5},{3,7},{5,1},{7,3},{8,12},{10,14},{12... | collective-permute-start | bytes 1572872 | tf_op jit(solution)/shard_map/ppermute | solution.py:228
  62.5 1.3 collective-permute-start.14
  63.8 1.4 select_bitcast_fusion.1
  66.0 1.3 bitcast_select_fusion.2
  67.5 9.4 %collective-permute-done.12 = bf16[256,1024]{0,1:T(8,128)(2,1)} collective-permute-done((bf16[256,1024]{0,1:T(8,128)(2,1)}, bf16[256,1024]{0,1:T(8,128)(2,1)}, u32[]{:S(2)}, u32[]{:S(2)}) %collective-permute-start.12) | collective-permute-done | bytes 524320 | tf_op jit(solution)/shard_map/ppermute | solution.py:228
  78.0 31.9 %all-gather.3.cloned.1.call-done = bf16[4096,512]{0,1:T(8,128)(2,1)} async-done(((bf16[256,512]{0,1:T(8,128)(2,1)}), bf16[4096,512]{0,1:T(8,128)(2,1)}) %all-gather.3.cloned.1.call-update) | async-done | bytes 4194320 | tf_op jit(solution)/shard_map/all_gather | solution.py:199
  109.9 1.1 broadcast.345
  111.0 21.4 %while.15 = (s32[]{:T(128)}, f32[2,4,256]{2,1,0:T(4,128)S(1)}, f32[2,4,256]{2,1,0:T(4,128)S(1)}, f32[2,4,256,128]{3,2,1,0:T(8,128)}, s32[]{:T(128)}, /*index=5*/...) while((s32[]{:T(128)}, f32[2,4,256]{2,1,0:T(4,128)S(1)}, ...), condition=%wide.region_5.8_spmd.clone, body=%wide.region_2.7_spmd.clone.sunk | while | flops 2203064576 | bytes 124405992 | solution.py:216
  111.5 4.2 %fusion.90 = (f32[2,4,256]{2,1,0:T(4,128)S(1)}, f32[2,2048,256,4]{2,1,3,0:T(8,128)S(1)}) fusion(pred[256,2048]{0,1:T(8,128)(4,1)S(1)} %broadcast_compare_fusion.3, bf16[256,2,4,128]{3,0,2,1:T(8,128)(2,1)S(1)} %get-tuple-element.244, bf16[4096,2,2,128]{0,3,2,1:T(8,128)(2,1)} %get-tuple-element.243, s32[]{:T(128)S(6)} %select_n.342), kind=kOutput, calls=%fused_computation.9.clone.1 | convolution fusion | flops 1086322688 | bytes 18882564 | tf_op jit(solution)/shard_map/while/body/rhgd,khd->hgrk/dot_general | solution.py:53
  115.8 4.1 %fusion.91 = f32[2,4,256]{2,1,0:T(4,128)S(1)} fusion(f32[2,2048,256,4]{2,1,3,0:T(8,128)S(1)} %get-tuple-element.209, f32[2,4,256]{2,1,0:T(4,128)S(1)} %max.13, pred[256,2048]{0,1:T(8,128)(4,1)S(1)} %broadcast_compare_fusion.3), kind=kLoop, calls=%fused_computation.11.clone.1 | loop fusion | flops 20969472 | bytes 17317888 | tf_op jit(solution)/shard_map/while/body/reduce_sum | solution.py:61
  119.8 2.4 %copy-done = f32[2,2048,256,4]{2,1,3,0:T(8,128)} copy-done((f32[2,2048,256,4]{2,1,3,0:T(8,128)}, f32[2,2048,256,4]{2,1,3,0:T(8,128)S(1)}, u32[]{:S(2)}) %copy-start) | copy-done | bytes 16777240 | tf_op jit(solution)/shard_map/while
  122.2 10.3 %fusion.92 = f32[2,4,256,128]{3,2,1,0:T(8,128)} fusion(f32[2,2048,256,4]{2,1,3,0:T(8,128)} %copy-done, f32[2,4,256]{2,1,0:T(4,128)S(1)} %max.13, pred[256,2048]{0,1:T(8,128)(4,1)S(1)} %broadcast_compare_fusion.3, bf16[4096,2,2,128]{0,3,2,1:T(8,128)(2,1)} %get-tuple-element.243, s32[]{:T(128)S(6)} %select_n.342, s32[]{:T(128)S(6)} %add.334, ...), kind=kOutput, calls=%fused_computation.14.clone.1 | convolution fusion | flops 1095237632 | bytes 20463624 | tf_op jit(solution)/shard_map/while/body/hgrk,khd->hgrd/dot_general | solution.py:62
  132.5 1.6 copy.42
  134.2 1.5 collective-permute-start.9
  135.7 1.1 constant_dynamic-update-slice_fusion.4
  136.7 1.8 collective-permute-start.10
  139.7 51.7 %all-gather.5.cloned.1.call-done = bf16[2048,1024]{1,0:T(8,128)(2,1)} async-done(((bf16[2048,256]{1,0:T(8,128)(2,1)}), bf16[2048,1024]{1,0:T(8,128)(2,1)}) %all-gather.5.cloned.1.call-update) | async-done | bytes 4194320 | tf_op jit(solution)/shard_map/all_gather | solution.py:242
  191.3 2.2 fusion.42
  194.8 4.0 %convolution_add_fusion = f32[768,512]{1,0:T(8,128)} fusion(f32[768,512]{1,0:T(8,128)S(1)} %fusion.42, bf16[768,1024]{0,1:T(8,128)(2,1)S(1)} %constant_dynamic-update-slice_fusion, bf16[2048,1024]{1,0:T(8,128)(2,1)} %all-gather.5.cloned.1.call-done, s32[]{:T(128)S(6)} %select_n.197), kind=kOutput, calls=%fused_computation.42 | convolution fusion | flops 805699584 | bytes 5767172 | tf_op jit(solution)/shard_map/dot_general | solution.py:251
  198.8 2.4 %fusion.45 = f32[768,512]{1,0:T(8,128)S(1)} fusion(bf16[768,1024]{0,1:T(8,128)(2,1)S(1)} %constant_dynamic-update-slice_fusion.3, bf16[2048,1024]{1,0:T(8,128)(2,1)} %all-gather.5.cloned.1.call-done, s32[]{:T(128)S(6)} %add.241, s32[]{:T(128)S(6)} %select_n.186), kind=kOutput, calls=%fused_computation.71 | convolution fusion | flops 805306368 | bytes 4194312 | tf_op jit(solution)/shard_map/dot_general | solution.py:251
  201.8 1.5 convolution_add_fusion.1
  204.9 1.9 add_convert_fusion.1
  206.8 1.6 collective-permute-start.16
  208.4 1.4 collective-permute-start.17
  209.8 1.5 collective-permute-start.18
  211.8 1.5 fusion.31
  213.3 3.7 %collective-permute-done.16 = bf16[256,512]{1,0:T(8,128)(2,1)S(1)} collective-permute-done((bf16[256,512]{1,0:T(8,128)(2,1)S(1)}, bf16[256,512]{1,0:T(8,128)(2,1)S(1)}, u32[]{:S(2)}, u32[]{:S(2)}) %collective-permute-start.16) | collective-permute-done | bytes 262176 | tf_op jit(solution)/shard_map/ppermute | solution.py:262
  217.0 4.6 %collective-permute-done.17 = bf16[256,512]{1,0:T(8,128)(2,1)S(1)} collective-permute-done((bf16[256,512]{1,0:T(8,128)(2,1)S(1)}, bf16[256,512]{1,0:T(8,128)(2,1)S(1)}, u32[]{:S(2)}, u32[]{:S(2)}) %collective-permute-start.17) | collective-permute-done | bytes 262176 | tf_op jit(solution)/shard_map/ppermute | solution.py:262
  223.7 1.4 copy.44
  225.1 1.6 reshape.371
  (126 shorter events, 24.0 us)
Async XLA Ops:
  6.5 4.6 %copy-start.13 = (s32[4]{0:T(128)S(1)}, s32[4]{0:T(128)}, u32[]{:S(2)}) copy-start(s32[4]{0:T(128)} %param.17) | copy-start | bytes 52
  6.5 103.4 %all-gather.3.cloned.1.call-start = ((), (), s32[]{:S(2)}) async-start(), calls=%async_computation | async-start | bytes 4456448 | tf_op jit(solution)/shard_map/all_gather | solution.py:199
  10.6 2.4 %collective-permute-start = (bf16[256,4,2,128]{0,3,1,2:T(8,128)(2,1)S(1)}, bf16[256,4,2,128]{0,3,1,2:T(8,128)(2,1)S(1)}, u32[]{:S(2)}, u32[]{:S(2)}) collective-permute-start(bf16[256,4,2,128]{0,3,1,2:T(8,128)(2,1)S(1)} %pad_maximum_fusion.5), channel_id=1, source_target_pairs={{0,1},{1,0},{2,3},{3,2},{4,5},{5,4},{6,7},{7,6},{8,9},{9,8},{10,11... | collective-permute-start | bytes 1572872 | tf_op jit(solution)/shard_map/ppermute | solution.py:139
  12.9 0.5 copy-start.11
  12.9 1.8 copy-start.8
  12.9 7.0 %copy-start.12 = (s32[2]{0:T(128)}, s32[2]{0:T(128)S(1)}, u32[]{:S(2)}) copy-start(s32[2]{0:T(128)S(1)} %get-tuple-element.143) | copy-start | bytes 28
  13.4 2.5 %copy-start.4 = (bf16[256,2048]{1,0:T(8,128)(2,1)S(1)}, bf16[256,2048]{1,0:T(8,128)(2,1)}, u32[]{:S(2)}) copy-start(bf16[256,2048]{1,0:T(8,128)(2,1)} %param.13) | copy-start | bytes 3145732
  15.7 175.6 %all-gather.5.cloned.1.call-start = ((), (), s32[]{:S(2)}) async-start(), calls=%async_computation.1 | async-start | bytes 5242880 | tf_op jit(solution)/shard_map/all_gather | solution.py:242
  18.6 1.2 copy-start.5
  19.2 23.9 %collective-permute-start.1 = (bf16[256,4,4,128]{3,0,2,1:T(8,128)(2,1)S(1)}, bf16[256,4,4,128]{3,0,2,1:T(8,128)(2,1)}, u32[]{:S(2)}, u32[]{:S(2)}) collective-permute-start(bf16[256,4,4,128]{3,0,2,1:T(8,128)(2,1)S(1)} %bitcast.188), channel_id=1, source_target_pairs={{0,1},{1,0},{2,3},{3,2},{4,5},{5,4},{6,7},{7,6},{8,9},{9,8},{10,11... | collective-permute-start | bytes 3145736 | tf_op jit(solution)/shard_map/ppermute | solution.py:139
  19.9 43.9 %collective-permute-start.2 = (bf16[4,512,256]{2,1,0:T(8,128)(2,1)S(1)}, bf16[4,512,256]{2,1,0:T(8,128)(2,1)}, u32[]{:S(2)}, u32[]{:S(2)}) collective-permute-start(bf16[4,512,256]{2,1,0:T(8,128)(2,1)S(1)} %bitcast.195), channel_id=1, source_target_pairs={{0,1},{1,0},{2,3},{3,2},{4,5},{5,4},{6,7},{7,6},{8,9},{9,8},{10,11... | collective-permute-start | bytes 3145736 | tf_op jit(solution)/shard_map/ppermute | solution.py:139
  21.6 7.9 %collective-permute-start.3 = (bf16[64,2,2,128]{3,0,1,2:T(8,128)(2,1)S(1)}, bf16[64,2,2,128]{3,0,1,2:T(8,128)(2,1)S(1)}, u32[]{:S(2)}, u32[]{:S(2)}) collective-permute-start(bf16[64,2,2,128]{3,0,1,2:T(8,128)(2,1)S(1)} %slice.87), channel_id=1, source_target_pairs={{0,2},{1,3}} | collective-permute-start | bytes 196616 | tf_op jit(solution)/shard_map/ppermute | solution.py:174
  29.5 3.2 %collective-permute-start.4 = (bf16[64,2,2,128]{3,0,1,2:T(8,128)(2,1)S(1)}, bf16[64,2,2,128]{3,0,1,2:T(8,128)(2,1)S(1)}, u32[]{:S(2)}, u32[]{:S(2)}) collective-permute-start(bf16[64,2,2,128]{3,0,1,2:T(8,128)(2,1)S(1)} %broadcast_select_fusion.1), channel_id=1, source_target_pairs={{0,4},{2,6},{1,5},{3,7}} | collective-permute-start | bytes 196616 | tf_op jit(solution)/shard_map/ppermute | solution.py:174
  32.7 5.8 %collective-permute-start.5 = (bf16[64,2,2,128]{3,0,1,2:T(8,128)(2,1)S(1)}, bf16[64,2,2,128]{3,0,1,2:T(8,128)(2,1)S(1)}, u32[]{:S(2)}, u32[]{:S(2)}) collective-permute-start(bf16[64,2,2,128]{3,0,1,2:T(8,128)(2,1)S(1)} %broadcast_select_fusion.2), channel_id=1, source_target_pairs={{0,8},{2,10},{4,12},{6,14},{1,9},{3,11},{5,13},{7,15}} | collective-permute-start | bytes 196616 | tf_op jit(solution)/shard_map/ppermute | solution.py:174
  34.0 8.3 %collective-permute-start.7 = (bf16[256,2,2,128]{3,0,1,2:T(8,128)(2,1)S(1)}, bf16[256,2,2,128]{3,0,1,2:T(8,128)(2,1)S(1)}, u32[]{:S(2)}, u32[]{:S(2)}) collective-permute-start(bf16[256,2,2,128]{3,0,1,2:T(8,128)(2,1)S(1)} %fusion.52), channel_id=1, source_target_pairs={{0,2},{2,4},{4,6},{6,8},{8,10},{10,12},{12,14},{14,16},{16,18},{18... | collective-permute-start | bytes 786440 | tf_op jit(solution)/shard_map/ppermute | solution.py:169
  38.5 3.2 %collective-permute-start.6 = (bf16[64,2,2,128]{3,0,1,2:T(8,128)(2,1)S(1)}, bf16[64,2,2,128]{3,0,1,2:T(8,128)(2,1)S(1)}, u32[]{:S(2)}, u32[]{:S(2)}) collective-permute-start(bf16[64,2,2,128]{3,0,1,2:T(8,128)(2,1)S(1)} %broadcast_select_fusion.3), channel_id=1, source_target_pairs={{0,16},{2,18},{4,20},{6,22},{8,24},{10,26},{12,28},{14,30},{1,17},... | collective-permute-start | bytes 196616 | tf_op jit(solution)/shard_map/ppermute | solution.py:174
  44.5 1.6 copy-start.10
  48.3 2.2 copy-start.2
  57.5 19.4 %collective-permute-start.12 = (bf16[256,1024]{0,1:T(8,128)(2,1)}, bf16[256,1024]{0,1:T(8,128)(2,1)}, u32[]{:S(2)}, u32[]{:S(2)}) collective-permute-start(bf16[256,1024]{0,1:T(8,128)(2,1)} %bitcast.42), channel_id=1, source_target_pairs={{0,2},{2,4},{4,6},{6,0},{1,3},{3,5},{5,7},{7,1},{8,10},{10,12},{12... | collective-permute-start | bytes 1572872 | tf_op jit(solution)/shard_map/ppermute | solution.py:228
  60.0 75.7 %collective-permute-start.13 = (bf16[256,1024]{0,1:T(8,128)(2,1)}, bf16[256,1024]{0,1:T(8,128)(2,1)}, u32[]{:S(2)}, u32[]{:S(2)}) collective-permute-start(bf16[256,1024]{0,1:T(8,128)(2,1)} %bitcast.42), channel_id=1, source_target_pairs={{0,4},{2,6},{4,0},{6,2},{1,5},{3,7},{5,1},{7,3},{8,12},{10,14},{12... | collective-permute-start | bytes 1572872 | tf_op jit(solution)/shard_map/ppermute | solution.py:228
  62.5 76.1 %collective-permute-start.14 = (bf16[256,1024]{0,1:T(8,128)(2,1)}, bf16[256,1024]{0,1:T(8,128)(2,1)}, u32[]{:S(2)}, u32[]{:S(2)}) collective-permute-start(bf16[256,1024]{0,1:T(8,128)(2,1)} %bitcast.42), channel_id=1, source_target_pairs={{0,6},{2,0},{4,2},{6,4},{1,7},{3,1},{5,3},{7,5},{8,14},{10,8},{12,... | collective-permute-start | bytes 1572872 | tf_op jit(solution)/shard_map/ppermute | solution.py:228
  66.0 1.4 copy-start.3
  66.0 1.4 copy-start.9
  115.8 6.5 %copy-start = (f32[2,2048,256,4]{2,1,3,0:T(8,128)}, f32[2,2048,256,4]{2,1,3,0:T(8,128)S(1)}, u32[]{:S(2)}) copy-start(f32[2,2048,256,4]{2,1,3,0:T(8,128)S(1)} %get-tuple-element.209) | copy-start | bytes 50331652 | tf_op jit(solution)/shard_map/while
  134.2 59.4 %collective-permute-start.9 = (bf16[256,1024]{0,1:T(8,128)(2,1)S(1)}, bf16[256,1024]{0,1:T(8,128)(2,1)S(1)}, u32[]{:S(2)}, u32[]{:S(2)}) collective-permute-start(bf16[256,1024]{0,1:T(8,128)(2,1)S(1)} %bitcast.180), channel_id=1, source_target_pairs={{0,2},{2,4},{4,6},{6,0},{1,3},{3,5},{5,7},{7,1},{8,10},{10,12},{12... | collective-permute-start | bytes 1572872 | tf_op jit(solution)/shard_map/ppermute | solution.py:228
  136.7 56.9 %collective-permute-start.10 = (bf16[256,1024]{0,1:T(8,128)(2,1)S(1)}, bf16[256,1024]{0,1:T(8,128)(2,1)S(1)}, u32[]{:S(2)}, u32[]{:S(2)}) collective-permute-start(bf16[256,1024]{0,1:T(8,128)(2,1)S(1)} %bitcast.181), channel_id=1, source_target_pairs={{0,4},{2,6},{4,0},{6,2},{1,5},{3,7},{5,1},{7,3},{8,12},{10,14},{12... | collective-permute-start | bytes 1572872 | tf_op jit(solution)/shard_map/ppermute | solution.py:228
  139.6 54.1 %collective-permute-start.11 = (bf16[256,1024]{0,1:T(8,128)(2,1)S(1)}, bf16[256,1024]{0,1:T(8,128)(2,1)}, u32[]{:S(2)}, u32[]{:S(2)}) collective-permute-start(bf16[256,1024]{0,1:T(8,128)(2,1)S(1)} %bitcast.182), channel_id=1, source_target_pairs={{0,6},{2,0},{4,2},{6,4},{1,7},{3,1},{5,3},{7,5},{8,14},{10,8},{12,... | collective-permute-start | bytes 1572872 | tf_op jit(solution)/shard_map/ppermute | solution.py:228
  194.8 4.0 %copy-start.6 = (bf16[768,1024]{0,1:T(8,128)(2,1)}, bf16[768,1024]{0,1:T(8,128)(2,1)S(1)}, u32[]{:S(2)}) copy-start(bf16[768,1024]{0,1:T(8,128)(2,1)S(1)} %constant_dynamic-update-slice_fusion) | copy-start | bytes 4718596
  198.8 6.1 %collective-permute-start.15 = (f32[768,512]{1,0:T(8,128)}, f32[768,512]{1,0:T(8,128)}, u32[]{:S(2)}, u32[]{:S(2)}) collective-permute-start(f32[768,512]{1,0:T(8,128)} %convolution_add_fusion), channel_id=1, source_target_pairs={{0,1},{1,0},{2,3},{3,2},{4,5},{5,4},{6,7},{7,6},{8,9},{9,8},{10,11... | collective-permute-start | bytes 4718600 | tf_op jit(solution)/shard_map/ppermute | solution.py:256
  198.8 2.5 %copy-start.1 = (bf16[2048,1024]{1,0:T(8,128)(2,1)S(1)}, bf16[2048,1024]{1,0:T(8,128)(2,1)}, u32[]{:S(2)}) copy-start(bf16[2048,1024]{1,0:T(8,128)(2,1)} %all-gather.5.cloned.1.call-done) | copy-start | bytes 12582916
  201.3 2.6 %copy-start.7 = (bf16[768,1024]{0,1:T(8,128)(2,1)S(1)}, bf16[768,1024]{0,1:T(8,128)(2,1)}, u32[]{:S(2)}) copy-start(bf16[768,1024]{0,1:T(8,128)(2,1)} %copy-done.6) | copy-start | bytes 4718596
  203.3 8.5 %collective-permute-start.8 = (f32[256,512]{1,0:T(8,128)S(1)}, f32[256,512]{1,0:T(8,128)S(1)}, u32[]{:S(2)}, u32[]{:S(2)}) collective-permute-start(f32[256,512]{1,0:T(8,128)S(1)} %convolution_add_fusion.1), channel_id=1, source_target_pairs={{0,1},{1,0},{2,3},{3,2},{4,5},{5,4},{6,7},{7,6},{8,9},{9,8},{10,11... | collective-permute-start | bytes 1572872 | tf_op jit(solution)/shard_map/ppermute | solution.py:256
  206.8 10.2 %collective-permute-start.16 = (bf16[256,512]{1,0:T(8,128)(2,1)S(1)}, bf16[256,512]{1,0:T(8,128)(2,1)S(1)}, u32[]{:S(2)}, u32[]{:S(2)}) collective-permute-start(bf16[256,512]{1,0:T(8,128)(2,1)S(1)} %get-tuple-element.133), channel_id=1, source_target_pairs={{0,2},{2,4},{4,6},{6,0},{1,3},{3,5},{5,7},{7,1},{8,10},{10,12},{12... | collective-permute-start | bytes 786440 | tf_op jit(solution)/shard_map/ppermute | solution.py:262
  208.4 13.2 %collective-permute-start.17 = (bf16[256,512]{1,0:T(8,128)(2,1)S(1)}, bf16[256,512]{1,0:T(8,128)(2,1)S(1)}, u32[]{:S(2)}, u32[]{:S(2)}) collective-permute-start(bf16[256,512]{1,0:T(8,128)(2,1)S(1)} %get-tuple-element.135), channel_id=1, source_target_pairs={{0,4},{2,6},{4,0},{6,2},{1,5},{3,7},{5,1},{7,3},{8,12},{10,14},{12... | collective-permute-start | bytes 786440 | tf_op jit(solution)/shard_map/ppermute | solution.py:262
  209.8 11.9 %collective-permute-start.18 = (bf16[256,512]{1,0:T(8,128)(2,1)S(1)}, bf16[256,512]{1,0:T(8,128)(2,1)S(1)}, u32[]{:S(2)}, u32[]{:S(2)}) collective-permute-start(bf16[256,512]{1,0:T(8,128)(2,1)S(1)} %get-tuple-element.134), channel_id=1, source_target_pairs={{0,6},{2,0},{4,2},{6,4},{1,7},{3,1},{5,3},{7,5},{8,14},{10,8},{12,... | collective-permute-start | bytes 786440 | tf_op jit(solution)/shard_map/ppermute | solution.py:262
Sparse Core Ops, SparseCore 0:
  15.8 94.0 all-gather.2
  111.5 79.7 all-gather.4

commit v13 on v12

--- a/solution.py
+++ b/solution.py
@@ -263,13 +263,13 @@
         for shift in range(1, plane)
     ]
     got[0] = reduced(ret_stack[:rows], run_stack[:rows])
-    got = jnp.take(jnp.stack(got), (me_cb - jnp.arange(plane)) % plane, axis=0)
     per_head = line // head_count
-    return (
-        got.reshape(plane, rows, per_head, col_width)
-        .transpose(1, 2, 0, 3)
-        .reshape(rows, per_head * plane * col_width)
-    )
+    out = jnp.zeros((rows, per_head, plane, col_width), jnp.bfloat16)
+    for shift, piece in enumerate(got):
+        out = lax.dynamic_update_slice_in_dim(
+            out, piece.reshape(rows, per_head, 1, col_width), (me_cb - shift) % plane, axis=2
+        )
+    return out.reshape(rows, per_head * plane * col_width)
 
 
 def plane_gather(block, plane):

time: 234 us -> 249 us (1.064)
  local copies, waits for them, and re-layouts: 25.9 us -> 50.3 us
  waiting for transfers between devices: 108 us -> 99.7 us
    dynamic_update_slice x0 -> x4, local copies, waits for them, and re-layouts: none -> 25.7 us  [project_assigned(): lax.dynamic_update_slice_in_dim(out, piece.reshape(rows, per_head, 1, col...]
    ppermute x3, waiting for transfers between devices: 8.39 us -> 0.01 us  [project_assigned(): lax.ppermute(far[-shift % plane - 1], 'cb', [(i, (i + shift) % plane) for...]
  transfers between devices with their start and end apart: 21 -> 21, of which waited for: 10 -> 7; matrix products, arithmetic and copies ran while one was open for 26% -> 33% of each run, Pallas kernels for 0% -> 0%
where the time goes in v13:
time: 249 us
  waiting for transfers between devices  99.7 us (40%)
  local copies, waits for them, and re-layouts  50.3 us (20%)
  matrix products  34.7 us (14%)
  starting transfers between devices  28.5 us (11%)
  other arithmetic  20.4 us (8%)
  between operations  14.8 us (6%)
    all_gather x1, waiting for transfers between devices, project_assigned(): w_line = lax.all_gather(w_mine, 'cz', axis=1, tiled=True)  51.8 us
    all_gather x1, waiting for transfers between devices, duo_attend(): lax.all_gather(ret_kv.reshape(rows, ret_per * 2 * HEAD_SIZE), CTX, axis=0...  32.1 us
    dynamic_update_slice x4, local copies, waits for them, and re-layouts, project_assigned(): lax.dynamic_update_slice_in_dim(out, piece.reshape(rows, per_head, 1, col...  25.7 us
    dot_general x2, matrix products, update(): jnp.einsum('hgrk,khd->hgrd', weights.astype(jnp.bfloat16), value_block, p...  14.7 us
    ppermute x6, starting transfers between devices, plane_pieces(): lax.ppermute(block, 'cb', [(i, (i + shift) % plane) for i in range(plane)])  9.64 us
    ppermute x6, waiting for transfers between devices, plane_pieces(): lax.ppermute(block, 'cb', [(i, (i + shift) % plane) for i in range(plane)])  9.17 us
    ppermute x4, starting transfers between devices, duo_attend(): got = lax.ppermute(sink_kv, CTX, pairs)  8.74 us
    unnamed x35, local copies, waits for them, and re-layouts  7.81 us
  transfers between devices with their start and end apart: 21, of which 7 were waited for; matrix products, arithmetic and copies ran while one was open for 33% of the time, Pallas kernels for 0%

profile of v13, /device:TPU:0, one launch (start us, length us, event | category | flops | bytes accessed | tf_op | source)
XLA Modules:
  0.0 248.5 jit_solution(10488585332465081028)
XLA Ops:
  9.1 1.1 copy.43
  17.3 1.4 subtract_convert_fusion
  21.5 4.9 %collective-permute-start.3 = (bf16[64,2,2,128]{3,0,1,2:T(8,128)(2,1)S(1)}, bf16[64,2,2,128]{3,0,1,2:T(8,128)(2,1)S(1)}, u32[]{:S(2)}, u32[]{:S(2)}) collective-permute-start(bf16[64,2,2,128]{3,0,1,2:T(8,128)(2,1)S(1)} %slice.85), channel_id=1, source_target_pairs={{0,2},{1,3}} | collective-permute-start | bytes 196616 | tf_op jit(solution)/shard_map/ppermute | solution.py:174
  26.4 3.0 %collective-permute-done.3 = bf16[64,2,2,128]{3,0,1,2:T(8,128)(2,1)S(1)} collective-permute-done((bf16[64,2,2,128]{3,0,1,2:T(8,128)(2,1)S(1)}, bf16[64,2,2,128]{3,0,1,2:T(8,128)(2,1)S(1)}, u32[]{:S(2)}, u32[]{:S(2)}) %collective-permute-start.3) | collective-permute-done | bytes 65568 | tf_op jit(solution)/shard_map/ppermute | solution.py:174
  29.4 1.3 collective-permute-start.4
  31.5 1.1 collective-permute-done.4
  32.6 1.3 collective-permute-start.5
  34.0 4.4 %collective-permute-start.7 = (bf16[256,2,2,128]{3,0,1,2:T(8,128)(2,1)S(1)}, bf16[256,2,2,128]{3,0,1,2:T(8,128)(2,1)S(1)}, u32[]{:S(2)}, u32[]{:S(2)}) collective-permute-start(bf16[256,2,2,128]{3,0,1,2:T(8,128)(2,1)S(1)} %fusion.50), channel_id=1, source_target_pairs={{0,2},{2,4},{4,6},{6,8},{8,10},{10,12},{12,14},{14,16},{16,18},{18... | collective-permute-start | bytes 786440 | tf_op jit(solution)/shard_map/ppermute | solution.py:169
  38.4 1.3 collective-permute-start.6
  39.8 1.8 collective-permute-done.6
  43.1 1.4 select_bitcast_fusion.3
  44.7 1.4 gather_fusion.4
  46.1 2.1 fusion.17
  48.2 2.1 copy-done.2
  50.4 1.1 fusion.18
  51.5 1.4 gather_fusion.2
  52.9 4.5 %divide_convert_fusion = bf16[256,2,4,128]{0,3,2,1:T(8,128)(2,1)} fusion(f32[2,576,256,4]{2,1,3,0:T(8,128)} %copy-done.2, f32[2,4,256]{2,1,0:T(4,128)S(1)} %get-tuple-element.139, pred[256,576]{0,1:T(8,128)(4,1)S(1)} %pad_add_fusion, f32[256,2,4]{0,2,1:T(4,128)S(1)} %bitcast_add_fusion, f32[256,2,4]{0,2,1:T(4,128)S(1)} %get-tuple-element.138, ...), kind=kOutput, calls=%fused_computation.50 | convolution fusion | flops 308674560 | bytes 5709824 | tf_op jit(solution)/shard_map/hgrk,khd->hgrd/dot_general | solution.py:62
  57.4 2.5 collective-permute-start.12
  59.9 2.5 collective-permute-start.13
  62.4 1.3 collective-permute-start.14
  63.7 1.4 select_bitcast_fusion.1
  65.9 1.3 bitcast_select_fusion.2
  67.4 9.2 %collective-permute-done.12 = bf16[256,1024]{0,1:T(8,128)(2,1)} collective-permute-done((bf16[256,1024]{0,1:T(8,128)(2,1)}, bf16[256,1024]{0,1:T(8,128)(2,1)}, u32[]{:S(2)}, u32[]{:S(2)}) %collective-permute-start.12) | collective-permute-done | bytes 524320 | tf_op jit(solution)/shard_map/ppermute | solution.py:228
  77.6 32.1 %all-gather.3.cloned.1.call-done = bf16[4096,512]{0,1:T(8,128)(2,1)} async-done(((bf16[256,512]{0,1:T(8,128)(2,1)}), bf16[4096,512]{0,1:T(8,128)(2,1)}) %all-gather.3.cloned.1.call-update) | async-done | bytes 4194320 | tf_op jit(solution)/shard_map/all_gather | solution.py:199
  110.9 21.4 %while.15 = (s32[]{:T(128)}, f32[2,4,256]{2,1,0:T(4,128)S(1)}, f32[2,4,256]{2,1,0:T(4,128)S(1)}, f32[2,4,256,128]{3,2,1,0:T(8,128)}, s32[]{:T(128)}, /*index=5*/...) while((s32[]{:T(128)}, f32[2,4,256]{2,1,0:T(4,128)S(1)}, ...), condition=%wide.region_5.8_spmd.clone, body=%wide.region_2.7_spmd.clone.sunk | while | flops 2203064576 | bytes 124405992 | solution.py:216
  111.3 4.2 %fusion.85 = (f32[2,4,256]{2,1,0:T(4,128)S(1)}, f32[2,2048,256,4]{2,1,3,0:T(8,128)S(1)}) fusion(pred[256,2048]{0,1:T(8,128)(4,1)S(1)} %broadcast_compare_fusion.3, bf16[256,2,4,128]{3,0,2,1:T(8,128)(2,1)S(1)} %get-tuple-element.244, bf16[4096,2,2,128]{0,3,2,1:T(8,128)(2,1)} %get-tuple-element.243, s32[]{:T(128)S(6)} %select_n.319), kind=kOutput, calls=%fused_computation.8.clone.1 | convolution fusion | flops 1086322688 | bytes 18882564 | tf_op jit(solution)/shard_map/while/body/rhgd,khd->hgrk/dot_general | solution.py:53
  115.6 4.1 %fusion.86 = f32[2,4,256]{2,1,0:T(4,128)S(1)} fusion(f32[2,2048,256,4]{2,1,3,0:T(8,128)S(1)} %get-tuple-element.209, f32[2,4,256]{2,1,0:T(4,128)S(1)} %max.13, pred[256,2048]{0,1:T(8,128)(4,1)S(1)} %broadcast_compare_fusion.3), kind=kLoop, calls=%fused_computation.10.clone.1 | loop fusion | flops 20969472 | bytes 17317888 | tf_op jit(solution)/shard_map/while/body/reduce_sum | solution.py:61
  119.6 2.4 copy-done
  122.0 10.2 %fusion.87 = f32[2,4,256,128]{3,2,1,0:T(8,128)} fusion(f32[2,2048,256,4]{2,1,3,0:T(8,128)} %copy-done, f32[2,4,256]{2,1,0:T(4,128)S(1)} %max.13, pred[256,2048]{0,1:T(8,128)(4,1)S(1)} %broadcast_compare_fusion.3, bf16[4096,2,2,128]{0,3,2,1:T(8,128)(2,1)} %get-tuple-element.243, s32[]{:T(128)S(6)} %select_n.319, s32[]{:T(128)S(6)} %add.314, ...), kind=kOutput, calls=%fused_computation.13.clone.1 | convolution fusion | flops 1095237632 | bytes 20463624 | tf_op jit(solution)/shard_map/while/body/hgrk,khd->hgrd/dot_general | solution.py:62
  132.2 1.6 copy.51
  133.9 1.5 collective-permute-start.9
  135.4 1.1 constant_dynamic-update-slice_fusion.4
  136.5 1.8 collective-permute-start.10
  139.4 51.8 %all-gather.5.cloned.1.call-done = bf16[2048,1024]{1,0:T(8,128)(2,1)} async-done(((bf16[2048,256]{1,0:T(8,128)(2,1)}), bf16[2048,1024]{1,0:T(8,128)(2,1)}) %all-gather.5.cloned.1.call-update) | async-done | bytes 4194320 | tf_op jit(solution)/shard_map/all_gather | solution.py:242
  191.2 2.2 fusion.40
  194.7 4.0 %convolution_add_fusion = f32[768,512]{1,0:T(8,128)} fusion(f32[768,512]{1,0:T(8,128)S(1)} %fusion.40, bf16[768,1024]{0,1:T(8,128)(2,1)S(1)} %constant_dynamic-update-slice_fusion, bf16[2048,1024]{1,0:T(8,128)(2,1)} %all-gather.5.cloned.1.call-done, s32[]{:T(128)S(6)} %select_n.188), kind=kOutput, calls=%fused_computation.40 | convolution fusion | flops 805699584 | bytes 5767172 | tf_op jit(solution)/shard_map/dot_general | solution.py:251
  198.7 2.4 fusion.43
  201.6 1.6 convolution_add_fusion.1
  205.4 1.9 add_convert_fusion.1
  207.3 1.5 collective-permute-start.16
  208.8 1.5 collective-permute-start.17
  210.3 1.5 collective-permute-start.18
  211.7 1.5 fusion.30
  213.7 6.4 %dynamic_update_slice.12 = bf16[256,2,4,256]{3,2,1,0:T(4,128)(2,1)S(1)} dynamic-update-slice(bf16[256,2,4,256]{3,2,1,0:T(4,128)(2,1)S(1)} %broadcast_in_dim.95, bf16[256,2,1,256]{3,2,1,0:T(2,128)(2,1)S(1)} %reshape.392, s32[]{:T(128)} %constant.135.clone.1, s32[]{:T(128)} %constant.135.clone.1, s32[]{:T(128)S(6)} %select_n.190, s32[]{:T(128)} %constant.135.clone.1) | dynamic-update-slice | bytes 524292 | tf_op jit(solution)/shard_map/dynamic_update_slice | solution.py:269
  220.4 6.4 %dynamic_update_slice.13 = bf16[256,2,4,256]{3,2,1,0:T(4,128)(2,1)S(1)} dynamic-update-slice(bf16[256,2,4,256]{3,2,1,0:T(4,128)(2,1)S(1)} %dynamic_update_slice.12, bf16[256,2,1,256]{3,2,1,0:T(2,128)(2,1)S(1)} %reshape.393, s32[]{:T(128)} %constant.135.clone.1, s32[]{:T(128)} %constant.135.clone.1, s32[]{:T(128)S(6)} %select_n.192, s32[]{:T(128)} %constant.135.clone.1) | dynamic-update-slice | bytes 524292 | tf_op jit(solution)/shard_map/dynamic_update_slice | solution.py:269
  227.0 6.4 %dynamic_update_slice.14 = bf16[256,2,4,256]{3,2,1,0:T(4,128)(2,1)S(1)} dynamic-update-slice(bf16[256,2,4,256]{3,2,1,0:T(4,128)(2,1)S(1)} %dynamic_update_slice.13, bf16[256,2,1,256]{3,2,1,0:T(2,128)(2,1)S(1)} %reshape.394, s32[]{:T(128)} %constant.135.clone.1, s32[]{:T(128)} %constant.135.clone.1, s32[]{:T(128)S(6)} %select_n.194, s32[]{:T(128)} %constant.135.clone.1) | dynamic-update-slice | bytes 524292 | tf_op jit(solution)/shard_map/dynamic_update_slice | solution.py:269
  233.6 6.4 %dynamic_update_slice.15 = bf16[256,2,4,256]{3,2,1,0:T(4,128)(2,1)S(1)} dynamic-update-slice(bf16[256,2,4,256]{3,2,1,0:T(4,128)(2,1)S(1)} %dynamic_update_slice.14, bf16[256,2,1,256]{3,2,1,0:T(2,128)(2,1)S(1)} %reshape.395, s32[]{:T(128)} %constant.135.clone.1, s32[]{:T(128)} %constant.135.clone.1, s32[]{:T(128)S(6)} %select_n.196, s32[]{:T(128)} %constant.135.clone.1) | dynamic-update-slice | bytes 524292 | tf_op jit(solution)/shard_map/dynamic_update_slice | solution.py:269
  240.1 1.6 reshape.331
  (127 shorter events, 23.8 us)
Async XLA Ops:
  6.5 4.6 %copy-start.13 = (s32[4]{0:T(128)S(1)}, s32[4]{0:T(128)}, u32[]{:S(2)}) copy-start(s32[4]{0:T(128)} %param.17) | copy-start | bytes 52
  6.5 103.3 %all-gather.3.cloned.1.call-start = ((), (), s32[]{:S(2)}) async-start(), calls=%async_computation | async-start | bytes 4456448 | tf_op jit(solution)/shard_map/all_gather | solution.py:199
  10.6 2.3 collective-permute-start
  12.9 0.6 copy-start.12
  12.9 1.8 copy-start.8
  12.9 7.1 %copy-start.11 = (s32[2]{0:T(128)}, s32[2]{0:T(128)S(1)}, u32[]{:S(2)}) copy-start(s32[2]{0:T(128)S(1)} %get-tuple-element.118) | copy-start | bytes 28
  13.4 2.5 %copy-start.4 = (bf16[256,2048]{1,0:T(8,128)(2,1)S(1)}, bf16[256,2048]{1,0:T(8,128)(2,1)}, u32[]{:S(2)}) copy-start(bf16[256,2048]{1,0:T(8,128)(2,1)} %param.13) | copy-start | bytes 3145732
  15.7 175.5 %all-gather.5.cloned.1.call-start = ((), (), s32[]{:S(2)}) async-start(), calls=%async_computation.1 | async-start | bytes 5242880 | tf_op jit(solution)/shard_map/all_gather | solution.py:242
  18.6 1.2 copy-start.5
  19.2 23.9 %collective-permute-start.1 = (bf16[256,4,4,128]{3,0,2,1:T(8,128)(2,1)S(1)}, bf16[256,4,4,128]{3,0,2,1:T(8,128)(2,1)}, u32[]{:S(2)}, u32[]{:S(2)}) collective-permute-start(bf16[256,4,4,128]{3,0,2,1:T(8,128)(2,1)S(1)} %bitcast.179), channel_id=1, source_target_pairs={{0,1},{1,0},{2,3},{3,2},{4,5},{5,4},{6,7},{7,6},{8,9},{9,8},{10,11... | collective-permute-start | bytes 3145736 | tf_op jit(solution)/shard_map/ppermute | solution.py:139
  19.9 43.8 %collective-permute-start.2 = (bf16[4,512,256]{2,1,0:T(8,128)(2,1)S(1)}, bf16[4,512,256]{2,1,0:T(8,128)(2,1)}, u32[]{:S(2)}, u32[]{:S(2)}) collective-permute-start(bf16[4,512,256]{2,1,0:T(8,128)(2,1)S(1)} %bitcast.186), channel_id=1, source_target_pairs={{0,1},{1,0},{2,3},{3,2},{4,5},{5,4},{6,7},{7,6},{8,9},{9,8},{10,11... | collective-permute-start | bytes 3145736 | tf_op jit(solution)/shard_map/ppermute | solution.py:139
  21.5 7.9 %collective-permute-start.3 = (bf16[64,2,2,128]{3,0,1,2:T(8,128)(2,1)S(1)}, bf16[64,2,2,128]{3,0,1,2:T(8,128)(2,1)S(1)}, u32[]{:S(2)}, u32[]{:S(2)}) collective-permute-start(bf16[64,2,2,128]{3,0,1,2:T(8,128)(2,1)S(1)} %slice.85), channel_id=1, source_target_pairs={{0,2},{1,3}} | collective-permute-start | bytes 196616 | tf_op jit(solution)/shard_map/ppermute | solution.py:174
  29.4 3.2 %collective-permute-start.4 = (bf16[64,2,2,128]{3,0,1,2:T(8,128)(2,1)S(1)}, bf16[64,2,2,128]{3,0,1,2:T(8,128)(2,1)S(1)}, u32[]{:S(2)}, u32[]{:S(2)}) collective-permute-start(bf16[64,2,2,128]{3,0,1,2:T(8,128)(2,1)S(1)} %broadcast_select_fusion), channel_id=1, source_target_pairs={{0,4},{2,6},{1,5},{3,7}} | collective-permute-start | bytes 196616 | tf_op jit(solution)/shard_map/ppermute | solution.py:174
  32.6 5.8 %collective-permute-start.5 = (bf16[64,2,2,128]{3,0,1,2:T(8,128)(2,1)S(1)}, bf16[64,2,2,128]{3,0,1,2:T(8,128)(2,1)S(1)}, u32[]{:S(2)}, u32[]{:S(2)}) collective-permute-start(bf16[64,2,2,128]{3,0,1,2:T(8,128)(2,1)S(1)} %broadcast_select_fusion.1), channel_id=1, source_target_pairs={{0,8},{2,10},{4,12},{6,14},{1,9},{3,11},{5,13},{7,15}} | collective-permute-start | bytes 196616 | tf_op jit(solution)/shard_map/ppermute | solution.py:174
  34.0 8.3 %collective-permute-start.7 = (bf16[256,2,2,128]{3,0,1,2:T(8,128)(2,1)S(1)}, bf16[256,2,2,128]{3,0,1,2:T(8,128)(2,1)S(1)}, u32[]{:S(2)}, u32[]{:S(2)}) collective-permute-start(bf16[256,2,2,128]{3,0,1,2:T(8,128)(2,1)S(1)} %fusion.50), channel_id=1, source_target_pairs={{0,2},{2,4},{4,6},{6,8},{8,10},{10,12},{12,14},{14,16},{16,18},{18... | collective-permute-start | bytes 786440 | tf_op jit(solution)/shard_map/ppermute | solution.py:169
  38.4 3.2 %collective-permute-start.6 = (bf16[64,2,2,128]{3,0,1,2:T(8,128)(2,1)S(1)}, bf16[64,2,2,128]{3,0,1,2:T(8,128)(2,1)S(1)}, u32[]{:S(2)}, u32[]{:S(2)}) collective-permute-start(bf16[64,2,2,128]{3,0,1,2:T(8,128)(2,1)S(1)} %broadcast_select_fusion.2), channel_id=1, source_target_pairs={{0,16},{2,18},{4,20},{6,22},{8,24},{10,26},{12,28},{14,30},{1,17},... | collective-permute-start | bytes 196616 | tf_op jit(solution)/shard_map/ppermute | solution.py:174
  44.5 1.6 copy-start.10
  48.2 2.2 copy-start.2
  57.4 19.2 %collective-permute-start.12 = (bf16[256,1024]{0,1:T(8,128)(2,1)}, bf16[256,1024]{0,1:T(8,128)(2,1)}, u32[]{:S(2)}, u32[]{:S(2)}) collective-permute-start(bf16[256,1024]{0,1:T(8,128)(2,1)} %bitcast.42), channel_id=1, source_target_pairs={{0,2},{2,4},{4,6},{6,0},{1,3},{3,5},{5,7},{7,1},{8,10},{10,12},{12... | collective-permute-start | bytes 1572872 | tf_op jit(solution)/shard_map/ppermute | solution.py:228
  59.9 75.6 %collective-permute-start.13 = (bf16[256,1024]{0,1:T(8,128)(2,1)}, bf16[256,1024]{0,1:T(8,128)(2,1)}, u32[]{:S(2)}, u32[]{:S(2)}) collective-permute-start(bf16[256,1024]{0,1:T(8,128)(2,1)} %bitcast.42), channel_id=1, source_target_pairs={{0,4},{2,6},{4,0},{6,2},{1,5},{3,7},{5,1},{7,3},{8,12},{10,14},{12... | collective-permute-start | bytes 1572872 | tf_op jit(solution)/shard_map/ppermute | solution.py:228
  62.4 75.9 %collective-permute-start.14 = (bf16[256,1024]{0,1:T(8,128)(2,1)}, bf16[256,1024]{0,1:T(8,128)(2,1)}, u32[]{:S(2)}, u32[]{:S(2)}) collective-permute-start(bf16[256,1024]{0,1:T(8,128)(2,1)} %bitcast.42), channel_id=1, source_target_pairs={{0,6},{2,0},{4,2},{6,4},{1,7},{3,1},{5,3},{7,5},{8,14},{10,8},{12,... | collective-permute-start | bytes 1572872 | tf_op jit(solution)/shard_map/ppermute | solution.py:228
  65.9 1.4 copy-start.3
  65.9 1.4 copy-start.9
  115.6 6.4 %copy-start = (f32[2,2048,256,4]{2,1,3,0:T(8,128)}, f32[2,2048,256,4]{2,1,3,0:T(8,128)S(1)}, u32[]{:S(2)}) copy-start(f32[2,2048,256,4]{2,1,3,0:T(8,128)S(1)} %get-tuple-element.209) | copy-start | bytes 50331652 | tf_op jit(solution)/shard_map/while
  133.9 59.5 %collective-permute-start.9 = (bf16[256,1024]{0,1:T(8,128)(2,1)S(1)}, bf16[256,1024]{0,1:T(8,128)(2,1)S(1)}, u32[]{:S(2)}, u32[]{:S(2)}) collective-permute-start(bf16[256,1024]{0,1:T(8,128)(2,1)S(1)} %bitcast.171), channel_id=1, source_target_pairs={{0,2},{2,4},{4,6},{6,0},{1,3},{3,5},{5,7},{7,1},{8,10},{10,12},{12... | collective-permute-start | bytes 1572872 | tf_op jit(solution)/shard_map/ppermute | solution.py:228
  136.5 57.0 %collective-permute-start.10 = (bf16[256,1024]{0,1:T(8,128)(2,1)S(1)}, bf16[256,1024]{0,1:T(8,128)(2,1)S(1)}, u32[]{:S(2)}, u32[]{:S(2)}) collective-permute-start(bf16[256,1024]{0,1:T(8,128)(2,1)S(1)} %bitcast.172), channel_id=1, source_target_pairs={{0,4},{2,6},{4,0},{6,2},{1,5},{3,7},{5,1},{7,3},{8,12},{10,14},{12... | collective-permute-start | bytes 1572872 | tf_op jit(solution)/shard_map/ppermute | solution.py:228
  139.4 54.2 %collective-permute-start.11 = (bf16[256,1024]{0,1:T(8,128)(2,1)S(1)}, bf16[256,1024]{0,1:T(8,128)(2,1)}, u32[]{:S(2)}, u32[]{:S(2)}) collective-permute-start(bf16[256,1024]{0,1:T(8,128)(2,1)S(1)} %bitcast.173), channel_id=1, source_target_pairs={{0,6},{2,0},{4,2},{6,4},{1,7},{3,1},{5,3},{7,5},{8,14},{10,8},{12,... | collective-permute-start | bytes 1572872 | tf_op jit(solution)/shard_map/ppermute | solution.py:228
  194.6 4.0 %copy-start.6 = (bf16[768,1024]{0,1:T(8,128)(2,1)}, bf16[768,1024]{0,1:T(8,128)(2,1)S(1)}, u32[]{:S(2)}) copy-start(bf16[768,1024]{0,1:T(8,128)(2,1)S(1)} %constant_dynamic-update-slice_fusion) | copy-start | bytes 4718596
  198.7 6.7 %collective-permute-start.15 = (f32[768,512]{1,0:T(8,128)}, f32[768,512]{1,0:T(8,128)}, u32[]{:S(2)}, u32[]{:S(2)}) collective-permute-start(f32[768,512]{1,0:T(8,128)} %convolution_add_fusion), channel_id=1, source_target_pairs={{0,1},{1,0},{2,3},{3,2},{4,5},{5,4},{6,7},{7,6},{8,9},{9,8},{10,11... | collective-permute-start | bytes 4718600 | tf_op jit(solution)/shard_map/ppermute | solution.py:256
  198.7 2.5 %copy-start.1 = (bf16[2048,1024]{1,0:T(8,128)(2,1)S(1)}, bf16[2048,1024]{1,0:T(8,128)(2,1)}, u32[]{:S(2)}) copy-start(bf16[2048,1024]{1,0:T(8,128)(2,1)} %all-gather.5.cloned.1.call-done) | copy-start | bytes 12582916
  201.6 2.7 %copy-start.7 = (bf16[768,1024]{0,1:T(8,128)(2,1)S(1)}, bf16[768,1024]{0,1:T(8,128)(2,1)}, u32[]{:S(2)}) copy-start(bf16[768,1024]{0,1:T(8,128)(2,1)} %copy-done.6) | copy-start | bytes 4718596
  203.3 8.5 %collective-permute-start.8 = (f32[256,512]{1,0:T(8,128)S(1)}, f32[256,512]{1,0:T(8,128)S(1)}, u32[]{:S(2)}, u32[]{:S(2)}) collective-permute-start(f32[256,512]{1,0:T(8,128)S(1)} %convolution_add_fusion.1), channel_id=1, source_target_pairs={{0,1},{1,0},{2,3},{3,2},{4,5},{5,4},{6,7},{7,6},{8,9},{9,8},{10,11... | collective-permute-start | bytes 1572872 | tf_op jit(solution)/shard_map/ppermute | solution.py:256
  207.3 12.9 %collective-permute-start.16 = (bf16[256,512]{1,0:T(8,128)(2,1)S(1)}, bf16[256,512]{1,0:T(8,128)(2,1)S(1)}, u32[]{:S(2)}, u32[]{:S(2)}) collective-permute-start(bf16[256,512]{1,0:T(8,128)(2,1)S(1)} %get-tuple-element.135), channel_id=1, source_target_pairs={{0,2},{2,4},{4,6},{6,0},{1,3},{3,5},{5,7},{7,1},{8,10},{10,12},{12... | collective-permute-start | bytes 786440 | tf_op jit(solution)/shard_map/ppermute | solution.py:262
  208.8 18.0 %collective-permute-start.17 = (bf16[256,512]{1,0:T(8,128)(2,1)S(1)}, bf16[256,512]{1,0:T(8,128)(2,1)S(1)}, u32[]{:S(2)}, u32[]{:S(2)}) collective-permute-start(bf16[256,512]{1,0:T(8,128)(2,1)S(1)} %get-tuple-element.134), channel_id=1, source_target_pairs={{0,4},{2,6},{4,0},{6,2},{1,5},{3,7},{5,1},{7,3},{8,12},{10,14},{12... | collective-permute-start | bytes 786440 | tf_op jit(solution)/shard_map/ppermute | solution.py:262
  210.3 23.2 %collective-permute-start.18 = (bf16[256,512]{1,0:T(8,128)(2,1)S(1)}, bf16[256,512]{1,0:T(8,128)(2,1)S(1)}, u32[]{:S(2)}, u32[]{:S(2)}) collective-permute-start(bf16[256,512]{1,0:T(8,128)(2,1)S(1)} %get-tuple-element.133), channel_id=1, source_target_pairs={{0,6},{2,0},{4,2},{6,4},{1,7},{3,1},{5,3},{7,5},{8,14},{10,8},{12,... | collective-permute-start | bytes 786440 | tf_op jit(solution)/shard_map/ppermute | solution.py:262
Sparse Core Ops, SparseCore 0:
  15.8 93.9 all-gather.2
  111.4 79.8 all-gather.4

commit v14 on v12

--- a/solution.py
+++ b/solution.py
@@ -151,7 +151,11 @@
     run_per = (kv_total - ret_count) // head_count
     me = lax.axis_index("head")
     is_ret = jnp.any(jnp.arange(kv_total, dtype=jnp.int32)[:, None] == retrieval[None, :], axis=1)
-    order = jnp.argsort(is_ret.astype(jnp.int32), stable=True)
+    heads = jnp.arange(kv_total, dtype=jnp.int32)
+    flag = is_ret.astype(jnp.int32)
+    before = (flag[None, :] < flag[:, None]) | ((flag[None, :] == flag[:, None]) & (heads[None, :] < heads[:, None]))
+    rank = jnp.sum(before.astype(jnp.int32), axis=1)
+    order = jnp.sum(jnp.where(rank[None, :] == heads[:, None], heads[None, :], 0), axis=1)
     run_ids = lax.dynamic_slice_in_dim(order, me * run_per, run_per)
     ret_ids = lax.dynamic_slice_in_dim(order, kv_total - ret_count + me * ret_per, ret_per)
 

time: 234 us -> 235 us (level)
  transfers between devices with their start and end apart: 21 -> 21, of which waited for: 10 -> 11; matrix products, arithmetic and copies ran while one was open for 26% -> 26% of each run, Pallas kernels for 0% -> 0%
where the time goes in v14:
time: 235 us; the launch traced here: 234 us
  waiting for transfers between devices  109 us (46%)
  matrix products  34.7 us (15%)
  starting transfers between devices  28.9 us (12%)
  local copies, waits for them, and re-layouts  25.5 us (11%)
  other arithmetic  20.9 us (9%)
  between operations  14.8 us (6%)
    all_gather x1, waiting for transfers between devices, project_assigned(): w_line = lax.all_gather(w_mine, 'cz', axis=1, tiled=True)  51.5 us
    all_gather x1, waiting for transfers between devices, duo_attend(): lax.all_gather(ret_kv.reshape(rows, ret_per * 2 * HEAD_SIZE), CTX, axis=0...  31.8 us
    dot_general x2, matrix products, update(): jnp.einsum('hgrk,khd->hgrd', weights.astype(jnp.bfloat16), value_block, p...  14.8 us
    ppermute x6, waiting for transfers between devices, plane_pieces(): lax.ppermute(block, 'cb', [(i, (i + shift) % plane) for i in range(plane)])  10.2 us
    ppermute x6, starting transfers between devices, plane_pieces(): lax.ppermute(block, 'cb', [(i, (i + shift) % plane) for i in range(plane)])  9.63 us
    ppermute x4, starting transfers between devices, duo_attend(): got = lax.ppermute(sink_kv, CTX, pairs)  8.4 us
    ppermute x3, waiting for transfers between devices, project_assigned(): lax.ppermute(far[-shift % plane - 1], 'cb', [(i, (i + shift) % plane) for...  8.39 us
    dot_general x4, matrix products, product(): jnp.dot(run_part, w_half[ret_rows:], preferred_element_type=jnp.float32)  7.64 us
  transfers between devices with their start and end apart: 21, of which 11 were waited for; matrix products, arithmetic and copies ran while one was open for 26% of the time, Pallas kernels for 0%

profile of v14, /device:TPU:0, one launch (start us, length us, event | category | flops | bytes accessed | tf_op | source)
XLA Modules:
  0.0 233.9 jit_solution(10261083789118509843)
XLA Ops:
  9.1 1.1 copy.34
  16.9 1.4 subtract_convert_fusion
  21.5 4.5 %collective-permute-start.3 = (bf16[64,2,2,128]{3,0,1,2:T(8,128)(2,1)S(1)}, bf16[64,2,2,128]{3,0,1,2:T(8,128)(2,1)S(1)}, u32[]{:S(2)}, u32[]{:S(2)}) collective-permute-start(bf16[64,2,2,128]{3,0,1,2:T(8,128)(2,1)S(1)} %slice.87), channel_id=1, source_target_pairs={{0,2},{1,3}} | collective-permute-start | bytes 196616 | tf_op jit(solution)/shard_map/ppermute | solution.py:178
  26.1 3.2 %collective-permute-done.3 = bf16[64,2,2,128]{3,0,1,2:T(8,128)(2,1)S(1)} collective-permute-done((bf16[64,2,2,128]{3,0,1,2:T(8,128)(2,1)S(1)}, bf16[64,2,2,128]{3,0,1,2:T(8,128)(2,1)S(1)}, u32[]{:S(2)}, u32[]{:S(2)}) %collective-permute-start.3) | collective-permute-done | bytes 65568 | tf_op jit(solution)/shard_map/ppermute | solution.py:178
  29.3 1.3 collective-permute-start.4
  31.3 1.1 collective-permute-done.4
  32.5 1.3 collective-permute-start.5
  33.8 4.4 %collective-permute-start.7 = (bf16[256,2,2,128]{3,0,1,2:T(8,128)(2,1)S(1)}, bf16[256,2,2,128]{3,0,1,2:T(8,128)(2,1)S(1)}, u32[]{:S(2)}, u32[]{:S(2)}) collective-permute-start(bf16[256,2,2,128]{3,0,1,2:T(8,128)(2,1)S(1)} %fusion.52), channel_id=1, source_target_pairs={{0,2},{2,4},{4,6},{6,8},{8,10},{10,12},{12,14},{14,16},{16,18},{18... | collective-permute-start | bytes 786440 | tf_op jit(solution)/shard_map/ppermute | solution.py:173
  38.3 1.3 collective-permute-start.6
  39.6 1.8 collective-permute-done.6
  42.9 1.4 select_bitcast_fusion.3
  44.5 1.4 gather_fusion.5
  45.9 2.1 fusion.17
  48.1 2.1 copy-done.2
  50.2 1.1 fusion.18
  51.3 1.5 gather_fusion.3
  52.8 4.5 %divide_convert_fusion = bf16[256,2,4,128]{0,3,2,1:T(8,128)(2,1)} fusion(f32[2,576,256,4]{2,1,3,0:T(8,128)} %copy-done.2, f32[2,4,256]{2,1,0:T(4,128)S(1)} %get-tuple-element.137, pred[256,576]{0,1:T(8,128)(4,1)S(1)} %pad_add_fusion, f32[256,2,4]{0,2,1:T(4,128)S(1)} %bitcast_add_fusion, f32[256,2,4]{0,2,1:T(4,128)S(1)} %get-tuple-element.136, ...), kind=kOutput, calls=%fused_computation.54 | convolution fusion | flops 308674560 | bytes 5709824 | tf_op jit(solution)/shard_map/hgrk,khd->hgrd/dot_general | solution.py:62
  57.3 2.5 %collective-permute-start.12 = (bf16[256,1024]{0,1:T(8,128)(2,1)}, bf16[256,1024]{0,1:T(8,128)(2,1)}, u32[]{:S(2)}, u32[]{:S(2)}) collective-permute-start(bf16[256,1024]{0,1:T(8,128)(2,1)} %bitcast.42), channel_id=1, source_target_pairs={{0,2},{2,4},{4,6},{6,0},{1,3},{3,5},{5,7},{7,1},{8,10},{10,12},{12... | collective-permute-start | bytes 1572872 | tf_op jit(solution)/shard_map/ppermute | solution.py:232
  59.8 2.6 %collective-permute-start.13 = (bf16[256,1024]{0,1:T(8,128)(2,1)}, bf16[256,1024]{0,1:T(8,128)(2,1)}, u32[]{:S(2)}, u32[]{:S(2)}) collective-permute-start(bf16[256,1024]{0,1:T(8,128)(2,1)} %bitcast.42), channel_id=1, source_target_pairs={{0,4},{2,6},{4,0},{6,2},{1,5},{3,7},{5,1},{7,3},{8,12},{10,14},{12... | collective-permute-start | bytes 1572872 | tf_op jit(solution)/shard_map/ppermute | solution.py:232
  62.4 1.1 collective-permute-start.14
  63.5 1.4 select_bitcast_fusion.1
  65.8 1.3 bitcast_select_fusion.2
  67.2 10.2 %collective-permute-done.12 = bf16[256,1024]{0,1:T(8,128)(2,1)} collective-permute-done((bf16[256,1024]{0,1:T(8,128)(2,1)}, bf16[256,1024]{0,1:T(8,128)(2,1)}, u32[]{:S(2)}, u32[]{:S(2)}) %collective-permute-start.12) | collective-permute-done | bytes 524320 | tf_op jit(solution)/shard_map/ppermute | solution.py:232
  78.5 31.8 %all-gather.3.cloned.1.call-done = bf16[4096,512]{0,1:T(8,128)(2,1)} async-done(((bf16[256,512]{0,1:T(8,128)(2,1)}), bf16[4096,512]{0,1:T(8,128)(2,1)}) %all-gather.3.cloned.1.call-update) | async-done | bytes 4194320 | tf_op jit(solution)/shard_map/all_gather | solution.py:203
  110.3 1.1 broadcast.346
  111.4 21.5 %while.15 = (s32[]{:T(128)}, f32[2,4,256]{2,1,0:T(4,128)S(1)}, f32[2,4,256]{2,1,0:T(4,128)S(1)}, f32[2,4,256,128]{3,2,1,0:T(8,128)}, s32[]{:T(128)}, /*index=5*/...) while((s32[]{:T(128)}, f32[2,4,256]{2,1,0:T(4,128)S(1)}, ...), condition=%wide.region_6.9_spmd.clone, body=%wide.region_3.8_spmd.clone.sunk | while | flops 2203064576 | bytes 124405992 | solution.py:220
  111.9 4.2 %fusion.92 = (f32[2,4,256]{2,1,0:T(4,128)S(1)}, f32[2,2048,256,4]{2,1,3,0:T(8,128)S(1)}) fusion(pred[256,2048]{0,1:T(8,128)(4,1)S(1)} %broadcast_compare_fusion.3, bf16[256,2,4,128]{3,0,2,1:T(8,128)(2,1)S(1)} %get-tuple-element.242, bf16[4096,2,2,128]{0,3,2,1:T(8,128)(2,1)} %get-tuple-element.241, s32[]{:T(128)S(6)} %select_n.348), kind=kOutput, calls=%fused_computation.9.clone.1 | convolution fusion | flops 1086322688 | bytes 18882564 | tf_op jit(solution)/shard_map/while/body/rhgd,khd->hgrk/dot_general | solution.py:53
  116.2 4.1 %fusion.93 = f32[2,4,256]{2,1,0:T(4,128)S(1)} fusion(f32[2,2048,256,4]{2,1,3,0:T(8,128)S(1)} %get-tuple-element.207, f32[2,4,256]{2,1,0:T(4,128)S(1)} %max.13, pred[256,2048]{0,1:T(8,128)(4,1)S(1)} %broadcast_compare_fusion.3), kind=kLoop, calls=%fused_computation.11.clone.1 | loop fusion | flops 20969472 | bytes 17317888 | tf_op jit(solution)/shard_map/while/body/reduce_sum | solution.py:61
  120.2 2.4 %copy-done = f32[2,2048,256,4]{2,1,3,0:T(8,128)} copy-done((f32[2,2048,256,4]{2,1,3,0:T(8,128)}, f32[2,2048,256,4]{2,1,3,0:T(8,128)S(1)}, u32[]{:S(2)}) %copy-start) | copy-done | bytes 16777240 | tf_op jit(solution)/shard_map/while
  122.6 10.3 %fusion.94 = f32[2,4,256,128]{3,2,1,0:T(8,128)} fusion(f32[2,2048,256,4]{2,1,3,0:T(8,128)} %copy-done, f32[2,4,256]{2,1,0:T(4,128)S(1)} %max.13, pred[256,2048]{0,1:T(8,128)(4,1)S(1)} %broadcast_compare_fusion.3, bf16[4096,2,2,128]{0,3,2,1:T(8,128)(2,1)} %get-tuple-element.241, s32[]{:T(128)S(6)} %select_n.348, s32[]{:T(128)S(6)} %add.334, ...), kind=kOutput, calls=%fused_computation.14.clone.1 | convolution fusion | flops 1095237632 | bytes 20463624 | tf_op jit(solution)/shard_map/while/body/hgrk,khd->hgrd/dot_general | solution.py:62
  132.9 1.6 copy.42
  134.6 1.4 collective-permute-start.9
  136.0 1.1 constant_dynamic-update-slice_fusion.4
  137.1 2.0 collective-permute-start.10
  140.2 51.5 %all-gather.5.cloned.1.call-done = bf16[2048,1024]{1,0:T(8,128)(2,1)} async-done(((bf16[2048,256]{1,0:T(8,128)(2,1)}), bf16[2048,1024]{1,0:T(8,128)(2,1)}) %all-gather.5.cloned.1.call-update) | async-done | bytes 4194320 | tf_op jit(solution)/shard_map/all_gather | solution.py:246
  191.7 2.2 fusion.42
  195.1 4.0 %convolution_add_fusion = f32[768,512]{1,0:T(8,128)} fusion(f32[768,512]{1,0:T(8,128)S(1)} %fusion.42, bf16[768,1024]{0,1:T(8,128)(2,1)S(1)} %constant_dynamic-update-slice_fusion, bf16[2048,1024]{1,0:T(8,128)(2,1)} %all-gather.5.cloned.1.call-done, s32[]{:T(128)S(6)} %select_n.202), kind=kOutput, calls=%fused_computation.42 | convolution fusion | flops 805699584 | bytes 5767172 | tf_op jit(solution)/shard_map/dot_general | solution.py:255
  199.2 2.4 %fusion.45 = f32[768,512]{1,0:T(8,128)S(1)} fusion(bf16[768,1024]{0,1:T(8,128)(2,1)S(1)} %constant_dynamic-update-slice_fusion.3, bf16[2048,1024]{1,0:T(8,128)(2,1)} %all-gather.5.cloned.1.call-done, s32[]{:T(128)S(6)} %add.241, s32[]{:T(128)S(6)} %select_n.191), kind=kOutput, calls=%fused_computation.71 | convolution fusion | flops 805306368 | bytes 4194312 | tf_op jit(solution)/shard_map/dot_general | solution.py:255
  202.2 1.5 convolution_add_fusion.1
  205.3 1.9 add_convert_fusion.1
  207.2 1.5 collective-permute-start.16
  208.7 1.5 collective-permute-start.17
  210.2 1.5 collective-permute-start.18
  212.2 1.5 fusion.31
  213.7 3.7 %collective-permute-done.16 = bf16[256,512]{1,0:T(8,128)(2,1)S(1)} collective-permute-done((bf16[256,512]{1,0:T(8,128)(2,1)S(1)}, bf16[256,512]{1,0:T(8,128)(2,1)S(1)}, u32[]{:S(2)}, u32[]{:S(2)}) %collective-permute-start.16) | collective-permute-done | bytes 262176 | tf_op jit(solution)/shard_map/ppermute | solution.py:266
  217.4 4.6 %collective-permute-done.17 = bf16[256,512]{1,0:T(8,128)(2,1)S(1)} collective-permute-done((bf16[256,512]{1,0:T(8,128)(2,1)S(1)}, bf16[256,512]{1,0:T(8,128)(2,1)S(1)}, u32[]{:S(2)}, u32[]{:S(2)}) %collective-permute-start.17) | collective-permute-done | bytes 262176 | tf_op jit(solution)/shard_map/ppermute | solution.py:266
  224.1 1.4 copy.44
  225.5 1.6 reshape.378
  (126 shorter events, 23.9 us)
Async XLA Ops:
  6.5 4.6 %copy-start.13 = (s32[4]{0:T(128)S(1)}, s32[4]{0:T(128)}, u32[]{:S(2)}) copy-start(s32[4]{0:T(128)} %param.17) | copy-start | bytes 52
  6.5 103.8 %all-gather.3.cloned.1.call-start = ((), (), s32[]{:S(2)}) async-start(), calls=%async_computation | async-start | bytes 4456448 | tf_op jit(solution)/shard_map/all_gather | solution.py:203
  10.6 2.1 collective-permute-start
  12.2 0.8 copy-start.11
  12.2 2.1 copy-start.8
  12.2 7.6 %copy-start.12 = (s32[2]{0:T(128)}, s32[2]{0:T(128)S(1)}, u32[]{:S(2)}) copy-start(s32[2]{0:T(128)S(1)} %get-tuple-element.141) | copy-start | bytes 28
  13.0 2.5 %copy-start.4 = (bf16[256,2048]{1,0:T(8,128)(2,1)S(1)}, bf16[256,2048]{1,0:T(8,128)(2,1)}, u32[]{:S(2)}) copy-start(bf16[256,2048]{1,0:T(8,128)(2,1)} %param.13) | copy-start | bytes 3145732
  15.3 176.4 %all-gather.5.cloned.1.call-start = ((), (), s32[]{:S(2)}) async-start(), calls=%async_computation.1 | async-start | bytes 5242880 | tf_op jit(solution)/shard_map/all_gather | solution.py:246
  18.3 1.2 copy-start.5
  18.9 24.1 %collective-permute-start.1 = (bf16[256,4,4,128]{3,0,2,1:T(8,128)(2,1)S(1)}, bf16[256,4,4,128]{3,0,2,1:T(8,128)(2,1)}, u32[]{:S(2)}, u32[]{:S(2)}) collective-permute-start(bf16[256,4,4,128]{3,0,2,1:T(8,128)(2,1)S(1)} %bitcast.188), channel_id=1, source_target_pairs={{0,1},{1,0},{2,3},{3,2},{4,5},{5,4},{6,7},{7,6},{8,9},{9,8},{10,11... | collective-permute-start | bytes 3145736 | tf_op jit(solution)/shard_map/ppermute | solution.py:139
  19.5 44.1 %collective-permute-start.2 = (bf16[4,512,256]{2,1,0:T(8,128)(2,1)S(1)}, bf16[4,512,256]{2,1,0:T(8,128)(2,1)}, u32[]{:S(2)}, u32[]{:S(2)}) collective-permute-start(bf16[4,512,256]{2,1,0:T(8,128)(2,1)S(1)} %bitcast.195), channel_id=1, source_target_pairs={{0,1},{1,0},{2,3},{3,2},{4,5},{5,4},{6,7},{7,6},{8,9},{9,8},{10,11... | collective-permute-start | bytes 3145736 | tf_op jit(solution)/shard_map/ppermute | solution.py:139
  21.5 7.7 %collective-permute-start.3 = (bf16[64,2,2,128]{3,0,1,2:T(8,128)(2,1)S(1)}, bf16[64,2,2,128]{3,0,1,2:T(8,128)(2,1)S(1)}, u32[]{:S(2)}, u32[]{:S(2)}) collective-permute-start(bf16[64,2,2,128]{3,0,1,2:T(8,128)(2,1)S(1)} %slice.87), channel_id=1, source_target_pairs={{0,2},{1,3}} | collective-permute-start | bytes 196616 | tf_op jit(solution)/shard_map/ppermute | solution.py:178
  29.3 3.2 %collective-permute-start.4 = (bf16[64,2,2,128]{3,0,1,2:T(8,128)(2,1)S(1)}, bf16[64,2,2,128]{3,0,1,2:T(8,128)(2,1)S(1)}, u32[]{:S(2)}, u32[]{:S(2)}) collective-permute-start(bf16[64,2,2,128]{3,0,1,2:T(8,128)(2,1)S(1)} %broadcast_select_fusion.1), channel_id=1, source_target_pairs={{0,4},{2,6},{1,5},{3,7}} | collective-permute-start | bytes 196616 | tf_op jit(solution)/shard_map/ppermute | solution.py:178
  32.5 5.8 %collective-permute-start.5 = (bf16[64,2,2,128]{3,0,1,2:T(8,128)(2,1)S(1)}, bf16[64,2,2,128]{3,0,1,2:T(8,128)(2,1)S(1)}, u32[]{:S(2)}, u32[]{:S(2)}) collective-permute-start(bf16[64,2,2,128]{3,0,1,2:T(8,128)(2,1)S(1)} %broadcast_select_fusion.2), channel_id=1, source_target_pairs={{0,8},{2,10},{4,12},{6,14},{1,9},{3,11},{5,13},{7,15}} | collective-permute-start | bytes 196616 | tf_op jit(solution)/shard_map/ppermute | solution.py:178
  33.8 8.3 %collective-permute-start.7 = (bf16[256,2,2,128]{3,0,1,2:T(8,128)(2,1)S(1)}, bf16[256,2,2,128]{3,0,1,2:T(8,128)(2,1)S(1)}, u32[]{:S(2)}, u32[]{:S(2)}) collective-permute-start(bf16[256,2,2,128]{3,0,1,2:T(8,128)(2,1)S(1)} %fusion.52), channel_id=1, source_target_pairs={{0,2},{2,4},{4,6},{6,8},{8,10},{10,12},{12,14},{14,16},{16,18},{18... | collective-permute-start | bytes 786440 | tf_op jit(solution)/shard_map/ppermute | solution.py:173
  38.3 3.2 %collective-permute-start.6 = (bf16[64,2,2,128]{3,0,1,2:T(8,128)(2,1)S(1)}, bf16[64,2,2,128]{3,0,1,2:T(8,128)(2,1)S(1)}, u32[]{:S(2)}, u32[]{:S(2)}) collective-permute-start(bf16[64,2,2,128]{3,0,1,2:T(8,128)(2,1)S(1)} %broadcast_select_fusion.3), channel_id=1, source_target_pairs={{0,16},{2,18},{4,20},{6,22},{8,24},{10,26},{12,28},{14,30},{1,17},... | collective-permute-start | bytes 196616 | tf_op jit(solution)/shard_map/ppermute | solution.py:178
  44.3 1.6 copy-start.10
  48.0 2.1 copy-start.2
  57.3 20.1 %collective-permute-start.12 = (bf16[256,1024]{0,1:T(8,128)(2,1)}, bf16[256,1024]{0,1:T(8,128)(2,1)}, u32[]{:S(2)}, u32[]{:S(2)}) collective-permute-start(bf16[256,1024]{0,1:T(8,128)(2,1)} %bitcast.42), channel_id=1, source_target_pairs={{0,2},{2,4},{4,6},{6,0},{1,3},{3,5},{5,7},{7,1},{8,10},{10,12},{12... | collective-permute-start | bytes 1572872 | tf_op jit(solution)/shard_map/ppermute | solution.py:232
  59.8 76.2 %collective-permute-start.13 = (bf16[256,1024]{0,1:T(8,128)(2,1)}, bf16[256,1024]{0,1:T(8,128)(2,1)}, u32[]{:S(2)}, u32[]{:S(2)}) collective-permute-start(bf16[256,1024]{0,1:T(8,128)(2,1)} %bitcast.42), channel_id=1, source_target_pairs={{0,4},{2,6},{4,0},{6,2},{1,5},{3,7},{5,1},{7,3},{8,12},{10,14},{12... | collective-permute-start | bytes 1572872 | tf_op jit(solution)/shard_map/ppermute | solution.py:232
  62.4 76.6 %collective-permute-start.14 = (bf16[256,1024]{0,1:T(8,128)(2,1)}, bf16[256,1024]{0,1:T(8,128)(2,1)}, u32[]{:S(2)}, u32[]{:S(2)}) collective-permute-start(bf16[256,1024]{0,1:T(8,128)(2,1)} %bitcast.42), channel_id=1, source_target_pairs={{0,6},{2,0},{4,2},{6,4},{1,7},{3,1},{5,3},{7,5},{8,14},{10,8},{12,... | collective-permute-start | bytes 1572872 | tf_op jit(solution)/shard_map/ppermute | solution.py:232
  65.7 1.4 copy-start.3
  65.7 1.4 copy-start.9
  116.1 6.5 %copy-start = (f32[2,2048,256,4]{2,1,3,0:T(8,128)}, f32[2,2048,256,4]{2,1,3,0:T(8,128)S(1)}, u32[]{:S(2)}) copy-start(f32[2,2048,256,4]{2,1,3,0:T(8,128)S(1)} %get-tuple-element.207) | copy-start | bytes 50331652 | tf_op jit(solution)/shard_map/while
  134.6 59.3 %collective-permute-start.9 = (bf16[256,1024]{0,1:T(8,128)(2,1)S(1)}, bf16[256,1024]{0,1:T(8,128)(2,1)S(1)}, u32[]{:S(2)}, u32[]{:S(2)}) collective-permute-start(bf16[256,1024]{0,1:T(8,128)(2,1)S(1)} %bitcast.180), channel_id=1, source_target_pairs={{0,2},{2,4},{4,6},{6,0},{1,3},{3,5},{5,7},{7,1},{8,10},{10,12},{12... | collective-permute-start | bytes 1572872 | tf_op jit(solution)/shard_map/ppermute | solution.py:232
  137.1 56.9 %collective-permute-start.10 = (bf16[256,1024]{0,1:T(8,128)(2,1)S(1)}, bf16[256,1024]{0,1:T(8,128)(2,1)S(1)}, u32[]{:S(2)}, u32[]{:S(2)}) collective-permute-start(bf16[256,1024]{0,1:T(8,128)(2,1)S(1)} %bitcast.181), channel_id=1, source_target_pairs={{0,4},{2,6},{4,0},{6,2},{1,5},{3,7},{5,1},{7,3},{8,12},{10,14},{12... | collective-permute-start | bytes 1572872 | tf_op jit(solution)/shard_map/ppermute | solution.py:232
  140.1 54.0 %collective-permute-start.11 = (bf16[256,1024]{0,1:T(8,128)(2,1)S(1)}, bf16[256,1024]{0,1:T(8,128)(2,1)}, u32[]{:S(2)}, u32[]{:S(2)}) collective-permute-start(bf16[256,1024]{0,1:T(8,128)(2,1)S(1)} %bitcast.182), channel_id=1, source_target_pairs={{0,6},{2,0},{4,2},{6,4},{1,7},{3,1},{5,3},{7,5},{8,14},{10,8},{12,... | collective-permute-start | bytes 1572872 | tf_op jit(solution)/shard_map/ppermute | solution.py:232
  195.1 4.0 %copy-start.6 = (bf16[768,1024]{0,1:T(8,128)(2,1)}, bf16[768,1024]{0,1:T(8,128)(2,1)S(1)}, u32[]{:S(2)}) copy-start(bf16[768,1024]{0,1:T(8,128)(2,1)S(1)} %constant_dynamic-update-slice_fusion) | copy-start | bytes 4718596
  199.1 6.2 %collective-permute-start.15 = (f32[768,512]{1,0:T(8,128)}, f32[768,512]{1,0:T(8,128)}, u32[]{:S(2)}, u32[]{:S(2)}) collective-permute-start(f32[768,512]{1,0:T(8,128)} %convolution_add_fusion), channel_id=1, source_target_pairs={{0,1},{1,0},{2,3},{3,2},{4,5},{5,4},{6,7},{7,6},{8,9},{9,8},{10,11... | collective-permute-start | bytes 4718600 | tf_op jit(solution)/shard_map/ppermute | solution.py:260
  199.2 2.5 %copy-start.1 = (bf16[2048,1024]{1,0:T(8,128)(2,1)S(1)}, bf16[2048,1024]{1,0:T(8,128)(2,1)}, u32[]{:S(2)}) copy-start(bf16[2048,1024]{1,0:T(8,128)(2,1)} %all-gather.5.cloned.1.call-done) | copy-start | bytes 12582916
  201.7 2.6 %copy-start.7 = (bf16[768,1024]{0,1:T(8,128)(2,1)S(1)}, bf16[768,1024]{0,1:T(8,128)(2,1)}, u32[]{:S(2)}) copy-start(bf16[768,1024]{0,1:T(8,128)(2,1)} %copy-done.6) | copy-start | bytes 4718596
  203.7 8.5 %collective-permute-start.8 = (f32[256,512]{1,0:T(8,128)S(1)}, f32[256,512]{1,0:T(8,128)S(1)}, u32[]{:S(2)}, u32[]{:S(2)}) collective-permute-start(f32[256,512]{1,0:T(8,128)S(1)} %convolution_add_fusion.1), channel_id=1, source_target_pairs={{0,1},{1,0},{2,3},{3,2},{4,5},{5,4},{6,7},{7,6},{8,9},{9,8},{10,11... | collective-permute-start | bytes 1572872 | tf_op jit(solution)/shard_map/ppermute | solution.py:260
  207.2 10.2 %collective-permute-start.16 = (bf16[256,512]{1,0:T(8,128)(2,1)S(1)}, bf16[256,512]{1,0:T(8,128)(2,1)S(1)}, u32[]{:S(2)}, u32[]{:S(2)}) collective-permute-start(bf16[256,512]{1,0:T(8,128)(2,1)S(1)} %get-tuple-element.131), channel_id=1, source_target_pairs={{0,2},{2,4},{4,6},{6,0},{1,3},{3,5},{5,7},{7,1},{8,10},{10,12},{12... | collective-permute-start | bytes 786440 | tf_op jit(solution)/shard_map/ppermute | solution.py:266
  208.7 13.3 %collective-permute-start.17 = (bf16[256,512]{1,0:T(8,128)(2,1)S(1)}, bf16[256,512]{1,0:T(8,128)(2,1)S(1)}, u32[]{:S(2)}, u32[]{:S(2)}) collective-permute-start(bf16[256,512]{1,0:T(8,128)(2,1)S(1)} %get-tuple-element.133), channel_id=1, source_target_pairs={{0,4},{2,6},{4,0},{6,2},{1,5},{3,7},{5,1},{7,3},{8,12},{10,14},{12... | collective-permute-start | bytes 786440 | tf_op jit(solution)/shard_map/ppermute | solution.py:266
  210.2 11.9 %collective-permute-start.18 = (bf16[256,512]{1,0:T(8,128)(2,1)S(1)}, bf16[256,512]{1,0:T(8,128)(2,1)S(1)}, u32[]{:S(2)}, u32[]{:S(2)}) collective-permute-start(bf16[256,512]{1,0:T(8,128)(2,1)S(1)} %get-tuple-element.132), channel_id=1, source_target_pairs={{0,6},{2,0},{4,2},{6,4},{1,7},{3,1},{5,3},{7,5},{8,14},{10,8},{12,... | collective-permute-start | bytes 786440 | tf_op jit(solution)/shard_map/ppermute | solution.py:266
Sparse Core Ops, SparseCore 0:
  15.4 94.8 all-gather.2
  111.9 79.7 all-gather.4

commit v15 on v12

--- a/solution.py
+++ b/solution.py
@@ -239,18 +239,20 @@
     w_all = head_exchange(w_local.reshape(-1, group_rows, col_width), head_count)
     w_all = w_all.reshape(-1, group_rows, col_width)
     w_mine = jnp.take(w_all, ids, axis=0).reshape(-1, col_width)
-    w_line = lax.all_gather(w_mine, "cz", axis=1, tiled=True)
+    w_stack = lax.all_gather(w_mine, "cz", axis=0, tiled=False)
     ret_rows = att_ret.shape[1]
     run_stack = jnp.concatenate(plane_pieces(att_run, plane), axis=0)
     ret_stack = jnp.concatenate(plane_pieces(att_ret, plane), axis=0)
-    half = w_line.shape[1] // 2
+    per_half = line // 2
+    half = per_half * col_width
     me = lax.axis_index("head")
 
     def product(ret_part, run_part, columns):
-        w_half = lax.dynamic_slice_in_dim(w_line, columns * half, half, axis=1)
-        return jnp.dot(ret_part, w_half[:ret_rows], preferred_element_type=jnp.float32) + jnp.dot(
-            run_part, w_half[ret_rows:], preferred_element_type=jnp.float32
-        )
+        w_half = lax.dynamic_slice_in_dim(w_stack, columns * per_half, per_half, axis=0)
+        both = jnp.einsum(
+            "tk,lkc->tlc", ret_part, w_half[:, :ret_rows], preferred_element_type=jnp.float32
+        ) + jnp.einsum("tk,lkc->tlc", run_part, w_half[:, ret_rows:], preferred_element_type=jnp.float32)
+        return both.reshape(both.shape[0], half)
 
     def reduced(ret_part, run_part):
         sent = lax.ppermute(product(ret_part, run_part, 1 - me), "head", [(0, 1), (1, 0)])

time: 234 us -> 235 us (level)
  waiting for transfers between devices: 108 us -> 114 us
  local copies, waits for them, and re-layouts: 25.9 us -> 21.2 us
    ppermute x6, waiting for transfers between devices: 9.43 us -> 0.02 us  [plane_pieces(): lax.ppermute(block, 'cb', [(i, (i + shift) % plane) for i in range(plane)])]
    all_gather x1, waiting for transfers between devices: 31.9 us -> 39.8 us  [duo_attend(): lax.all_gather(ret_kv.reshape(rows, ret_per * 2 * HEAD_SIZE), CTX, axis=0...]
    all_gather x1, waiting for transfers between devices: 51.7 us -> 56.4 us  [project_assigned(): w_stack = lax.all_gather(w_mine, 'cz', axis=0, tiled=False)]
    dot_general x8, matrix products: 13.6 us -> 16.1 us  [the longest x4 8.83 us: product(): jnp.einsum('tk,lkc->tlc', run_part, w_half[:, ret_rows:], preferred_eleme...]
    unnamed x35 -> x41, local copies, waits for them, and re-layouts: 7.76 us -> 5.51 us
  transfers between devices with their start and end apart: 21 -> 21, of which waited for: 10 -> 9; matrix products, arithmetic and copies ran while one was open for 26% -> 26% of each run, Pallas kernels for 0% -> 0%
where the time goes in v15:
time: 235 us
  waiting for transfers between devices  114 us (49%)
  matrix products  35.2 us (15%)
  starting transfers between devices  27.9 us (12%)
  local copies, waits for them, and re-layouts  21.2 us (9%)
  other arithmetic  21 us (9%)
  between operations  14.9 us (6%)
    all_gather x1, waiting for transfers between devices, project_assigned(): w_stack = lax.all_gather(w_mine, 'cz', axis=0, tiled=False)  56.4 us
    all_gather x1, waiting for transfers between devices, duo_attend(): lax.all_gather(ret_kv.reshape(rows, ret_per * 2 * HEAD_SIZE), CTX, axis=0...  39.8 us
    dot_general x2, matrix products, update(): jnp.einsum('hgrk,khd->hgrd', weights.astype(jnp.bfloat16), value_block, p...  12.9 us
    ppermute x3, waiting for transfers between devices, project_assigned(): lax.ppermute(far[-shift % plane - 1], 'cb', [(i, (i + shift) % plane) for...  9.75 us
    ppermute x6, starting transfers between devices, plane_pieces(): lax.ppermute(block, 'cb', [(i, (i + shift) % plane) for i in range(plane)])  8.95 us
    dot_general x4, matrix products, product(): jnp.einsum('tk,lkc->tlc', run_part, w_half[:, ret_rows:], preferred_eleme...  8.83 us
    ppermute x4, starting transfers between devices, duo_attend(): got = lax.ppermute(sink_kv, CTX, pairs)  8.34 us
    dot_general x4, matrix products, product(): jnp.einsum('tk,lkc->tlc', ret_part, w_half[:, :ret_rows], preferred_eleme...  7.27 us
  transfers between devices with their start and end apart: 21, of which 9 were waited for; matrix products, arithmetic and copies ran while one was open for 26% of the time, Pallas kernels for 0%

profile of v15, /device:TPU:0, one launch (start us, length us, event | category | flops | bytes accessed | tf_op | source)
XLA Modules:
  0.0 234.7 jit_solution(15791932035367465527)
XLA Ops:
  7.9 1.1 copy.71
  9.1 1.1 copy.72
  11.5 1.0 sort.17
  14.9 0.9 copy.74
  17.1 1.4 subtract_convert_fusion
  22.6 4.5 %collective-permute-start.3 = (bf16[64,2,2,128]{3,0,1,2:T(8,128)(2,1)S(1)}, bf16[64,2,2,128]{3,0,1,2:T(8,128)(2,1)S(1)}, u32[]{:S(2)}, u32[]{:S(2)}) collective-permute-start(bf16[64,2,2,128]{3,0,1,2:T(8,128)(2,1)S(1)} %slice.87), channel_id=1, source_target_pairs={{0,2},{1,3}} | collective-permute-start | bytes 196616 | tf_op jit(solution)/shard_map/ppermute | solution.py:174
  27.8 2.8 %collective-permute-done.3 = bf16[64,2,2,128]{3,0,1,2:T(8,128)(2,1)S(1)} collective-permute-done((bf16[64,2,2,128]{3,0,1,2:T(8,128)(2,1)S(1)}, bf16[64,2,2,128]{3,0,1,2:T(8,128)(2,1)S(1)}, u32[]{:S(2)}, u32[]{:S(2)}) %collective-permute-start.3) | collective-permute-done | bytes 65568 | tf_op jit(solution)/shard_map/ppermute | solution.py:174
  30.6 1.3 collective-permute-start.4
  31.9 1.9 collective-permute-done.4
  33.8 1.3 collective-permute-start.5
  35.8 4.4 %collective-permute-start.7 = (bf16[256,2,2,128]{3,0,1,2:T(8,128)(2,1)S(1)}, bf16[256,2,2,128]{3,0,1,2:T(8,128)(2,1)S(1)}, u32[]{:S(2)}, u32[]{:S(2)}) collective-permute-start(bf16[256,2,2,128]{3,0,1,2:T(8,128)(2,1)S(1)} %fusion.50), channel_id=1, source_target_pairs={{0,2},{2,4},{4,6},{6,8},{8,10},{10,12},{12,14},{14,16},{16,18},{18... | collective-permute-start | bytes 786440 | tf_op jit(solution)/shard_map/ppermute | solution.py:169
  40.3 1.3 collective-permute-start.6
  41.6 1.8 collective-permute-done.6
  43.5 1.7 collective-permute-done.7
  45.2 0.9 pad_maximum_fusion.4
  46.4 1.5 gather_fusion.5
  47.9 2.0 fusion.17
  50.0 2.1 copy-done.1
  52.1 1.1 fusion.18
  54.0 3.7 %divide_convert_fusion = bf16[256,2,4,128]{0,3,2,1:T(8,128)(2,1)S(1)} fusion(f32[2,576,256,4]{2,1,3,0:T(8,128)} %copy-done.1, f32[2,4,256]{2,1,0:T(4,128)S(1)} %get-tuple-element.147, pred[256,576]{0,1:T(8,128)(4,1)S(1)} %pad_add_fusion, f32[256,2,4]{0,2,1:T(4,128)S(1)} %bitcast_add_fusion.2, f32[256,2,4]{0,2,1:T(4,128)S(1)} %get-tuple-element.146, ...), kind=kOutput, calls=%fused_computation.55 | convolution fusion | flops 308674560 | bytes 5709824 | tf_op jit(solution)/shard_map/hgrk,khd->hgrd/dot_general | solution.py:62
  57.8 1.0 copy.86
  58.8 2.4 %collective-permute-start.12 = (bf16[256,1024]{1,0:T(8,128)(2,1)}, bf16[256,1024]{1,0:T(8,128)(2,1)}, u32[]{:S(2)}, u32[]{:S(2)}) collective-permute-start(bf16[256,1024]{1,0:T(8,128)(2,1)} %copy.86), channel_id=1, source_target_pairs={{0,2},{2,4},{4,6},{6,0},{1,3},{3,5},{5,7},{7,1},{8,10},{10,12},{12... | collective-permute-start | bytes 1572872 | tf_op jit(solution)/shard_map/ppermute | solution.py:228
  61.2 2.1 collective-permute-start.13
  63.3 1.2 collective-permute-start.14
  64.5 1.7 select_bitcast_fusion.2
  66.4 1.6 gather_fusion
  68.1 2.3 bitcast_select_fusion.2
  70.4 39.8 %all-gather.3.cloned.1.call-done = bf16[4096,512]{0,1:T(8,128)(2,1)} async-done(((bf16[256,512]{0,1:T(8,128)(2,1)}), bf16[4096,512]{0,1:T(8,128)(2,1)}) %all-gather.3.cloned.1.call-update) | async-done | bytes 4194320 | tf_op jit(solution)/shard_map/all_gather | solution.py:199
  110.3 20.8 %while.15 = (s32[]{:T(128)}, f32[2,4,256]{2,1,0:T(4,128)S(1)}, f32[2,4,256]{2,1,0:T(4,128)S(1)}, f32[2,4,256,128]{3,2,1,0:T(8,128)S(1)}, s32[]{:T(128)}, /*index...) while((s32[]{:T(128)}, f32[2,4,256]{2,1,0:T(4,128)S(1)}, ...), condition=%wide.region_5.8_spmd.clone, body=%wide.region_2.7_spmd.clone.sunk | while | flops 2203064576 | bytes 124405992 | solution.py:216
  111.0 4.2 %fusion.92 = (f32[2,4,256]{2,1,0:T(4,128)S(1)}, f32[2,2048,256,4]{2,1,3,0:T(8,128)S(1)}) fusion(pred[256,2048]{0,1:T(8,128)(4,1)S(1)} %broadcast_compare_fusion.3, bf16[256,2,4,128]{3,0,2,1:T(8,128)(2,1)S(1)} %get-tuple-element.250, bf16[4096,2,2,128]{0,3,2,1:T(8,128)(2,1)} %get-tuple-element.249, s32[]{:T(128)S(6)} %select_n.346), kind=kOutput, calls=%fused_computation.9.clone.1 | convolution fusion | flops 1086322688 | bytes 18882564 | tf_op jit(solution)/shard_map/while/body/rhgd,khd->hgrk/dot_general | solution.py:53
  115.3 4.1 %fusion.93 = f32[2,4,256]{2,1,0:T(4,128)S(1)} fusion(f32[2,2048,256,4]{2,1,3,0:T(8,128)S(1)} %get-tuple-element.215, f32[2,4,256]{2,1,0:T(4,128)S(1)} %max.13, pred[256,2048]{0,1:T(8,128)(4,1)S(1)} %broadcast_compare_fusion.3), kind=kLoop, calls=%fused_computation.11.clone.1 | loop fusion | flops 20969472 | bytes 17317888 | tf_op jit(solution)/shard_map/while/body/reduce_sum | solution.py:61
  119.3 2.5 %copy-done = f32[2,2048,256,4]{2,1,3,0:T(8,128)} copy-done((f32[2,2048,256,4]{2,1,3,0:T(8,128)}, f32[2,2048,256,4]{2,1,3,0:T(8,128)S(1)}, u32[]{:S(2)}) %copy-start) | copy-done | bytes 16777240 | tf_op jit(solution)/shard_map/while
  121.9 9.2 %fusion.94 = f32[2,4,256,128]{3,2,1,0:T(8,128)S(1)} fusion(f32[2,2048,256,4]{2,1,3,0:T(8,128)} %copy-done, f32[2,4,256]{2,1,0:T(4,128)S(1)} %max.13, pred[256,2048]{0,1:T(8,128)(4,1)S(1)} %broadcast_compare_fusion.3, bf16[4096,2,2,128]{0,3,2,1:T(8,128)(2,1)} %get-tuple-element.249, s32[]{:T(128)S(6)} %select_n.346, s32[]{:T(128)S(6)} %add.325, ...), kind=kOutput, calls=%fused_computation.14.clone.1 | convolution fusion | flops 1095237632 | bytes 20463624 | tf_op jit(solution)/shard_map/while/body/hgrk,khd->hgrd/dot_general | solution.py:62
  132.3 2.8 %collective-permute-start.11 = (bf16[256,1024]{1,0:T(8,128)(2,1)S(1)}, bf16[256,1024]{1,0:T(8,128)(2,1)S(1)}, u32[]{:S(2)}, u32[]{:S(2)}) collective-permute-start(bf16[256,1024]{1,0:T(8,128)(2,1)S(1)} %convert_element_type.61), channel_id=1, source_target_pairs={{0,6},{2,0},{4,2},{6,4},{1,7},{3,1},{5,3},{7,5},{8,14},{10,8},{12,... | collective-permute-start | bytes 1572872 | tf_op jit(solution)/shard_map/ppermute | solution.py:228
  135.5 56.4 %all-gather.5.cloned.1.call-done = bf16[4,2048,256]{2,1,0:T(8,128)(2,1)} async-done(((bf16[1,2048,256]{2,1,0:T(8,128)(2,1)}), bf16[4,2048,256]{2,1,0:T(8,128)(2,1)}) %all-gather.5.cloned.1.call-update) | async-done | bytes 4194320 | tf_op jit(solution)/shard_map/all_gather | solution.py:242
  191.8 2.9 %fusion.39 = f32[768,2,256]{0,2,1:T(8,128)S(1)} fusion(bf16[4,2048,256]{2,1,0:T(8,128)(2,1)} %all-gather.5.cloned.1.call-done, s32[]{:T(128)S(6)} %select_n.203, s32[]{:T(128)S(6)} %add.238, bf16[256,1024]{1,0:T(8,128)(2,1)} %collective-permute-done.14, bf16[256,1024]{1,0:T(8,128)(2,1)} %collective-permute-done.13, ...), kind=kOutput, calls=%fused_computation.68 | convolution fusion | flops 810024960 | bytes 4194312 | tf_op jit(solution)/shard_map/tk,lkc->tlc/dot_general | solution.py:254
  194.8 2.3 convolution_add_fusion
  197.2 3.6 %fusion.42 = f32[768,2,256]{0,2,1:T(8,128)} fusion(bf16[4,2048,256]{2,1,0:T(8,128)(2,1)S(1)} %copy-done.2, s32[]{:T(128)S(6)} %select_n.192, s32[]{:T(128)S(6)} %add.238, bf16[256,1024]{1,0:T(8,128)(2,1)} %collective-permute-done.14, bf16[256,1024]{1,0:T(8,128)(2,1)} %collective-permute-done.13, bf16[256,1024]{1,0:T(8,128)(2,1)} %collective-permute-done.12), kind=kOutput, calls=%fused_computation.71 | convolution fusion | flops 810024960 | bytes 4194312 | tf_op jit(solution)/shard_map/tk,lkc->tlc/dot_general | solution.py:254
  201.2 1.9 fusion.32
  203.1 1.8 convolution_add_fusion.2
  206.1 2.5 %convolution_add_fusion.1 = f32[768,2,256]{0,2,1:T(8,128)S(1)} fusion(f32[768,2,256]{0,2,1:T(8,128)} %fusion.42, bf16[4,2048,256]{2,1,0:T(8,128)(2,1)S(1)} %copy-done.3, s32[]{:T(128)S(6)} %select_n.192, bf16[256,1024]{1,0:T(8,128)(2,1)S(1)} %copy-done.15, bf16[256,1024]{1,0:T(8,128)(2,1)S(1)} %copy-done.13, bf16[256,1024]{1,0:T(8,128)(2,1)S(1)} %copy-done.17), kind=kOutput, calls=%fused_computation.45 | convolution fusion | flops 810418176 | bytes 5767172 | tf_op jit(solution)/shard_map/tk,lkc->tlc/dot_general | solution.py:252
  209.0 1.5 collective-permute-start.16
  210.5 1.5 collective-permute-start.17
  212.0 1.5 collective-permute-start.18
  214.1 5.1 %collective-permute-done.16 = bf16[256,512]{0,1:T(8,128)(2,1)S(1)} collective-permute-done((bf16[256,512]{0,1:T(8,128)(2,1)S(1)}, bf16[256,512]{0,1:T(8,128)(2,1)S(1)}, u32[]{:S(2)}, u32[]{:S(2)}) %collective-permute-start.16) | collective-permute-done | bytes 262176 | tf_op jit(solution)/shard_map/ppermute | solution.py:264
  219.2 4.6 %collective-permute-done.17 = bf16[256,512]{0,1:T(8,128)(2,1)S(1)} collective-permute-done((bf16[256,512]{0,1:T(8,128)(2,1)S(1)}, bf16[256,512]{0,1:T(8,128)(2,1)S(1)}, u32[]{:S(2)}, u32[]{:S(2)}) %collective-permute-start.17) | collective-permute-done | bytes 262176 | tf_op jit(solution)/shard_map/ppermute | solution.py:264
  224.6 1.1 copy.89
  226.2 1.6 reshape.416
  (134 shorter events, 18.8 us)
Async XLA Ops:
  6.5 4.8 %copy-start.18 = (s32[4]{0:T(128)S(1)}, s32[4]{0:T(128)}, u32[]{:S(2)}) copy-start(s32[4]{0:T(128)} %param.17) | copy-start | bytes 52
  6.5 103.7 %all-gather.3.cloned.1.call-start = ((), (), s32[]{:S(2)}) async-start(), calls=%async_computation | async-start | bytes 4456448 | tf_op jit(solution)/shard_map/all_gather | solution.py:199
  10.6 2.5 %collective-permute-start = (bf16[256,4,2,128]{0,3,1,2:T(8,128)(2,1)S(1)}, bf16[256,4,2,128]{0,3,1,2:T(8,128)(2,1)S(1)}, u32[]{:S(2)}, u32[]{:S(2)}) collective-permute-start(bf16[256,4,2,128]{0,3,1,2:T(8,128)(2,1)S(1)} %pad_maximum_fusion.5), channel_id=1, source_target_pairs={{0,1},{1,0},{2,3},{3,2},{4,5},{5,4},{6,7},{7,6},{8,9},{9,8},{10,11... | collective-permute-start | bytes 1572872 | tf_op jit(solution)/shard_map/ppermute | solution.py:139
  13.1 1.7 copy-start.7
  13.1 6.6 %copy-start.10 = (s32[2]{0:T(128)}, s32[2]{0:T(128)S(1)}, u32[]{:S(2)}) copy-start(s32[2]{0:T(128)S(1)} %get-tuple-element.126) | copy-start | bytes 28
  13.1 7.2 %copy-start.11 = (s32[2]{0:T(128)}, s32[2]{0:T(128)S(1)}, u32[]{:S(2)}) copy-start(s32[2]{0:T(128)S(1)} %get-tuple-element.151) | copy-start | bytes 28
  13.1 1.0 copy-start.6
  13.4 2.4 %copy-start.4 = (bf16[256,2048]{1,0:T(8,128)(2,1)S(1)}, bf16[256,2048]{1,0:T(8,128)(2,1)}, u32[]{:S(2)}) copy-start(bf16[256,2048]{1,0:T(8,128)(2,1)} %param.13) | copy-start | bytes 3145732
  15.7 176.1 %all-gather.5.cloned.1.call-start = ((), (), s32[]{:S(2)}) async-start(), calls=%async_computation.1 | async-start | bytes 5242880 | tf_op jit(solution)/shard_map/all_gather | solution.py:242
  19.1 26.9 %collective-permute-start.1 = (bf16[256,4,4,128]{3,0,2,1:T(8,128)(2,1)S(1)}, bf16[256,4,4,128]{3,0,2,1:T(8,128)(2,1)S(1)}, u32[]{:S(2)}, u32[]{:S(2)}) collective-permute-start(bf16[256,4,4,128]{3,0,2,1:T(8,128)(2,1)S(1)} %bitcast.203), channel_id=1, source_target_pairs={{0,1},{1,0},{2,3},{3,2},{4,5},{5,4},{6,7},{7,6},{8,9},{9,8},{10,11... | collective-permute-start | bytes 3145736 | tf_op jit(solution)/shard_map/ppermute | solution.py:139
  19.2 45.4 %collective-permute-start.2 = (bf16[4,512,256]{2,1,0:T(8,128)(2,1)}, bf16[4,512,256]{2,1,0:T(8,128)(2,1)}, u32[]{:S(2)}, u32[]{:S(2)}) collective-permute-start(bf16[4,512,256]{2,1,0:T(8,128)(2,1)} %bitcast.20), channel_id=1, source_target_pairs={{0,1},{1,0},{2,3},{3,2},{4,5},{5,4},{6,7},{7,6},{8,9},{9,8},{10,11... | collective-permute-start | bytes 3145736 | tf_op jit(solution)/shard_map/ppermute | solution.py:139
  22.6 8.0 %collective-permute-start.3 = (bf16[64,2,2,128]{3,0,1,2:T(8,128)(2,1)S(1)}, bf16[64,2,2,128]{3,0,1,2:T(8,128)(2,1)S(1)}, u32[]{:S(2)}, u32[]{:S(2)}) collective-permute-start(bf16[64,2,2,128]{3,0,1,2:T(8,128)(2,1)S(1)} %slice.87), channel_id=1, source_target_pairs={{0,2},{1,3}} | collective-permute-start | bytes 196616 | tf_op jit(solution)/shard_map/ppermute | solution.py:174
  30.6 3.2 %collective-permute-start.4 = (bf16[64,2,2,128]{3,0,1,2:T(8,128)(2,1)S(1)}, bf16[64,2,2,128]{3,0,1,2:T(8,128)(2,1)S(1)}, u32[]{:S(2)}, u32[]{:S(2)}) collective-permute-start(bf16[64,2,2,128]{3,0,1,2:T(8,128)(2,1)S(1)} %broadcast_select_fusion), channel_id=1, source_target_pairs={{0,4},{2,6},{1,5},{3,7}} | collective-permute-start | bytes 196616 | tf_op jit(solution)/shard_map/ppermute | solution.py:174
  33.8 6.4 %collective-permute-start.5 = (bf16[64,2,2,128]{3,0,1,2:T(8,128)(2,1)S(1)}, bf16[64,2,2,128]{3,0,1,2:T(8,128)(2,1)S(1)}, u32[]{:S(2)}, u32[]{:S(2)}) collective-permute-start(bf16[64,2,2,128]{3,0,1,2:T(8,128)(2,1)S(1)} %broadcast_select_fusion.1), channel_id=1, source_target_pairs={{0,8},{2,10},{4,12},{6,14},{1,9},{3,11},{5,13},{7,15}} | collective-permute-start | bytes 196616 | tf_op jit(solution)/shard_map/ppermute | solution.py:174
  35.8 9.3 %collective-permute-start.7 = (bf16[256,2,2,128]{3,0,1,2:T(8,128)(2,1)S(1)}, bf16[256,2,2,128]{3,0,1,2:T(8,128)(2,1)S(1)}, u32[]{:S(2)}, u32[]{:S(2)}) collective-permute-start(bf16[256,2,2,128]{3,0,1,2:T(8,128)(2,1)S(1)} %fusion.50), channel_id=1, source_target_pairs={{0,2},{2,4},{4,6},{6,8},{8,10},{10,12},{12,14},{14,16},{16,18},{18... | collective-permute-start | bytes 786440 | tf_op jit(solution)/shard_map/ppermute | solution.py:169
  40.3 3.2 %collective-permute-start.6 = (bf16[64,2,2,128]{3,0,1,2:T(8,128)(2,1)S(1)}, bf16[64,2,2,128]{3,0,1,2:T(8,128)(2,1)S(1)}, u32[]{:S(2)}, u32[]{:S(2)}) collective-permute-start(bf16[64,2,2,128]{3,0,1,2:T(8,128)(2,1)S(1)} %broadcast_select_fusion.2), channel_id=1, source_target_pairs={{0,16},{2,18},{4,20},{6,22},{8,24},{10,26},{12,28},{14,30},{1,17},... | collective-permute-start | bytes 196616 | tf_op jit(solution)/shard_map/ppermute | solution.py:174
  46.2 1.8 copy-start.5
  46.2 1.7 copy-start.9
  49.9 2.1 copy-start.1
  58.8 76.4 %collective-permute-start.12 = (bf16[256,1024]{1,0:T(8,128)(2,1)}, bf16[256,1024]{1,0:T(8,128)(2,1)}, u32[]{:S(2)}, u32[]{:S(2)}) collective-permute-start(bf16[256,1024]{1,0:T(8,128)(2,1)} %copy.86), channel_id=1, source_target_pairs={{0,2},{2,4},{4,6},{6,0},{1,3},{3,5},{5,7},{7,1},{8,10},{10,12},{12... | collective-permute-start | bytes 1572872 | tf_op jit(solution)/shard_map/ppermute | solution.py:228
  61.2 74.2 %collective-permute-start.13 = (bf16[256,1024]{1,0:T(8,128)(2,1)}, bf16[256,1024]{1,0:T(8,128)(2,1)}, u32[]{:S(2)}, u32[]{:S(2)}) collective-permute-start(bf16[256,1024]{1,0:T(8,128)(2,1)} %copy.86), channel_id=1, source_target_pairs={{0,4},{2,6},{4,0},{6,2},{1,5},{3,7},{5,1},{7,3},{8,12},{10,14},{12... | collective-permute-start | bytes 1572872 | tf_op jit(solution)/shard_map/ppermute | solution.py:228
  63.3 72.2 %collective-permute-start.14 = (bf16[256,1024]{1,0:T(8,128)(2,1)}, bf16[256,1024]{1,0:T(8,128)(2,1)}, u32[]{:S(2)}, u32[]{:S(2)}) collective-permute-start(bf16[256,1024]{1,0:T(8,128)(2,1)} %copy.86), channel_id=1, source_target_pairs={{0,6},{2,0},{4,2},{6,4},{1,7},{3,1},{5,3},{7,5},{8,14},{10,8},{12,... | collective-permute-start | bytes 1572872 | tf_op jit(solution)/shard_map/ppermute | solution.py:228
  66.2 1.8 copy-start.8
  115.2 6.6 %copy-start = (f32[2,2048,256,4]{2,1,3,0:T(8,128)}, f32[2,2048,256,4]{2,1,3,0:T(8,128)S(1)}, u32[]{:S(2)}) copy-start(f32[2,2048,256,4]{2,1,3,0:T(8,128)S(1)} %get-tuple-element.215) | copy-start | bytes 50331652 | tf_op jit(solution)/shard_map/while
  132.2 62.5 %collective-permute-start.10 = (bf16[256,1024]{1,0:T(8,128)(2,1)S(1)}, bf16[256,1024]{1,0:T(8,128)(2,1)S(1)}, u32[]{:S(2)}, u32[]{:S(2)}) collective-permute-start(bf16[256,1024]{1,0:T(8,128)(2,1)S(1)} %convert_element_type.61), channel_id=1, source_target_pairs={{0,4},{2,6},{4,0},{6,2},{1,5},{3,7},{5,1},{7,3},{8,12},{10,14},{12... | collective-permute-start | bytes 1572872 | tf_op jit(solution)/shard_map/ppermute | solution.py:228
  132.3 62.4 %collective-permute-start.11 = (bf16[256,1024]{1,0:T(8,128)(2,1)S(1)}, bf16[256,1024]{1,0:T(8,128)(2,1)S(1)}, u32[]{:S(2)}, u32[]{:S(2)}) collective-permute-start(bf16[256,1024]{1,0:T(8,128)(2,1)S(1)} %convert_element_type.61), channel_id=1, source_target_pairs={{0,6},{2,0},{4,2},{6,4},{1,7},{3,1},{5,3},{7,5},{8,14},{10,8},{12,... | collective-permute-start | bytes 1572872 | tf_op jit(solution)/shard_map/ppermute | solution.py:228
  135.1 59.6 %collective-permute-start.9 = (bf16[256,1024]{1,0:T(8,128)(2,1)S(1)}, bf16[256,1024]{1,0:T(8,128)(2,1)S(1)}, u32[]{:S(2)}, u32[]{:S(2)}) collective-permute-start(bf16[256,1024]{1,0:T(8,128)(2,1)S(1)} %convert_element_type.61), channel_id=1, source_target_pairs={{0,2},{2,4},{4,6},{6,0},{1,3},{3,5},{5,7},{7,1},{8,10},{10,12},{12... | collective-permute-start | bytes 1572872 | tf_op jit(solution)/shard_map/ppermute | solution.py:228
  191.8 3.0 %copy-start.2 = (bf16[4,2048,256]{2,1,0:T(8,128)(2,1)S(1)}, bf16[4,2048,256]{2,1,0:T(8,128)(2,1)}, u32[]{:S(2)}) copy-start(bf16[4,2048,256]{2,1,0:T(8,128)(2,1)} %all-gather.5.cloned.1.call-done) | copy-start | bytes 12582916
  194.7 2.4 %copy-start.12 = (bf16[256,1024]{1,0:T(8,128)(2,1)}, bf16[256,1024]{1,0:T(8,128)(2,1)S(1)}, u32[]{:S(2)}) copy-start(bf16[256,1024]{1,0:T(8,128)(2,1)S(1)} %collective-permute-done.10) | copy-start | bytes 1572868
  194.7 2.4 %copy-start.14 = (bf16[256,1024]{1,0:T(8,128)(2,1)}, bf16[256,1024]{1,0:T(8,128)(2,1)S(1)}, u32[]{:S(2)}) copy-start(bf16[256,1024]{1,0:T(8,128)(2,1)S(1)} %collective-permute-done.11) | copy-start | bytes 1572868
  194.8 2.3 copy-start.16
  197.1 11.5 %collective-permute-start.15 = (f32[768,512]{0,1:T(8,128)}, f32[768,512]{0,1:T(8,128)S(1)}, u32[]{:S(2)}, u32[]{:S(2)}) collective-permute-start(f32[768,512]{0,1:T(8,128)} %bitcast.50), channel_id=1, source_target_pairs={{0,1},{1,0},{2,3},{3,2},{4,5},{5,4},{6,7},{7,6},{8,9},{9,8},{10,11... | collective-permute-start | bytes 4718600 | tf_op jit(solution)/shard_map/ppermute | solution.py:258
  201.2 4.4 %copy-start.3 = (bf16[4,2048,256]{2,1,0:T(8,128)(2,1)S(1)}, bf16[4,2048,256]{2,1,0:T(8,128)(2,1)}, u32[]{:S(2)}) copy-start(bf16[4,2048,256]{2,1,0:T(8,128)(2,1)} %all-gather.5.cloned.1.call-done) | copy-start | bytes 12582916
  201.2 4.9 %copy-start.13 = (bf16[256,1024]{1,0:T(8,128)(2,1)S(1)}, bf16[256,1024]{1,0:T(8,128)(2,1)}, u32[]{:S(2)}) copy-start(bf16[256,1024]{1,0:T(8,128)(2,1)} %copy-done.12) | copy-start | bytes 1572868
  201.2 4.9 %copy-start.15 = (bf16[256,1024]{1,0:T(8,128)(2,1)S(1)}, bf16[256,1024]{1,0:T(8,128)(2,1)}, u32[]{:S(2)}) copy-start(bf16[256,1024]{1,0:T(8,128)(2,1)} %copy-done.14) | copy-start | bytes 1572868
  201.2 4.9 %copy-start.17 = (bf16[256,1024]{1,0:T(8,128)(2,1)S(1)}, bf16[256,1024]{1,0:T(8,128)(2,1)}, u32[]{:S(2)}) copy-start(bf16[256,1024]{1,0:T(8,128)(2,1)} %copy-done.16) | copy-start | bytes 1572868
  205.0 9.0 %collective-permute-start.8 = (f32[256,512]{0,1:T(8,128)S(1)}, f32[256,512]{0,1:T(8,128)S(1)}, u32[]{:S(2)}, u32[]{:S(2)}) collective-permute-start(f32[256,512]{0,1:T(8,128)S(1)} %bitcast.217), channel_id=1, source_target_pairs={{0,1},{1,0},{2,3},{3,2},{4,5},{5,4},{6,7},{7,6},{8,9},{9,8},{10,11... | collective-permute-start | bytes 1572872 | tf_op jit(solution)/shard_map/ppermute | solution.py:258
  209.0 10.2 %collective-permute-start.16 = (bf16[256,512]{0,1:T(8,128)(2,1)S(1)}, bf16[256,512]{0,1:T(8,128)(2,1)S(1)}, u32[]{:S(2)}, u32[]{:S(2)}) collective-permute-start(bf16[256,512]{0,1:T(8,128)(2,1)S(1)} %get-tuple-element.141), channel_id=1, source_target_pairs={{0,2},{2,4},{4,6},{6,0},{1,3},{3,5},{5,7},{7,1},{8,10},{10,12},{12... | collective-permute-start | bytes 786440 | tf_op jit(solution)/shard_map/ppermute | solution.py:264
  210.5 13.3 %collective-permute-start.17 = (bf16[256,512]{0,1:T(8,128)(2,1)S(1)}, bf16[256,512]{0,1:T(8,128)(2,1)S(1)}, u32[]{:S(2)}, u32[]{:S(2)}) collective-permute-start(bf16[256,512]{0,1:T(8,128)(2,1)S(1)} %get-tuple-element.143), channel_id=1, source_target_pairs={{0,4},{2,6},{4,0},{6,2},{1,5},{3,7},{5,1},{7,3},{8,12},{10,14},{12... | collective-permute-start | bytes 786440 | tf_op jit(solution)/shard_map/ppermute | solution.py:264
  212.0 11.9 %collective-permute-start.18 = (bf16[256,512]{0,1:T(8,128)(2,1)S(1)}, bf16[256,512]{0,1:T(8,128)(2,1)S(1)}, u32[]{:S(2)}, u32[]{:S(2)}) collective-permute-start(bf16[256,512]{0,1:T(8,128)(2,1)S(1)} %get-tuple-element.142), channel_id=1, source_target_pairs={{0,6},{2,0},{4,2},{6,4},{1,7},{3,1},{5,3},{7,5},{8,14},{10,8},{12,... | collective-permute-start | bytes 786440 | tf_op jit(solution)/shard_map/ppermute | solution.py:264
Sparse Core Ops, SparseCore 0:
  15.9 94.3 all-gather.2
  111.8 79.9 all-gather.4

commit v16 on v12

--- a/solution.py
+++ b/solution.py
@@ -253,8 +253,10 @@
         )
 
     def reduced(ret_part, run_part):
-        sent = lax.ppermute(product(ret_part, run_part, 1 - me), "head", [(0, 1), (1, 0)])
-        return (product(ret_part, run_part, me) + sent).astype(jnp.bfloat16)
+        sent = lax.ppermute(
+            product(ret_part, run_part, 1 - me).astype(jnp.bfloat16), "head", [(0, 1), (1, 0)]
+        )
+        return (product(ret_part, run_part, me) + sent.astype(jnp.float32)).astype(jnp.bfloat16)
 
     me_cb = lax.axis_index("cb")
     far = reduced(ret_stack[rows:], run_stack[rows:]).reshape(plane - 1, rows, half)

time: 234 us -> 238 us (1.017)
  waiting for transfers between devices: 108 us -> 118 us
  matrix products: 34.6 us -> 28 us
    ppermute x6, waiting for transfers between devices: 9.43 us -> 32.5 us  [plane_pieces(): lax.ppermute(block, 'cb', [(i, (i + shift) % plane) for i in range(plane)])]
    all_gather x1, waiting for transfers between devices: 31.9 us -> 15.4 us  [duo_attend(): lax.all_gather(ret_kv.reshape(rows, ret_per * 2 * HEAD_SIZE), CTX, axis=0...]
    dot_general x4, matrix products: 5.93 us -> 2.96 us  [product(): jnp.dot(ret_part, w_half[:ret_rows], preferred_element_type=jnp.float32)]
    dot_general x2, matrix products: 14.7 us -> 12.3 us  [update(): jnp.einsum('hgrk,khd->hgrd', weights.astype(jnp.bfloat16), value_block, p...]
    unnamed x35 -> x29, local copies, waits for them, and re-layouts: 7.76 us -> 6.69 us
  transfers between devices with their start and end apart: 21 -> 21, of which waited for: 10 -> 11; matrix products, arithmetic and copies ran while one was open for 26% -> 25% of each run, Pallas kernels for 0% -> 0%
where the time goes in v16:
time: 238 us; the launch traced here: 237 us
  waiting for transfers between devices  118 us (50%)
  starting transfers between devices  29.7 us (12%)
  matrix products  28 us (12%)
  local copies, waits for them, and re-layouts  25 us (11%)
  other arithmetic  20.7 us (9%)
  between operations  14.8 us (6%)
    all_gather x1, waiting for transfers between devices, project_assigned(): w_line = lax.all_gather(w_mine, 'cz', axis=1, tiled=True)  54 us
    ppermute x6, waiting for transfers between devices, plane_pieces(): lax.ppermute(block, 'cb', [(i, (i + shift) % plane) for i in range(plane)])  32.5 us
    all_gather x1, waiting for transfers between devices, duo_attend(): lax.all_gather(ret_kv.reshape(rows, ret_per * 2 * HEAD_SIZE), CTX, axis=0...  15.4 us
    dot_general x2, matrix products, update(): jnp.einsum('hgrk,khd->hgrd', weights.astype(jnp.bfloat16), value_block, p...  12.3 us
    ppermute x6, starting transfers between devices, plane_pieces(): lax.ppermute(block, 'cb', [(i, (i + shift) % plane) for i in range(plane)])  10.6 us
    ppermute x3, waiting for transfers between devices, project_assigned(): lax.ppermute(far[-shift % plane - 1], 'cb', [(i, (i + shift) % plane) for...  8.98 us
    ppermute x4, starting transfers between devices, duo_attend(): got = lax.ppermute(sink_kv, CTX, pairs)  8.74 us
    unnamed x29, local copies, waits for them, and re-layouts  6.69 us
  transfers between devices with their start and end apart: 21, of which 11 were waited for; matrix products, arithmetic and copies ran while one was open for 25% of the time, Pallas kernels for 0%

profile of v16, /device:TPU:0, one launch (start us, length us, event | category | flops | bytes accessed | tf_op | source)
XLA Modules:
  0.0 236.7 jit_solution(11675686360534061368)
XLA Ops:
  7.9 1.1 copy.33
  9.1 1.1 copy.34
  17.7 1.4 subtract_convert_fusion
  23.5 4.9 %collective-permute-start.3 = (bf16[64,2,2,128]{3,0,1,2:T(8,128)(2,1)S(1)}, bf16[64,2,2,128]{3,0,1,2:T(8,128)(2,1)S(1)}, u32[]{:S(2)}, u32[]{:S(2)}) collective-permute-start(bf16[64,2,2,128]{3,0,1,2:T(8,128)(2,1)S(1)} %slice.87), channel_id=1, source_target_pairs={{0,2},{1,3}} | collective-permute-start | bytes 196616 | tf_op jit(solution)/shard_map/ppermute | solution.py:174
  28.3 3.5 %collective-permute-done.3 = bf16[64,2,2,128]{3,0,1,2:T(8,128)(2,1)S(1)} collective-permute-done((bf16[64,2,2,128]{3,0,1,2:T(8,128)(2,1)S(1)}, bf16[64,2,2,128]{3,0,1,2:T(8,128)(2,1)S(1)}, u32[]{:S(2)}, u32[]{:S(2)}) %collective-permute-start.3) | collective-permute-done | bytes 65568 | tf_op jit(solution)/shard_map/ppermute | solution.py:174
  31.8 1.3 collective-permute-start.4
  33.2 1.9 collective-permute-done.4
  35.0 1.3 collective-permute-start.5
  36.3 4.4 %collective-permute-start.7 = (bf16[256,2,2,128]{3,0,1,2:T(8,128)(2,1)S(1)}, bf16[256,2,2,128]{3,0,1,2:T(8,128)(2,1)S(1)}, u32[]{:S(2)}, u32[]{:S(2)}) collective-permute-start(bf16[256,2,2,128]{3,0,1,2:T(8,128)(2,1)S(1)} %fusion.51), channel_id=1, source_target_pairs={{0,2},{2,4},{4,6},{6,8},{8,10},{10,12},{12,14},{14,16},{16,18},{18... | collective-permute-start | bytes 786440 | tf_op jit(solution)/shard_map/ppermute | solution.py:169
  40.8 1.3 collective-permute-start.6
  42.8 1.2 collective-permute-done.6
  45.8 1.4 select_bitcast_fusion.3
  47.5 1.5 gather_fusion.5
  49.0 2.1 fusion.17
  51.2 1.1 fusion.18
  52.3 2.1 divide_convert_fusion
  54.4 2.5 %collective-permute-start.12 = (bf16[256,1024]{0,1:T(8,128)(2,1)}, bf16[256,1024]{0,1:T(8,128)(2,1)}, u32[]{:S(2)}, u32[]{:S(2)}) collective-permute-start(bf16[256,1024]{0,1:T(8,128)(2,1)} %bitcast.42), channel_id=1, source_target_pairs={{0,2},{2,4},{4,6},{6,0},{1,3},{3,5},{5,7},{7,1},{8,10},{10,12},{12... | collective-permute-start | bytes 1572872 | tf_op jit(solution)/shard_map/ppermute | solution.py:228
  56.9 2.4 %collective-permute-start.13 = (bf16[256,1024]{0,1:T(8,128)(2,1)}, bf16[256,1024]{0,1:T(8,128)(2,1)}, u32[]{:S(2)}, u32[]{:S(2)}) collective-permute-start(bf16[256,1024]{0,1:T(8,128)(2,1)} %bitcast.42), channel_id=1, source_target_pairs={{0,4},{2,6},{4,0},{6,2},{1,5},{3,7},{5,1},{7,3},{8,12},{10,14},{12... | collective-permute-start | bytes 1572872 | tf_op jit(solution)/shard_map/ppermute | solution.py:228
  60.2 1.4 select_bitcast_fusion.1
  62.5 1.3 bitcast_select_fusion.2
  63.9 2.4 gather_fusion.3
  66.4 6.3 %collective-permute-done.12 = bf16[256,1024]{0,1:T(8,128)(2,1)} collective-permute-done((bf16[256,1024]{0,1:T(8,128)(2,1)}, bf16[256,1024]{0,1:T(8,128)(2,1)}, u32[]{:S(2)}, u32[]{:S(2)}) %collective-permute-start.12) | collective-permute-done | bytes 524320 | tf_op jit(solution)/shard_map/ppermute | solution.py:228
  72.7 1.1 constant_dynamic-update-slice_fusion.5
  73.8 16.1 %collective-permute-done.13 = bf16[256,1024]{0,1:T(8,128)(2,1)} collective-permute-done((bf16[256,1024]{0,1:T(8,128)(2,1)}, bf16[256,1024]{0,1:T(8,128)(2,1)}, u32[]{:S(2)}, u32[]{:S(2)}) %collective-permute-start.13) | collective-permute-done | bytes 524320 | tf_op jit(solution)/shard_map/ppermute | solution.py:228
  89.9 1.1 constant_dynamic-update-slice_fusion.4
  90.9 1.1 constant_dynamic-update-slice_fusion.3
  92.0 15.4 %all-gather.3.cloned.1.call-done = bf16[4096,512]{0,1:T(8,128)(2,1)} async-done(((bf16[256,512]{0,1:T(8,128)(2,1)}), bf16[4096,512]{0,1:T(8,128)(2,1)}) %all-gather.3.cloned.1.call-update) | async-done | bytes 4194320 | tf_op jit(solution)/shard_map/all_gather | solution.py:199
  107.5 1.1 broadcast.345
  108.6 21.3 %while.15 = (s32[]{:T(128)}, f32[2,4,256]{2,1,0:T(4,128)S(1)}, f32[2,4,256]{2,1,0:T(4,128)S(1)}, f32[2,4,256,128]{3,2,1,0:T(8,128)}, s32[]{:T(128)}, /*index=5*/...) while((s32[]{:T(128)}, f32[2,4,256]{2,1,0:T(4,128)S(1)}, ...), condition=%wide.region_5.8_spmd.clone, body=%wide.region_2.7_spmd.clone.sunk | while | flops 2203064576 | bytes 124405992 | solution.py:216
  109.1 4.2 %fusion.91 = (f32[2,4,256]{2,1,0:T(4,128)S(1)}, f32[2,2048,256,4]{2,1,3,0:T(8,128)S(1)}) fusion(pred[256,2048]{0,1:T(8,128)(4,1)S(1)} %broadcast_compare_fusion.3, bf16[256,2,4,128]{3,0,2,1:T(8,128)(2,1)S(1)} %get-tuple-element.244, bf16[4096,2,2,128]{0,3,2,1:T(8,128)(2,1)} %get-tuple-element.243, s32[]{:T(128)S(6)} %select_n.342), kind=kOutput, calls=%fused_computation.9.clone.1 | convolution fusion | flops 1086322688 | bytes 18882564 | tf_op jit(solution)/shard_map/while/body/rhgd,khd->hgrk/dot_general | solution.py:53
  113.3 4.1 %fusion.92 = f32[2,4,256]{2,1,0:T(4,128)S(1)} fusion(f32[2,2048,256,4]{2,1,3,0:T(8,128)S(1)} %get-tuple-element.209, f32[2,4,256]{2,1,0:T(4,128)S(1)} %max.13, pred[256,2048]{0,1:T(8,128)(4,1)S(1)} %broadcast_compare_fusion.3), kind=kLoop, calls=%fused_computation.11.clone.1 | loop fusion | flops 20969472 | bytes 17317888 | tf_op jit(solution)/shard_map/while/body/reduce_sum | solution.py:61
  117.4 2.3 copy-done
  119.7 10.2 %fusion.93 = f32[2,4,256,128]{3,2,1,0:T(8,128)} fusion(f32[2,2048,256,4]{2,1,3,0:T(8,128)} %copy-done, f32[2,4,256]{2,1,0:T(4,128)S(1)} %max.13, pred[256,2048]{0,1:T(8,128)(4,1)S(1)} %broadcast_compare_fusion.3, bf16[4096,2,2,128]{0,3,2,1:T(8,128)(2,1)} %get-tuple-element.243, s32[]{:T(128)S(6)} %select_n.342, s32[]{:T(128)S(6)} %add.330, ...), kind=kOutput, calls=%fused_computation.14.clone.1 | convolution fusion | flops 1095237632 | bytes 20463624 | tf_op jit(solution)/shard_map/while/body/hgrk,khd->hgrd/dot_general | solution.py:62
  129.9 1.6 copy.42
  132.3 1.7 collective-permute-start.10
  134.0 54.0 %all-gather.5.cloned.1.call-done = bf16[2048,1024]{1,0:T(8,128)(2,1)} async-done(((bf16[2048,256]{1,0:T(8,128)(2,1)}), bf16[2048,1024]{1,0:T(8,128)(2,1)}) %all-gather.5.cloned.1.call-update) | async-done | bytes 4194320 | tf_op jit(solution)/shard_map/all_gather | solution.py:242
  188.0 2.4 %fusion.40 = f32[768,512]{1,0:T(8,128)S(1)} fusion(bf16[768,1024]{0,1:T(8,128)(2,1)S(1)} %constant_dynamic-update-slice_fusion.3, bf16[2048,1024]{1,0:T(8,128)(2,1)} %all-gather.5.cloned.1.call-done, s32[]{:T(128)S(6)} %add.241, s32[]{:T(128)S(6)} %select_n.197), kind=kOutput, calls=%fused_computation.66 | convolution fusion | flops 805306368 | bytes 4194312 | tf_op jit(solution)/shard_map/dot_general | solution.py:251
  190.4 2.4 %collective-permute-start.11 = (bf16[256,1024]{0,1:T(8,128)(2,1)S(1)}, bf16[256,1024]{0,1:T(8,128)(2,1)S(1)}, u32[]{:S(2)}, u32[]{:S(2)}) collective-permute-start(bf16[256,1024]{0,1:T(8,128)(2,1)S(1)} %bitcast.182), channel_id=1, source_target_pairs={{0,6},{2,0},{4,2},{6,4},{1,7},{3,1},{5,3},{7,5},{8,14},{10,8},{12,... | collective-permute-start | bytes 1572872 | tf_op jit(solution)/shard_map/ppermute | solution.py:228
  193.9 10.1 %collective-permute-done.11 = bf16[256,1024]{0,1:T(8,128)(2,1)S(1)} collective-permute-done((bf16[256,1024]{0,1:T(8,128)(2,1)S(1)}, bf16[256,1024]{0,1:T(8,128)(2,1)S(1)}, u32[]{:S(2)}, u32[]{:S(2)}) %collective-permute-start.11) | collective-permute-done | bytes 524320 | tf_op jit(solution)/shard_map/ppermute | solution.py:228
  204.1 1.0 add_convert_fusion.2
  205.7 1.5 fusion.29
  209.3 2.5 %collective-permute-start.16 = (bf16[256,512]{1,0:T(8,128)(2,1)S(1)}, bf16[256,512]{1,0:T(8,128)(2,1)S(1)}, u32[]{:S(2)}, u32[]{:S(2)}) collective-permute-start(bf16[256,512]{1,0:T(8,128)(2,1)S(1)} %get-tuple-element.133), channel_id=1, source_target_pairs={{0,2},{2,4},{4,6},{6,0},{1,3},{3,5},{5,7},{7,1},{8,10},{10,12},{12... | collective-permute-start | bytes 786440 | tf_op jit(solution)/shard_map/ppermute | solution.py:264
  211.8 1.5 collective-permute-start.17
  214.3 1.5 fusion.50
  215.9 4.1 %collective-permute-done.16 = bf16[256,512]{1,0:T(8,128)(2,1)S(1)} collective-permute-done((bf16[256,512]{1,0:T(8,128)(2,1)S(1)}, bf16[256,512]{1,0:T(8,128)(2,1)S(1)}, u32[]{:S(2)}, u32[]{:S(2)}) %collective-permute-start.16) | collective-permute-done | bytes 262176 | tf_op jit(solution)/shard_map/ppermute | solution.py:264
  219.9 4.9 %collective-permute-done.17 = bf16[256,512]{1,0:T(8,128)(2,1)S(1)} collective-permute-done((bf16[256,512]{1,0:T(8,128)(2,1)S(1)}, bf16[256,512]{1,0:T(8,128)(2,1)S(1)}, u32[]{:S(2)}, u32[]{:S(2)}) %collective-permute-start.17) | collective-permute-done | bytes 262176 | tf_op jit(solution)/shard_map/ppermute | solution.py:264
  226.9 1.4 copy.44
  228.3 1.6 reshape.371
  (120 shorter events, 25.4 us)
Async XLA Ops:
  6.5 4.6 %copy-start.10 = (s32[4]{0:T(128)S(1)}, s32[4]{0:T(128)}, u32[]{:S(2)}) copy-start(s32[4]{0:T(128)} %param.17) | copy-start | bytes 52
  6.5 100.9 %all-gather.3.cloned.1.call-start = ((), (), s32[]{:S(2)}) async-start(), calls=%async_computation | async-start | bytes 4456448 | tf_op jit(solution)/shard_map/all_gather | solution.py:199
  10.6 3.0 %collective-permute-start = (bf16[256,4,2,128]{0,3,1,2:T(8,128)(2,1)S(1)}, bf16[256,4,2,128]{0,3,1,2:T(8,128)(2,1)S(1)}, u32[]{:S(2)}, u32[]{:S(2)}) collective-permute-start(bf16[256,4,2,128]{0,3,1,2:T(8,128)(2,1)S(1)} %pad_maximum_fusion.5), channel_id=1, source_target_pairs={{0,1},{1,0},{2,3},{3,2},{4,5},{5,4},{6,7},{7,6},{8,9},{9,8},{10,11... | collective-permute-start | bytes 1572872 | tf_op jit(solution)/shard_map/ppermute | solution.py:139
  12.9 2.3 copy-start.7
  13.6 1.0 copy-start.6
  13.9 2.5 %copy-start.3 = (bf16[256,2048]{1,0:T(8,128)(2,1)S(1)}, bf16[256,2048]{1,0:T(8,128)(2,1)}, u32[]{:S(2)}) copy-start(bf16[256,2048]{1,0:T(8,128)(2,1)} %param.13) | copy-start | bytes 3145732
  16.2 171.9 %all-gather.5.cloned.1.call-start = ((), (), s32[]{:S(2)}) async-start(), calls=%async_computation.1 | async-start | bytes 5242880 | tf_op jit(solution)/shard_map/all_gather | solution.py:242
  19.1 1.2 copy-start.4
  19.7 26.1 %collective-permute-start.1 = (bf16[256,4,4,128]{3,0,2,1:T(8,128)(2,1)S(1)}, bf16[256,4,4,128]{3,0,2,1:T(8,128)(2,1)}, u32[]{:S(2)}, u32[]{:S(2)}) collective-permute-start(bf16[256,4,4,128]{3,0,2,1:T(8,128)(2,1)S(1)} %bitcast.188), channel_id=1, source_target_pairs={{0,1},{1,0},{2,3},{3,2},{4,5},{5,4},{6,7},{7,6},{8,9},{9,8},{10,11... | collective-permute-start | bytes 3145736 | tf_op jit(solution)/shard_map/ppermute | solution.py:139
  20.3 39.9 %collective-permute-start.2 = (bf16[4,512,256]{2,1,0:T(8,128)(2,1)S(1)}, bf16[4,512,256]{2,1,0:T(8,128)(2,1)}, u32[]{:S(2)}, u32[]{:S(2)}) collective-permute-start(bf16[4,512,256]{2,1,0:T(8,128)(2,1)S(1)} %bitcast.195), channel_id=1, source_target_pairs={{0,1},{1,0},{2,3},{3,2},{4,5},{5,4},{6,7},{7,6},{8,9},{9,8},{10,11... | collective-permute-start | bytes 3145736 | tf_op jit(solution)/shard_map/ppermute | solution.py:139
  23.5 8.4 %collective-permute-start.3 = (bf16[64,2,2,128]{3,0,1,2:T(8,128)(2,1)S(1)}, bf16[64,2,2,128]{3,0,1,2:T(8,128)(2,1)S(1)}, u32[]{:S(2)}, u32[]{:S(2)}) collective-permute-start(bf16[64,2,2,128]{3,0,1,2:T(8,128)(2,1)S(1)} %slice.87), channel_id=1, source_target_pairs={{0,2},{1,3}} | collective-permute-start | bytes 196616 | tf_op jit(solution)/shard_map/ppermute | solution.py:174
  31.8 3.2 %collective-permute-start.4 = (bf16[64,2,2,128]{3,0,1,2:T(8,128)(2,1)S(1)}, bf16[64,2,2,128]{3,0,1,2:T(8,128)(2,1)S(1)}, u32[]{:S(2)}, u32[]{:S(2)}) collective-permute-start(bf16[64,2,2,128]{3,0,1,2:T(8,128)(2,1)S(1)} %broadcast_select_fusion.1), channel_id=1, source_target_pairs={{0,4},{2,6},{1,5},{3,7}} | collective-permute-start | bytes 196616 | tf_op jit(solution)/shard_map/ppermute | solution.py:174
  35.0 5.7 %collective-permute-start.5 = (bf16[64,2,2,128]{3,0,1,2:T(8,128)(2,1)S(1)}, bf16[64,2,2,128]{3,0,1,2:T(8,128)(2,1)S(1)}, u32[]{:S(2)}, u32[]{:S(2)}) collective-permute-start(bf16[64,2,2,128]{3,0,1,2:T(8,128)(2,1)S(1)} %broadcast_select_fusion.2), channel_id=1, source_target_pairs={{0,8},{2,10},{4,12},{6,14},{1,9},{3,11},{5,13},{7,15}} | collective-permute-start | bytes 196616 | tf_op jit(solution)/shard_map/ppermute | solution.py:174
  36.3 8.6 %collective-permute-start.7 = (bf16[256,2,2,128]{3,0,1,2:T(8,128)(2,1)S(1)}, bf16[256,2,2,128]{3,0,1,2:T(8,128)(2,1)S(1)}, u32[]{:S(2)}, u32[]{:S(2)}) collective-permute-start(bf16[256,2,2,128]{3,0,1,2:T(8,128)(2,1)S(1)} %fusion.51), channel_id=1, source_target_pairs={{0,2},{2,4},{4,6},{6,8},{8,10},{10,12},{12,14},{14,16},{16,18},{18... | collective-permute-start | bytes 786440 | tf_op jit(solution)/shard_map/ppermute | solution.py:169
  40.8 3.2 %collective-permute-start.6 = (bf16[64,2,2,128]{3,0,1,2:T(8,128)(2,1)S(1)}, bf16[64,2,2,128]{3,0,1,2:T(8,128)(2,1)S(1)}, u32[]{:S(2)}, u32[]{:S(2)}) collective-permute-start(bf16[64,2,2,128]{3,0,1,2:T(8,128)(2,1)S(1)} %broadcast_select_fusion.3), channel_id=1, source_target_pairs={{0,16},{2,18},{4,20},{6,22},{8,24},{10,26},{12,28},{14,30},{1,17},... | collective-permute-start | bytes 196616 | tf_op jit(solution)/shard_map/ppermute | solution.py:174
  47.3 1.8 copy-start.9
  47.5 3.7 %copy-start.2 = (bf16[2,256,4,4,128]{4,1,3,2,0:T(8,128)(2,1)}, bf16[2,256,4,4,128]{4,1,3,2,0:T(8,128)(2,1)S(1)}, u32[]{:S(2)}) copy-start(bf16[2,256,4,4,128]{4,1,3,2,0:T(8,128)(2,1)S(1)} %pad_maximum_fusion) | copy-start | bytes 6291460
  51.1 1.2 copy-start.5
  54.4 18.3 %collective-permute-start.12 = (bf16[256,1024]{0,1:T(8,128)(2,1)}, bf16[256,1024]{0,1:T(8,128)(2,1)}, u32[]{:S(2)}, u32[]{:S(2)}) collective-permute-start(bf16[256,1024]{0,1:T(8,128)(2,1)} %bitcast.42), channel_id=1, source_target_pairs={{0,2},{2,4},{4,6},{6,0},{1,3},{3,5},{5,7},{7,1},{8,10},{10,12},{12... | collective-permute-start | bytes 1572872 | tf_op jit(solution)/shard_map/ppermute | solution.py:228
  56.9 33.0 %collective-permute-start.13 = (bf16[256,1024]{0,1:T(8,128)(2,1)}, bf16[256,1024]{0,1:T(8,128)(2,1)}, u32[]{:S(2)}, u32[]{:S(2)}) collective-permute-start(bf16[256,1024]{0,1:T(8,128)(2,1)} %bitcast.42), channel_id=1, source_target_pairs={{0,4},{2,6},{4,0},{6,2},{1,5},{3,7},{5,1},{7,3},{8,12},{10,14},{12... | collective-permute-start | bytes 1572872 | tf_op jit(solution)/shard_map/ppermute | solution.py:228
  59.3 31.6 %collective-permute-start.14 = (bf16[256,1024]{0,1:T(8,128)(2,1)}, bf16[256,1024]{0,1:T(8,128)(2,1)}, u32[]{:S(2)}, u32[]{:S(2)}) collective-permute-start(bf16[256,1024]{0,1:T(8,128)(2,1)} %bitcast.42), channel_id=1, source_target_pairs={{0,6},{2,0},{4,2},{6,4},{1,7},{3,1},{5,3},{7,5},{8,14},{10,8},{12,... | collective-permute-start | bytes 1572872 | tf_op jit(solution)/shard_map/ppermute | solution.py:228
  62.5 3.7 %copy-start.8 = (pred[2]{0:T(512)(128)(4,1)S(1)}, pred[2]{0:T(512)(128)(4,1)}, u32[]{:S(2)}) copy-start(pred[2]{0:T(512)(128)(4,1)} %copy-done.7) | copy-start | bytes 10
  113.3 6.4 %copy-start = (f32[2,2048,256,4]{2,1,3,0:T(8,128)}, f32[2,2048,256,4]{2,1,3,0:T(8,128)S(1)}, u32[]{:S(2)}) copy-start(f32[2,2048,256,4]{2,1,3,0:T(8,128)S(1)} %get-tuple-element.209) | copy-start | bytes 50331652 | tf_op jit(solution)/shard_map/while
  131.6 62.3 %collective-permute-start.9 = (bf16[256,1024]{0,1:T(8,128)(2,1)S(1)}, bf16[256,1024]{0,1:T(8,128)(2,1)S(1)}, u32[]{:S(2)}, u32[]{:S(2)}) collective-permute-start(bf16[256,1024]{0,1:T(8,128)(2,1)S(1)} %bitcast.180), channel_id=1, source_target_pairs={{0,2},{2,4},{4,6},{6,0},{1,3},{3,5},{5,7},{7,1},{8,10},{10,12},{12... | collective-permute-start | bytes 1572872 | tf_op jit(solution)/shard_map/ppermute | solution.py:228
  132.3 61.6 %collective-permute-start.10 = (bf16[256,1024]{0,1:T(8,128)(2,1)S(1)}, bf16[256,1024]{0,1:T(8,128)(2,1)S(1)}, u32[]{:S(2)}, u32[]{:S(2)}) collective-permute-start(bf16[256,1024]{0,1:T(8,128)(2,1)S(1)} %bitcast.181), channel_id=1, source_target_pairs={{0,4},{2,6},{4,0},{6,2},{1,5},{3,7},{5,1},{7,3},{8,12},{10,14},{12... | collective-permute-start | bytes 1572872 | tf_op jit(solution)/shard_map/ppermute | solution.py:228
  188.0 4.8 %copy-start.1 = (bf16[2048,1024]{1,0:T(8,128)(2,1)S(1)}, bf16[2048,1024]{1,0:T(8,128)(2,1)}, u32[]{:S(2)}) copy-start(bf16[2048,1024]{1,0:T(8,128)(2,1)} %all-gather.5.cloned.1.call-done) | copy-start | bytes 12582916
  190.4 13.7 %collective-permute-start.11 = (bf16[256,1024]{0,1:T(8,128)(2,1)S(1)}, bf16[256,1024]{0,1:T(8,128)(2,1)S(1)}, u32[]{:S(2)}, u32[]{:S(2)}) collective-permute-start(bf16[256,1024]{0,1:T(8,128)(2,1)S(1)} %bitcast.182), channel_id=1, source_target_pairs={{0,6},{2,0},{4,2},{6,4},{1,7},{3,1},{5,3},{7,5},{8,14},{10,8},{12,... | collective-permute-start | bytes 1572872 | tf_op jit(solution)/shard_map/ppermute | solution.py:228
  205.1 3.7 %collective-permute-start.15 = (bf16[768,512]{1,0:T(8,128)(2,1)S(1)}, bf16[768,512]{1,0:T(8,128)(2,1)S(1)}, u32[]{:S(2)}, u32[]{:S(2)}) collective-permute-start(bf16[768,512]{1,0:T(8,128)(2,1)S(1)} %add_convert_fusion.2), channel_id=1, source_target_pairs={{0,1},{1,0},{2,3},{3,2},{4,5},{5,4},{6,7},{7,6},{8,9},{9,8},{10,11... | collective-permute-start | bytes 2359304 | tf_op jit(solution)/shard_map/ppermute | solution.py:256
  207.2 7.1 %collective-permute-start.8 = (bf16[256,512]{1,0:T(8,128)(2,1)S(1)}, bf16[256,512]{1,0:T(8,128)(2,1)S(1)}, u32[]{:S(2)}, u32[]{:S(2)}) collective-permute-start(bf16[256,512]{1,0:T(8,128)(2,1)S(1)} %fusion.29), channel_id=1, source_target_pairs={{0,1},{1,0},{2,3},{3,2},{4,5},{5,4},{6,7},{7,6},{8,9},{9,8},{10,11... | collective-permute-start | bytes 786440 | tf_op jit(solution)/shard_map/ppermute | solution.py:256
  209.3 10.6 %collective-permute-start.16 = (bf16[256,512]{1,0:T(8,128)(2,1)S(1)}, bf16[256,512]{1,0:T(8,128)(2,1)S(1)}, u32[]{:S(2)}, u32[]{:S(2)}) collective-permute-start(bf16[256,512]{1,0:T(8,128)(2,1)S(1)} %get-tuple-element.133), channel_id=1, source_target_pairs={{0,2},{2,4},{4,6},{6,0},{1,3},{3,5},{5,7},{7,1},{8,10},{10,12},{12... | collective-permute-start | bytes 786440 | tf_op jit(solution)/shard_map/ppermute | solution.py:264
  211.8 13.0 %collective-permute-start.17 = (bf16[256,512]{1,0:T(8,128)(2,1)S(1)}, bf16[256,512]{1,0:T(8,128)(2,1)S(1)}, u32[]{:S(2)}, u32[]{:S(2)}) collective-permute-start(bf16[256,512]{1,0:T(8,128)(2,1)S(1)} %get-tuple-element.135), channel_id=1, source_target_pairs={{0,4},{2,6},{4,0},{6,2},{1,5},{3,7},{5,1},{7,3},{8,12},{10,14},{12... | collective-permute-start | bytes 786440 | tf_op jit(solution)/shard_map/ppermute | solution.py:264
  213.3 11.6 %collective-permute-start.18 = (bf16[256,512]{1,0:T(8,128)(2,1)S(1)}, bf16[256,512]{1,0:T(8,128)(2,1)S(1)}, u32[]{:S(2)}, u32[]{:S(2)}) collective-permute-start(bf16[256,512]{1,0:T(8,128)(2,1)S(1)} %get-tuple-element.134), channel_id=1, source_target_pairs={{0,6},{2,0},{4,2},{6,4},{1,7},{3,1},{5,3},{7,5},{8,14},{10,8},{12,... | collective-permute-start | bytes 786440 | tf_op jit(solution)/shard_map/ppermute | solution.py:264
Sparse Core Ops, SparseCore 0:
  16.3 91.1 all-gather.2
  109.0 78.9 all-gather.4
